TPU v7x, 256 devices: a whole 4x4x8 slice. The times are simulated.
256 devices in a mesh: seq: 32 (over z, y), dp: 8 (over x, core).
Axes of the slice: x: 4, y: 4, z: 8, core: 2. Of those that a mesh axis runs over, the one named last changes fastest.
Arguments:
- queries: bfloat16 [8, 12288, 2048], P('dp', 'seq'), may hold values from -0.59765625 to 0.59765625
- keys: bfloat16 [8, 12288, 2048], P('dp', 'seq'), may hold values from -0.59765625 to 0.59765625
- values: bfloat16 [8, 12288, 2048], P('dp', 'seq'), may hold values from -6 to 6
- output_gradient: bfloat16 [8, 12288, 2048], P('dp', 'seq'), may hold values from -0.59765625 to 0.59765625
- document_lengths: int32 [8, 8], P('dp'), may hold values from 1 to 3072, 12288 in all within a row
- cutoff_rows: int32 [8, 12288], P('dp', 'seq'), may hold values 0 or 1
- head_decay_rate: float32 [16], replicated, may hold values from 4.06901042e-06 to 0.04, as said below
Outputs:
- query_grad: bfloat16 [8, 12288, 2048], P('dp', 'seq')
- key_grad: bfloat16 [8, 12288, 2048], P('dp', 'seq')
- value_grad: bfloat16 [8, 12288, 2048], P('dp', 'seq')
- rate_grad: float32 [16], replicated
Inputs may be any that keep to these rules, and one draw needn't show every extreme that they name: `head_decay_rate`: a positive rate for each head.
All inputs are finite; a program needn't handle non-finite values. No bound on the sum of `cutoff_rows` on one device may be relied on, other than what follows from the above.
Results may differ from a plain program's by a relative error of at most 0.0034.
Values sent between devices are 32-bit elements; how exact they have to be, the bound alone decides.
No kernel may reach another device: no remote copies, remote signals or barrier semaphores. Data moves between devices by JAX's collectives and lax.ppermute only.
A program may use at most 192 MiB of HBM per device.

v0:
```python
import math

import jax
import jax.numpy as jnp
from jax import lax
from jax.sharding import PartitionSpec as P

HEADS = 16
HEAD_DIM = 128


cutoff_logarithm = math.log(0.7)
state_mode = lax.Precision.HIGH


def carried_in(part, axis, combine, identity, reverse):
    count = lax.axis_size(axis)
    place = lax.axis_index(axis)
    ahead = count - 1 - place if reverse else place
    gathered = jax.tree.map(lambda a: lax.all_gather(a, axis), part)
    state = jax.tree.map(lambda a, e: jnp.zeros_like(a) + jnp.asarray(e, a.dtype), part, identity)

    def one(step, state):
        source = count - 1 - step if reverse else step
        return combine(
            state, jax.tree.map(lambda a: lax.dynamic_index_in_dim(a, source, 0, False), gathered)
        )

    return lax.fori_loop(0, ahead, one, state)


def block_mask_list(head_decay_rate, cutoff_list, row_position, start_list):
    is_start = jnp.any(row_position[:, None] == start_list[None, :], axis=1)
    seg_local = jnp.cumsum(is_start.astype(jnp.int32))
    begin = jnp.max(
        jnp.where(start_list[None, :] <= row_position[:, None], start_list[None, :], 0), axis=1
    )
    position = (row_position - begin).astype(jnp.float32)
    logarithm_step = (
        cutoff_list.astype(jnp.float32)[:, None] * cutoff_logarithm - head_decay_rate[None, :]
    )
    cum_log = jnp.cumsum(logarithm_step, axis=0)
    carry_in = jnp.where((seg_local == 0)[:, None], jnp.exp(cum_log), 0.0)
    carry_out = jnp.where(
        (seg_local == seg_local[-1])[:, None], jnp.exp(cum_log[-1][None, :] - cum_log), 0.0
    )
    decay_all = jnp.where(seg_local[-1] == 0, jnp.exp(cum_log[-1]), 0.0)
    return (cum_log, seg_local, position, carry_in, carry_out, decay_all)


def weights_of(cum_log, seg_local):
    count = seg_local.shape[0]
    index = jnp.arange(count, dtype=jnp.int32)
    allowed = (seg_local[:, None] == seg_local[None, :]) & (index[:, None] >= index[None, :])
    spread = cum_log.T[:, :, None] - cum_log.T[:, None, :]
    return jnp.where(allowed[None], jnp.exp(jnp.where(allowed[None], spread, 0.0)), 0.0)


def forward_combine(earlier, later):
    return (earlier[0] * later[0], later[0][:, None, None] * earlier[1] + later[1])


def backward_combine(earlier, later):
    return (later[0] * earlier[0], later[1] + later[0][:, None, None] * earlier[1])


def on_device(
    queries, keys, values, output_gradient, document_lengths, cutoff_rows, head_decay_rate
):
    row_count = queries.shape[1]
    query_block = queries.reshape(row_count, HEADS, HEAD_DIM)
    key_block = keys.reshape(row_count, HEADS, HEAD_DIM)
    value_block = values.reshape(row_count, HEADS, HEAD_DIM)
    gradient_block = output_gradient.reshape(row_count, HEADS, HEAD_DIM)
    block_piece = lax.axis_index("seq")
    row_position = block_piece * row_count + jnp.arange(row_count, dtype=jnp.int32)
    length_list = document_lengths[0]
    start_list = jnp.cumsum(length_list) - length_list
    cum_log, seg_local, position, carry_in, carry_out, decay_all = block_mask_list(
        head_decay_rate, cutoff_rows[0], row_position, start_list
    )
    key_f = key_block.astype(jnp.float32)
    value_f = value_block.astype(jnp.float32)
    grad_f = gradient_block.astype(jnp.float32)
    query_f = query_block.astype(jnp.float32)
    state_local = jnp.einsum(
        "the,thf->hef", carry_out[:, :, None] * key_f, value_f, precision=state_mode
    )
    back_local = jnp.einsum(
        "she,shf->hef", carry_in[:, :, None] * query_f, grad_f, precision=state_mode
    )
    identity = (jnp.ones_like(decay_all), jnp.zeros_like(state_local))
    state_input = carried_in((decay_all, state_local), "seq", forward_combine, identity, False)[1]
    backward_input = carried_in((decay_all, back_local), "seq", backward_combine, identity, True)[1]
    weight = weights_of(cum_log, seg_local)
    scores = jnp.einsum("she,the->hst", query_block, key_block, preferred_element_type=jnp.float32)
    grad_scores = jnp.einsum(
        "shf,thf->hst", gradient_block, value_block, preferred_element_type=jnp.float32
    )
    attn_prob = (weight * scores).astype(jnp.bfloat16)
    grad_prob = (weight * grad_scores).astype(jnp.bfloat16)
    value_full = jnp.einsum(
        "hst,shf->thf", attn_prob, gradient_block, preferred_element_type=jnp.float32
    )
    value_full = value_full + carry_out[:, :, None] * jnp.einsum(
        "the,hef->thf", key_f, backward_input, precision=state_mode
    )
    query_full = jnp.einsum(
        "hst,the->she", grad_prob, key_block, preferred_element_type=jnp.float32
    )
    query_full = query_full + carry_in[:, :, None] * jnp.einsum(
        "shf,hef->she", grad_f, state_input, precision=state_mode
    )
    key_full = jnp.einsum(
        "hst,she->the", grad_prob, query_block, preferred_element_type=jnp.float32
    )
    key_full = key_full + carry_out[:, :, None] * jnp.einsum(
        "thf,hef->the", value_f, backward_input, precision=state_mode
    )
    inner_step = jnp.sum(key_f * key_full, axis=2) - jnp.sum(query_f * query_full, axis=2)
    rate_part = jnp.sum(position[:, None] * inner_step, axis=0)
    rate_total = lax.psum(rate_part, ("seq", "dp"))
    token_total = row_count * lax.axis_size("seq") * lax.axis_size("dp")
    rate_grad = head_decay_rate * rate_total / math.sqrt(token_total)
    out_shape = (1, row_count, HEADS * HEAD_DIM)
    return (
        query_full.astype(jnp.bfloat16).reshape(out_shape),
        key_full.astype(jnp.bfloat16).reshape(out_shape),
        value_full.astype(jnp.bfloat16).reshape(out_shape),
        rate_grad,
    )


def solution(mesh):
    in_specs = (
        P("dp", "seq", None),
        P("dp", "seq", None),
        P("dp", "seq", None),
        P("dp", "seq", None),
        P("dp", None),
        P("dp", "seq"),
        P(),
    )
    out_specs = (P("dp", "seq", None), P("dp", "seq", None), P("dp", "seq", None), P())
    return jax.shard_map(
        on_device, mesh=mesh, in_specs=in_specs, out_specs=out_specs, check_vma=False
    )
```

profile of v0, /device:TPU:6, one launch (start us, length us, event | category | flops | bytes accessed | tf_op | source)
XLA Modules:
  0.0 645.0 jit_solution(15343796747295576941)
XLA Ops:
  7.2 0.8 reduce-window_clone.1
  8.0 0.7 subtract_bitcast_fusion
  8.8 0.3 reduce-window.16
  9.4 0.6 slice.25
  10.7 0.7 broadcast_compare_fusion
  11.3 0.7 multiply_reduce_fusion.1
  12.0 0.7 broadcast_subtract_fusion
  12.7 0.9 reduce-window.24
  13.9 1.9 copy.84
  15.8 2.4 copy.99
  18.2 0.2 slice_reduce_fusion.1
  18.5 2.4 fusion.9
  21.0 1.9 copy.81
  22.8 1.8 copy.101
  24.7 1.1 copy-done.3
  25.8 2.4 fusion.7
  28.2 42.1 %all-gather.2 = f32[32,1,16]{2,1,0:T(1,128)S(1)} all-gather(f32[1,1,16]{2,1,0:T(1,128)S(1)} %bitcast.115), channel_id=1, replica_groups=mesh['seq'=32,'dp'=8] {'seq'}, dimensions={0}, use_global_device_ids=true | all-gather | bytes 2112 | tf_op jit(solution)/shard_map/all_gather | solution.py:20
  70.6 6.9 %multiply_convert_fusion.1 = bf16[16,384,384]{2,1,0:T(8,128)(2,1)} fusion(f32[16,384]{1,0:T(8,128)S(1)} %get-tuple-element.184, pred[384,384]{1,0:T(8,128)(4,1)S(1)} %fusion.21, bf16[384,16,128]{0,2,1:T(8,128)(2,1)S(1)} %bitcast.99, bf16[384,16,128]{2,1,0:T(8,128)(2,1)} %bitcast.103), kind=kOutput, calls=%fused_computation.5 | convolution fusion | flops 615776256 | bytes 8036352 | tf_op jit(solution)/shard_map/shf,thf->hst/dot_general | solution.py:97
  77.5 179.8 %all-gather.8.cloned.1.call-done = f32[512,128,128]{2,1,0:T(8,128)} async-done(((f32[16,128,128]{2,1,0:T(8,128)}), f32[512,128,128]{2,1,0:T(8,128)}) %all-gather.8.cloned.1.call-update) | async-done | bytes 33554448 | tf_op jit(solution)/shard_map/all_gather | solution.py:20
  257.4 47.1 %while.27 = (s32[]{:T(128)}, f32[16,128,128]{2,1,0:T(8,128)S(1)}, s32[]{:T(128)}, f32[32,16,128,128]{3,2,1,0:T(8,128)}, f32[32,16]{1,0:T(8,128)S(1)}, /*index=5*/s32[]{:T(128)}, s32[]{:T(128)}, s32[]{:T(128)}, s32[]{:T(128)}) while((s32[]{:T(128)}, f32[16,128,128]{2,1,0:T(8,128)S(1)}, s32[]{:T(128)}, f32[32,16,128,128]{3,2,1,0:T(8,128)}, ...), condition=%wide.region_9.10_spmd, body=%wide.region_8.9_spmd.sunk | while | flops 524294 | bytes 3146075 | solution.py:29
  257.4 1.4 bitcast_add_fusion.5
  258.9 1.4 bitcast_add_fusion.5
  260.4 1.4 bitcast_add_fusion.5
  261.9 1.4 bitcast_add_fusion.5
  263.4 1.4 bitcast_add_fusion.5
  264.9 1.4 bitcast_add_fusion.5
  266.4 1.5 bitcast_add_fusion.5
  267.9 1.6 bitcast_add_fusion.5
  269.5 1.6 bitcast_add_fusion.5
  271.1 1.7 bitcast_add_fusion.5
  272.8 1.4 bitcast_add_fusion.5
  274.3 1.4 bitcast_add_fusion.5
  275.8 1.5 bitcast_add_fusion.5
  277.3 1.5 bitcast_add_fusion.5
  278.9 1.5 bitcast_add_fusion.5
  280.4 1.5 bitcast_add_fusion.5
  281.9 1.4 bitcast_add_fusion.5
  283.4 1.4 bitcast_add_fusion.5
  284.9 1.4 bitcast_add_fusion.5
  286.4 1.4 bitcast_add_fusion.5
  287.9 1.4 bitcast_add_fusion.5
  289.4 1.5 bitcast_add_fusion.5
  290.9 1.5 bitcast_add_fusion.5
  292.4 1.5 bitcast_add_fusion.5
  293.9 1.5 bitcast_add_fusion.5
  295.5 1.5 bitcast_add_fusion.5
  297.0 1.5 bitcast_add_fusion.5
  298.5 1.5 bitcast_add_fusion.5
  300.0 1.5 bitcast_add_fusion.5
  301.5 1.4 bitcast_add_fusion.5
  303.0 1.4 bitcast_add_fusion.5
  304.5 4.5 fusion.17
  309.0 2.7 fusion.25
  311.6 178.6 %all-gather.6.cloned.1.call-done = f32[512,128,128]{2,1,0:T(8,128)} async-done(((f32[16,128,128]{2,1,0:T(8,128)}), f32[512,128,128]{2,1,0:T(8,128)}) %all-gather.6.cloned.1.call-update) | async-done | bytes 33554448 | tf_op jit(solution)/shard_map/all_gather | solution.py:20
  490.3 0.2 while.26
  490.5 4.1 fusion.24
  494.6 8.2 %fusion.12 = bf16[384,16,128]{0,2,1:T(8,128)(2,1)} fusion(f32[16,128,384]{2,1,0:T(8,128)} %fusion.25, bf16[384,16,128]{0,2,1:T(8,128)(2,1)} %bitcast.101, f32[16,384]{1,0:T(8,128)S(1)} %get-tuple-element.184, pred[384,384]{1,0:T(8,128)(4,1)S(1)} %fusion.21, bf16[384,16,128]{0,2,1:T(8,128)(2,1)} %bitcast.95, bf16[384,16,128]{0,2,1:T(8,128)(2,1)S(1)} %bitcast.91, ...), kind=kOutput, calls=%fused_computation.23 | convolution fusion | flops 1222115328 | bytes 9633792 | tf_op jit(solution)/shard_map/hst,shf->thf/dot_general | solution.py:102
  502.8 2.7 copy.94
  505.5 5.9 fusion.8
  511.4 5.1 fusion.10
  516.6 2.7 copy.92
  519.3 116.7 %psum.7 = f32[16]{0:T(128)S(1)} all-reduce(f32[16]{0:T(128)S(1)} %multiply_reduce_fusion), channel_id=1, replica_groups=mesh['seq'=32,'dp'=8] {'seq','dp'}, use_global_device_ids=true, to_apply=%region_14.15 | all-reduce | flops 16 | bytes 128 | tf_op jit(solution)/shard_map/psum | solution.py:122
  636.0 0.5 multiply_multiply_fusion
  636.6 1.6 copy.93
  (65 shorter events, 1.8 us)
Async XLA Ops:
  7.2 250.1 %all-gather.8.cloned.1.call-start = ((), (), s32[]{:S(2)}) async-start(), calls=%async_computation.1 | async-start | bytes 34603008 | tf_op jit(solution)/shard_map/all_gather | solution.py:20
  15.8 5.1 copy-start
  18.2 52.4 %copy-start.2 = (bf16[1,384,2048]{1,2,0:T(8,128)(2,1)}, bf16[1,384,2048]{1,2,0:T(8,128)(2,1)S(1)}, u32[]{:S(2)}) copy-start(bf16[1,384,2048]{1,2,0:T(8,128)(2,1)S(1)} %copy.99) | copy-start | bytes 4718596
  20.9 469.3 %all-gather.6.cloned.1.call-start = ((), (), s32[]{:S(2)}) async-start(), calls=%async_computation | async-start | bytes 34603008 | tf_op jit(solution)/shard_map/all_gather | solution.py:20
  24.7 1.1 copy-start.3
  502.8 2.7 copy-start.1
  505.5 5.9 copy-start.4
  516.5 119.5 %copy-start.6 = (f32[16]{0:T(128)S(1)}, f32[16]{0:T(128)}, u32[]{:S(2)}) copy-start(f32[16]{0:T(128)} %param.17) | copy-start | bytes 196
  516.5 120.0 %copy-start.5 = (bf16[384,16,128]{0,2,1:T(8,128)(2,1)S(1)}, bf16[384,16,128]{0,2,1:T(8,128)(2,1)}, u32[]{:S(2)}) copy-start(bf16[384,16,128]{0,2,1:T(8,128)(2,1)} %get-tuple-element.181) | copy-start | bytes 4718596
Sparse Core Ops, SparseCore 0:
  21.0 236.1 all-gather.7
  259.8 230.3 all-gather.5
where the time goes:
time: 649 us; the launch traced here: 645 us
  waiting for transfers between devices  358 us (55%)
  blocking collectives  159 us (24%)
  other arithmetic  51.8 us (8%)
  matrix products  42 us (6%)
  local copies, waits for them, and re-layouts  17.7 us (3%)
  between operations  14.8 us (2%)
    all_gather x2, waiting for transfers between devices, carried_in(): gathered = jax.tree.map(lambda a: lax.all_gather(a, axis), part)  358 us
    psum x1, blocking collectives, on_device(): rate_total = lax.psum(rate_part, ('seq', 'dp'))  117 us
    add x31, other arithmetic, backward_combine(): later[1] + later[0][:, None, None] * earlier[1]  45.6 us
    all_gather x1, blocking collectives, carried_in(): gathered = jax.tree.map(lambda a: lax.all_gather(a, axis), part)  42.1 us
    unnamed x20, local copies, waits for them, and re-layouts  13.7 us
  transfers between devices with their start and end apart: 2, of which 2 were waited for; matrix products, arithmetic and copies ran while one was open for 10% of the time, Pallas kernels for 0%

commit v1 on v0

--- a/solution.py
+++ b/solution.py
@@ -13,20 +13,31 @@
 state_mode = lax.Precision.HIGH
 
 
-def carried_in(part, axis, combine, identity, reverse):
+def carried_both(decay, forward_part, backward_part, axis):
     count = lax.axis_size(axis)
-    place = lax.axis_index(axis)
-    ahead = count - 1 - place if reverse else place
-    gathered = jax.tree.map(lambda a: lax.all_gather(a, axis), part)
-    state = jax.tree.map(lambda a, e: jnp.zeros_like(a) + jnp.asarray(e, a.dtype), part, identity)
-
-    def one(step, state):
-        source = count - 1 - step if reverse else step
-        return combine(
-            state, jax.tree.map(lambda a: lax.dynamic_index_in_dim(a, source, 0, False), gathered)
-        )
-
-    return lax.fori_loop(0, ahead, one, state)
+    ones = jnp.ones_like(decay)
+    zeros = jnp.zeros_like(forward_part)
+    fwd_decay, fwd_state = decay, forward_part
+    bwd_decay, bwd_state = decay, backward_part
+    excl_decay, excl_state = ones, zeros
+    rexcl_decay, rexcl_state = ones, zeros
+    shift = 1
+    while shift < count:
+        up = [(i, i + shift) for i in range(count - shift)]
+        down = [(i + shift, i) for i in range(count - shift)]
+        got_decay, got_state = lax.ppermute((fwd_decay, fwd_state), axis, up)
+        rgot_decay, rgot_state = lax.ppermute((bwd_decay, bwd_state), axis, down)
+        excl_state = excl_decay[:, None, None] * got_state + excl_state
+        excl_decay = got_decay * excl_decay
+        rexcl_state = rexcl_state + rexcl_decay[:, None, None] * rgot_state
+        rexcl_decay = rexcl_decay * rgot_decay
+        if 2 * shift < count:
+            fwd_state = fwd_decay[:, None, None] * got_state + fwd_state
+            fwd_decay = got_decay * fwd_decay
+            bwd_state = bwd_state + bwd_decay[:, None, None] * rgot_state
+            bwd_decay = bwd_decay * rgot_decay
+        shift *= 2
+    return excl_state, rexcl_state
 
 
 def block_mask_list(head_decay_rate, cutoff_list, row_position, start_list):
@@ -56,14 +67,6 @@
     return jnp.where(allowed[None], jnp.exp(jnp.where(allowed[None], spread, 0.0)), 0.0)
 
 
-def forward_combine(earlier, later):
-    return (earlier[0] * later[0], later[0][:, None, None] * earlier[1] + later[1])
-
-
-def backward_combine(earlier, later):
-    return (later[0] * earlier[0], later[1] + later[0][:, None, None] * earlier[1])
-
-
 def on_device(
     queries, keys, values, output_gradient, document_lengths, cutoff_rows, head_decay_rate
 ):
@@ -89,9 +92,7 @@
     back_local = jnp.einsum(
         "she,shf->hef", carry_in[:, :, None] * query_f, grad_f, precision=state_mode
     )
-    identity = (jnp.ones_like(decay_all), jnp.zeros_like(state_local))
-    state_input = carried_in((decay_all, state_local), "seq", forward_combine, identity, False)[1]
-    backward_input = carried_in((decay_all, back_local), "seq", backward_combine, identity, True)[1]
+    state_input, backward_input = carried_both(decay_all, state_local, back_local, "seq")
     weight = weights_of(cum_log, seg_local)
     scores = jnp.einsum("she,the->hst", query_block, key_block, preferred_element_type=jnp.float32)
     grad_scores = jnp.einsum(

time: 649 us -> 396 us (0.61)
  waiting for transfers between devices: 358 us -> 127 us
  starting transfers between devices: 0.08 us -> 110 us
  blocking collectives: 159 us -> 99.3 us
  other arithmetic: 51.8 us -> 11.4 us
  between operations: 14.8 us -> 1.77 us
  matrix products: 42 us -> 30 us
    all_gather x2 -> x0, waiting for transfers between devices: 358 us -> none  [carried_in(): gathered = jax.tree.map(lambda a: lax.all_gather(a, axis), part)]
    ppermute x0 -> x18, waiting for transfers between devices: none -> 127 us  [the longest x9 65.3 us: carried_both(): got_decay, got_state = lax.ppermute((fwd_decay, fwd_state), axis, up)]
    ppermute x0 -> x18, starting transfers between devices: none -> 110 us  [the longest x9 97.9 us: carried_both(): got_decay, got_state = lax.ppermute((fwd_decay, fwd_state), axis, up)]
    all_gather x1 -> x0, blocking collectives: 42.1 us -> none  [carried_in(): gathered = jax.tree.map(lambda a: lax.all_gather(a, axis), part)]
    add x31 -> x8, other arithmetic: 45.6 us -> 5.39 us  [the longest x4 3.23 us: carried_both(): bwd_state = bwd_state + bwd_decay[:, None, None] * rgot_state]
    psum x1, blocking collectives: 117 us -> 99.3 us  [on_device(): rate_total = lax.psum(rate_part, ('seq', 'dp'))]
  transfers between devices with their start and end apart: 2 -> 18, of which waited for: 2 -> 7; matrix products, arithmetic and copies ran while one was open for 10% -> 5% of each run, Pallas kernels for 0% -> 0%
where the time goes in v1:
time: 396 us; the launch traced here: 393 us
  waiting for transfers between devices  127 us (32%)
  starting transfers between devices  110 us (28%)
  blocking collectives  99.3 us (25%)
  matrix products  30 us (8%)
  local copies, waits for them, and re-layouts  14.2 us (4%)
  other arithmetic  11.4 us (3%)
    psum x1, blocking collectives, on_device(): rate_total = lax.psum(rate_part, ('seq', 'dp'))  99.3 us
    ppermute x9, starting transfers between devices, carried_both(): got_decay, got_state = lax.ppermute((fwd_decay, fwd_state), axis, up)  97.9 us
    ppermute x9, waiting for transfers between devices, carried_both(): got_decay, got_state = lax.ppermute((fwd_decay, fwd_state), axis, up)  65.3 us
    ppermute x9, waiting for transfers between devices, carried_both(): rgot_decay, rgot_state = lax.ppermute((bwd_decay, bwd_state), axis, down)  61.6 us
    ppermute x9, starting transfers between devices, carried_both(): rgot_decay, rgot_state = lax.ppermute((bwd_decay, bwd_state), axis, down)  11.8 us
    unnamed x20, local copies, waits for them, and re-layouts  10.5 us
  transfers between devices with their start and end apart: 18, of which 7 were waited for; matrix products, arithmetic and copies ran while one was open for 5% of the time, Pallas kernels for 0%

profile of v1, /device:TPU:6, one launch (start us, length us, event | category | flops | bytes accessed | tf_op | source)
XLA Modules:
  0.0 393.3 jit_solution(1536534105192003341)
XLA Ops:
  0.6 0.8 reduce-window_clone.1
  1.5 0.7 subtract_bitcast_fusion
  2.2 0.3 reduce-window.16
  2.7 0.1 slice_reduce_fusion.2
  2.9 0.6 slice.25
  3.4 0.6 broadcast_compare_fusion
  4.1 0.7 multiply_reduce_fusion.1
  4.8 0.7 broadcast_subtract_fusion
  5.5 0.9 reduce-window.24
  6.4 0.2 slice_reduce_fusion
  6.6 0.2 slice_reduce_fusion.1
  6.8 1.9 copy.81
  8.7 1.8 copy.101
  10.7 2.4 fusion.7
  13.0 4.5 %collective-permute-start.4 = (f32[16,128,128]{2,1,0:T(8,128)}, f32[16,128,128]{2,1,0:T(8,128)}, u32[]{:S(2)}, u32[]{:S(2)}) collective-permute-start(f32[16,128,128]{2,1,0:T(8,128)} %fusion.7), channel_id=1, source_target_pairs={{0,8},{8,16},{16,24},{24,32},{32,40},{40,48},{48,56},{56,64},{64,7... | collective-permute-start | bytes 3145736 | tf_op jit(solution)/shard_map/ppermute | solution.py:28
  17.5 2.6 copy.99
  20.1 1.9 copy.84
  21.9 3.8 fusion.9
  25.8 1.3 collective-permute-start.9
  27.7 11.5 %collective-permute-done.4 = f32[16,128,128]{2,1,0:T(8,128)} collective-permute-done((f32[16,128,128]{2,1,0:T(8,128)}, f32[16,128,128]{2,1,0:T(8,128)}, u32[]{:S(2)}, u32[]{:S(2)}) %collective-permute-start.4) | collective-permute-done | bytes 1048608 | tf_op jit(solution)/shard_map/ppermute | solution.py:28
  39.2 13.4 %collective-permute-done.9 = f32[16,128,128]{2,1,0:T(8,128)} collective-permute-done((f32[16,128,128]{2,1,0:T(8,128)}, f32[16,128,128]{2,1,0:T(8,128)}, u32[]{:S(2)}, u32[]{:S(2)}) %collective-permute-start.9) | collective-permute-done | bytes 1048608 | tf_op jit(solution)/shard_map/ppermute | solution.py:29
  52.6 2.7 multiply_add_fusion.4
  55.3 1.3 collective-permute-start.11
  56.6 6.1 %collective-permute-start.5 = (f32[16,128,128]{2,1,0:T(8,128)S(1)}, f32[16,128,128]{2,1,0:T(8,128)S(1)}, u32[]{:S(2)}, u32[]{:S(2)}) collective-permute-start(f32[16,128,128]{2,1,0:T(8,128)S(1)} %get-tuple-element.43), channel_id=1, source_target_pairs={{0,16},{8,24},{16,32},{24,40},{32,48},{40,56},{48,64},{56,72},{64,... | collective-permute-start | bytes 3145736 | tf_op jit(solution)/shard_map/ppermute | solution.py:28
  62.8 3.4 collective-permute-start
  66.1 1.3 collective-permute-start.10
  67.4 36.3 %collective-permute-done = f32[16]{0:T(128)S(1)} collective-permute-done((f32[16]{0:T(128)S(1)}, f32[16]{0:T(128)S(1)}, u32[]{:S(2)}, u32[]{:S(2)}) %collective-permute-start) | collective-permute-done | bytes 96 | tf_op jit(solution)/shard_map/ppermute | solution.py:28
  103.8 3.5 collective-permute-done.10
  107.3 0.2 multiply_add_fusion.3
  107.4 1.3 collective-permute-start.13
  108.7 0.1 fusion.28
  108.9 1.3 collective-permute-start.12
  110.2 0.2 multiply_add_fusion.7
  110.4 5.4 %collective-permute-start.6 = (f32[16,128,128]{2,1,0:T(8,128)S(1)}, f32[16,128,128]{2,1,0:T(8,128)S(1)}, u32[]{:S(2)}, u32[]{:S(2)}) collective-permute-start(f32[16,128,128]{2,1,0:T(8,128)S(1)} %multiply_add_fusion.7), channel_id=1, source_target_pairs={{0,32},{8,40},{16,48},{24,56},{32,64},{40,72},{48,80},{56,88},{64,... | collective-permute-start | bytes 3145736 | tf_op jit(solution)/shard_map/ppermute | solution.py:28
  115.8 3.7 multiply_convert_fusion.1
  119.6 14.7 %collective-permute-done.13 = f32[16,128,128]{2,1,0:T(8,128)S(1)} collective-permute-done((f32[16,128,128]{2,1,0:T(8,128)S(1)}, f32[16,128,128]{2,1,0:T(8,128)S(1)}, u32[]{:S(2)}, u32[]{:S(2)}) %collective-permute-start.13) | collective-permute-done | bytes 1048608 | tf_op jit(solution)/shard_map/ppermute | solution.py:29
  134.3 0.2 multiply_add_fusion.2
  134.5 1.3 collective-permute-start.15
  135.8 1.2 fusion.39
  137.0 4.9 %collective-permute-start.1 = (f32[16]{0:T(128)S(1)}, f32[16]{0:T(128)S(1)}, u32[]{:S(2)}, u32[]{:S(2)}) collective-permute-start(f32[16]{0:T(128)S(1)} %get-tuple-element.41), channel_id=1, source_target_pairs={{0,16},{8,24},{16,32},{24,40},{32,48},{40,56},{48,64},{56,72},{64,... | collective-permute-start | bytes 200 | tf_op jit(solution)/shard_map/ppermute | solution.py:28
  141.9 1.3 collective-permute-start.14
  143.2 0.2 multiply_add_fusion.6
  143.4 10.8 %collective-permute-start.7 = (f32[16,128,128]{2,1,0:T(8,128)S(1)}, f32[16,128,128]{2,1,0:T(8,128)S(1)}, u32[]{:S(2)}, u32[]{:S(2)}) collective-permute-start(f32[16,128,128]{2,1,0:T(8,128)S(1)} %multiply_add_fusion.6), channel_id=1, source_target_pairs={{0,64},{8,72},{16,80},{24,88},{32,96},{40,104},{48,112},{56,120},{... | collective-permute-start | bytes 3145736 | tf_op jit(solution)/shard_map/ppermute | solution.py:28
  154.2 1.6 fusion.38
  155.7 30.0 %collective-permute-done.15 = f32[16,128,128]{2,1,0:T(8,128)S(1)} collective-permute-done((f32[16,128,128]{2,1,0:T(8,128)S(1)}, f32[16,128,128]{2,1,0:T(8,128)S(1)}, u32[]{:S(2)}, u32[]{:S(2)}) %collective-permute-start.15) | collective-permute-done | bytes 1048608 | tf_op jit(solution)/shard_map/ppermute | solution.py:29
  185.7 0.2 multiply_add_fusion.1
  185.9 1.5 collective-permute-start.17
  187.5 6.6 %collective-permute-start.2 = (f32[16]{0:T(128)S(1)}, f32[16]{0:T(128)S(1)}, u32[]{:S(2)}, u32[]{:S(2)}) collective-permute-start(f32[16]{0:T(128)S(1)} %mul.243), channel_id=1, source_target_pairs={{0,32},{8,40},{16,48},{24,56},{32,64},{40,72},{48,80},{56,88},{64,... | collective-permute-start | bytes 200 | tf_op jit(solution)/shard_map/ppermute | solution.py:28
  194.0 1.3 collective-permute-start.16
  195.4 8.5 %collective-permute-start.3 = (f32[16]{0:T(128)S(1)}, f32[16]{0:T(128)S(1)}, u32[]{:S(2)}, u32[]{:S(2)}) collective-permute-start(f32[16]{0:T(128)S(1)} %mul.244), channel_id=1, source_target_pairs={{0,64},{8,72},{16,80},{24,88},{32,96},{40,104},{48,112},{56,120},{... | collective-permute-start | bytes 200 | tf_op jit(solution)/shard_map/ppermute | solution.py:28
  203.9 0.2 multiply_add_fusion.5
  204.1 47.9 %collective-permute-start.8 = (f32[16,128,128]{2,1,0:T(8,128)S(1)}, f32[16,128,128]{2,1,0:T(8,128)S(1)}, u32[]{:S(2)}, u32[]{:S(2)}) collective-permute-start(f32[16,128,128]{2,1,0:T(8,128)S(1)} %multiply_add_fusion.5), channel_id=1, source_target_pairs={{0,128},{8,136},{16,144},{24,152},{32,160},{40,168},{48,176},{56,1... | collective-permute-start | bytes 3145736 | tf_op jit(solution)/shard_map/ppermute | solution.py:28
  252.0 1.7 multiply_add_fusion
  253.7 3.1 fusion.8
  256.8 17.5 %collective-permute-done.8 = f32[16,128,128]{2,1,0:T(8,128)S(1)} collective-permute-done((f32[16,128,128]{2,1,0:T(8,128)S(1)}, f32[16,128,128]{2,1,0:T(8,128)S(1)}, u32[]{:S(2)}, u32[]{:S(2)}) %collective-permute-start.8) | collective-permute-done | bytes 1048608 | tf_op jit(solution)/shard_map/ppermute | solution.py:28
  274.2 3.9 %fusion.10 = (f32[384,16]{0,1:T(8,128)S(1)}, bf16[384,16,128]{0,2,1:T(8,128)(2,1)}) fusion(bf16[384,16,128]{0,2,1:T(8,128)(2,1)S(1)} %bitcast.75, bf16[384,16,128]{0,2,1:T(8,128)(2,1)S(1)} %bitcast.80, f32[16,128,128]{2,1,0:T(8,128)} %collective-permute-done.4, f32[16,128,128]{2,1,0:T(8,128)S(1)} %collective-permute-done.5, ...), kind=kOutput, calls=%fused_computation.16 | convolution fusion | flops 610789376 | bytes 13156608 | tf_op jit(solution)/shard_map/shf,hef->she/dot_general | solution.py:112
  278.2 0.1 multiply_reduce_fusion
  278.3 6.8 %fusion = f32[16,384,128]{1,2,0:T(8,128)} fusion(bf16[384,16,128]{0,2,1:T(8,128)(2,1)} %bitcast.78, f32[16,384]{1,0:T(8,128)S(1)} %get-tuple-element.39, pred[384,384]{1,0:T(8,128)(4,1)S(1)} %fusion.28, bf16[384,16,128]{0,2,1:T(8,128)(2,1)S(1)} %bitcast.76, bf16[384,16,128]{0,2,1:T(8,128)(2,1)S(1)} %bitcast.71), kind=kOutput, calls=%fused_computation.3 | convolution fusion | flops 1219756032 | bytes 8036352 | tf_op jit(solution)/shard_map/hst,shf->thf/dot_general | solution.py:103
  285.1 99.3 %psum.7 = f32[16]{0:T(128)S(1)} all-reduce(f32[16]{0:T(128)S(1)} %multiply_reduce_fusion), channel_id=1, replica_groups=mesh['seq'=32,'dp'=8] {'seq','dp'}, use_global_device_ids=true, to_apply=%region_10.11 | all-reduce | flops 16 | bytes 128 | tf_op jit(solution)/shard_map/psum | solution.py:123
  384.4 0.5 multiply_multiply_fusion
  384.9 3.4 fusion.12
  388.4 1.6 copy.94
  390.0 1.6 copy.93
  391.6 1.6 copy.92
  (44 shorter events, 0.7 us)
Async XLA Ops:
  10.6 2.5 copy-start.1
  13.0 26.2 %collective-permute-start.4 = (f32[16,128,128]{2,1,0:T(8,128)}, f32[16,128,128]{2,1,0:T(8,128)}, u32[]{:S(2)}, u32[]{:S(2)}) collective-permute-start(f32[16,128,128]{2,1,0:T(8,128)} %fusion.7), channel_id=1, source_target_pairs={{0,8},{8,16},{16,24},{24,32},{32,40},{40,48},{48,56},{56,64},{64,7... | collective-permute-start | bytes 3145736 | tf_op jit(solution)/shard_map/ppermute | solution.py:28
  25.8 26.8 %collective-permute-start.9 = (f32[16,128,128]{2,1,0:T(8,128)}, f32[16,128,128]{2,1,0:T(8,128)}, u32[]{:S(2)}, u32[]{:S(2)}) collective-permute-start(f32[16,128,128]{2,1,0:T(8,128)} %fusion.9), channel_id=1, source_target_pairs={{8,0},{16,8},{24,16},{32,24},{40,32},{48,40},{56,48},{64,56},{72,6... | collective-permute-start | bytes 3145736 | tf_op jit(solution)/shard_map/ppermute | solution.py:29
  55.3 51.9 %collective-permute-start.11 = (f32[16,128,128]{2,1,0:T(8,128)S(1)}, f32[16,128,128]{2,1,0:T(8,128)S(1)}, u32[]{:S(2)}, u32[]{:S(2)}) collective-permute-start(f32[16,128,128]{2,1,0:T(8,128)S(1)} %get-tuple-element.42), channel_id=1, source_target_pairs={{16,0},{24,8},{32,16},{40,24},{48,32},{56,40},{64,48},{72,56},{80,... | collective-permute-start | bytes 3145736 | tf_op jit(solution)/shard_map/ppermute | solution.py:29
  56.6 53.6 %collective-permute-start.5 = (f32[16,128,128]{2,1,0:T(8,128)S(1)}, f32[16,128,128]{2,1,0:T(8,128)S(1)}, u32[]{:S(2)}, u32[]{:S(2)}) collective-permute-start(f32[16,128,128]{2,1,0:T(8,128)S(1)} %get-tuple-element.43), channel_id=1, source_target_pairs={{0,16},{8,24},{16,32},{24,40},{32,48},{40,56},{48,64},{56,72},{64,... | collective-permute-start | bytes 3145736 | tf_op jit(solution)/shard_map/ppermute | solution.py:28
  62.8 41.0 %collective-permute-start = (f32[16]{0:T(128)S(1)}, f32[16]{0:T(128)S(1)}, u32[]{:S(2)}, u32[]{:S(2)}) collective-permute-start(f32[16]{0:T(128)S(1)} %broadcast_select_fusion), channel_id=1, source_target_pairs={{0,8},{8,16},{16,24},{24,32},{32,40},{40,48},{48,56},{56,64},{64,7... | collective-permute-start | bytes 200 | tf_op jit(solution)/shard_map/ppermute | solution.py:28
  66.1 41.1 %collective-permute-start.10 = (f32[16]{0:T(128)S(1)}, f32[16]{0:T(128)S(1)}, u32[]{:S(2)}, u32[]{:S(2)}) collective-permute-start(f32[16]{0:T(128)S(1)} %broadcast_select_fusion), channel_id=1, source_target_pairs={{8,0},{16,8},{24,16},{32,24},{40,32},{48,40},{56,48},{64,56},{72,6... | collective-permute-start | bytes 200 | tf_op jit(solution)/shard_map/ppermute | solution.py:29
  107.4 26.9 %collective-permute-start.13 = (f32[16,128,128]{2,1,0:T(8,128)S(1)}, f32[16,128,128]{2,1,0:T(8,128)S(1)}, u32[]{:S(2)}, u32[]{:S(2)}) collective-permute-start(f32[16,128,128]{2,1,0:T(8,128)S(1)} %multiply_add_fusion.3), channel_id=1, source_target_pairs={{32,0},{40,8},{48,16},{56,24},{64,32},{72,40},{80,48},{88,56},{96,... | collective-permute-start | bytes 3145736 | tf_op jit(solution)/shard_map/ppermute | solution.py:29
  108.9 10.7 %collective-permute-start.12 = (f32[16]{0:T(128)S(1)}, f32[16]{0:T(128)S(1)}, u32[]{:S(2)}, u32[]{:S(2)}) collective-permute-start(f32[16]{0:T(128)S(1)} %get-tuple-element.40), channel_id=1, source_target_pairs={{16,0},{24,8},{32,16},{40,24},{48,32},{56,40},{64,48},{72,56},{80,... | collective-permute-start | bytes 200 | tf_op jit(solution)/shard_map/ppermute | solution.py:29
  110.2 5.6 %copy-start = (bf16[1,384,2048]{1,2,0:T(8,128)(2,1)S(1)}, bf16[1,384,2048]{1,2,0:T(8,128)(2,1)}, u32[]{:S(2)}) copy-start(bf16[1,384,2048]{1,2,0:T(8,128)(2,1)} %copy.99) | copy-start | bytes 4718596
  110.2 5.6 %copy-start.2 = (bf16[48,8,16,128]{3,2,1,0:T(8,128)(2,1)S(1)}, bf16[48,8,16,128]{3,2,1,0:T(8,128)(2,1)}, u32[]{:S(2)}) copy-start(bf16[48,8,16,128]{3,2,1,0:T(8,128)(2,1)} %copy-done.1) | copy-start | bytes 4718596
  110.4 32.8 %collective-permute-start.6 = (f32[16,128,128]{2,1,0:T(8,128)S(1)}, f32[16,128,128]{2,1,0:T(8,128)S(1)}, u32[]{:S(2)}, u32[]{:S(2)}) collective-permute-start(f32[16,128,128]{2,1,0:T(8,128)S(1)} %multiply_add_fusion.7), channel_id=1, source_target_pairs={{0,32},{8,40},{16,48},{24,56},{32,64},{40,72},{48,80},{56,88},{64,... | collective-permute-start | bytes 3145736 | tf_op jit(solution)/shard_map/ppermute | solution.py:28
  134.5 51.2 %collective-permute-start.15 = (f32[16,128,128]{2,1,0:T(8,128)S(1)}, f32[16,128,128]{2,1,0:T(8,128)S(1)}, u32[]{:S(2)}, u32[]{:S(2)}) collective-permute-start(f32[16,128,128]{2,1,0:T(8,128)S(1)} %multiply_add_fusion.2), channel_id=1, source_target_pairs={{64,0},{72,8},{80,16},{88,24},{96,32},{104,40},{112,48},{120,56},{... | collective-permute-start | bytes 3145736 | tf_op jit(solution)/shard_map/ppermute | solution.py:29
  137.0 6.2 %collective-permute-start.1 = (f32[16]{0:T(128)S(1)}, f32[16]{0:T(128)S(1)}, u32[]{:S(2)}, u32[]{:S(2)}) collective-permute-start(f32[16]{0:T(128)S(1)} %get-tuple-element.41), channel_id=1, source_target_pairs={{0,16},{8,24},{16,32},{24,40},{32,48},{40,56},{48,64},{56,72},{64,... | collective-permute-start | bytes 200 | tf_op jit(solution)/shard_map/ppermute | solution.py:28
  141.9 13.9 %collective-permute-start.14 = (f32[16]{0:T(128)S(1)}, f32[16]{0:T(128)S(1)}, u32[]{:S(2)}, u32[]{:S(2)}) collective-permute-start(f32[16]{0:T(128)S(1)} %mul.277), channel_id=1, source_target_pairs={{32,0},{40,8},{48,16},{56,24},{64,32},{72,40},{80,48},{88,56},{96,... | collective-permute-start | bytes 200 | tf_op jit(solution)/shard_map/ppermute | solution.py:29
  143.4 60.5 %collective-permute-start.7 = (f32[16,128,128]{2,1,0:T(8,128)S(1)}, f32[16,128,128]{2,1,0:T(8,128)S(1)}, u32[]{:S(2)}, u32[]{:S(2)}) collective-permute-start(f32[16,128,128]{2,1,0:T(8,128)S(1)} %multiply_add_fusion.6), channel_id=1, source_target_pairs={{0,64},{8,72},{16,80},{24,88},{32,96},{40,104},{48,112},{56,120},{... | collective-permute-start | bytes 3145736 | tf_op jit(solution)/shard_map/ppermute | solution.py:28
  185.9 66.1 %collective-permute-start.17 = (f32[16,128,128]{2,1,0:T(8,128)S(1)}, f32[16,128,128]{2,1,0:T(8,128)S(1)}, u32[]{:S(2)}, u32[]{:S(2)}) collective-permute-start(f32[16,128,128]{2,1,0:T(8,128)S(1)} %multiply_add_fusion.1), channel_id=1, source_target_pairs={{128,0},{136,8},{144,16},{152,24},{160,32},{168,40},{176,48},{184,... | collective-permute-start | bytes 3145736 | tf_op jit(solution)/shard_map/ppermute | solution.py:29
  187.5 7.9 %collective-permute-start.2 = (f32[16]{0:T(128)S(1)}, f32[16]{0:T(128)S(1)}, u32[]{:S(2)}, u32[]{:S(2)}) collective-permute-start(f32[16]{0:T(128)S(1)} %mul.243), channel_id=1, source_target_pairs={{0,32},{8,40},{16,48},{24,56},{32,64},{40,72},{48,80},{56,88},{64,... | collective-permute-start | bytes 200 | tf_op jit(solution)/shard_map/ppermute | solution.py:28
  194.0 9.8 %collective-permute-start.16 = (f32[16]{0:T(128)S(1)}, f32[16]{0:T(128)S(1)}, u32[]{:S(2)}, u32[]{:S(2)}) collective-permute-start(f32[16]{0:T(128)S(1)} %mul.283), channel_id=1, source_target_pairs={{64,0},{72,8},{80,16},{88,24},{96,32},{104,40},{112,48},{120,56},{... | collective-permute-start | bytes 200 | tf_op jit(solution)/shard_map/ppermute | solution.py:29
  195.4 56.6 %collective-permute-start.3 = (f32[16]{0:T(128)S(1)}, f32[16]{0:T(128)S(1)}, u32[]{:S(2)}, u32[]{:S(2)}) collective-permute-start(f32[16]{0:T(128)S(1)} %mul.244), channel_id=1, source_target_pairs={{0,64},{8,72},{16,80},{24,88},{32,96},{40,104},{48,112},{56,120},{... | collective-permute-start | bytes 200 | tf_op jit(solution)/shard_map/ppermute | solution.py:28
  204.1 70.1 %collective-permute-start.8 = (f32[16,128,128]{2,1,0:T(8,128)S(1)}, f32[16,128,128]{2,1,0:T(8,128)S(1)}, u32[]{:S(2)}, u32[]{:S(2)}) collective-permute-start(f32[16,128,128]{2,1,0:T(8,128)S(1)} %multiply_add_fusion.5), channel_id=1, source_target_pairs={{0,128},{8,136},{16,144},{24,152},{32,160},{40,168},{48,176},{56,1... | collective-permute-start | bytes 3145736 | tf_op jit(solution)/shard_map/ppermute | solution.py:28
  253.7 3.1 copy-start.3
  278.3 106.1 %copy-start.6 = (f32[16]{0:T(128)S(1)}, f32[16]{0:T(128)}, u32[]{:S(2)}) copy-start(f32[16]{0:T(128)} %param.13) | copy-start | bytes 196
  388.4 1.6 copy-start.4
  390.0 1.6 copy-start.5

commit v2 on v1

--- a/solution.py
+++ b/solution.py
@@ -13,31 +13,47 @@
 state_mode = lax.Precision.HIGH
 
 
+def packed(decay, state):
+    pad = jnp.broadcast_to(decay[:, None, None], (state.shape[0], 8, state.shape[2]))
+    return jnp.concatenate([state, pad], axis=1)
+
+
+def combine(far, near):
+    rows = far.shape[1] - 8
+    state = near[:, rows : rows + 1, 0:1] * far[:, :rows] + near[:, :rows]
+    return jnp.concatenate([state, far[:, rows:] * near[:, rows:]], axis=1)
+
+
 def carried_both(decay, forward_part, backward_part, axis):
     count = lax.axis_size(axis)
-    ones = jnp.ones_like(decay)
-    zeros = jnp.zeros_like(forward_part)
-    fwd_decay, fwd_state = decay, forward_part
-    bwd_decay, bwd_state = decay, backward_part
-    excl_decay, excl_state = ones, zeros
-    rexcl_decay, rexcl_state = ones, zeros
+    fwd = packed(decay, forward_part)
+    bwd = packed(decay, backward_part)
+    excl = packed(jnp.ones_like(decay), jnp.zeros_like(forward_part))
+    rexcl = excl
     shift = 1
     while shift < count:
         up = [(i, i + shift) for i in range(count - shift)]
         down = [(i + shift, i) for i in range(count - shift)]
-        got_decay, got_state = lax.ppermute((fwd_decay, fwd_state), axis, up)
-        rgot_decay, rgot_state = lax.ppermute((bwd_decay, bwd_state), axis, down)
-        excl_state = excl_decay[:, None, None] * got_state + excl_state
-        excl_decay = got_decay * excl_decay
-        rexcl_state = rexcl_state + rexcl_decay[:, None, None] * rgot_state
-        rexcl_decay = rexcl_decay * rgot_decay
+        got = lax.ppermute(fwd, axis, up)
+        rgot = lax.ppermute(bwd, axis, down)
+        excl = combine(got, excl)
+        rexcl = combine(rgot, rexcl)
         if 2 * shift < count:
-            fwd_state = fwd_decay[:, None, None] * got_state + fwd_state
-            fwd_decay = got_decay * fwd_decay
-            bwd_state = bwd_state + bwd_decay[:, None, None] * rgot_state
-            bwd_decay = bwd_decay * rgot_decay
+            fwd = combine(got, fwd)
+            bwd = combine(rgot, bwd)
         shift *= 2
-    return excl_state, rexcl_state
+    rows = forward_part.shape[1]
+    return excl[:, :rows], rexcl[:, :rows]
+
+
+def all_sum(value, axes):
+    for axis in axes:
+        count = lax.axis_size(axis)
+        step = 1
+        while step < count:
+            value = value + lax.ppermute(value, axis, [(i, i ^ step) for i in range(count)])
+            step *= 2
+    return value
 
 
 def block_mask_list(head_decay_rate, cutoff_list, row_position, start_list):
@@ -120,7 +136,7 @@
     )
     inner_step = jnp.sum(key_f * key_full, axis=2) - jnp.sum(query_f * query_full, axis=2)
     rate_part = jnp.sum(position[:, None] * inner_step, axis=0)
-    rate_total = lax.psum(rate_part, ("seq", "dp"))
+    rate_total = all_sum(rate_part, ("seq", "dp"))
     token_total = row_count * lax.axis_size("seq") * lax.axis_size("dp")
     rate_grad = head_decay_rate * rate_total / math.sqrt(token_total)
     out_shape = (1, row_count, HEADS * HEAD_DIM)

time: 396 us -> 299 us (0.76)
  blocking collectives: 99.3 us -> 0 us
  waiting for transfers between devices: 127 us -> 183 us
  starting transfers between devices: 110 us -> 60.1 us
    psum x1 -> x0, blocking collectives: 99.3 us -> none  [on_device(): rate_total = lax.psum(rate_part, ('seq', 'dp'))]
    ppermute x18, waiting for transfers between devices: 127 us -> 183 us  [the longest x5 106 us: carried_both(): rgot = lax.ppermute(bwd, axis, down)]
    ppermute x18, starting transfers between devices: 110 us -> 60.1 us  [the longest x5 42.1 us: carried_both(): got = lax.ppermute(fwd, axis, up)]
    unnamed x20 -> x18, local copies, waits for them, and re-layouts: 10.5 us -> 11.4 us
  transfers between devices with their start and end apart: 18 -> 18, of which waited for: 7 -> 13; matrix products, arithmetic and copies ran while one was open for 5% -> 10% of each run, Pallas kernels for 0% -> 0%
where the time goes in v2:
time: 299 us; the launch traced here: 298 us
  waiting for transfers between devices  183 us (61%)
  starting transfers between devices  60.1 us (20%)
  matrix products  26.8 us (9%)
  local copies, waits for them, and re-layouts  17.2 us (6%)
  other arithmetic  9.23 us (3%)
    ppermute x5, waiting for transfers between devices, carried_both(): rgot = lax.ppermute(bwd, axis, down)  106 us
    ppermute x5, waiting for transfers between devices, carried_both(): got = lax.ppermute(fwd, axis, up)  62.4 us
    ppermute x5, starting transfers between devices, carried_both(): got = lax.ppermute(fwd, axis, up)  42.1 us
    ppermute x8, waiting for transfers between devices, all_sum(): lax.ppermute(value, axis, [(i, i ^ step) for i in range(count)])  14 us
    unnamed x18, local copies, waits for them, and re-layouts  11.4 us
    ppermute x8, starting transfers between devices, all_sum(): lax.ppermute(value, axis, [(i, i ^ step) for i in range(count)])  11.4 us
    dot_general x1, matrix products, on_device(): jnp.einsum('hst,shf->thf', attn_prob, gradient_block, preferred_element_t...  6.76 us
    ppermute x5, starting transfers between devices, carried_both(): rgot = lax.ppermute(bwd, axis, down)  6.64 us
  transfers between devices with their start and end apart: 18, of which 13 were waited for; matrix products, arithmetic and copies ran while one was open for 10% of the time, Pallas kernels for 0%

profile of v2, /device:TPU:6, one launch (start us, length us, event | category | flops | bytes accessed | tf_op | source)
XLA Modules:
  0.0 297.7 jit_solution(11624890540259133332)
XLA Ops:
  0.6 0.8 reduce-window_clone.1
  1.5 0.7 subtract_bitcast_fusion
  2.2 0.3 reduce-window.16
  2.9 0.6 slice.141
  3.4 0.6 broadcast_compare_fusion
  4.7 0.7 multiply_reduce_fusion.1
  5.4 0.7 broadcast_subtract_fusion
  6.2 0.9 reduce-window.24
  7.5 2.0 copy.81
  9.5 1.6 copy.101
  11.1 2.6 copy.99
  13.7 1.9 copy.84
  15.7 2.9 fusion.7
  18.6 1.4 fusion.9
  20.2 3.7 %collective-permute-start = (f32[16,136,128]{2,1,0:T(8,128)S(1)}, f32[16,136,128]{2,1,0:T(8,128)S(1)}, u32[]{:S(2)}, u32[]{:S(2)}) collective-permute-start(f32[16,136,128]{2,1,0:T(8,128)S(1)} %get-tuple-element.45), channel_id=1, source_target_pairs={{0,8},{8,16},{16,24},{24,32},{32,40},{40,48},{48,56},{56,64},{64,7... | collective-permute-start | bytes 3342344 | tf_op jit(solution)/shard_map/ppermute | solution.py:37
  23.9 1.3 collective-permute-start.5
  25.4 3.7 %multiply_convert_fusion.1 = bf16[16,384,384]{2,1,0:T(8,128)(2,1)S(1)} fusion(f32[16,384]{1,0:T(8,128)S(1)} %get-tuple-element.49, pred[384,384]{1,0:T(8,128)(4,1)S(1)} %fusion.33, bf16[384,16,128]{0,2,1:T(8,128)(2,1)S(1)} %bitcast.79, bf16[384,16,128]{2,1,0:T(8,128)(2,1)S(1)} %bitcast.82), kind=kOutput, calls=%fused_computation.1 | convolution fusion | flops 615776256 | bytes 8036352 | tf_op jit(solution)/shard_map/shf,thf->hst/dot_general | solution.py:114
  29.1 18.6 %collective-permute-done = f32[16,136,128]{2,1,0:T(8,128)S(1)} collective-permute-done((f32[16,136,128]{2,1,0:T(8,128)S(1)}, f32[16,136,128]{2,1,0:T(8,128)S(1)}, u32[]{:S(2)}, u32[]{:S(2)}) %collective-permute-start) | collective-permute-done | bytes 1114144 | tf_op jit(solution)/shard_map/ppermute | solution.py:37
  47.7 4.2 %collective-permute-done.5 = f32[16,136,128]{2,1,0:T(8,128)S(1)} collective-permute-done((f32[16,136,128]{2,1,0:T(8,128)S(1)}, f32[16,136,128]{2,1,0:T(8,128)S(1)}, u32[]{:S(2)}, u32[]{:S(2)}) %collective-permute-start.5) | collective-permute-done | bytes 1114144 | tf_op jit(solution)/shard_map/ppermute | solution.py:38
  51.8 0.3 multiply_add_fusion.3
  52.3 1.3 collective-permute-start.6
  53.6 1.2 fusion.45
  54.9 6.1 %collective-permute-start.1 = (f32[16,136,128]{2,1,0:T(8,128)S(1)}, f32[16,136,128]{2,1,0:T(8,128)S(1)}, u32[]{:S(2)}, u32[]{:S(2)}) collective-permute-start(f32[16,136,128]{2,1,0:T(8,128)S(1)} %pad_maximum_fusion.2), channel_id=1, source_target_pairs={{0,16},{8,24},{16,32},{24,40},{32,48},{40,56},{48,64},{56,72},{64,... | collective-permute-start | bytes 3342344 | tf_op jit(solution)/shard_map/ppermute | solution.py:37
  61.1 1.6 fusion.44
  62.7 0.2 slice_reduce_fusion.4
  62.9 0.2 slice_reduce_fusion.9
  63.1 17.7 %collective-permute-done.6 = f32[16,136,128]{2,1,0:T(8,128)S(1)} collective-permute-done((f32[16,136,128]{2,1,0:T(8,128)S(1)}, f32[16,136,128]{2,1,0:T(8,128)S(1)}, u32[]{:S(2)}, u32[]{:S(2)}) %collective-permute-start.6) | collective-permute-done | bytes 1114144 | tf_op jit(solution)/shard_map/ppermute | solution.py:38
  81.1 1.3 collective-permute-start.7
  82.4 22.0 %collective-permute-done.1 = f32[16,136,128]{2,1,0:T(8,128)S(1)} collective-permute-done((f32[16,136,128]{2,1,0:T(8,128)S(1)}, f32[16,136,128]{2,1,0:T(8,128)S(1)}, u32[]{:S(2)}, u32[]{:S(2)}) %collective-permute-start.1) | collective-permute-done | bytes 1114144 | tf_op jit(solution)/shard_map/ppermute | solution.py:37
  104.7 6.4 %collective-permute-start.2 = (f32[16,136,128]{2,1,0:T(8,128)S(1)}, f32[16,136,128]{2,1,0:T(8,128)S(1)}, u32[]{:S(2)}, u32[]{:S(2)}) collective-permute-start(f32[16,136,128]{2,1,0:T(8,128)S(1)} %pad_maximum_fusion.3), channel_id=1, source_target_pairs={{0,32},{8,40},{16,48},{24,56},{32,64},{40,72},{48,80},{56,88},{64,... | collective-permute-start | bytes 3342344 | tf_op jit(solution)/shard_map/ppermute | solution.py:37
  111.1 0.2 slice_reduce_fusion.1
  111.5 19.7 %collective-permute-done.7 = f32[16,136,128]{2,1,0:T(8,128)S(1)} collective-permute-done((f32[16,136,128]{2,1,0:T(8,128)S(1)}, f32[16,136,128]{2,1,0:T(8,128)S(1)}, u32[]{:S(2)}, u32[]{:S(2)}) %collective-permute-start.7) | collective-permute-done | bytes 1114144 | tf_op jit(solution)/shard_map/ppermute | solution.py:38
  131.5 1.5 collective-permute-start.8
  133.0 0.2 slice_reduce_fusion.10
  133.5 7.4 %collective-permute-start.3 = (f32[16,136,128]{2,1,0:T(8,128)S(1)}, f32[16,136,128]{2,1,0:T(8,128)S(1)}, u32[]{:S(2)}, u32[]{:S(2)}) collective-permute-start(f32[16,136,128]{2,1,0:T(8,128)S(1)} %pad_maximum_fusion.4), channel_id=1, source_target_pairs={{0,64},{8,72},{16,80},{24,88},{32,96},{40,104},{48,112},{56,120},{... | collective-permute-start | bytes 3342344 | tf_op jit(solution)/shard_map/ppermute | solution.py:37
  140.9 0.2 slice_reduce_fusion.6
  141.6 43.0 %collective-permute-done.8 = f32[16,136,128]{2,1,0:T(8,128)S(1)} collective-permute-done((f32[16,136,128]{2,1,0:T(8,128)S(1)}, f32[16,136,128]{2,1,0:T(8,128)S(1)}, u32[]{:S(2)}, u32[]{:S(2)}) %collective-permute-start.8) | collective-permute-done | bytes 1114144 | tf_op jit(solution)/shard_map/ppermute | solution.py:38
  184.8 1.3 collective-permute-start.9
  186.1 0.2 slice_reduce_fusion.2
  186.6 18.5 %collective-permute-start.4 = (f32[16,136,128]{2,1,0:T(8,128)S(1)}, f32[16,136,128]{2,1,0:T(8,128)S(1)}, u32[]{:S(2)}, u32[]{:S(2)}) collective-permute-start(f32[16,136,128]{2,1,0:T(8,128)S(1)} %pad_maximum_fusion.5), channel_id=1, source_target_pairs={{0,128},{8,136},{16,144},{24,152},{32,160},{40,168},{48,176},{56,1... | collective-permute-start | bytes 3342344 | tf_op jit(solution)/shard_map/ppermute | solution.py:37
  205.1 0.2 slice_reduce_fusion.7
  205.3 0.2 fusion.39
  205.5 0.2 fusion.38
  205.7 21.6 %collective-permute-done.9 = f32[16,136,128]{2,1,0:T(8,128)S(1)} collective-permute-done((f32[16,136,128]{2,1,0:T(8,128)S(1)}, f32[16,136,128]{2,1,0:T(8,128)S(1)}, u32[]{:S(2)}, u32[]{:S(2)}) %collective-permute-start.9) | collective-permute-done | bytes 1114144 | tf_op jit(solution)/shard_map/ppermute | solution.py:38
  227.4 0.5 fusion.20
  227.9 3.1 %fusion.8 = (f32[384,16]{0,1:T(8,128)S(1)}, bf16[384,16,128]{0,2,1:T(8,128)(2,1)}) fusion(bf16[384,16,128]{0,2,1:T(8,128)(2,1)S(1)} %bitcast.70, f32[16,128,128]{2,1,0:T(8,128)S(1)} %fusion.20, bf16[384,16,128]{2,1,0:T(8,128)(2,1)S(1)} %bitcast.83, f32[384,16]{0,1:T(8,128)S(1)} %get-tuple-element.46, f32[16,384,128]{1,2,0:T(8,128)S(1)} %fusion.45), kind=kOutput, calls=%fused_computation.14 | convolution fusion | flops 608692224 | bytes 8962048 | tf_op jit(solution)/shard_map/thf,hef->the/dot_general | solution.py:134
  231.0 21.8 %collective-permute-done.4 = f32[16,136,128]{2,1,0:T(8,128)S(1)} collective-permute-done((f32[16,136,128]{2,1,0:T(8,128)S(1)}, f32[16,136,128]{2,1,0:T(8,128)S(1)}, u32[]{:S(2)}, u32[]{:S(2)}) %collective-permute-start.4) | collective-permute-done | bytes 1114144 | tf_op jit(solution)/shard_map/ppermute | solution.py:37
  252.8 2.8 fusion.10
  255.6 2.1 collective-permute-start.10
  257.8 1.5 collective-permute-done.10
  259.5 4.9 %collective-permute-done.11 = f32[16]{0:T(128)S(1)} collective-permute-done((f32[16]{0:T(128)S(1)}, f32[16]{0:T(128)S(1)}, u32[]{:S(2)}, u32[]{:S(2)}) %collective-permute-start.11) | collective-permute-done | bytes 96 | tf_op jit(solution)/shard_map/ppermute | solution.py:54
  264.4 3.5 %collective-permute-done.12 = f32[16]{0:T(128)S(1)} collective-permute-done((f32[16]{0:T(128)S(1)}, f32[16]{0:T(128)S(1)}, u32[]{:S(2)}, u32[]{:S(2)}) %collective-permute-start.12) | collective-permute-done | bytes 96 | tf_op jit(solution)/shard_map/ppermute | solution.py:54
  267.9 4.5 %collective-permute-start.13 = (f32[16]{0:T(128)S(1)}, f32[16]{0:T(128)S(1)}, u32[]{:S(2)}, u32[]{:S(2)}) collective-permute-start(f32[16]{0:T(128)S(1)} %add.117), channel_id=1, source_target_pairs={{0,64},{8,72},{16,80},{24,88},{32,96},{40,104},{48,112},{56,120},{... | collective-permute-start | bytes 200 | tf_op jit(solution)/shard_map/ppermute | solution.py:54
  272.3 6.8 %fusion = f32[16,384,128]{1,2,0:T(8,128)} fusion(bf16[384,16,128]{0,2,1:T(8,128)(2,1)} %bitcast.77, f32[16,384]{1,0:T(8,128)S(1)} %get-tuple-element.49, pred[384,384]{1,0:T(8,128)(4,1)S(1)} %fusion.33, bf16[384,16,128]{0,2,1:T(8,128)(2,1)S(1)} %bitcast.76, bf16[384,16,128]{0,2,1:T(8,128)(2,1)S(1)} %bitcast.71), kind=kOutput, calls=%fused_computation.3 | convolution fusion | flops 1219756032 | bytes 8036352 | tf_op jit(solution)/shard_map/hst,shf->thf/dot_general | solution.py:119
  279.1 2.4 collective-permute-start.14
  281.5 3.4 %fusion.12 = bf16[384,16,128]{0,2,1:T(8,128)(2,1)S(1)} fusion(f32[16,384,128]{1,2,0:T(8,128)} %fusion, f32[16,128,128]{2,1,0:T(8,128)} %copy-done.2, bf16[384,16,128]{0,2,1:T(8,128)(2,1)S(1)} %bitcast.72, f32[384,16]{0,1:T(8,128)S(1)} %get-tuple-element.46), kind=kOutput, calls=%fused_computation.19 | convolution fusion | flops 606339072 | bytes 7364608 | tf_op jit(solution)/shard_map/the,hef->thf/dot_general | solution.py:122
  284.9 2.0 collective-permute-done.14
  286.9 1.6 copy.94
  288.5 0.8 collective-permute-start.16
  289.3 2.7 copy.93
  292.0 1.4 collective-permute-start.17
  293.5 1.6 copy.92
  295.1 2.1 collective-permute-done.17
  297.2 0.5 multiply_multiply_fusion
  (70 shorter events, 4.2 us)
Async XLA Ops:
  7.5 2.0 copy-start.4
  15.6 2.9 copy-start
  20.1 5.3 %copy-start.1 = (bf16[48,8,16,128]{3,2,1,0:T(8,128)(2,1)S(1)}, bf16[48,8,16,128]{3,2,1,0:T(8,128)(2,1)}, u32[]{:S(2)}) copy-start(bf16[48,8,16,128]{3,2,1,0:T(8,128)(2,1)} %copy.101) | copy-start | bytes 4718596
  20.2 27.4 %collective-permute-start = (f32[16,136,128]{2,1,0:T(8,128)S(1)}, f32[16,136,128]{2,1,0:T(8,128)S(1)}, u32[]{:S(2)}, u32[]{:S(2)}) collective-permute-start(f32[16,136,128]{2,1,0:T(8,128)S(1)} %get-tuple-element.45), channel_id=1, source_target_pairs={{0,8},{8,16},{16,24},{24,32},{32,40},{40,48},{48,56},{56,64},{64,7... | collective-permute-start | bytes 3342344 | tf_op jit(solution)/shard_map/ppermute | solution.py:37
  23.9 27.9 %collective-permute-start.5 = (f32[16,136,128]{2,1,0:T(8,128)S(1)}, f32[16,136,128]{2,1,0:T(8,128)S(1)}, u32[]{:S(2)}, u32[]{:S(2)}) collective-permute-start(f32[16,136,128]{2,1,0:T(8,128)S(1)} %get-tuple-element.44), channel_id=1, source_target_pairs={{8,0},{16,8},{24,16},{32,24},{40,32},{48,40},{56,48},{64,56},{72,6... | collective-permute-start | bytes 3342344 | tf_op jit(solution)/shard_map/ppermute | solution.py:38
  52.3 28.5 %collective-permute-start.6 = (f32[16,136,128]{2,1,0:T(8,128)S(1)}, f32[16,136,128]{2,1,0:T(8,128)S(1)}, u32[]{:S(2)}, u32[]{:S(2)}) collective-permute-start(f32[16,136,128]{2,1,0:T(8,128)S(1)} %pad_maximum_fusion.6), channel_id=1, source_target_pairs={{16,0},{24,8},{32,16},{40,24},{48,32},{56,40},{64,48},{72,56},{80,... | collective-permute-start | bytes 3342344 | tf_op jit(solution)/shard_map/ppermute | solution.py:38
  54.9 49.5 %collective-permute-start.1 = (f32[16,136,128]{2,1,0:T(8,128)S(1)}, f32[16,136,128]{2,1,0:T(8,128)S(1)}, u32[]{:S(2)}, u32[]{:S(2)}) collective-permute-start(f32[16,136,128]{2,1,0:T(8,128)S(1)} %pad_maximum_fusion.2), channel_id=1, source_target_pairs={{0,16},{8,24},{16,32},{24,40},{32,48},{40,56},{48,64},{56,72},{64,... | collective-permute-start | bytes 3342344 | tf_op jit(solution)/shard_map/ppermute | solution.py:37
  81.1 50.2 %collective-permute-start.7 = (f32[16,136,128]{2,1,0:T(8,128)S(1)}, f32[16,136,128]{2,1,0:T(8,128)S(1)}, u32[]{:S(2)}, u32[]{:S(2)}) collective-permute-start(f32[16,136,128]{2,1,0:T(8,128)S(1)} %pad_maximum_fusion.7), channel_id=1, source_target_pairs={{32,0},{40,8},{48,16},{56,24},{64,32},{72,40},{80,48},{88,56},{96,... | collective-permute-start | bytes 3342344 | tf_op jit(solution)/shard_map/ppermute | solution.py:38
  104.7 28.5 %collective-permute-start.2 = (f32[16,136,128]{2,1,0:T(8,128)S(1)}, f32[16,136,128]{2,1,0:T(8,128)S(1)}, u32[]{:S(2)}, u32[]{:S(2)}) collective-permute-start(f32[16,136,128]{2,1,0:T(8,128)S(1)} %pad_maximum_fusion.3), channel_id=1, source_target_pairs={{0,32},{8,40},{16,48},{24,56},{32,64},{40,72},{48,80},{56,88},{64,... | collective-permute-start | bytes 3342344 | tf_op jit(solution)/shard_map/ppermute | solution.py:37
  131.5 53.0 %collective-permute-start.8 = (f32[16,136,128]{2,1,0:T(8,128)S(1)}, f32[16,136,128]{2,1,0:T(8,128)S(1)}, u32[]{:S(2)}, u32[]{:S(2)}) collective-permute-start(f32[16,136,128]{2,1,0:T(8,128)S(1)} %pad_maximum_fusion.8), channel_id=1, source_target_pairs={{64,0},{72,8},{80,16},{88,24},{96,32},{104,40},{112,48},{120,56},{... | collective-permute-start | bytes 3342344 | tf_op jit(solution)/shard_map/ppermute | solution.py:38
  133.5 52.8 %collective-permute-start.3 = (f32[16,136,128]{2,1,0:T(8,128)S(1)}, f32[16,136,128]{2,1,0:T(8,128)S(1)}, u32[]{:S(2)}, u32[]{:S(2)}) collective-permute-start(f32[16,136,128]{2,1,0:T(8,128)S(1)} %pad_maximum_fusion.4), channel_id=1, source_target_pairs={{0,64},{8,72},{16,80},{24,88},{32,96},{40,104},{48,112},{56,120},{... | collective-permute-start | bytes 3342344 | tf_op jit(solution)/shard_map/ppermute | solution.py:37
  184.8 42.5 %collective-permute-start.9 = (f32[16,136,128]{2,1,0:T(8,128)S(1)}, f32[16,136,128]{2,1,0:T(8,128)S(1)}, u32[]{:S(2)}, u32[]{:S(2)}) collective-permute-start(f32[16,136,128]{2,1,0:T(8,128)S(1)} %pad_maximum_fusion.9), channel_id=1, source_target_pairs={{128,0},{136,8},{144,16},{152,24},{160,32},{168,40},{176,48},{184,... | collective-permute-start | bytes 3342344 | tf_op jit(solution)/shard_map/ppermute | solution.py:38
  186.6 66.1 %collective-permute-start.4 = (f32[16,136,128]{2,1,0:T(8,128)S(1)}, f32[16,136,128]{2,1,0:T(8,128)S(1)}, u32[]{:S(2)}, u32[]{:S(2)}) collective-permute-start(f32[16,136,128]{2,1,0:T(8,128)S(1)} %pad_maximum_fusion.5), channel_id=1, source_target_pairs={{0,128},{8,136},{16,144},{24,152},{32,160},{40,168},{48,176},{56,1... | collective-permute-start | bytes 3342344 | tf_op jit(solution)/shard_map/ppermute | solution.py:37
  227.9 27.6 %copy-start.2 = (f32[16,128,128]{2,1,0:T(8,128)}, f32[16,128,128]{2,1,0:T(8,128)S(1)}, u32[]{:S(2)}) copy-start(f32[16,128,128]{2,1,0:T(8,128)S(1)} %fusion.20) | copy-start | bytes 3145732
  255.6 3.7 %collective-permute-start.10 = (f32[16]{0:T(128)S(1)}, f32[16]{0:T(128)S(1)}, u32[]{:S(2)}, u32[]{:S(2)}) collective-permute-start(f32[16]{0:T(128)S(1)} %multiply_reduce_fusion), channel_id=1, source_target_pairs={{0,8},{8,0},{16,24},{24,16},{32,40},{40,32},{48,56},{56,48},{64,72... | collective-permute-start | bytes 200 | tf_op jit(solution)/shard_map/ppermute | solution.py:54
  259.3 5.0 %collective-permute-start.11 = (f32[16]{0:T(128)S(1)}, f32[16]{0:T(128)S(1)}, u32[]{:S(2)}, u32[]{:S(2)}) collective-permute-start(f32[16]{0:T(128)S(1)} %add.115), channel_id=1, source_target_pairs={{0,16},{8,24},{16,0},{24,8},{32,48},{40,56},{48,32},{56,40},{64,80... | collective-permute-start | bytes 200 | tf_op jit(solution)/shard_map/ppermute | solution.py:54
  264.3 3.5 %collective-permute-start.12 = (f32[16]{0:T(128)S(1)}, f32[16]{0:T(128)S(1)}, u32[]{:S(2)}, u32[]{:S(2)}) collective-permute-start(f32[16]{0:T(128)S(1)} %add.116), channel_id=1, source_target_pairs={{0,32},{8,40},{16,48},{24,56},{32,0},{40,8},{48,16},{56,24},{64,96... | collective-permute-start | bytes 200 | tf_op jit(solution)/shard_map/ppermute | solution.py:54
  267.9 11.2 %collective-permute-start.13 = (f32[16]{0:T(128)S(1)}, f32[16]{0:T(128)S(1)}, u32[]{:S(2)}, u32[]{:S(2)}) collective-permute-start(f32[16]{0:T(128)S(1)} %add.117), channel_id=1, source_target_pairs={{0,64},{8,72},{16,80},{24,88},{32,96},{40,104},{48,112},{56,120},{... | collective-permute-start | bytes 200 | tf_op jit(solution)/shard_map/ppermute | solution.py:54
  279.1 7.8 %collective-permute-start.14 = (f32[16]{0:T(128)S(1)}, f32[16]{0:T(128)S(1)}, u32[]{:S(2)}, u32[]{:S(2)}) collective-permute-start(f32[16]{0:T(128)S(1)} %add.118), channel_id=1, source_target_pairs={{0,128},{8,136},{16,144},{24,152},{32,160},{40,168},{48,176},{56,1... | collective-permute-start | bytes 200 | tf_op jit(solution)/shard_map/ppermute | solution.py:54
  286.9 1.6 collective-permute-start.15
  288.5 3.5 %collective-permute-start.16 = (f32[16]{0:T(128)S(1)}, f32[16]{0:T(128)S(1)}, u32[]{:S(2)}, u32[]{:S(2)}) collective-permute-start(f32[16]{0:T(128)S(1)} %add.120), channel_id=1, source_target_pairs={{0,2},{1,3},{2,0},{3,1},{4,6},{5,7},{6,4},{7,5},{8,10},{9,11},{10,... | collective-permute-start | bytes 200 | tf_op jit(solution)/shard_map/ppermute | solution.py:54
  289.3 4.2 %copy-start.3 = (bf16[384,16,128]{0,2,1:T(8,128)(2,1)S(1)}, bf16[384,16,128]{0,2,1:T(8,128)(2,1)}, u32[]{:S(2)}) copy-start(bf16[384,16,128]{0,2,1:T(8,128)(2,1)} %get-tuple-element.35) | copy-start | bytes 4718596
  292.0 5.1 %collective-permute-start.17 = (f32[16]{0:T(128)S(1)}, f32[16]{0:T(128)S(1)}, u32[]{:S(2)}, u32[]{:S(2)}) collective-permute-start(f32[16]{0:T(128)S(1)} %add.121), channel_id=1, source_target_pairs={{0,4},{1,5},{2,6},{3,7},{4,0},{5,1},{6,2},{7,3},{8,12},{9,13},{10,... | collective-permute-start | bytes 200 | tf_op jit(solution)/shard_map/ppermute | solution.py:54
  293.5 3.7 %copy-start.5 = (f32[16]{0:T(128)S(1)}, f32[16]{0:T(128)}, u32[]{:S(2)}) copy-start(f32[16]{0:T(128)} %param.13) | copy-start | bytes 196

commit v3 on v2

--- a/solution.py
+++ b/solution.py
@@ -24,13 +24,11 @@
     return jnp.concatenate([state, far[:, rows:] * near[:, rows:]], axis=1)
 
 
-def carried_both(decay, forward_part, backward_part, axis):
+def group_scan(fwd, bwd, axis, stride):
     count = lax.axis_size(axis)
-    fwd = packed(decay, forward_part)
-    bwd = packed(decay, backward_part)
-    excl = packed(jnp.ones_like(decay), jnp.zeros_like(forward_part))
+    excl = jnp.concatenate([jnp.zeros_like(fwd[:, :-8]), jnp.ones_like(fwd[:, -8:])], axis=1)
     rexcl = excl
-    shift = 1
+    shift = stride
     while shift < count:
         up = [(i, i + shift) for i in range(count - shift)]
         down = [(i + shift, i) for i in range(count - shift)]
@@ -42,8 +40,70 @@
             fwd = combine(got, fwd)
             bwd = combine(rgot, bwd)
         shift *= 2
-    rows = forward_part.shape[1]
-    return excl[:, :rows], rexcl[:, :rows]
+    return excl, rexcl
+
+
+def row_exchange(parts, axis, group):
+    count = lax.axis_size(axis)
+    place = lax.axis_index(axis) % group
+    got = [lax.dynamic_index_in_dim(parts, place, 0, False)]
+    for step in range(1, group):
+        pairs = [
+            (base + j, base + (j + step) % group)
+            for base in range(0, count, group)
+            for j in range(group)
+        ]
+        send = lax.dynamic_index_in_dim(parts, (place + step) % group, 0, False)
+        got.append(lax.ppermute(send, axis, pairs))
+    order = (place - jnp.arange(group)) % group
+    return jnp.take(jnp.stack(got), order, axis=0)
+
+
+def carried_both(decay, forward_part, backward_part, axis):
+    count = lax.axis_size(axis)
+    group = 4 if count % 4 == 0 and forward_part.shape[0] % 4 == 0 else 1
+    heads, rows, cols = forward_part.shape
+    share = heads // group
+    pad = jnp.broadcast_to(decay[:, None, None], (heads, 8, cols))
+    parts = jnp.concatenate([forward_part, backward_part, pad], axis=1)
+    mine = row_exchange(parts.reshape(group, share, 2 * rows + 8, cols), axis, group)
+    own_s = mine[:, :, :rows]
+    own_b = mine[:, :, rows : 2 * rows]
+    own_a = mine[:, :, 2 * rows, 0]
+    excl = [jnp.zeros_like(own_s[0])]
+    excl_a = [jnp.ones_like(own_a[0])]
+    for j in range(1, group):
+        excl.append(own_a[j - 1][:, None, None] * excl[j - 1] + own_s[j - 1])
+        excl_a.append(excl_a[j - 1] * own_a[j - 1])
+    total = own_a[group - 1][:, None, None] * excl[group - 1] + own_s[group - 1]
+    total_a = excl_a[group - 1] * own_a[group - 1]
+    later = [None] * group
+    later_a = [None] * group
+    later[group - 1] = jnp.zeros_like(own_b[0])
+    later_a[group - 1] = jnp.ones_like(own_a[0])
+    for j in range(group - 2, -1, -1):
+        later[j] = own_b[j + 1] + own_a[j + 1][:, None, None] * later[j + 1]
+        later_a[j] = own_a[j + 1] * later_a[j + 1]
+    rtotal = own_b[0] + own_a[0][:, None, None] * later[0]
+    before, after = group_scan(
+        packed(total_a, total), packed(total_a, rtotal), axis, group
+    )
+    before = before[:, :rows]
+    after = after[:, :rows]
+    result = jnp.stack(
+        [
+            jnp.concatenate(
+                [
+                    excl_a[j][:, None, None] * before + excl[j],
+                    later[j] + later_a[j][:, None, None] * after,
+                ],
+                axis=1,
+            )
+            for j in range(group)
+        ]
+    )
+    full = row_exchange(result, axis, group).reshape(heads, 2 * rows, cols)
+    return full[:, :rows], full[:, rows:]
 
 
 def all_sum(value, axes):

time: 299 us -> 205 us (0.69)
  waiting for transfers between devices: 183 us -> 87.5 us
  starting transfers between devices: 60.1 us -> 34.7 us
  local copies, waits for them, and re-layouts: 17.2 us -> 31.2 us
  other arithmetic: 9.23 us -> 21.1 us
    ppermute x10 -> x12, waiting for transfers between devices: 169 us -> 72.5 us  [the longest x6 43.4 us: row_exchange(): got.append(lax.ppermute(send, axis, pairs))]
    ppermute x10 -> x12, starting transfers between devices: 48.7 us -> 29.3 us  [the longest x3 18.5 us: group_scan(): got = lax.ppermute(fwd, axis, up)]
    gather x0 -> x3, local copies, waits for them, and re-layouts: none -> 10.2 us  [row_exchange(): return jnp.take(jnp.stack(got), order, axis=0)]
    ppermute x8, starting transfers between devices: 11.4 us -> 5.41 us  [all_sum(): lax.ppermute(value, axis, [(i, i ^ step) for i in range(count)])]
    add x0 -> x3, other arithmetic: none -> 4 us  [the longest x1 1.46 us: carried_both(): excl_a[j][:, None, None] * before + excl[j]]
    select_n x0 -> x3, other arithmetic: none -> 3.82 us  [row_exchange(): return jnp.take(jnp.stack(got), order, axis=0)]
    another operation x6 -> x11, other arithmetic: 2.15 us -> 5.67 us  [the longest x2 3.08 us: row_exchange(): return jnp.take(jnp.stack(got), order, axis=0)]
    unnamed x18 -> x38, local copies, waits for them, and re-layouts: 11.4 us -> 12.7 us
  transfers between devices with their start and end apart: 18 -> 20, of which waited for: 13 -> 16; matrix products, arithmetic and copies ran while one was open for 10% -> 13% of each run, Pallas kernels for 0% -> 0%
where the time goes in v3:
time: 205 us
  waiting for transfers between devices  87.5 us (43%)
  starting transfers between devices  34.7 us (17%)
  local copies, waits for them, and re-layouts  31.2 us (15%)
  matrix products  28.3 us (14%)
  other arithmetic  21.1 us (10%)
    ppermute x6, waiting for transfers between devices, row_exchange(): got.append(lax.ppermute(send, axis, pairs))  43.4 us
    ppermute x3, waiting for transfers between devices, group_scan(): rgot = lax.ppermute(bwd, axis, down)  22.9 us
    ppermute x3, starting transfers between devices, group_scan(): got = lax.ppermute(fwd, axis, up)  18.5 us
    ppermute x8, waiting for transfers between devices, all_sum(): lax.ppermute(value, axis, [(i, i ^ step) for i in range(count)])  14.9 us
    unnamed x38, local copies, waits for them, and re-layouts  12.7 us
    gather x3, local copies, waits for them, and re-layouts, row_exchange(): return jnp.take(jnp.stack(got), order, axis=0)  10.2 us
    dot_general x1, matrix products, on_device(): jnp.einsum('hst,shf->thf', attn_prob, gradient_block, preferred_element_t...  7.07 us
    ppermute x6, starting transfers between devices, row_exchange(): got.append(lax.ppermute(send, axis, pairs))  6.82 us
  transfers between devices with their start and end apart: 20, of which 16 were waited for; matrix products, arithmetic and copies ran while one was open for 13% of the time, Pallas kernels for 0%

profile of v3, /device:TPU:6, one launch (start us, length us, event | category | flops | bytes accessed | tf_op | source)
XLA Modules:
  0.0 204.6 jit_solution(1751087563997691393)
XLA Ops:
  0.7 0.9 reduce-window_clone.1
  4.9 1.9 copy.90
  6.9 1.6 copy.108
  8.5 0.9 reduce-window.24
  9.8 1.9 copy.88
  11.7 3.0 %copy.110 = bf16[48,8,16,128]{3,2,1,0:T(8,128)(2,1)} copy(bf16[48,8,16,128]{3,1,2,0:T(8,128)(2,1)} %bitcast.170) | data formatting | bytes 3145728
  14.8 2.9 %fusion.9 = f32[16,128,128]{2,1,0:T(8,128)S(1)} fusion(bf16[384,16,128]{0,2,1:T(8,128)(2,1)} %bitcast.160, bf16[384,16,128]{0,2,1:T(8,128)(2,1)S(1)} %bitcast.154, f32[384,16]{0,1:T(8,128)S(1)} %get-tuple-element.74), kind=kOutput, calls=%fused_computation.17 | convolution fusion | flops 605552640 | bytes 4218880 | tf_op jit(solution)/shard_map/she,shf->hef/dot_general | solution.py:168
  17.8 1.4 fusion.7
  19.6 3.1 %collective-permute-start.2 = (f32[4,264,128]{2,1,0:T(8,128)S(1)}, f32[4,264,128]{2,1,0:T(8,128)S(1)}, u32[]{:S(2)}, u32[]{:S(2)}) collective-permute-start(f32[4,264,128]{2,1,0:T(8,128)S(1)} %get-tuple-element.54), channel_id=1, source_target_pairs={{0,24},{8,0},{16,8},{24,16},{32,56},{40,32},{48,40},{56,48},{64,88... | collective-permute-start | bytes 1622024 | tf_op jit(solution)/shard_map/ppermute | solution.py:57
  23.3 1.0 collective-permute-start
  25.1 20.7 %collective-permute-done.2 = f32[4,264,128]{2,1,0:T(8,128)S(1)} collective-permute-done((f32[4,264,128]{2,1,0:T(8,128)S(1)}, f32[4,264,128]{2,1,0:T(8,128)S(1)}, u32[]{:S(2)}, u32[]{:S(2)}) %collective-permute-start.2) | collective-permute-done | bytes 540704 | tf_op jit(solution)/shard_map/ppermute | solution.py:57
  45.8 3.7 %collective-permute-done = f32[4,264,128]{2,1,0:T(8,128)S(1)} collective-permute-done((f32[4,264,128]{2,1,0:T(8,128)S(1)}, f32[4,264,128]{2,1,0:T(8,128)S(1)}, u32[]{:S(2)}, u32[]{:S(2)}) %collective-permute-start) | collective-permute-done | bytes 540704 | tf_op jit(solution)/shard_map/ppermute | solution.py:57
  49.5 1.5 pad_maximum_fusion.1
  51.0 3.6 %gather_fusion = f32[4,4,264,128]{3,2,1,0:T(8,128)} fusion(f32[4,4,264,128]{3,2,1,0:T(8,128)} %pad_maximum_fusion.1, s32[1024]{0:T(1024)S(1)} %pad_clamp_fusion), kind=kCustom, calls=%fused_computation | custom fusion | bytes 4325392 | tf_op jit(solution)/shard_map/jit(_take)/gather | solution.py:59
  54.6 1.8 broadcast_select_fusion
  56.6 1.3 fusion.33
  58.0 0.9 pad_maximum_fusion.5
  58.9 4.5 %collective-permute-start.3 = (f32[4,136,128]{2,1,0:T(8,128)}, f32[4,136,128]{2,1,0:T(8,128)}, u32[]{:S(2)}, u32[]{:S(2)}) collective-permute-start(f32[4,136,128]{2,1,0:T(8,128)} %get-tuple-element.75), channel_id=1, source_target_pairs={{0,32},{8,40},{16,48},{24,56},{32,64},{40,72},{48,80},{56,88},{64,... | collective-permute-start | bytes 835592 | tf_op jit(solution)/shard_map/ppermute | solution.py:35
  63.5 1.3 collective-permute-start.6
  64.9 4.1 %collective-permute-done.3 = f32[4,136,128]{2,1,0:T(8,128)} collective-permute-done((f32[4,136,128]{2,1,0:T(8,128)}, f32[4,136,128]{2,1,0:T(8,128)}, u32[]{:S(2)}, u32[]{:S(2)}) %collective-permute-start.3) | collective-permute-done | bytes 278560 | tf_op jit(solution)/shard_map/ppermute | solution.py:35
  69.1 0.8 fusion.51
  69.9 4.1 %collective-permute-done.6 = f32[4,136,128]{2,1,0:T(8,128)} collective-permute-done((f32[4,136,128]{2,1,0:T(8,128)}, f32[4,136,128]{2,1,0:T(8,128)}, u32[]{:S(2)}, u32[]{:S(2)}) %collective-permute-start.6) | collective-permute-done | bytes 278560 | tf_op jit(solution)/shard_map/ppermute | solution.py:36
  74.0 1.2 multiply_add_fusion.9
  75.3 6.0 %collective-permute-start.4 = (f32[4,136,128]{2,1,0:T(8,128)S(1)}, f32[4,136,128]{2,1,0:T(8,128)S(1)}, u32[]{:S(2)}, u32[]{:S(2)}) collective-permute-start(f32[4,136,128]{2,1,0:T(8,128)S(1)} %pad_maximum_fusion.6), channel_id=1, source_target_pairs={{0,64},{8,72},{16,80},{24,88},{32,96},{40,104},{48,112},{56,120},{... | collective-permute-start | bytes 835592 | tf_op jit(solution)/shard_map/ppermute | solution.py:35
  81.3 0.8 fusion.53
  82.2 1.3 collective-permute-start.7
  83.6 0.8 slice_reduce_fusion.4
  84.4 2.1 %collective-permute-done.4 = f32[4,136,128]{2,1,0:T(8,128)S(1)} collective-permute-done((f32[4,136,128]{2,1,0:T(8,128)S(1)}, f32[4,136,128]{2,1,0:T(8,128)S(1)}, u32[]{:S(2)}, u32[]{:S(2)}) %collective-permute-start.4) | collective-permute-done | bytes 278560 | tf_op jit(solution)/shard_map/ppermute | solution.py:35
  86.7 7.9 %collective-permute-start.5 = (f32[4,136,128]{2,1,0:T(8,128)S(1)}, f32[4,136,128]{2,1,0:T(8,128)S(1)}, u32[]{:S(2)}, u32[]{:S(2)}) collective-permute-start(f32[4,136,128]{2,1,0:T(8,128)S(1)} %pad_maximum_fusion.7), channel_id=1, source_target_pairs={{0,128},{8,136},{16,144},{24,152},{32,160},{40,168},{48,176},{56,1... | collective-permute-start | bytes 835592 | tf_op jit(solution)/shard_map/ppermute | solution.py:35
  94.6 3.0 %collective-permute-done.7 = f32[4,136,128]{2,1,0:T(8,128)S(1)} collective-permute-done((f32[4,136,128]{2,1,0:T(8,128)S(1)}, f32[4,136,128]{2,1,0:T(8,128)S(1)}, u32[]{:S(2)}, u32[]{:S(2)}) %collective-permute-start.7) | collective-permute-done | bytes 278560 | tf_op jit(solution)/shard_map/ppermute | solution.py:36
  97.7 1.4 collective-permute-start.8
  99.1 0.8 slice_reduce_fusion.2
  100.2 15.8 %collective-permute-done.8 = f32[4,136,128]{2,1,0:T(8,128)S(1)} collective-permute-done((f32[4,136,128]{2,1,0:T(8,128)S(1)}, f32[4,136,128]{2,1,0:T(8,128)S(1)}, u32[]{:S(2)}, u32[]{:S(2)}) %collective-permute-start.8) | collective-permute-done | bytes 278560 | tf_op jit(solution)/shard_map/ppermute | solution.py:36
  116.0 1.5 multiply_add_fusion.4
  117.5 1.2 multiply_add_fusion.1
  120.1 1.3 collective-permute-start.9
  121.4 5.1 %multiply_convert_fusion.1 = bf16[16,384,384]{2,1,0:T(8,128)(2,1)} fusion(f32[16,384]{1,0:T(8,128)S(1)} %get-tuple-element.71, pred[384,384]{1,0:T(8,128)(4,1)S(1)} %copy-done.11, bf16[384,16,128]{0,2,1:T(8,128)(2,1)S(1)} %bitcast.163, bf16[384,16,128]{2,1,0:T(8,128)(2,1)S(1)} %bitcast.165), kind=kOutput, calls=%fused_computation.3 | convolution fusion | flops 615776256 | bytes 8036352 | tf_op jit(solution)/shard_map/shf,thf->hst/dot_general | solution.py:174
  126.5 7.7 %collective-permute-done.11 = f32[4,256,128]{2,1,0:T(8,128)S(1)} collective-permute-done((f32[4,256,128]{2,1,0:T(8,128)S(1)}, f32[4,256,128]{2,1,0:T(8,128)S(1)}, u32[]{:S(2)}, u32[]{:S(2)}) %collective-permute-start.11) | collective-permute-done | bytes 524320 | tf_op jit(solution)/shard_map/ppermute | solution.py:57
  134.2 1.6 collective-permute-done.10
  135.8 9.7 %collective-permute-done.9 = f32[4,256,128]{2,1,0:T(8,128)S(1)} collective-permute-done((f32[4,256,128]{2,1,0:T(8,128)S(1)}, f32[4,256,128]{2,1,0:T(8,128)S(1)}, u32[]{:S(2)}, u32[]{:S(2)}) %collective-permute-start.9) | collective-permute-done | bytes 524320 | tf_op jit(solution)/shard_map/ppermute | solution.py:57
  145.6 1.6 pad_maximum_fusion.3
  147.2 2.9 %copy.92 = f32[4,4,256,128]{2,3,1,0:T(8,128)} copy(f32[4,4,256,128]{3,2,1,0:T(8,128)} %pad_maximum_fusion.3) | data formatting | bytes 4194304 | tf_op jit(solution)/shard_map/stack | solution.py:59
  150.1 3.7 %gather_fusion.1 = f32[4,4,256,128]{2,3,1,0:T(8,128)} fusion(f32[4,4,256,128]{2,3,1,0:T(8,128)} %copy.92, s32[1024]{0:T(1024)S(1)} %pad_clamp_fusion), kind=kCustom, calls=%fused_computation.1 | custom fusion | bytes 4194320 | tf_op jit(solution)/shard_map/jit(_take)/gather | solution.py:59
  153.8 2.9 %copy.93 = f32[4,4,256,128]{3,2,1,0:T(8,128)} copy(f32[4,4,256,128]{2,3,1,0:T(8,128)} %gather_fusion.1) | data formatting | bytes 4194304 | tf_op jit(solution)/shard_map/jit(_take)/gather | solution.py:59
  156.7 2.0 bitcast_select_fusion
  158.7 2.5 %fusion.21 = f32[16,128,384]{2,1,0:T(8,128)S(1)} fusion(bf16[384,16,128]{0,2,1:T(8,128)(2,1)} %bitcast.161, f32[16,256,128]{2,1,0:T(8,128)S(1)} %bitcast_select_fusion), kind=kOutput, calls=%fused_computation.38 | convolution fusion | flops 603979776 | bytes 5767168 | tf_op jit(solution)/shard_map/shf,hef->she/dot_general | solution.py:188
  161.3 1.4 fusion.17
  162.7 2.8 %fusion.10 = (f32[384,16]{0,1:T(8,128)S(1)}, bf16[384,16,128]{0,2,1:T(8,128)(2,1)}) fusion(bf16[384,16,128]{0,2,1:T(8,128)(2,1)S(1)} %bitcast.155, f32[16,128,384]{2,1,0:T(8,128)S(1)} %fusion.21, f32[384,16]{0,1:T(8,128)S(1)} %get-tuple-element.74, bf16[16,384,384]{2,1,0:T(8,128)(2,1)S(1)} %bitcast.159, bf16[384,16,128]{0,2,1:T(8,128)(2,1)S(1)} %bitcast.150), kind=kOutput, calls=%fused_computation.18 | convolution fusion | flops 608692224 | bytes 12632064 | tf_op jit(solution)/shard_map/hst,the->she/dot_general | solution.py:185
  165.5 2.4 %fusion.8 = (f32[384,16]{0,1:T(8,128)S(1)}, bf16[384,16,128]{0,2,1:T(8,128)(2,1)}) fusion(bf16[384,16,128]{0,2,1:T(8,128)(2,1)S(1)} %bitcast.151, f32[16,128,384]{2,1,0:T(8,128)S(1)} %fusion.17, f32[384,16]{0,1:T(8,128)S(1)} %get-tuple-element.73, bf16[384,16,128]{0,2,1:T(8,128)(2,1)S(1)} %bitcast.156, bf16[16,384,384]{2,1,0:T(8,128)(2,1)S(1)} %bitcast.159), kind=kOutput, calls=%fused_computation.16 | convolution fusion | flops 608692224 | bytes 12632064 | tf_op jit(solution)/shard_map/hst,she->the/dot_general | solution.py:191
  168.1 3.5 %collective-permute-done.12 = f32[16]{0:T(128)S(1)} collective-permute-done((f32[16]{0:T(128)S(1)}, f32[16]{0:T(128)S(1)}, u32[]{:S(2)}, u32[]{:S(2)}) %collective-permute-start.12) | collective-permute-done | bytes 96 | tf_op jit(solution)/shard_map/ppermute | solution.py:114
  172.3 4.4 %collective-permute-done.13 = f32[16]{0:T(128)S(1)} collective-permute-done((f32[16]{0:T(128)S(1)}, f32[16]{0:T(128)S(1)}, u32[]{:S(2)}, u32[]{:S(2)}) %collective-permute-start.13) | collective-permute-done | bytes 96 | tf_op jit(solution)/shard_map/ppermute | solution.py:114
  176.7 1.0 collective-permute-start.14
  177.7 2.5 %collective-permute-done.14 = f32[16]{0:T(128)S(1)} collective-permute-done((f32[16]{0:T(128)S(1)}, f32[16]{0:T(128)S(1)}, u32[]{:S(2)}, u32[]{:S(2)}) %collective-permute-start.14) | collective-permute-done | bytes 96 | tf_op jit(solution)/shard_map/ppermute | solution.py:114
  180.6 2.7 %fusion.23 = f32[16,128,384]{2,1,0:T(8,128)} fusion(bf16[384,16,128]{0,2,1:T(8,128)(2,1)S(1)} %bitcast.152, f32[16,256,128]{2,1,0:T(8,128)S(1)} %bitcast_select_fusion), kind=kOutput, calls=%fused_computation.40 | convolution fusion | flops 603979776 | bytes 5767168 | tf_op jit(solution)/shard_map/the,hef->thf/dot_general | solution.py:182
  183.3 1.4 collective-permute-done.15
  184.7 0.8 collective-permute-start.16
  185.5 7.1 %fusion.12 = bf16[384,16,128]{0,2,1:T(8,128)(2,1)} fusion(f32[16,128,384]{2,1,0:T(8,128)} %fusion.23, bf16[384,16,128]{0,2,1:T(8,128)(2,1)} %bitcast.162, f32[16,384]{1,0:T(8,128)S(1)} %get-tuple-element.71, pred[384,384]{1,0:T(8,128)(4,1)S(1)} %copy-done.11, bf16[384,16,128]{0,2,1:T(8,128)(2,1)S(1)} %bitcast.157, bf16[384,16,128]{0,2,1:T(8,128)(2,1)S(1)} %bitcast.153, ...), kind=kOutput, calls=%fused_computation.21 | convolution fusion | flops 1222115328 | bytes 9633792 | tf_op jit(solution)/shard_map/hst,shf->thf/dot_general | solution.py:179
  192.7 2.7 %copy.101 = bf16[1,384,2048]{2,1,0:T(8,128)(2,1)} copy(bf16[1,384,2048]{1,2,0:T(8,128)(2,1)} %bitcast.169) | data formatting | bytes 3145728
  195.3 1.0 collective-permute-start.18
  196.3 1.6 copy.102
  197.9 1.1 collective-permute-done.18
  199.0 1.4 collective-permute-start.19
  200.4 1.6 copy.103
  202.0 2.0 collective-permute-done.19
  (102 shorter events, 9.5 us)
Async XLA Ops:
  0.6 6.2 %copy-start.8 = (bf16[1,384,2048]{2,1,0:T(8,128)(2,1)S(1)}, bf16[1,384,2048]{2,1,0:T(8,128)(2,1)}, u32[]{:S(2)}) copy-start(bf16[1,384,2048]{2,1,0:T(8,128)(2,1)} %param.10) | copy-start | bytes 4718596
  6.8 1.6 copy-start.13
  6.8 1.6 copy-start.12
  14.8 2.9 %copy-start.1 = (bf16[48,8,16,128]{3,2,1,0:T(8,128)(2,1)S(1)}, bf16[48,8,16,128]{3,2,1,0:T(8,128)(2,1)}, u32[]{:S(2)}) copy-start(bf16[48,8,16,128]{3,2,1,0:T(8,128)(2,1)} %copy.110) | copy-start | bytes 4718596
  19.6 26.2 %collective-permute-start.2 = (f32[4,264,128]{2,1,0:T(8,128)S(1)}, f32[4,264,128]{2,1,0:T(8,128)S(1)}, u32[]{:S(2)}, u32[]{:S(2)}) collective-permute-start(f32[4,264,128]{2,1,0:T(8,128)S(1)} %get-tuple-element.54), channel_id=1, source_target_pairs={{0,24},{8,0},{16,8},{24,16},{32,56},{40,32},{48,40},{56,48},{64,88... | collective-permute-start | bytes 1622024 | tf_op jit(solution)/shard_map/ppermute | solution.py:57
  22.7 23.1 %collective-permute-start.1 = (f32[4,264,128]{2,1,0:T(8,128)S(1)}, f32[4,264,128]{2,1,0:T(8,128)S(1)}, u32[]{:S(2)}, u32[]{:S(2)}) collective-permute-start(f32[4,264,128]{2,1,0:T(8,128)S(1)} %get-tuple-element.55), channel_id=1, source_target_pairs={{0,16},{8,24},{16,0},{24,8},{32,48},{40,56},{48,32},{56,40},{64,80... | collective-permute-start | bytes 1622024 | tf_op jit(solution)/shard_map/ppermute | solution.py:57
  23.3 26.2 %collective-permute-start = (f32[4,264,128]{2,1,0:T(8,128)S(1)}, f32[4,264,128]{2,1,0:T(8,128)S(1)}, u32[]{:S(2)}, u32[]{:S(2)}) collective-permute-start(f32[4,264,128]{2,1,0:T(8,128)S(1)} %get-tuple-element.56), channel_id=1, source_target_pairs={{0,8},{8,16},{16,24},{24,0},{32,40},{40,48},{48,56},{56,32},{64,72... | collective-permute-start | bytes 1622024 | tf_op jit(solution)/shard_map/ppermute | solution.py:57
  56.5 2.4 %copy-start.4 = (f32[4,4,264,128]{3,2,1,0:T(8,128)}, f32[4,4,264,128]{3,2,1,0:T(8,128)S(1)}, u32[]{:S(2)}) copy-start(f32[4,4,264,128]{3,2,1,0:T(8,128)S(1)} %broadcast_select_fusion) | copy-start | bytes 6488068
  57.9 1.0 copy-start.6
  58.9 10.2 %collective-permute-start.3 = (f32[4,136,128]{2,1,0:T(8,128)}, f32[4,136,128]{2,1,0:T(8,128)}, u32[]{:S(2)}, u32[]{:S(2)}) collective-permute-start(f32[4,136,128]{2,1,0:T(8,128)} %get-tuple-element.75), channel_id=1, source_target_pairs={{0,32},{8,40},{16,48},{24,56},{32,64},{40,72},{48,80},{56,88},{64,... | collective-permute-start | bytes 835592 | tf_op jit(solution)/shard_map/ppermute | solution.py:35
  63.5 10.5 %collective-permute-start.6 = (f32[4,136,128]{2,1,0:T(8,128)}, f32[4,136,128]{2,1,0:T(8,128)}, u32[]{:S(2)}, u32[]{:S(2)}) collective-permute-start(f32[4,136,128]{2,1,0:T(8,128)} %get-tuple-element.76), channel_id=1, source_target_pairs={{32,0},{40,8},{48,16},{56,24},{64,32},{72,40},{80,48},{88,56},{96,... | collective-permute-start | bytes 835592 | tf_op jit(solution)/shard_map/ppermute | solution.py:36
  75.2 40.8 %copy-start.7 = (f32[4,128,128]{2,1,0:T(8,128)S(1)}, f32[4,128,128]{2,1,0:T(8,128)}, u32[]{:S(2)}) copy-start(f32[4,128,128]{2,1,0:T(8,128)} %get-tuple-element.48) | copy-start | bytes 786436
  75.3 11.3 %collective-permute-start.4 = (f32[4,136,128]{2,1,0:T(8,128)S(1)}, f32[4,136,128]{2,1,0:T(8,128)S(1)}, u32[]{:S(2)}, u32[]{:S(2)}) collective-permute-start(f32[4,136,128]{2,1,0:T(8,128)S(1)} %pad_maximum_fusion.6), channel_id=1, source_target_pairs={{0,64},{8,72},{16,80},{24,88},{32,96},{40,104},{48,112},{56,120},{... | collective-permute-start | bytes 835592 | tf_op jit(solution)/shard_map/ppermute | solution.py:35
  82.2 15.3 %collective-permute-start.7 = (f32[4,136,128]{2,1,0:T(8,128)S(1)}, f32[4,136,128]{2,1,0:T(8,128)S(1)}, u32[]{:S(2)}, u32[]{:S(2)}) collective-permute-start(f32[4,136,128]{2,1,0:T(8,128)S(1)} %pad_maximum_fusion.8), channel_id=1, source_target_pairs={{64,0},{72,8},{80,16},{88,24},{96,32},{104,40},{112,48},{120,56},{... | collective-permute-start | bytes 835592 | tf_op jit(solution)/shard_map/ppermute | solution.py:36
  86.7 13.5 %collective-permute-start.5 = (f32[4,136,128]{2,1,0:T(8,128)S(1)}, f32[4,136,128]{2,1,0:T(8,128)S(1)}, u32[]{:S(2)}, u32[]{:S(2)}) collective-permute-start(f32[4,136,128]{2,1,0:T(8,128)S(1)} %pad_maximum_fusion.7), channel_id=1, source_target_pairs={{0,128},{8,136},{16,144},{24,152},{32,160},{40,168},{48,176},{56,1... | collective-permute-start | bytes 835592 | tf_op jit(solution)/shard_map/ppermute | solution.py:35
  97.6 19.8 %copy-start.10 = (f32[4,128,128]{2,1,0:T(8,128)S(1)}, f32[4,128,128]{2,1,0:T(8,128)}, u32[]{:S(2)}) copy-start(f32[4,128,128]{2,1,0:T(8,128)} %get-tuple-element.35) | copy-start | bytes 786436
  97.7 18.3 %collective-permute-start.8 = (f32[4,136,128]{2,1,0:T(8,128)S(1)}, f32[4,136,128]{2,1,0:T(8,128)S(1)}, u32[]{:S(2)}, u32[]{:S(2)}) collective-permute-start(f32[4,136,128]{2,1,0:T(8,128)S(1)} %pad_maximum_fusion.9), channel_id=1, source_target_pairs={{128,0},{136,8},{144,16},{152,24},{160,32},{168,40},{176,48},{184,... | collective-permute-start | bytes 835592 | tf_op jit(solution)/shard_map/ppermute | solution.py:36
  119.1 2.3 %copy-start = (bf16[1,384,2048]{1,2,0:T(8,128)(2,1)S(1)}, bf16[1,384,2048]{1,2,0:T(8,128)(2,1)}, u32[]{:S(2)}) copy-start(bf16[1,384,2048]{1,2,0:T(8,128)(2,1)} %copy.108) | copy-start | bytes 4718596
  119.1 2.3 %copy-start.2 = (bf16[48,8,16,128]{3,2,1,0:T(8,128)(2,1)S(1)}, bf16[48,8,16,128]{3,2,1,0:T(8,128)(2,1)}, u32[]{:S(2)}) copy-start(bf16[48,8,16,128]{3,2,1,0:T(8,128)(2,1)} %copy.110) | copy-start | bytes 4718596
  119.1 2.3 %copy-start.11 = (pred[384,384]{1,0:T(8,128)(4,1)S(1)}, pred[384,384]{1,0:T(8,128)(4,1)}, u32[]{:S(2)}) copy-start(pred[384,384]{1,0:T(8,128)(4,1)} %fusion.26) | copy-start | bytes 442372
  119.3 14.9 %collective-permute-start.11 = (f32[4,256,128]{2,1,0:T(8,128)S(1)}, f32[4,256,128]{2,1,0:T(8,128)S(1)}, u32[]{:S(2)}, u32[]{:S(2)}) collective-permute-start(f32[4,256,128]{2,1,0:T(8,128)S(1)} %get-tuple-element.58), channel_id=1, source_target_pairs={{0,24},{8,0},{16,8},{24,16},{32,56},{40,32},{48,40},{56,48},{64,88... | collective-permute-start | bytes 1572872 | tf_op jit(solution)/shard_map/ppermute | solution.py:57
  119.4 16.5 %collective-permute-start.10 = (f32[4,256,128]{2,1,0:T(8,128)S(1)}, f32[4,256,128]{2,1,0:T(8,128)S(1)}, u32[]{:S(2)}, u32[]{:S(2)}) collective-permute-start(f32[4,256,128]{2,1,0:T(8,128)S(1)} %get-tuple-element.59), channel_id=1, source_target_pairs={{0,16},{8,24},{16,0},{24,8},{32,48},{40,56},{48,32},{56,40},{64,80... | collective-permute-start | bytes 1572872 | tf_op jit(solution)/shard_map/ppermute | solution.py:57
  120.1 25.5 %collective-permute-start.9 = (f32[4,256,128]{2,1,0:T(8,128)S(1)}, f32[4,256,128]{2,1,0:T(8,128)S(1)}, u32[]{:S(2)}, u32[]{:S(2)}) collective-permute-start(f32[4,256,128]{2,1,0:T(8,128)S(1)} %get-tuple-element.60), channel_id=1, source_target_pairs={{0,8},{8,16},{16,24},{24,0},{32,40},{40,48},{48,56},{56,32},{64,72... | collective-permute-start | bytes 1572872 | tf_op jit(solution)/shard_map/ppermute | solution.py:57
  156.7 6.0 %slice-start = ((s8[4718592]{0:T(1024)(128)(4,1)}), s8[4194304]{0:T(1024)(128)(4,1)S(1)}, s32[]{:S(2)}) async-start(s8[4718592]{0:T(1024)(128)(4,1)} %bitcast.158), calls=%async_computation | async-start | bytes 8388608
  158.7 2.6 %copy-start.3 = (bf16[48,8,16,128]{3,2,1,0:T(8,128)(2,1)S(1)}, bf16[48,8,16,128]{3,2,1,0:T(8,128)(2,1)}, u32[]{:S(2)}) copy-start(bf16[48,8,16,128]{3,2,1,0:T(8,128)(2,1)} %copy.110) | copy-start | bytes 4718596
  158.7 4.0 %slice-start.1 = ((s8[4718592]{0:T(1024)(128)(4,1)}), s8[524288]{0:T(1024)(128)(4,1)S(1)}, s32[]{:S(2)}) async-start(s8[4718592]{0:T(1024)(128)(4,1)} %bitcast.158), calls=%async_computation.1 | async-start | bytes 1048576
  168.0 3.6 %collective-permute-start.12 = (f32[16]{0:T(128)S(1)}, f32[16]{0:T(128)S(1)}, u32[]{:S(2)}, u32[]{:S(2)}) collective-permute-start(f32[16]{0:T(128)S(1)} %multiply_reduce_fusion), channel_id=1, source_target_pairs={{0,8},{8,0},{16,24},{24,16},{32,40},{40,32},{48,56},{56,48},{64,72... | collective-permute-start | bytes 200 | tf_op jit(solution)/shard_map/ppermute | solution.py:114
  171.6 5.0 %collective-permute-start.13 = (f32[16]{0:T(128)S(1)}, f32[16]{0:T(128)S(1)}, u32[]{:S(2)}, u32[]{:S(2)}) collective-permute-start(f32[16]{0:T(128)S(1)} %add.237), channel_id=1, source_target_pairs={{0,16},{8,24},{16,0},{24,8},{32,48},{40,56},{48,32},{56,40},{64,80... | collective-permute-start | bytes 200 | tf_op jit(solution)/shard_map/ppermute | solution.py:114
  176.7 3.5 %collective-permute-start.14 = (f32[16]{0:T(128)S(1)}, f32[16]{0:T(128)S(1)}, u32[]{:S(2)}, u32[]{:S(2)}) collective-permute-start(f32[16]{0:T(128)S(1)} %add.238), channel_id=1, source_target_pairs={{0,32},{8,40},{16,48},{24,56},{32,0},{40,8},{48,16},{56,24},{64,96... | collective-permute-start | bytes 200 | tf_op jit(solution)/shard_map/ppermute | solution.py:114
  180.2 4.4 %collective-permute-start.15 = (f32[16]{0:T(128)S(1)}, f32[16]{0:T(128)S(1)}, u32[]{:S(2)}, u32[]{:S(2)}) collective-permute-start(f32[16]{0:T(128)S(1)} %add.239), channel_id=1, source_target_pairs={{0,64},{8,72},{16,80},{24,88},{32,96},{40,104},{48,112},{56,120},{... | collective-permute-start | bytes 200 | tf_op jit(solution)/shard_map/ppermute | solution.py:114
  184.7 7.9 %collective-permute-start.16 = (f32[16]{0:T(128)S(1)}, f32[16]{0:T(128)S(1)}, u32[]{:S(2)}, u32[]{:S(2)}) collective-permute-start(f32[16]{0:T(128)S(1)} %add.240), channel_id=1, source_target_pairs={{0,128},{8,136},{16,144},{24,152},{32,160},{40,168},{48,176},{56,1... | collective-permute-start | bytes 200 | tf_op jit(solution)/shard_map/ppermute | solution.py:114
  192.5 3.8 %copy-start.5 = (bf16[384,16,128]{0,2,1:T(8,128)(2,1)S(1)}, bf16[384,16,128]{0,2,1:T(8,128)(2,1)}, u32[]{:S(2)}) copy-start(bf16[384,16,128]{0,2,1:T(8,128)(2,1)} %get-tuple-element.46) | copy-start | bytes 4718596
  192.6 2.8 %collective-permute-start.17 = (f32[16]{0:T(128)S(1)}, f32[16]{0:T(128)S(1)}, u32[]{:S(2)}, u32[]{:S(2)}) collective-permute-start(f32[16]{0:T(128)S(1)} %add.241), channel_id=1, source_target_pairs={{0,1},{1,0},{2,3},{3,2},{4,5},{5,4},{6,7},{7,6},{8,9},{9,8},{10,11... | collective-permute-start | bytes 200 | tf_op jit(solution)/shard_map/ppermute | solution.py:114
  195.3 5.1 %copy-start.9 = (bf16[384,16,128]{0,2,1:T(8,128)(2,1)S(1)}, bf16[384,16,128]{0,2,1:T(8,128)(2,1)}, u32[]{:S(2)}) copy-start(bf16[384,16,128]{0,2,1:T(8,128)(2,1)} %fusion.12) | copy-start | bytes 4718596
  195.3 3.7 %collective-permute-start.18 = (f32[16]{0:T(128)S(1)}, f32[16]{0:T(128)S(1)}, u32[]{:S(2)}, u32[]{:S(2)}) collective-permute-start(f32[16]{0:T(128)S(1)} %add.242), channel_id=1, source_target_pairs={{0,2},{1,3},{2,0},{3,1},{4,6},{5,7},{6,4},{7,5},{8,10},{9,11},{10,... | collective-permute-start | bytes 200 | tf_op jit(solution)/shard_map/ppermute | solution.py:114
  199.0 5.0 %collective-permute-start.19 = (f32[16]{0:T(128)S(1)}, f32[16]{0:T(128)S(1)}, u32[]{:S(2)}, u32[]{:S(2)}) collective-permute-start(f32[16]{0:T(128)S(1)} %add.243), channel_id=1, source_target_pairs={{0,4},{1,5},{2,6},{3,7},{4,0},{5,1},{6,2},{7,3},{8,12},{9,13},{10,... | collective-permute-start | bytes 200 | tf_op jit(solution)/shard_map/ppermute | solution.py:114

commit v4 on v3

--- a/solution.py
+++ b/solution.py
@@ -182,20 +182,37 @@
     value_full = value_full + carry_out[:, :, None] * jnp.einsum(
         "the,hef->thf", key_f, backward_input, precision=state_mode
     )
-    query_full = jnp.einsum(
+    query_local = jnp.einsum(
         "hst,the->she", grad_prob, key_block, preferred_element_type=jnp.float32
     )
-    query_full = query_full + carry_in[:, :, None] * jnp.einsum(
+    key_local = jnp.einsum(
+        "hst,she->the", grad_prob, query_block, preferred_element_type=jnp.float32
+    )
+    local_step = jnp.sum(key_f * key_local, axis=2) - jnp.sum(query_f * query_local, axis=2)
+    rate_local = jnp.sum(position[:, None] * local_step, axis=0)
+    key_moment = jnp.einsum(
+        "the,thf->hef",
+        (position[:, None] * carry_out)[:, :, None] * key_f,
+        value_f,
+        precision=state_mode,
+    )
+    query_moment = jnp.einsum(
+        "she,shf->hef",
+        (position[:, None] * carry_in)[:, :, None] * query_f,
+        grad_f,
+        precision=state_mode,
+    )
+    rate_part = (
+        rate_local
+        + jnp.sum(key_moment * backward_input, axis=(1, 2))
+        - jnp.sum(query_moment * state_input, axis=(1, 2))
+    )
+    query_full = query_local + carry_in[:, :, None] * jnp.einsum(
         "shf,hef->she", grad_f, state_input, precision=state_mode
     )
-    key_full = jnp.einsum(
-        "hst,she->the", grad_prob, query_block, preferred_element_type=jnp.float32
-    )
-    key_full = key_full + carry_out[:, :, None] * jnp.einsum(
+    key_full = key_local + carry_out[:, :, None] * jnp.einsum(
         "thf,hef->the", value_f, backward_input, precision=state_mode
     )
-    inner_step = jnp.sum(key_f * key_full, axis=2) - jnp.sum(query_f * query_full, axis=2)
-    rate_part = jnp.sum(position[:, None] * inner_step, axis=0)
     rate_total = all_sum(rate_part, ("seq", "dp"))
     token_total = row_count * lax.axis_size("seq") * lax.axis_size("dp")
     rate_grad = head_decay_rate * rate_total / math.sqrt(token_total)

time: 205 us -> 213 us (1.039)
  waiting for transfers between devices: 87.5 us -> 93.7 us
  matrix products: 28.3 us -> 33.7 us
  other arithmetic: 21.1 us -> 18 us
  local copies, waits for them, and re-layouts: 31.2 us -> 28.5 us
  starting transfers between devices: 34.7 us -> 36.9 us
    ppermute x6, waiting for transfers between devices: 43.4 us -> 48.6 us  [row_exchange(): got.append(lax.ppermute(send, axis, pairs))]
    dot_general x0 -> x2, matrix products: none -> 3.05 us  [the longest x1 1.53 us: on_device(): jnp.einsum('the,thf->hef', (position[:, None] * carry_out)[:, :, None] *...]
    ppermute x8, starting transfers between devices: 5.41 us -> 7.98 us  [all_sum(): lax.ppermute(value, axis, [(i, i ^ step) for i in range(count)])]
    unnamed x38 -> x29, local copies, waits for them, and re-layouts: 12.7 us -> 11.9 us
  transfers between devices with their start and end apart: 20 -> 20, of which waited for: 16 -> 15; matrix products, arithmetic and copies ran while one was open for 13% -> 10% of each run, Pallas kernels for 0% -> 0%
where the time goes in v4:
time: 213 us
  waiting for transfers between devices  93.7 us (44%)
  starting transfers between devices  36.9 us (17%)
  matrix products  33.7 us (16%)
  local copies, waits for them, and re-layouts  28.5 us (13%)
  other arithmetic  18 us (8%)
    ppermute x6, waiting for transfers between devices, row_exchange(): got.append(lax.ppermute(send, axis, pairs))  48.6 us
    ppermute x3, waiting for transfers between devices, group_scan(): rgot = lax.ppermute(bwd, axis, down)  23 us
    ppermute x3, starting transfers between devices, group_scan(): got = lax.ppermute(fwd, axis, up)  18.2 us
    ppermute x8, waiting for transfers between devices, all_sum(): lax.ppermute(value, axis, [(i, i ^ step) for i in range(count)])  14 us
    unnamed x29, local copies, waits for them, and re-layouts  11.9 us
    gather x3, local copies, waits for them, and re-layouts, row_exchange(): return jnp.take(jnp.stack(got), order, axis=0)  10.2 us
    ppermute x3, waiting for transfers between devices, group_scan(): got = lax.ppermute(fwd, axis, up)  8.14 us
    ppermute x8, starting transfers between devices, all_sum(): lax.ppermute(value, axis, [(i, i ^ step) for i in range(count)])  7.98 us
  transfers between devices with their start and end apart: 20, of which 15 were waited for; matrix products, arithmetic and copies ran while one was open for 10% of the time, Pallas kernels for 0%

profile of v4, /device:TPU:6, one launch (start us, length us, event | category | flops | bytes accessed | tf_op | source)
XLA Modules:
  0.0 212.6 jit_solution(9076166632247957380)
XLA Ops:
  0.7 0.8 reduce-window_clone.1
  1.5 0.7 subtract_bitcast_fusion
  4.2 0.7 broadcast_compare_fusion
  5.0 0.7 multiply_reduce_fusion.1
  5.7 0.7 broadcast_subtract_fusion
  6.5 0.9 reduce-window.24
  7.6 1.9 copy.79
  9.5 1.9 copy.77
  11.4 1.9 copy.101
  13.8 4.0 %multiply_convert_fusion.1 = bf16[16,384,384]{2,1,0:T(8,128)(2,1)S(1)} fusion(f32[16,384]{1,0:T(8,128)S(1)} %get-tuple-element.68, pred[384,384]{1,0:T(8,128)(4,1)S(1)} %fusion.40, bf16[384,16,128]{2,1,0:T(8,128)(2,1)S(1)} %bitcast.169, bf16[384,16,128]{2,1,0:T(8,128)(2,1)S(1)} %bitcast.173), kind=kOutput, calls=%fused_computation.3 | convolution fusion | flops 615776256 | bytes 8036352 | tf_op jit(solution)/shard_map/shf,thf->hst/dot_general | solution.py:174
  17.8 3.3 %fusion.11 = (f32[384,16]{0,1:T(8,128)S(1)}, f32[16,384,128]{1,2,0:T(8,128)}) fusion(bf16[384,16,128]{0,2,1:T(8,128)(2,1)S(1)} %bitcast.164, bf16[16,384,384]{2,1,0:T(8,128)(2,1)S(1)} %multiply_convert_fusion.1, bf16[384,16,128]{0,2,1:T(8,128)(2,1)S(1)} %bitcast.158), kind=kOutput, calls=%fused_computation.21 | convolution fusion | flops 606332928 | bytes 11034624 | tf_op jit(solution)/shard_map/hst,the->she/dot_general | solution.py:185
  21.1 2.9 %fusion.8 = (f32[384,16]{0,1:T(8,128)S(1)}, f32[16,384,128]{1,2,0:T(8,128)}) fusion(bf16[384,16,128]{0,2,1:T(8,128)(2,1)S(1)} %bitcast.159, bf16[384,16,128]{0,2,1:T(8,128)(2,1)S(1)} %bitcast.165, bf16[16,384,384]{2,1,0:T(8,128)(2,1)S(1)} %multiply_convert_fusion.1), kind=kOutput, calls=%fused_computation.18 | convolution fusion | flops 606332928 | bytes 11034624 | tf_op jit(solution)/shard_map/hst,she->the/dot_general | solution.py:188
  24.4 2.4 %fusion.10 = f32[16,128,128]{2,1,0:T(8,128)} fusion(bf16[384,16,128]{0,2,1:T(8,128)(2,1)S(1)} %bitcast.166, f32[384,16]{0,1:T(8,128)S(1)} %get-tuple-element.25, bf16[384,16,128]{2,1,0:T(8,128)(2,1)S(1)} %bitcast.174), kind=kOutput, calls=%fused_computation.20 | convolution fusion | flops 605552640 | bytes 4218880 | tf_op jit(solution)/shard_map/she,shf->hef/dot_general | solution.py:168
  26.8 2.4 %fusion.7 = f32[16,128,128]{2,1,0:T(8,128)} fusion(bf16[384,16,128]{0,2,1:T(8,128)(2,1)S(1)} %bitcast.160, f32[384,16]{0,1:T(8,128)S(1)} %get-tuple-element.66, bf16[384,16,128]{2,1,0:T(8,128)(2,1)S(1)} %bitcast.170), kind=kOutput, calls=%fused_computation.17 | convolution fusion | flops 605552640 | bytes 4218880 | tf_op jit(solution)/shard_map/the,thf->hef/dot_general | solution.py:165
  29.2 1.7 pad_maximum_fusion
  31.1 3.1 %collective-permute-start.2 = (f32[4,264,128]{2,1,0:T(8,128)S(1)}, f32[4,264,128]{2,1,0:T(8,128)S(1)}, u32[]{:S(2)}, u32[]{:S(2)}) collective-permute-start(f32[4,264,128]{2,1,0:T(8,128)S(1)} %get-tuple-element.48), channel_id=1, source_target_pairs={{0,24},{8,0},{16,8},{24,16},{32,56},{40,32},{48,40},{56,48},{64,88... | collective-permute-start | bytes 1622024 | tf_op jit(solution)/shard_map/ppermute | solution.py:57
  34.2 0.6 collective-permute-start.1
  34.8 1.0 collective-permute-start
  35.8 21.5 %collective-permute-done.2 = f32[4,264,128]{2,1,0:T(8,128)S(1)} collective-permute-done((f32[4,264,128]{2,1,0:T(8,128)S(1)}, f32[4,264,128]{2,1,0:T(8,128)S(1)}, u32[]{:S(2)}, u32[]{:S(2)}) %collective-permute-start.2) | collective-permute-done | bytes 540704 | tf_op jit(solution)/shard_map/ppermute | solution.py:57
  57.3 3.7 %collective-permute-done = f32[4,264,128]{2,1,0:T(8,128)S(1)} collective-permute-done((f32[4,264,128]{2,1,0:T(8,128)S(1)}, f32[4,264,128]{2,1,0:T(8,128)S(1)}, u32[]{:S(2)}, u32[]{:S(2)}) %collective-permute-start) | collective-permute-done | bytes 540704 | tf_op jit(solution)/shard_map/ppermute | solution.py:57
  61.0 1.5 pad_maximum_fusion.1
  62.5 3.7 %gather_fusion = f32[4,4,264,128]{3,2,1,0:T(8,128)} fusion(f32[4,4,264,128]{3,2,1,0:T(8,128)} %pad_maximum_fusion.1, s32[1024]{0:T(1024)S(1)} %pad_clamp_fusion), kind=kCustom, calls=%fused_computation | custom fusion | bytes 4325392 | tf_op jit(solution)/shard_map/jit(_take)/gather | solution.py:59
  66.2 1.8 broadcast_select_fusion
  68.5 3.8 %collective-permute-start.3 = (f32[4,136,128]{2,1,0:T(8,128)S(1)}, f32[4,136,128]{2,1,0:T(8,128)S(1)}, u32[]{:S(2)}, u32[]{:S(2)}) collective-permute-start(f32[4,136,128]{2,1,0:T(8,128)S(1)} %get-tuple-element.69), channel_id=1, source_target_pairs={{0,32},{8,40},{16,48},{24,56},{32,64},{40,72},{48,80},{56,88},{64,... | collective-permute-start | bytes 835592 | tf_op jit(solution)/shard_map/ppermute | solution.py:35
  72.4 1.5 collective-permute-start.6
  73.8 4.6 %collective-permute-done.3 = f32[4,136,128]{2,1,0:T(8,128)S(1)} collective-permute-done((f32[4,136,128]{2,1,0:T(8,128)S(1)}, f32[4,136,128]{2,1,0:T(8,128)S(1)}, u32[]{:S(2)}, u32[]{:S(2)}) %collective-permute-start.3) | collective-permute-done | bytes 278560 | tf_op jit(solution)/shard_map/ppermute | solution.py:35
  78.5 4.2 %collective-permute-done.6 = f32[4,136,128]{2,1,0:T(8,128)S(1)} collective-permute-done((f32[4,136,128]{2,1,0:T(8,128)S(1)}, f32[4,136,128]{2,1,0:T(8,128)S(1)}, u32[]{:S(2)}, u32[]{:S(2)}) %collective-permute-start.6) | collective-permute-done | bytes 278560 | tf_op jit(solution)/shard_map/ppermute | solution.py:36
  82.9 6.4 %collective-permute-start.4 = (f32[4,136,128]{2,1,0:T(8,128)S(1)}, f32[4,136,128]{2,1,0:T(8,128)S(1)}, u32[]{:S(2)}, u32[]{:S(2)}) collective-permute-start(f32[4,136,128]{2,1,0:T(8,128)S(1)} %pad_maximum_fusion.6), channel_id=1, source_target_pairs={{0,64},{8,72},{16,80},{24,88},{32,96},{40,104},{48,112},{56,120},{... | collective-permute-start | bytes 835592 | tf_op jit(solution)/shard_map/ppermute | solution.py:35
  89.5 1.3 collective-permute-start.7
  91.0 3.5 %collective-permute-done.4 = f32[4,136,128]{2,1,0:T(8,128)S(1)} collective-permute-done((f32[4,136,128]{2,1,0:T(8,128)S(1)}, f32[4,136,128]{2,1,0:T(8,128)S(1)}, u32[]{:S(2)}, u32[]{:S(2)}) %collective-permute-start.4) | collective-permute-done | bytes 278560 | tf_op jit(solution)/shard_map/ppermute | solution.py:35
  94.7 7.9 %collective-permute-start.5 = (f32[4,136,128]{2,1,0:T(8,128)S(1)}, f32[4,136,128]{2,1,0:T(8,128)S(1)}, u32[]{:S(2)}, u32[]{:S(2)}) collective-permute-start(f32[4,136,128]{2,1,0:T(8,128)S(1)} %pad_maximum_fusion.7), channel_id=1, source_target_pairs={{0,128},{8,136},{16,144},{24,152},{32,160},{40,168},{48,176},{56,1... | collective-permute-start | bytes 835592 | tf_op jit(solution)/shard_map/ppermute | solution.py:35
  102.6 2.2 %collective-permute-done.7 = f32[4,136,128]{2,1,0:T(8,128)S(1)} collective-permute-done((f32[4,136,128]{2,1,0:T(8,128)S(1)}, f32[4,136,128]{2,1,0:T(8,128)S(1)}, u32[]{:S(2)}, u32[]{:S(2)}) %collective-permute-start.7) | collective-permute-done | bytes 278560 | tf_op jit(solution)/shard_map/ppermute | solution.py:36
  105.0 1.3 collective-permute-start.8
  106.7 16.5 %collective-permute-done.8 = f32[4,136,128]{2,1,0:T(8,128)S(1)} collective-permute-done((f32[4,136,128]{2,1,0:T(8,128)S(1)}, f32[4,136,128]{2,1,0:T(8,128)S(1)}, u32[]{:S(2)}, u32[]{:S(2)}) %collective-permute-start.8) | collective-permute-done | bytes 278560 | tf_op jit(solution)/shard_map/ppermute | solution.py:36
  124.0 1.4 constant_dynamic-slice_fusion
  125.3 0.6 collective-permute-start.10
  126.0 1.4 collective-permute-start.9
  127.5 13.0 %collective-permute-done.11 = f32[4,256,128]{2,1,0:T(8,128)} collective-permute-done((f32[4,256,128]{2,1,0:T(8,128)}, f32[4,256,128]{2,1,0:T(8,128)}, u32[]{:S(2)}, u32[]{:S(2)}) %collective-permute-start.11) | collective-permute-done | bytes 524320 | tf_op jit(solution)/shard_map/ppermute | solution.py:57
  140.5 1.6 collective-permute-done.10
  142.1 8.9 %collective-permute-done.9 = f32[4,256,128]{2,1,0:T(8,128)} collective-permute-done((f32[4,256,128]{2,1,0:T(8,128)}, f32[4,256,128]{2,1,0:T(8,128)}, u32[]{:S(2)}, u32[]{:S(2)}) %collective-permute-start.9) | collective-permute-done | bytes 524320 | tf_op jit(solution)/shard_map/ppermute | solution.py:57
  150.9 3.1 %pad_maximum_fusion.3 = f32[4,4,256,128]{3,2,1,0:T(8,128)} fusion(f32[1,4,256,128]{3,2,1,0:T(8,128)} %bitcast.33, f32[1,4,256,128]{3,2,1,0:T(8,128)} %bitcast.31, f32[1,4,256,128]{3,2,1,0:T(8,128)} %bitcast.29, f32[1,4,256,128]{3,2,1,0:T(8,128)} %get-tuple-element.51), kind=kLoop, calls=%fused_computation.35 | loop fusion | flops 1572864 | bytes 4194304 | tf_op jit(solution)/shard_map/stack | solution.py:59
  154.0 3.0 %copy.81 = f32[4,4,256,128]{2,3,1,0:T(8,128)} copy(f32[4,4,256,128]{3,2,1,0:T(8,128)} %pad_maximum_fusion.3) | data formatting | bytes 4194304 | tf_op jit(solution)/shard_map/stack | solution.py:59
  156.9 3.6 %gather_fusion.1 = f32[4,4,256,128]{2,3,1,0:T(8,128)} fusion(f32[4,4,256,128]{2,3,1,0:T(8,128)} %copy.81, s32[1024]{0:T(1024)S(1)} %pad_clamp_fusion), kind=kCustom, calls=%fused_computation.1 | custom fusion | bytes 4194320 | tf_op jit(solution)/shard_map/jit(_take)/gather | solution.py:59
  160.6 3.0 %copy.82 = f32[4,4,256,128]{3,2,1,0:T(8,128)} copy(f32[4,4,256,128]{2,3,1,0:T(8,128)} %gather_fusion.1) | data formatting | bytes 4194304 | tf_op jit(solution)/shard_map/jit(_take)/gather | solution.py:59
  163.5 2.0 bitcast_select_fusion
  165.6 1.5 fusion.25
  167.7 1.5 fusion.26
  169.3 3.5 %collective-permute-done.12 = f32[16]{0:T(128)S(1)} collective-permute-done((f32[16]{0:T(128)S(1)}, f32[16]{0:T(128)S(1)}, u32[]{:S(2)}, u32[]{:S(2)}) %collective-permute-start.12) | collective-permute-done | bytes 96 | tf_op jit(solution)/shard_map/ppermute | solution.py:114
  172.9 0.6 collective-permute-start.13
  173.5 2.8 %fusion.32 = f32[16,128,384]{2,1,0:T(8,128)} fusion(bf16[384,16,128]{0,2,1:T(8,128)(2,1)S(1)} %bitcast.162, f32[16,256,128]{2,1,0:T(8,128)S(1)} %bitcast_select_fusion), kind=kOutput, calls=%fused_computation.51 | convolution fusion | flops 603979776 | bytes 5767168 | tf_op jit(solution)/shard_map/the,hef->thf/dot_general | solution.py:182
  176.3 1.7 collective-permute-done.13
  177.9 2.9 %collective-permute-start.14 = (f32[16]{0:T(128)S(1)}, f32[16]{0:T(128)S(1)}, u32[]{:S(2)}, u32[]{:S(2)}) collective-permute-start(f32[16]{0:T(128)S(1)} %add.242), channel_id=1, source_target_pairs={{0,32},{8,40},{16,48},{24,56},{32,0},{40,8},{48,16},{56,24},{64,96... | collective-permute-start | bytes 200 | tf_op jit(solution)/shard_map/ppermute | solution.py:114
  180.8 7.0 %fusion.14 = bf16[384,16,128]{0,2,1:T(8,128)(2,1)} fusion(f32[16,128,384]{2,1,0:T(8,128)} %fusion.32, f32[16,384]{1,0:T(8,128)S(1)} %get-tuple-element.68, pred[384,384]{1,0:T(8,128)(4,1)S(1)} %fusion.40, bf16[384,16,128]{0,2,1:T(8,128)(2,1)S(1)} %bitcast.168, bf16[384,16,128]{0,2,1:T(8,128)(2,1)S(1)} %bitcast.163, f32[384,16]{0,1:T(8,128)S(1)} %get-tuple-element.66, ...), kind=kOutput, calls=%fused_computation.25 | convolution fusion | flops 1222115328 | bytes 9633792 | tf_op jit(solution)/shard_map/hst,shf->thf/dot_general | solution.py:179
  187.8 2.0 collective-permute-start.15
  189.9 4.3 %fusion.18 = bf16[384,16,128]{0,2,1:T(8,128)(2,1)S(1)} fusion(f32[16,384,128]{1,2,0:T(8,128)} %get-tuple-element.81, f32[384,16]{0,1:T(8,128)S(1)} %get-tuple-element.25, f32[16,256,128]{2,1,0:T(8,128)} %copy-done.5, bf16[384,16,128]{2,1,0:T(8,128)(2,1)} %bitcast.176), kind=kOutput, calls=%fused_computation.31 | convolution fusion | flops 606339072 | bytes 7364608 | tf_op jit(solution)/shard_map/shf,hef->she/dot_general | solution.py:210
  194.6 1.5 fusion.16
  196.1 5.7 %collective-permute-done.16 = f32[16]{0:T(128)S(1)} collective-permute-done((f32[16]{0:T(128)S(1)}, f32[16]{0:T(128)S(1)}, u32[]{:S(2)}, u32[]{:S(2)}) %collective-permute-start.16) | collective-permute-done | bytes 96 | tf_op jit(solution)/shard_map/ppermute | solution.py:114
  201.8 1.6 copy.93
  203.4 0.9 collective-permute-start.18
  204.3 1.6 copy.92
  205.9 1.1 collective-permute-done.18
  207.0 1.4 collective-permute-start.19
  208.4 1.6 copy.94
  210.0 2.0 collective-permute-done.19
  (93 shorter events, 7.1 us)
Async XLA Ops:
  11.4 2.0 copy-start.8
  13.3 13.5 %copy-start = (bf16[48,8,16,128]{3,2,1,0:T(8,128)(2,1)}, bf16[48,8,16,128]{3,2,1,0:T(8,128)(2,1)S(1)}, u32[]{:S(2)}) copy-start(bf16[48,8,16,128]{3,2,1,0:T(8,128)(2,1)S(1)} %copy.101) | copy-start | bytes 4718596
  13.7 10.7 %copy-start.3 = (bf16[48,8,16,128]{3,2,1,0:T(8,128)(2,1)}, bf16[48,8,16,128]{3,2,1,0:T(8,128)(2,1)S(1)}, u32[]{:S(2)}) copy-start(bf16[48,8,16,128]{3,2,1,0:T(8,128)(2,1)S(1)} %copy.100) | copy-start | bytes 4718596
  31.1 26.2 %collective-permute-start.2 = (f32[4,264,128]{2,1,0:T(8,128)S(1)}, f32[4,264,128]{2,1,0:T(8,128)S(1)}, u32[]{:S(2)}, u32[]{:S(2)}) collective-permute-start(f32[4,264,128]{2,1,0:T(8,128)S(1)} %get-tuple-element.48), channel_id=1, source_target_pairs={{0,24},{8,0},{16,8},{24,16},{32,56},{40,32},{48,40},{56,48},{64,88... | collective-permute-start | bytes 1622024 | tf_op jit(solution)/shard_map/ppermute | solution.py:57
  34.2 23.1 %collective-permute-start.1 = (f32[4,264,128]{2,1,0:T(8,128)S(1)}, f32[4,264,128]{2,1,0:T(8,128)S(1)}, u32[]{:S(2)}, u32[]{:S(2)}) collective-permute-start(f32[4,264,128]{2,1,0:T(8,128)S(1)} %get-tuple-element.49), channel_id=1, source_target_pairs={{0,16},{8,24},{16,0},{24,8},{32,48},{40,56},{48,32},{56,40},{64,80... | collective-permute-start | bytes 1622024 | tf_op jit(solution)/shard_map/ppermute | solution.py:57
  34.8 26.2 %collective-permute-start = (f32[4,264,128]{2,1,0:T(8,128)S(1)}, f32[4,264,128]{2,1,0:T(8,128)S(1)}, u32[]{:S(2)}, u32[]{:S(2)}) collective-permute-start(f32[4,264,128]{2,1,0:T(8,128)S(1)} %get-tuple-element.50), channel_id=1, source_target_pairs={{0,8},{8,16},{16,24},{24,0},{32,40},{40,48},{48,56},{56,32},{64,72... | collective-permute-start | bytes 1622024 | tf_op jit(solution)/shard_map/ppermute | solution.py:57
  68.5 9.9 %collective-permute-start.3 = (f32[4,136,128]{2,1,0:T(8,128)S(1)}, f32[4,136,128]{2,1,0:T(8,128)S(1)}, u32[]{:S(2)}, u32[]{:S(2)}) collective-permute-start(f32[4,136,128]{2,1,0:T(8,128)S(1)} %get-tuple-element.69), channel_id=1, source_target_pairs={{0,32},{8,40},{16,48},{24,56},{32,64},{40,72},{48,80},{56,88},{64,... | collective-permute-start | bytes 835592 | tf_op jit(solution)/shard_map/ppermute | solution.py:35
  72.4 10.4 %collective-permute-start.6 = (f32[4,136,128]{2,1,0:T(8,128)S(1)}, f32[4,136,128]{2,1,0:T(8,128)S(1)}, u32[]{:S(2)}, u32[]{:S(2)}) collective-permute-start(f32[4,136,128]{2,1,0:T(8,128)S(1)} %get-tuple-element.70), channel_id=1, source_target_pairs={{32,0},{40,8},{48,16},{56,24},{64,32},{72,40},{80,48},{88,56},{96,... | collective-permute-start | bytes 835592 | tf_op jit(solution)/shard_map/ppermute | solution.py:36
  82.9 11.7 %collective-permute-start.4 = (f32[4,136,128]{2,1,0:T(8,128)S(1)}, f32[4,136,128]{2,1,0:T(8,128)S(1)}, u32[]{:S(2)}, u32[]{:S(2)}) collective-permute-start(f32[4,136,128]{2,1,0:T(8,128)S(1)} %pad_maximum_fusion.6), channel_id=1, source_target_pairs={{0,64},{8,72},{16,80},{24,88},{32,96},{40,104},{48,112},{56,120},{... | collective-permute-start | bytes 835592 | tf_op jit(solution)/shard_map/ppermute | solution.py:35
  89.5 15.3 %collective-permute-start.7 = (f32[4,136,128]{2,1,0:T(8,128)S(1)}, f32[4,136,128]{2,1,0:T(8,128)S(1)}, u32[]{:S(2)}, u32[]{:S(2)}) collective-permute-start(f32[4,136,128]{2,1,0:T(8,128)S(1)} %pad_maximum_fusion.8), channel_id=1, source_target_pairs={{64,0},{72,8},{80,16},{88,24},{96,32},{104,40},{112,48},{120,56},{... | collective-permute-start | bytes 835592 | tf_op jit(solution)/shard_map/ppermute | solution.py:36
  94.7 12.0 %collective-permute-start.5 = (f32[4,136,128]{2,1,0:T(8,128)S(1)}, f32[4,136,128]{2,1,0:T(8,128)S(1)}, u32[]{:S(2)}, u32[]{:S(2)}) collective-permute-start(f32[4,136,128]{2,1,0:T(8,128)S(1)} %pad_maximum_fusion.7), channel_id=1, source_target_pairs={{0,128},{8,136},{16,144},{24,152},{32,160},{40,168},{48,176},{56,1... | collective-permute-start | bytes 835592 | tf_op jit(solution)/shard_map/ppermute | solution.py:35
  105.0 18.2 %collective-permute-start.8 = (f32[4,136,128]{2,1,0:T(8,128)S(1)}, f32[4,136,128]{2,1,0:T(8,128)S(1)}, u32[]{:S(2)}, u32[]{:S(2)}) collective-permute-start(f32[4,136,128]{2,1,0:T(8,128)S(1)} %pad_maximum_fusion.9), channel_id=1, source_target_pairs={{128,0},{136,8},{144,16},{152,24},{160,32},{168,40},{176,48},{184,... | collective-permute-start | bytes 835592 | tf_op jit(solution)/shard_map/ppermute | solution.py:36
  125.3 15.2 %collective-permute-start.11 = (f32[4,256,128]{2,1,0:T(8,128)}, f32[4,256,128]{2,1,0:T(8,128)}, u32[]{:S(2)}, u32[]{:S(2)}) collective-permute-start(f32[4,256,128]{2,1,0:T(8,128)} %get-tuple-element.52), channel_id=1, source_target_pairs={{0,24},{8,0},{16,8},{24,16},{32,56},{40,32},{48,40},{56,48},{64,88... | collective-permute-start | bytes 1572872 | tf_op jit(solution)/shard_map/ppermute | solution.py:57
  125.3 16.7 %collective-permute-start.10 = (f32[4,256,128]{2,1,0:T(8,128)}, f32[4,256,128]{2,1,0:T(8,128)}, u32[]{:S(2)}, u32[]{:S(2)}) collective-permute-start(f32[4,256,128]{2,1,0:T(8,128)} %get-tuple-element.53), channel_id=1, source_target_pairs={{0,16},{8,24},{16,0},{24,8},{32,48},{40,56},{48,32},{56,40},{64,80... | collective-permute-start | bytes 1572872 | tf_op jit(solution)/shard_map/ppermute | solution.py:57
  126.0 25.0 %collective-permute-start.9 = (f32[4,256,128]{2,1,0:T(8,128)}, f32[4,256,128]{2,1,0:T(8,128)}, u32[]{:S(2)}, u32[]{:S(2)}) collective-permute-start(f32[4,256,128]{2,1,0:T(8,128)} %get-tuple-element.54), channel_id=1, source_target_pairs={{0,8},{8,16},{16,24},{24,0},{32,40},{40,48},{48,56},{56,32},{64,72... | collective-permute-start | bytes 1572872 | tf_op jit(solution)/shard_map/ppermute | solution.py:57
  163.5 2.0 copy-start.1
  165.5 7.9 %copy-start.5 = (f32[16,256,128]{2,1,0:T(8,128)}, f32[16,256,128]{2,1,0:T(8,128)S(1)}, u32[]{:S(2)}) copy-start(f32[16,256,128]{2,1,0:T(8,128)S(1)} %bitcast_select_fusion) | copy-start | bytes 6291460
  165.6 2.2 %copy-start.4 = (bf16[48,8,16,128]{3,2,1,0:T(8,128)(2,1)S(1)}, bf16[48,8,16,128]{3,2,1,0:T(8,128)(2,1)}, u32[]{:S(2)}) copy-start(bf16[48,8,16,128]{3,2,1,0:T(8,128)(2,1)} %copy-done.3) | copy-start | bytes 4718596
  169.3 3.6 %collective-permute-start.12 = (f32[16]{0:T(128)S(1)}, f32[16]{0:T(128)S(1)}, u32[]{:S(2)}, u32[]{:S(2)}) collective-permute-start(f32[16]{0:T(128)S(1)} %add_subtract_fusion), channel_id=1, source_target_pairs={{0,8},{8,0},{16,24},{24,16},{32,40},{40,32},{48,56},{56,48},{64,72... | collective-permute-start | bytes 200 | tf_op jit(solution)/shard_map/ppermute | solution.py:114
  172.9 5.0 %collective-permute-start.13 = (f32[16]{0:T(128)S(1)}, f32[16]{0:T(128)S(1)}, u32[]{:S(2)}, u32[]{:S(2)}) collective-permute-start(f32[16]{0:T(128)S(1)} %add.241), channel_id=1, source_target_pairs={{0,16},{8,24},{16,0},{24,8},{32,48},{40,56},{48,32},{56,40},{64,80... | collective-permute-start | bytes 200 | tf_op jit(solution)/shard_map/ppermute | solution.py:114
  177.9 9.9 %collective-permute-start.14 = (f32[16]{0:T(128)S(1)}, f32[16]{0:T(128)S(1)}, u32[]{:S(2)}, u32[]{:S(2)}) collective-permute-start(f32[16]{0:T(128)S(1)} %add.242), channel_id=1, source_target_pairs={{0,32},{8,40},{16,48},{24,56},{32,0},{40,8},{48,16},{56,24},{64,96... | collective-permute-start | bytes 200 | tf_op jit(solution)/shard_map/ppermute | solution.py:114
  187.8 6.4 %collective-permute-start.15 = (f32[16]{0:T(128)S(1)}, f32[16]{0:T(128)S(1)}, u32[]{:S(2)}, u32[]{:S(2)}) collective-permute-start(f32[16]{0:T(128)S(1)} %add.243), channel_id=1, source_target_pairs={{0,64},{8,72},{16,80},{24,88},{32,96},{40,104},{48,112},{56,120},{... | collective-permute-start | bytes 200 | tf_op jit(solution)/shard_map/ppermute | solution.py:114
  189.9 4.5 %copy-start.2 = (bf16[48,8,16,128]{3,2,1,0:T(8,128)(2,1)S(1)}, bf16[48,8,16,128]{3,2,1,0:T(8,128)(2,1)}, u32[]{:S(2)}) copy-start(bf16[48,8,16,128]{3,2,1,0:T(8,128)(2,1)} %copy-done) | copy-start | bytes 4718596
  189.9 4.5 %copy-start.6 = (f32[16,256,128]{2,1,0:T(8,128)S(1)}, f32[16,256,128]{2,1,0:T(8,128)}, u32[]{:S(2)}) copy-start(f32[16,256,128]{2,1,0:T(8,128)} %copy-done.5) | copy-start | bytes 6291460
  189.9 4.7 %copy-start.7 = (f32[16,384,128]{1,2,0:T(8,128)S(1)}, f32[16,384,128]{1,2,0:T(8,128)}, u32[]{:S(2)}) copy-start(f32[16,384,128]{1,2,0:T(8,128)} %get-tuple-element.79) | copy-start | bytes 9437188
  194.2 7.5 %collective-permute-start.16 = (f32[16]{0:T(128)S(1)}, f32[16]{0:T(128)S(1)}, u32[]{:S(2)}, u32[]{:S(2)}) collective-permute-start(f32[16]{0:T(128)S(1)} %add.244), channel_id=1, source_target_pairs={{0,128},{8,136},{16,144},{24,152},{32,160},{40,168},{48,176},{56,1... | collective-permute-start | bytes 200 | tf_op jit(solution)/shard_map/ppermute | solution.py:114
  201.8 1.6 collective-permute-start.17
  203.4 5.0 %copy-start.9 = (bf16[384,16,128]{0,2,1:T(8,128)(2,1)S(1)}, bf16[384,16,128]{0,2,1:T(8,128)(2,1)}, u32[]{:S(2)}) copy-start(bf16[384,16,128]{0,2,1:T(8,128)(2,1)} %fusion.14) | copy-start | bytes 4718596
  203.4 3.6 %collective-permute-start.18 = (f32[16]{0:T(128)S(1)}, f32[16]{0:T(128)S(1)}, u32[]{:S(2)}, u32[]{:S(2)}) collective-permute-start(f32[16]{0:T(128)S(1)} %add.246), channel_id=1, source_target_pairs={{0,2},{1,3},{2,0},{3,1},{4,6},{5,7},{6,4},{7,5},{8,10},{9,11},{10,... | collective-permute-start | bytes 200 | tf_op jit(solution)/shard_map/ppermute | solution.py:114
  205.9 6.2 %copy-start.10 = (f32[16]{0:T(128)S(1)}, f32[16]{0:T(128)}, u32[]{:S(2)}) copy-start(f32[16]{0:T(128)} %param.13) | copy-start | bytes 196
  207.0 5.0 %collective-permute-start.19 = (f32[16]{0:T(128)S(1)}, f32[16]{0:T(128)S(1)}, u32[]{:S(2)}, u32[]{:S(2)}) collective-permute-start(f32[16]{0:T(128)S(1)} %add.247), channel_id=1, source_target_pairs={{0,4},{1,5},{2,6},{3,7},{4,0},{5,1},{6,2},{7,3},{8,12},{9,13},{10,... | collective-permute-start | bytes 200 | tf_op jit(solution)/shard_map/ppermute | solution.py:114

commit v5 on v3

--- a/solution.py
+++ b/solution.py
@@ -55,8 +55,7 @@
         ]
         send = lax.dynamic_index_in_dim(parts, (place + step) % group, 0, False)
         got.append(lax.ppermute(send, axis, pairs))
-    order = (place - jnp.arange(group)) % group
-    return jnp.take(jnp.stack(got), order, axis=0)
+    return jnp.stack([lax.select_n((place - j) % group, *got) for j in range(group)])
 
 
 def carried_both(decay, forward_part, backward_part, axis):
@@ -106,13 +105,26 @@
     return full[:, :rows], full[:, rows:]
 
 
+def digit_sum(value, axis, step, radix):
+    count = lax.axis_size(axis)
+    digit = (lax.axis_index(axis) // step) % radix
+    got = [value]
+    for k in range(1, radix):
+        got.append(lax.ppermute(value, axis, [(i, i ^ (k * step)) for i in range(count)]))
+    total = lax.select_n(digit, *got)
+    for m in range(1, radix):
+        total = total + lax.select_n(digit ^ m, *got)
+    return total
+
+
 def all_sum(value, axes):
     for axis in axes:
         count = lax.axis_size(axis)
         step = 1
         while step < count:
-            value = value + lax.ppermute(value, axis, [(i, i ^ step) for i in range(count)])
-            step *= 2
+            radix = 4 if count % (step * 4) == 0 else 2
+            value = digit_sum(value, axis, step, radix)
+            step *= radix
     return value
 
 

time: 205 us -> 196 us (0.956)
  starting transfers between devices: 34.7 us -> 65.4 us
  waiting for transfers between devices: 87.5 us -> 65.9 us
  local copies, waits for them, and re-layouts: 31.2 us -> 19.7 us
  other arithmetic: 21.1 us -> 16.6 us
  matrix products: 28.3 us -> 25.4 us
    ppermute x8 -> x11, starting transfers between devices: 5.41 us -> 20.7 us  [digit_sum(): lax.ppermute(value, axis, [(i, i ^ k * step) for i in range(count)])]
    ppermute x3, waiting for transfers between devices: 22.9 us -> 11.4 us  [group_scan(): rgot = lax.ppermute(bwd, axis, down)]
    gather x3 -> x0, local copies, waits for them, and re-layouts: 10.2 us -> none  [row_exchange(): return jnp.take(jnp.stack(got), order, axis=0)]
    ppermute x3, starting transfers between devices: 18.5 us -> 28.3 us  [group_scan(): got = lax.ppermute(fwd, axis, up)]
    ppermute x6, waiting for transfers between devices: 43.4 us -> 35.6 us  [row_exchange(): got.append(lax.ppermute(send, axis, pairs))]
    ppermute x6, starting transfers between devices: 6.82 us -> 12.4 us  [row_exchange(): got.append(lax.ppermute(send, axis, pairs))]
    select_n x3 -> x0, other arithmetic: 3.82 us -> none  [row_exchange(): return jnp.take(jnp.stack(got), order, axis=0)]
    another operation x3 -> x2, local copies, waits for them, and re-layouts: 3.21 us -> 0.27 us  [the longest x1 2.93 us: row_exchange(): return jnp.take(jnp.stack(got), order, axis=0)]
  transfers between devices with their start and end apart: 20 -> 23, of which waited for: 16 -> 15; matrix products, arithmetic and copies ran while one was open for 13% -> 11% of each run, Pallas kernels for 0% -> 0%
where the time goes in v5:
time: 196 us; the launch traced here: 195 us
  waiting for transfers between devices  65.9 us (34%)
  starting transfers between devices  65.4 us (33%)
  matrix products  25.4 us (13%)
  local copies, waits for them, and re-layouts  19.7 us (10%)
  other arithmetic  16.6 us (8%)
  between operations  2.09 us (1%)
    ppermute x6, waiting for transfers between devices, row_exchange(): got.append(lax.ppermute(send, axis, pairs))  35.6 us
    ppermute x3, starting transfers between devices, group_scan(): got = lax.ppermute(fwd, axis, up)  28.3 us
    ppermute x11, starting transfers between devices, digit_sum(): lax.ppermute(value, axis, [(i, i ^ k * step) for i in range(count)])  20.7 us
    ppermute x11, waiting for transfers between devices, digit_sum(): lax.ppermute(value, axis, [(i, i ^ k * step) for i in range(count)])  14.1 us
    unnamed x42, local copies, waits for them, and re-layouts  14.1 us
    ppermute x6, starting transfers between devices, row_exchange(): got.append(lax.ppermute(send, axis, pairs))  12.4 us
    ppermute x3, waiting for transfers between devices, group_scan(): rgot = lax.ppermute(bwd, axis, down)  11.4 us
    dot_general x1, matrix products, on_device(): jnp.einsum('hst,shf->thf', attn_prob, gradient_block, preferred_element_t...  7.06 us
  transfers between devices with their start and end apart: 23, of which 15 were waited for; matrix products, arithmetic and copies ran while one was open for 11% of the time, Pallas kernels for 0%

profile of v5, /device:TPU:6, one launch (start us, length us, event | category | flops | bytes accessed | tf_op | source)
XLA Modules:
  0.0 195.0 jit_solution(13708206593413989405)
XLA Ops:
  0.7 0.9 reduce-window_clone.1
  1.6 0.7 subtract_bitcast_fusion
  4.2 0.7 broadcast_compare_fusion
  4.9 1.9 copy.87
  6.8 1.6 copy.103
  8.5 0.9 reduce-window.24
  9.8 1.9 copy.85
  11.7 3.0 %copy.105 = bf16[48,8,16,128]{3,2,1,0:T(8,128)(2,1)} copy(bf16[48,8,16,128]{3,1,2,0:T(8,128)(2,1)} %bitcast.221) | data formatting | bytes 3145728
  14.8 2.9 %fusion.9 = f32[16,128,128]{2,1,0:T(8,128)S(1)} fusion(bf16[384,16,128]{0,2,1:T(8,128)(2,1)} %bitcast.207, bf16[384,16,128]{0,2,1:T(8,128)(2,1)S(1)} %bitcast.203, f32[384,16]{0,1:T(8,128)S(1)} %get-tuple-element.74), kind=kOutput, calls=%fused_computation.15 | convolution fusion | flops 605552640 | bytes 4218880 | tf_op jit(solution)/shard_map/she,shf->hef/dot_general | solution.py:180
  17.8 1.4 fusion.7
  19.4 1.3 copy-done.3
  20.8 1.2 dynamic-slice_bitcast_fusion
  22.0 1.6 collective-permute-start
  23.6 2.9 %collective-permute-start.1 = (f32[4,264,128]{2,1,0:T(8,128)}, f32[4,264,128]{2,1,0:T(8,128)}, u32[]{:S(2)}, u32[]{:S(2)}) collective-permute-start(f32[4,264,128]{2,1,0:T(8,128)} %get-tuple-element.54), channel_id=1, source_target_pairs={{0,16},{8,24},{16,0},{24,8},{32,48},{40,56},{48,32},{56,40},{64,80... | collective-permute-start | bytes 1622024 | tf_op jit(solution)/shard_map/ppermute | solution.py:57
  26.5 1.3 collective-permute-start.2
  27.9 9.7 %collective-permute-done = f32[4,264,128]{2,1,0:T(8,128)} collective-permute-done((f32[4,264,128]{2,1,0:T(8,128)}, f32[4,264,128]{2,1,0:T(8,128)}, u32[]{:S(2)}, u32[]{:S(2)}) %collective-permute-start) | collective-permute-done | bytes 540704 | tf_op jit(solution)/shard_map/ppermute | solution.py:57
  37.6 12.8 %collective-permute-done.1 = f32[4,264,128]{2,1,0:T(8,128)} collective-permute-done((f32[4,264,128]{2,1,0:T(8,128)}, f32[4,264,128]{2,1,0:T(8,128)}, u32[]{:S(2)}, u32[]{:S(2)}) %collective-permute-start.1) | collective-permute-done | bytes 540704 | tf_op jit(solution)/shard_map/ppermute | solution.py:57
  50.4 1.8 fusion.28
  52.4 1.1 fusion.49
  53.6 0.9 pad_maximum_fusion.4
  54.6 1.3 collective-permute-start.6
  56.3 4.6 %collective-permute-start.3 = (f32[4,136,128]{2,1,0:T(8,128)}, f32[4,136,128]{2,1,0:T(8,128)S(1)}, u32[]{:S(2)}, u32[]{:S(2)}) collective-permute-start(f32[4,136,128]{2,1,0:T(8,128)} %get-tuple-element.75), channel_id=1, source_target_pairs={{0,32},{8,40},{16,48},{24,56},{32,64},{40,72},{48,80},{56,88},{64,... | collective-permute-start | bytes 835592 | tf_op jit(solution)/shard_map/ppermute | solution.py:35
  60.8 3.7 %collective-permute-done.6 = f32[4,136,128]{2,1,0:T(8,128)} collective-permute-done((f32[4,136,128]{2,1,0:T(8,128)}, f32[4,136,128]{2,1,0:T(8,128)}, u32[]{:S(2)}, u32[]{:S(2)}) %collective-permute-start.6) | collective-permute-done | bytes 278560 | tf_op jit(solution)/shard_map/ppermute | solution.py:36
  64.5 0.8 fusion.79
  65.4 0.6 collective-permute-done.3
  66.0 1.2 multiply_add_fusion.9
  67.4 5.6 %collective-permute-start.4 = (f32[4,136,128]{2,1,0:T(8,128)S(1)}, f32[4,136,128]{2,1,0:T(8,128)S(1)}, u32[]{:S(2)}, u32[]{:S(2)}) collective-permute-start(f32[4,136,128]{2,1,0:T(8,128)S(1)} %pad_maximum_fusion.5), channel_id=1, source_target_pairs={{0,64},{8,72},{16,80},{24,88},{32,96},{40,104},{48,112},{56,120},{... | collective-permute-start | bytes 835592 | tf_op jit(solution)/shard_map/ppermute | solution.py:35
  73.2 1.3 collective-permute-start.7
  74.5 0.8 slice_reduce_fusion.2
  75.4 1.8 collective-permute-done.4
  77.3 18.1 %collective-permute-start.5 = (f32[4,136,128]{2,1,0:T(8,128)S(1)}, f32[4,136,128]{2,1,0:T(8,128)S(1)}, u32[]{:S(2)}, u32[]{:S(2)}) collective-permute-start(f32[4,136,128]{2,1,0:T(8,128)S(1)} %pad_maximum_fusion.6), channel_id=1, source_target_pairs={{0,128},{8,136},{16,144},{24,152},{32,160},{40,168},{48,176},{56,1... | collective-permute-start | bytes 835592 | tf_op jit(solution)/shard_map/ppermute | solution.py:35
  95.6 1.3 collective-permute-start.8
  97.2 2.3 %collective-permute-done.5 = f32[4,136,128]{2,1,0:T(8,128)S(1)} collective-permute-done((f32[4,136,128]{2,1,0:T(8,128)S(1)}, f32[4,136,128]{2,1,0:T(8,128)S(1)}, u32[]{:S(2)}, u32[]{:S(2)}) %collective-permute-start.5) | collective-permute-done | bytes 278560 | tf_op jit(solution)/shard_map/ppermute | solution.py:35
  99.5 1.1 multiply_add_fusion.4
  100.6 1.1 multiply_add_fusion.2
  101.7 7.7 %collective-permute-done.8 = f32[4,136,128]{2,1,0:T(8,128)S(1)} collective-permute-done((f32[4,136,128]{2,1,0:T(8,128)S(1)}, f32[4,136,128]{2,1,0:T(8,128)S(1)}, u32[]{:S(2)}, u32[]{:S(2)}) %collective-permute-start.8) | collective-permute-done | bytes 278560 | tf_op jit(solution)/shard_map/ppermute | solution.py:36
  109.4 1.2 multiply_add_fusion.5
  110.6 1.1 multiply_add_fusion.3
  112.2 1.7 collective-permute-start.9
  113.9 4.9 %collective-permute-start.10 = (f32[4,256,128]{2,1,0:T(8,128)S(1)}, f32[4,256,128]{2,1,0:T(8,128)S(1)}, u32[]{:S(2)}, u32[]{:S(2)}) collective-permute-start(f32[4,256,128]{2,1,0:T(8,128)S(1)} %get-tuple-element.57), channel_id=1, source_target_pairs={{0,16},{8,24},{16,0},{24,8},{32,48},{40,56},{48,32},{56,40},{64,80... | collective-permute-start | bytes 1572872 | tf_op jit(solution)/shard_map/ppermute | solution.py:57
  118.8 3.7 %multiply_convert_fusion.1 = bf16[16,384,384]{2,1,0:T(8,128)(2,1)S(1)} fusion(f32[16,384]{1,0:T(8,128)S(1)} %get-tuple-element.71, pred[384,384]{1,0:T(8,128)(4,1)S(1)} %fusion.26, bf16[384,16,128]{0,2,1:T(8,128)(2,1)S(1)} %bitcast.209, bf16[384,16,128]{2,1,0:T(8,128)(2,1)S(1)} %bitcast.212), kind=kOutput, calls=%fused_computation.1 | convolution fusion | flops 615776256 | bytes 8036352 | tf_op jit(solution)/shard_map/shf,thf->hst/dot_general | solution.py:186
  122.5 7.5 %collective-permute-done.9 = f32[4,256,128]{2,1,0:T(8,128)S(1)} collective-permute-done((f32[4,256,128]{2,1,0:T(8,128)S(1)}, f32[4,256,128]{2,1,0:T(8,128)S(1)}, u32[]{:S(2)}, u32[]{:S(2)}) %collective-permute-start.9) | collective-permute-done | bytes 524320 | tf_op jit(solution)/shard_map/ppermute | solution.py:57
  130.1 5.6 %collective-permute-done.10 = f32[4,256,128]{2,1,0:T(8,128)S(1)} collective-permute-done((f32[4,256,128]{2,1,0:T(8,128)S(1)}, f32[4,256,128]{2,1,0:T(8,128)S(1)}, u32[]{:S(2)}, u32[]{:S(2)}) %collective-permute-start.10) | collective-permute-done | bytes 524320 | tf_op jit(solution)/shard_map/ppermute | solution.py:57
  136.1 1.0 fusion.21
  137.1 1.4 fusion.17
  138.6 2.7 %fusion.23 = f32[16,128,384]{2,1,0:T(8,128)} fusion(bf16[384,16,128]{0,2,1:T(8,128)(2,1)S(1)} %bitcast.199, f32[16,256,128]{2,1,0:T(8,128)S(1)} %bitcast.216), kind=kOutput, calls=%fused_computation.35 | convolution fusion | flops 603979776 | bytes 5767168 | tf_op jit(solution)/shard_map/the,hef->thf/dot_general | solution.py:194
  141.3 2.8 %fusion.10 = (f32[384,16]{0,1:T(8,128)S(1)}, bf16[384,16,128]{0,2,1:T(8,128)(2,1)}) fusion(bf16[384,16,128]{0,2,1:T(8,128)(2,1)S(1)} %bitcast.204, f32[16,128,384]{2,1,0:T(8,128)S(1)} %fusion.21, f32[384,16]{0,1:T(8,128)S(1)} %get-tuple-element.74, bf16[16,384,384]{2,1,0:T(8,128)(2,1)S(1)} %multiply_convert_fusion.1, bf16[384,16,128]{0,2,1:T(8,128)(2,1)S(1)} %bitcast.200), kind=kOutput, calls=%fused_computation.16 | convolution fusion | flops 608692224 | bytes 12632064 | tf_op jit(solution)/shard_map/hst,the->she/dot_general | solution.py:197
  144.0 2.4 %fusion.8 = (f32[384,16]{0,1:T(8,128)S(1)}, bf16[384,16,128]{0,2,1:T(8,128)(2,1)}) fusion(bf16[384,16,128]{0,2,1:T(8,128)(2,1)S(1)} %bitcast.201, f32[16,128,384]{2,1,0:T(8,128)S(1)} %fusion.17, f32[384,16]{0,1:T(8,128)S(1)} %get-tuple-element.73, bf16[384,16,128]{0,2,1:T(8,128)(2,1)S(1)} %bitcast.205, bf16[16,384,384]{2,1,0:T(8,128)(2,1)S(1)} %multiply_convert_fusion.1), kind=kOutput, calls=%fused_computation.14 | convolution fusion | flops 608692224 | bytes 12632064 | tf_op jit(solution)/shard_map/hst,she->the/dot_general | solution.py:203
  146.9 3.3 %collective-permute-start.13 = (f32[16]{0:T(128)S(1)}, f32[16]{0:T(128)S(1)}, u32[]{:S(2)}, u32[]{:S(2)}) collective-permute-start(f32[16]{0:T(128)S(1)} %multiply_reduce_fusion), channel_id=1, source_target_pairs={{0,16},{8,24},{16,0},{24,8},{32,48},{40,56},{48,32},{56,40},{64,80... | collective-permute-start | bytes 200 | tf_op jit(solution)/shard_map/ppermute | solution.py:113
  150.3 1.1 collective-permute-start.14
  151.3 7.1 %fusion.12 = bf16[384,16,128]{0,2,1:T(8,128)(2,1)} fusion(f32[16,128,384]{2,1,0:T(8,128)} %fusion.23, bf16[384,16,128]{0,2,1:T(8,128)(2,1)} %bitcast.208, f32[16,384]{1,0:T(8,128)S(1)} %get-tuple-element.71, pred[384,384]{1,0:T(8,128)(4,1)S(1)} %copy-done.15, bf16[384,16,128]{0,2,1:T(8,128)(2,1)S(1)} %bitcast.206, bf16[384,16,128]{0,2,1:T(8,128)(2,1)S(1)} %bitcast.202, ...), kind=kOutput, calls=%fused_computation.19 | convolution fusion | flops 1222115328 | bytes 9633792 | tf_op jit(solution)/shard_map/hst,shf->thf/dot_general | solution.py:191
  158.4 2.7 %copy.96 = bf16[1,384,2048]{2,1,0:T(8,128)(2,1)} copy(bf16[1,384,2048]{1,2,0:T(8,128)(2,1)} %bitcast.220) | data formatting | bytes 3145728
  161.2 2.7 %collective-permute-start.15 = (f32[16]{0:T(128)S(1)}, f32[16]{0:T(128)S(1)}, u32[]{:S(2)}, u32[]{:S(2)}) collective-permute-start(f32[16]{0:T(128)S(1)} %fusion.66), channel_id=1, source_target_pairs={{0,32},{8,40},{16,48},{24,56},{32,0},{40,8},{48,16},{56,24},{64,96... | collective-permute-start | bytes 200 | tf_op jit(solution)/shard_map/ppermute | solution.py:113
  163.8 8.8 %collective-permute-start.16 = (f32[16]{0:T(128)S(1)}, f32[16]{0:T(128)S(1)}, u32[]{:S(2)}, u32[]{:S(2)}) collective-permute-start(f32[16]{0:T(128)S(1)} %fusion.66), channel_id=1, source_target_pairs={{0,64},{8,72},{16,80},{24,88},{32,96},{40,104},{48,112},{56,120},{... | collective-permute-start | bytes 200 | tf_op jit(solution)/shard_map/ppermute | solution.py:113
  172.6 1.4 collective-permute-start.17
  174.1 3.8 %collective-permute-done.17 = f32[16]{0:T(128)S(1)} collective-permute-done((f32[16]{0:T(128)S(1)}, f32[16]{0:T(128)S(1)}, u32[]{:S(2)}, u32[]{:S(2)}) %collective-permute-start.17) | collective-permute-done | bytes 96 | tf_op jit(solution)/shard_map/ppermute | solution.py:113
  178.0 1.6 copy.97
  179.7 5.8 %collective-permute-done.18 = f32[16]{0:T(128)S(1)} collective-permute-done((f32[16]{0:T(128)S(1)}, f32[16]{0:T(128)S(1)}, u32[]{:S(2)}, u32[]{:S(2)}) %collective-permute-start.18) | collective-permute-done | bytes 96 | tf_op jit(solution)/shard_map/ppermute | solution.py:113
  185.5 0.9 collective-permute-start.20
  186.4 0.9 collective-permute-start.21
  187.3 1.7 collective-permute-done.20
  189.4 1.2 collective-permute-start.22
  190.6 1.6 copy.98
  192.2 2.3 %collective-permute-done.22 = f32[16]{0:T(128)S(1)} collective-permute-done((f32[16]{0:T(128)S(1)}, f32[16]{0:T(128)S(1)}, u32[]{:S(2)}, u32[]{:S(2)}) %collective-permute-start.22) | collective-permute-done | bytes 96 | tf_op jit(solution)/shard_map/ppermute | solution.py:113
  (103 shorter events, 6.2 us)
Async XLA Ops:
  0.6 6.2 %copy-start.11 = (bf16[1,384,2048]{2,1,0:T(8,128)(2,1)S(1)}, bf16[1,384,2048]{2,1,0:T(8,128)(2,1)}, u32[]{:S(2)}) copy-start(bf16[1,384,2048]{2,1,0:T(8,128)(2,1)} %param.10) | copy-start | bytes 4718596
  6.8 1.6 copy-start.17
  6.8 1.6 copy-start.16
  14.8 2.9 %copy-start.1 = (bf16[48,8,16,128]{3,2,1,0:T(8,128)(2,1)S(1)}, bf16[48,8,16,128]{3,2,1,0:T(8,128)(2,1)}, u32[]{:S(2)}) copy-start(bf16[48,8,16,128]{3,2,1,0:T(8,128)(2,1)} %copy.105) | copy-start | bytes 4718596
  19.4 1.4 copy-start.3
  22.0 15.6 %collective-permute-start = (f32[4,264,128]{2,1,0:T(8,128)}, f32[4,264,128]{2,1,0:T(8,128)}, u32[]{:S(2)}, u32[]{:S(2)}) collective-permute-start(f32[4,264,128]{2,1,0:T(8,128)} %get-tuple-element.55), channel_id=1, source_target_pairs={{0,8},{8,16},{16,24},{24,0},{32,40},{40,48},{48,56},{56,32},{64,72... | collective-permute-start | bytes 1622024 | tf_op jit(solution)/shard_map/ppermute | solution.py:57
  23.6 26.8 %collective-permute-start.1 = (f32[4,264,128]{2,1,0:T(8,128)}, f32[4,264,128]{2,1,0:T(8,128)}, u32[]{:S(2)}, u32[]{:S(2)}) collective-permute-start(f32[4,264,128]{2,1,0:T(8,128)} %get-tuple-element.54), channel_id=1, source_target_pairs={{0,16},{8,24},{16,0},{24,8},{32,48},{40,56},{48,32},{56,40},{64,80... | collective-permute-start | bytes 1622024 | tf_op jit(solution)/shard_map/ppermute | solution.py:57
  26.5 23.9 %collective-permute-start.2 = (f32[4,264,128]{2,1,0:T(8,128)}, f32[4,264,128]{2,1,0:T(8,128)}, u32[]{:S(2)}, u32[]{:S(2)}) collective-permute-start(f32[4,264,128]{2,1,0:T(8,128)} %get-tuple-element.53), channel_id=1, source_target_pairs={{0,24},{8,0},{16,8},{24,16},{32,56},{40,32},{48,40},{56,48},{64,88... | collective-permute-start | bytes 1622024 | tf_op jit(solution)/shard_map/ppermute | solution.py:57
  52.1 2.4 %copy-start.5 = (f32[1,4,264,128]{3,2,1,0:T(8,128)}, f32[1,4,264,128]{3,2,1,0:T(8,128)S(1)}, u32[]{:S(2)}) copy-start(f32[1,4,264,128]{3,2,1,0:T(8,128)S(1)} %get-tuple-element.40) | copy-start | bytes 1622020
  52.1 2.4 %copy-start.6 = (f32[1,4,264,128]{3,2,1,0:T(8,128)}, f32[1,4,264,128]{3,2,1,0:T(8,128)S(1)}, u32[]{:S(2)}) copy-start(f32[1,4,264,128]{3,2,1,0:T(8,128)S(1)} %get-tuple-element.42) | copy-start | bytes 1622020
  52.2 2.4 %copy-start.7 = (f32[1,4,264,128]{3,2,1,0:T(8,128)}, f32[1,4,264,128]{3,2,1,0:T(8,128)S(1)}, u32[]{:S(2)}) copy-start(f32[1,4,264,128]{3,2,1,0:T(8,128)S(1)} %get-tuple-element.41) | copy-start | bytes 1622020
  52.2 2.4 %copy-start.8 = (f32[1,4,264,128]{3,2,1,0:T(8,128)}, f32[1,4,264,128]{3,2,1,0:T(8,128)S(1)}, u32[]{:S(2)}) copy-start(f32[1,4,264,128]{3,2,1,0:T(8,128)S(1)} %get-tuple-element.39) | copy-start | bytes 1622020
  53.5 1.0 copy-start.9
  53.5 2.4 %copy-start.10 = (f32[4,128,128]{2,1,0:T(8,128)}, f32[4,128,128]{2,1,0:T(8,128)S(1)}, u32[]{:S(2)}) copy-start(f32[4,128,128]{2,1,0:T(8,128)S(1)} %get-tuple-element.51) | copy-start | bytes 786436
  54.6 9.9 %collective-permute-start.6 = (f32[4,136,128]{2,1,0:T(8,128)}, f32[4,136,128]{2,1,0:T(8,128)}, u32[]{:S(2)}, u32[]{:S(2)}) collective-permute-start(f32[4,136,128]{2,1,0:T(8,128)} %get-tuple-element.76), channel_id=1, source_target_pairs={{32,0},{40,8},{48,16},{56,24},{64,32},{72,40},{80,48},{88,56},{96,... | collective-permute-start | bytes 835592 | tf_op jit(solution)/shard_map/ppermute | solution.py:36
  56.2 62.6 %copy-start.14 = (pred[384,384]{1,0:T(8,128)(4,1)}, pred[384,384]{1,0:T(8,128)(4,1)S(1)}, u32[]{:S(2)}) copy-start(pred[384,384]{1,0:T(8,128)(4,1)S(1)} %fusion.26) | copy-start | bytes 442372
  56.3 9.8 %collective-permute-start.3 = (f32[4,136,128]{2,1,0:T(8,128)}, f32[4,136,128]{2,1,0:T(8,128)S(1)}, u32[]{:S(2)}, u32[]{:S(2)}) collective-permute-start(f32[4,136,128]{2,1,0:T(8,128)} %get-tuple-element.75), channel_id=1, source_target_pairs={{0,32},{8,40},{16,48},{24,56},{32,64},{40,72},{48,80},{56,88},{64,... | collective-permute-start | bytes 835592 | tf_op jit(solution)/shard_map/ppermute | solution.py:35
  67.4 9.8 %collective-permute-start.4 = (f32[4,136,128]{2,1,0:T(8,128)S(1)}, f32[4,136,128]{2,1,0:T(8,128)S(1)}, u32[]{:S(2)}, u32[]{:S(2)}) collective-permute-start(f32[4,136,128]{2,1,0:T(8,128)S(1)} %pad_maximum_fusion.5), channel_id=1, source_target_pairs={{0,64},{8,72},{16,80},{24,88},{32,96},{40,104},{48,112},{56,120},{... | collective-permute-start | bytes 835592 | tf_op jit(solution)/shard_map/ppermute | solution.py:35
  73.2 22.3 %collective-permute-start.7 = (f32[4,136,128]{2,1,0:T(8,128)S(1)}, f32[4,136,128]{2,1,0:T(8,128)S(1)}, u32[]{:S(2)}, u32[]{:S(2)}) collective-permute-start(f32[4,136,128]{2,1,0:T(8,128)S(1)} %pad_maximum_fusion.7), channel_id=1, source_target_pairs={{64,0},{72,8},{80,16},{88,24},{96,32},{104,40},{112,48},{120,56},{... | collective-permute-start | bytes 835592 | tf_op jit(solution)/shard_map/ppermute | solution.py:36
  75.4 25.2 %copy-start.13 = (f32[4,128,128]{2,1,0:T(8,128)S(1)}, f32[4,128,128]{2,1,0:T(8,128)}, u32[]{:S(2)}) copy-start(f32[4,128,128]{2,1,0:T(8,128)} %get-tuple-element.31) | copy-start | bytes 786436
  77.3 22.2 %collective-permute-start.5 = (f32[4,136,128]{2,1,0:T(8,128)S(1)}, f32[4,136,128]{2,1,0:T(8,128)S(1)}, u32[]{:S(2)}, u32[]{:S(2)}) collective-permute-start(f32[4,136,128]{2,1,0:T(8,128)S(1)} %pad_maximum_fusion.6), channel_id=1, source_target_pairs={{0,128},{8,136},{16,144},{24,152},{32,160},{40,168},{48,176},{56,1... | collective-permute-start | bytes 835592 | tf_op jit(solution)/shard_map/ppermute | solution.py:35
  95.6 13.8 %collective-permute-start.8 = (f32[4,136,128]{2,1,0:T(8,128)S(1)}, f32[4,136,128]{2,1,0:T(8,128)S(1)}, u32[]{:S(2)}, u32[]{:S(2)}) collective-permute-start(f32[4,136,128]{2,1,0:T(8,128)S(1)} %pad_maximum_fusion.8), channel_id=1, source_target_pairs={{128,0},{136,8},{144,16},{152,24},{160,32},{168,40},{176,48},{184,... | collective-permute-start | bytes 835592 | tf_op jit(solution)/shard_map/ppermute | solution.py:36
  112.0 6.8 %copy-start = (bf16[1,384,2048]{1,2,0:T(8,128)(2,1)S(1)}, bf16[1,384,2048]{1,2,0:T(8,128)(2,1)}, u32[]{:S(2)}) copy-start(bf16[1,384,2048]{1,2,0:T(8,128)(2,1)} %copy.103) | copy-start | bytes 4718596
  112.0 6.8 %copy-start.2 = (bf16[48,8,16,128]{3,2,1,0:T(8,128)(2,1)S(1)}, bf16[48,8,16,128]{3,2,1,0:T(8,128)(2,1)}, u32[]{:S(2)}) copy-start(bf16[48,8,16,128]{3,2,1,0:T(8,128)(2,1)} %copy.105) | copy-start | bytes 4718596
  112.2 17.9 %collective-permute-start.9 = (f32[4,256,128]{2,1,0:T(8,128)S(1)}, f32[4,256,128]{2,1,0:T(8,128)S(1)}, u32[]{:S(2)}, u32[]{:S(2)}) collective-permute-start(f32[4,256,128]{2,1,0:T(8,128)S(1)} %get-tuple-element.58), channel_id=1, source_target_pairs={{0,8},{8,16},{16,24},{24,0},{32,40},{40,48},{48,56},{56,32},{64,72... | collective-permute-start | bytes 1572872 | tf_op jit(solution)/shard_map/ppermute | solution.py:57
  113.9 21.8 %collective-permute-start.10 = (f32[4,256,128]{2,1,0:T(8,128)S(1)}, f32[4,256,128]{2,1,0:T(8,128)S(1)}, u32[]{:S(2)}, u32[]{:S(2)}) collective-permute-start(f32[4,256,128]{2,1,0:T(8,128)S(1)} %get-tuple-element.57), channel_id=1, source_target_pairs={{0,16},{8,24},{16,0},{24,8},{32,48},{40,56},{48,32},{56,40},{64,80... | collective-permute-start | bytes 1572872 | tf_op jit(solution)/shard_map/ppermute | solution.py:57
  118.8 16.9 %collective-permute-start.11 = (f32[4,256,128]{2,1,0:T(8,128)S(1)}, f32[4,256,128]{2,1,0:T(8,128)S(1)}, u32[]{:S(2)}, u32[]{:S(2)}) collective-permute-start(f32[4,256,128]{2,1,0:T(8,128)S(1)} %get-tuple-element.56), channel_id=1, source_target_pairs={{0,24},{8,0},{16,8},{24,16},{32,56},{40,32},{48,40},{56,48},{64,88... | collective-permute-start | bytes 1572872 | tf_op jit(solution)/shard_map/ppermute | solution.py:57
  144.0 7.3 %copy-start.15 = (pred[384,384]{1,0:T(8,128)(4,1)S(1)}, pred[384,384]{1,0:T(8,128)(4,1)}, u32[]{:S(2)}) copy-start(pred[384,384]{1,0:T(8,128)(4,1)} %copy-done.14) | copy-start | bytes 442372
  146.6 14.5 %collective-permute-start.12 = (f32[16]{0:T(128)S(1)}, f32[16]{0:T(128)S(1)}, u32[]{:S(2)}, u32[]{:S(2)}) collective-permute-start(f32[16]{0:T(128)S(1)} %multiply_reduce_fusion), channel_id=1, source_target_pairs={{0,8},{8,0},{16,24},{24,16},{32,40},{40,32},{48,56},{56,48},{64,72... | collective-permute-start | bytes 200 | tf_op jit(solution)/shard_map/ppermute | solution.py:113
  146.9 14.2 %collective-permute-start.13 = (f32[16]{0:T(128)S(1)}, f32[16]{0:T(128)S(1)}, u32[]{:S(2)}, u32[]{:S(2)}) collective-permute-start(f32[16]{0:T(128)S(1)} %multiply_reduce_fusion), channel_id=1, source_target_pairs={{0,16},{8,24},{16,0},{24,8},{32,48},{40,56},{48,32},{56,40},{64,80... | collective-permute-start | bytes 200 | tf_op jit(solution)/shard_map/ppermute | solution.py:113
  150.3 10.9 %collective-permute-start.14 = (f32[16]{0:T(128)S(1)}, f32[16]{0:T(128)S(1)}, u32[]{:S(2)}, u32[]{:S(2)}) collective-permute-start(f32[16]{0:T(128)S(1)} %multiply_reduce_fusion), channel_id=1, source_target_pairs={{0,24},{8,16},{16,8},{24,0},{32,56},{40,48},{48,40},{56,32},{64,88... | collective-permute-start | bytes 200 | tf_op jit(solution)/shard_map/ppermute | solution.py:113
  158.4 19.6 %copy-start.4 = (bf16[384,16,128]{0,2,1:T(8,128)(2,1)S(1)}, bf16[384,16,128]{0,2,1:T(8,128)(2,1)}, u32[]{:S(2)}) copy-start(bf16[384,16,128]{0,2,1:T(8,128)(2,1)} %get-tuple-element.50) | copy-start | bytes 4718596
  161.1 29.5 %copy-start.12 = (bf16[384,16,128]{0,2,1:T(8,128)(2,1)S(1)}, bf16[384,16,128]{0,2,1:T(8,128)(2,1)}, u32[]{:S(2)}) copy-start(bf16[384,16,128]{0,2,1:T(8,128)(2,1)} %fusion.12) | copy-start | bytes 4718596
  161.2 12.8 %collective-permute-start.15 = (f32[16]{0:T(128)S(1)}, f32[16]{0:T(128)S(1)}, u32[]{:S(2)}, u32[]{:S(2)}) collective-permute-start(f32[16]{0:T(128)S(1)} %fusion.66), channel_id=1, source_target_pairs={{0,32},{8,40},{16,48},{24,56},{32,0},{40,8},{48,16},{56,24},{64,96... | collective-permute-start | bytes 200 | tf_op jit(solution)/shard_map/ppermute | solution.py:113
  163.8 10.3 %collective-permute-start.16 = (f32[16]{0:T(128)S(1)}, f32[16]{0:T(128)S(1)}, u32[]{:S(2)}, u32[]{:S(2)}) collective-permute-start(f32[16]{0:T(128)S(1)} %fusion.66), channel_id=1, source_target_pairs={{0,64},{8,72},{16,80},{24,88},{32,96},{40,104},{48,112},{56,120},{... | collective-permute-start | bytes 200 | tf_op jit(solution)/shard_map/ppermute | solution.py:113
  172.6 5.3 %collective-permute-start.17 = (f32[16]{0:T(128)S(1)}, f32[16]{0:T(128)S(1)}, u32[]{:S(2)}, u32[]{:S(2)}) collective-permute-start(f32[16]{0:T(128)S(1)} %fusion.66), channel_id=1, source_target_pairs={{0,96},{8,104},{16,112},{24,120},{32,64},{40,72},{48,80},{56,88},{... | collective-permute-start | bytes 200 | tf_op jit(solution)/shard_map/ppermute | solution.py:113
  177.9 7.5 %collective-permute-start.18 = (f32[16]{0:T(128)S(1)}, f32[16]{0:T(128)S(1)}, u32[]{:S(2)}, u32[]{:S(2)}) collective-permute-start(f32[16]{0:T(128)S(1)} %fusion.63), channel_id=1, source_target_pairs={{0,128},{8,136},{16,144},{24,152},{32,160},{40,168},{48,176},{56,1... | collective-permute-start | bytes 200 | tf_op jit(solution)/shard_map/ppermute | solution.py:113
  185.5 1.9 collective-permute-start.19
  185.5 3.6 %collective-permute-start.20 = (f32[16]{0:T(128)S(1)}, f32[16]{0:T(128)S(1)}, u32[]{:S(2)}, u32[]{:S(2)}) collective-permute-start(f32[16]{0:T(128)S(1)} %fusion.60), channel_id=1, source_target_pairs={{0,2},{1,3},{2,0},{3,1},{4,6},{5,7},{6,4},{7,5},{8,10},{9,11},{10,... | collective-permute-start | bytes 200 | tf_op jit(solution)/shard_map/ppermute | solution.py:113
  186.4 3.0 %collective-permute-start.21 = (f32[16]{0:T(128)S(1)}, f32[16]{0:T(128)S(1)}, u32[]{:S(2)}, u32[]{:S(2)}) collective-permute-start(f32[16]{0:T(128)S(1)} %fusion.60), channel_id=1, source_target_pairs={{0,3},{1,2},{2,1},{3,0},{4,7},{5,6},{6,5},{7,4},{8,11},{9,10},{10,... | collective-permute-start | bytes 200 | tf_op jit(solution)/shard_map/ppermute | solution.py:113
  189.4 5.1 %collective-permute-start.22 = (f32[16]{0:T(128)S(1)}, f32[16]{0:T(128)S(1)}, u32[]{:S(2)}, u32[]{:S(2)}) collective-permute-start(f32[16]{0:T(128)S(1)} %fusion.59), channel_id=1, source_target_pairs={{0,4},{1,5},{2,6},{3,7},{4,0},{5,1},{6,2},{7,3},{8,12},{9,13},{10,... | collective-permute-start | bytes 200 | tf_op jit(solution)/shard_map/ppermute | solution.py:113

commit v6 on v5

--- a/solution.py
+++ b/solution.py
@@ -4,6 +4,7 @@
 import jax.numpy as jnp
 from jax import lax
 from jax.sharding import PartitionSpec as P
+from jax.experimental import pallas as pl
 
 HEADS = 16
 HEAD_DIM = 128
@@ -32,6 +33,13 @@
     while shift < count:
         up = [(i, i + shift) for i in range(count - shift)]
         down = [(i + shift, i) for i in range(count - shift)]
+        if 2 * shift >= count:
+            place = lax.axis_index(axis)
+            sent = jnp.where(place < count - shift, fwd, bwd)
+            got = lax.ppermute(sent, axis, up + down)
+            excl = jnp.where(place >= shift, combine(got, excl), excl)
+            rexcl = jnp.where(place < count - shift, combine(got, rexcl), rexcl)
+            break
         got = lax.ppermute(fwd, axis, up)
         rgot = lax.ppermute(bwd, axis, down)
         excl = combine(got, excl)
@@ -128,6 +136,42 @@
     return value
 
 
+def split_dot(scaled, other):
+    high = scaled.astype(jnp.bfloat16)
+    low = (scaled - high.astype(jnp.float32)).astype(jnp.bfloat16)
+    return jnp.dot(high, other, preferred_element_type=jnp.float32) + jnp.dot(
+        low, other, preferred_element_type=jnp.float32
+    )
+
+
+def summary_kernel(out_ref, in_ref, key_ref, value_ref, query_ref, grad_ref, state_ref, back_ref):
+    per = state_ref.shape[0]
+    width = state_ref.shape[2]
+    for j in range(per):
+        cols = slice(j * width, (j + 1) * width)
+        keys_t = (out_ref[j] * key_ref[0, :, cols].astype(jnp.float32)).T
+        state_ref[j] = split_dot(keys_t, value_ref[0, :, cols])
+        query_t = (in_ref[j] * query_ref[0, :, cols].astype(jnp.float32)).T
+        back_ref[j] = split_dot(query_t, grad_ref[0, :, cols])
+
+
+def block_summaries(carry_out, carry_in, keys, values, queries, output_gradient):
+    rows = keys.shape[1]
+    per = 4
+    steps = HEADS // per
+    carry_spec = pl.BlockSpec((per, rows, 1), lambda i: (i, 0, 0))
+    data_spec = pl.BlockSpec((1, rows, per * HEAD_DIM), lambda i: (0, 0, i))
+    out_spec = pl.BlockSpec((per, HEAD_DIM, HEAD_DIM), lambda i: (i, 0, 0))
+    shape = jax.ShapeDtypeStruct((HEADS, HEAD_DIM, HEAD_DIM), jnp.float32)
+    return pl.pallas_call(
+        summary_kernel,
+        grid=(steps,),
+        in_specs=[carry_spec, carry_spec, data_spec, data_spec, data_spec, data_spec],
+        out_specs=[out_spec, out_spec],
+        out_shape=[shape, shape],
+    )(carry_out.T[:, :, None], carry_in.T[:, :, None], keys, values, queries, output_gradient)
+
+
 def block_mask_list(head_decay_rate, cutoff_list, row_position, start_list):
     is_start = jnp.any(row_position[:, None] == start_list[None, :], axis=1)
     seg_local = jnp.cumsum(is_start.astype(jnp.int32))
@@ -174,11 +218,8 @@
     value_f = value_block.astype(jnp.float32)
     grad_f = gradient_block.astype(jnp.float32)
     query_f = query_block.astype(jnp.float32)
-    state_local = jnp.einsum(
-        "the,thf->hef", carry_out[:, :, None] * key_f, value_f, precision=state_mode
-    )
-    back_local = jnp.einsum(
-        "she,shf->hef", carry_in[:, :, None] * query_f, grad_f, precision=state_mode
+    state_local, back_local = block_summaries(
+        carry_out, carry_in, keys, values, queries, output_gradient
     )
     state_input, backward_input = carried_both(decay_all, state_local, back_local, "seq")
     weight = weights_of(cum_log, seg_local)

time: 196 us -> 204 us (1.041)
  Pallas kernels: 0 us -> 8.21 us
  other arithmetic: 16.6 us -> 24.5 us
  matrix products: 25.4 us -> 21 us
  starting transfers between devices: 65.4 us -> 61.5 us
  waiting for transfers between devices: 65.9 us -> 62 us
  local copies, waits for them, and re-layouts: 19.7 us -> 23.3 us
    ppermute x3 -> x2, starting transfers between devices: 28.3 us -> 10.4 us  [group_scan(): got = lax.ppermute(fwd, axis, up)]
    ppermute x0 -> x1, starting transfers between devices: none -> 11.8 us  [group_scan(): got = lax.ppermute(sent, axis, up + down)]
    pallas_call x0 -> x1, Pallas kernels: none -> 8.21 us  [block_summaries(): pl.pallas_call(summary_kernel, grid=(steps,), in_specs=[carry_spec, carry...]
    ppermute x3 -> x2, waiting for transfers between devices: 11.4 us -> 16.7 us  [group_scan(): rgot = lax.ppermute(bwd, axis, down)]
    ppermute x11, starting transfers between devices: 20.7 us -> 25.3 us  [digit_sum(): lax.ppermute(value, axis, [(i, i ^ k * step) for i in range(count)])]
    ppermute x11, waiting for transfers between devices: 14.1 us -> 9.68 us  [digit_sum(): lax.ppermute(value, axis, [(i, i ^ k * step) for i in range(count)])]
    dot_general x2 -> x0, matrix products: 4.33 us -> none  [the longest x1 2.91 us: on_device(): jnp.einsum('she,shf->hef', carry_in[:, :, None] * query_f, grad_f, precis...]
    select_n x0 -> x2, other arithmetic: none -> 4.23 us  [the longest x1 3.46 us: block_mask_list(): carry_in = jnp.where((seg_local == 0)[:, None], jnp.exp(cum_log), 0.0)]
  transfers between devices with their start and end apart: 23 -> 22, of which waited for: 15 -> 14; matrix products, arithmetic and copies ran while one was open for 11% -> 14% of each run, Pallas kernels for 0% -> 0%
where the time goes in v6:
time: 204 us; the launch traced here: 203 us
  waiting for transfers between devices  62 us (30%)
  starting transfers between devices  61.5 us (30%)
  other arithmetic  24.5 us (12%)
  local copies, waits for them, and re-layouts  23.3 us (11%)
  matrix products  21 us (10%)
  Pallas kernels  8.21 us (4%)
  between operations  2.18 us (1%)
    ppermute x6, waiting for transfers between devices, row_exchange(): got.append(lax.ppermute(send, axis, pairs))  32 us
    ppermute x11, starting transfers between devices, digit_sum(): lax.ppermute(value, axis, [(i, i ^ k * step) for i in range(count)])  25.3 us
    ppermute x2, waiting for transfers between devices, group_scan(): rgot = lax.ppermute(bwd, axis, down)  16.7 us
    unnamed x82, local copies, waits for them, and re-layouts  12.4 us
    ppermute x1, starting transfers between devices, group_scan(): got = lax.ppermute(sent, axis, up + down)  11.8 us
    ppermute x6, starting transfers between devices, row_exchange(): got.append(lax.ppermute(send, axis, pairs))  11.4 us
    ppermute x2, starting transfers between devices, group_scan(): got = lax.ppermute(fwd, axis, up)  10.4 us
    ppermute x11, waiting for transfers between devices, digit_sum(): lax.ppermute(value, axis, [(i, i ^ k * step) for i in range(count)])  9.68 us
  transfers between devices with their start and end apart: 22, of which 14 were waited for; matrix products, arithmetic and copies ran while one was open for 14% of the time, Pallas kernels for 0%

profile of v6, /device:TPU:6, one launch (start us, length us, event | category | flops | bytes accessed | tf_op | source)
XLA Modules:
  0.0 202.7 jit_solution(8416130101034604426)
XLA Ops:
  1.3 0.7 broadcast_subtract_fusion
  2.1 0.9 reduce-window.24
  3.9 0.8 reduce-window_clone.1
  8.3 3.1 %reduce_window_sum.75 = f32[16,384,1]{2,1,0:T(8,128)S(1)} reshape(f32[16,3,128]{2,1,0:T(4,128)S(1)} %copy.84) | data formatting | bytes 49152 | tf_op jit(solution)/shard_map/reduce_window_sum
  11.4 3.5 %exponential_select_fusion.1 = (f32[16,384,1]{2,1,0:T(8,128)}, f32[16,384,1]{2,1,0:T(8,128)}) fusion(f32[16,384,1]{2,1,0:T(8,128)S(1)} %reduce_window_sum.75, pred[384]{0:T(512)(128)(4,1)S(1)} %get-tuple-element.49, f32[16]{0:T(128)S(1)} %slice_reduce_fusion.1, pred[384]{0:T(512)(128)(4,1)S(1)} %broadcast_compare_fusion), kind=kLoop, calls=%fused_computation.18 | loop fusion | flops 18432 | bytes 74560 | tf_op jit(solution)/shard_map/jit(_where)/select_n | solution.py:186
  14.8 8.2 %shard_map.102 = (f32[16,128,128]{2,1,0:T(8,128)}, f32[16,128,128]{2,1,0:T(8,128)}) custom-call(f32[16,384,1]{2,1,0:T(8,128)} %get-tuple-element.64.out_ref, f32[16,384,1]{2,1,0:T(8,128)} %get-tuple-element.63.in_ref, bf16[1,384,2048]{2,1,0:T(8,128)(2,1)} %key_ref.1, bf16[1,384,2048]{2,1,0:T(8,128)(2,1)} %value_ref.1, bf16[1,384,2048]{2,1,0:T(8,128)(2,1)} %query_ref.1, ...), custom_call_target="tpu_custom_call" | custom-call | tf_op jit(solution)/shard_map/pallas_call | solution.py:166
  23.1 1.7 pad_maximum_fusion
  24.8 1.2 dynamic-slice_bitcast_fusion
  26.0 1.6 collective-permute-start
  27.6 2.9 %collective-permute-start.1 = (f32[4,264,128]{2,1,0:T(8,128)}, f32[4,264,128]{2,1,0:T(8,128)}, u32[]{:S(2)}, u32[]{:S(2)}) collective-permute-start(f32[4,264,128]{2,1,0:T(8,128)} %get-tuple-element.68), channel_id=1, source_target_pairs={{0,16},{8,24},{16,0},{24,8},{32,48},{40,56},{48,32},{56,40},{64,80... | collective-permute-start | bytes 1622024 | tf_op jit(solution)/shard_map/ppermute | solution.py:65
  30.5 1.3 collective-permute-start.2
  31.9 0.7 exponential_select_fusion.3
  32.6 9.0 %collective-permute-done = f32[4,264,128]{2,1,0:T(8,128)S(1)} collective-permute-done((f32[4,264,128]{2,1,0:T(8,128)}, f32[4,264,128]{2,1,0:T(8,128)S(1)}, u32[]{:S(2)}, u32[]{:S(2)}) %collective-permute-start) | collective-permute-done | bytes 540704 | tf_op jit(solution)/shard_map/ppermute | solution.py:65
  41.5 12.9 %collective-permute-done.1 = f32[4,264,128]{2,1,0:T(8,128)} collective-permute-done((f32[4,264,128]{2,1,0:T(8,128)}, f32[4,264,128]{2,1,0:T(8,128)}, u32[]{:S(2)}, u32[]{:S(2)}) %collective-permute-start.1) | collective-permute-done | bytes 540704 | tf_op jit(solution)/shard_map/ppermute | solution.py:65
  54.4 1.4 fusion.21
  56.4 0.8 fusion.66
  57.2 0.9 fusion.42
  58.3 1.3 collective-permute-start.5
  59.6 4.6 %collective-permute-start.3 = (f32[4,136,128]{2,1,0:T(8,128)S(1)}, f32[4,136,128]{2,1,0:T(8,128)S(1)}, u32[]{:S(2)}, u32[]{:S(2)}) collective-permute-start(f32[4,136,128]{2,1,0:T(8,128)S(1)} %get-tuple-element.86), channel_id=1, source_target_pairs={{0,32},{8,40},{16,48},{24,56},{32,64},{40,72},{48,80},{56,88},{64,... | collective-permute-start | bytes 835592 | tf_op jit(solution)/shard_map/ppermute | solution.py:43
  65.0 2.9 %collective-permute-done.5 = f32[4,136,128]{2,1,0:T(8,128)S(1)} collective-permute-done((f32[4,136,128]{2,1,0:T(8,128)S(1)}, f32[4,136,128]{2,1,0:T(8,128)S(1)}, u32[]{:S(2)}, u32[]{:S(2)}) %collective-permute-start.5) | collective-permute-done | bytes 278560 | tf_op jit(solution)/shard_map/ppermute | solution.py:44
  67.9 1.2 collective-permute-done.3
  70.0 5.9 %collective-permute-start.4 = (f32[4,136,128]{2,1,0:T(8,128)S(1)}, f32[4,136,128]{2,1,0:T(8,128)S(1)}, u32[]{:S(2)}, u32[]{:S(2)}) collective-permute-start(f32[4,136,128]{2,1,0:T(8,128)S(1)} %pad_maximum_fusion.5), channel_id=1, source_target_pairs={{0,64},{8,72},{16,80},{24,88},{32,96},{40,104},{48,112},{56,120},{... | collective-permute-start | bytes 835592 | tf_op jit(solution)/shard_map/ppermute | solution.py:43
  75.9 1.3 collective-permute-start.6
  77.5 2.5 %collective-permute-done.4 = f32[4,136,128]{2,1,0:T(8,128)S(1)} collective-permute-done((f32[4,136,128]{2,1,0:T(8,128)S(1)}, f32[4,136,128]{2,1,0:T(8,128)S(1)}, u32[]{:S(2)}, u32[]{:S(2)}) %collective-permute-start.4) | collective-permute-done | bytes 278560 | tf_op jit(solution)/shard_map/ppermute | solution.py:43
  80.0 13.7 %collective-permute-done.6 = f32[4,136,128]{2,1,0:T(8,128)S(1)} collective-permute-done((f32[4,136,128]{2,1,0:T(8,128)S(1)}, f32[4,136,128]{2,1,0:T(8,128)S(1)}, u32[]{:S(2)}, u32[]{:S(2)}) %collective-permute-start.6) | collective-permute-done | bytes 278560 | tf_op jit(solution)/shard_map/ppermute | solution.py:44
  93.9 0.8 maximum_select_fusion
  94.7 11.8 %collective-permute-start.7 = (f32[4,136,128]{2,1,0:T(8,128)}, f32[4,136,128]{2,1,0:T(8,128)}, u32[]{:S(2)}, u32[]{:S(2)}) collective-permute-start(f32[4,136,128]{2,1,0:T(8,128)} %maximum_select_fusion), channel_id=1, source_target_pairs={{0,128},{8,136},{16,144},{24,152},{32,160},{40,168},{48,176},{56,1... | collective-permute-start | bytes 835592 | tf_op jit(solution)/shard_map/ppermute | solution.py:39
  107.1 0.9 copy.92
  108.0 2.6 %copy.106 = bf16[1,384,2048]{1,2,0:T(8,128)(2,1)} copy(bf16[1,384,2048]{2,1,0:T(8,128)(2,1)} %grad_ref.1) | data formatting | bytes 3145728 | tf_op jit(solution)/shard_map/reshape | solution.py:209
  110.5 1.9 copy.87
  112.6 3.0 %copy.108 = bf16[48,8,16,128]{3,2,1,0:T(8,128)(2,1)} copy(bf16[48,8,16,128]{3,1,2,0:T(8,128)(2,1)} %bitcast.209) | data formatting | bytes 3145728
  115.6 0.8 slice_reduce_fusion.4
  116.4 0.8 slice_reduce_fusion.2
  117.2 0.8 slice_multiply_fusion.1
  118.3 1.5 multiply_add_fusion.9
  119.8 1.1 multiply_add_fusion.4
  120.9 1.1 multiply_add_fusion.5
  122.1 1.2 multiply_add_fusion.2
  123.8 1.8 collective-permute-start.8
  125.6 3.7 %collective-permute-start.9 = (f32[4,256,128]{2,1,0:T(8,128)S(1)}, f32[4,256,128]{2,1,0:T(8,128)S(1)}, u32[]{:S(2)}, u32[]{:S(2)}) collective-permute-start(f32[4,256,128]{2,1,0:T(8,128)S(1)} %get-tuple-element.71), channel_id=1, source_target_pairs={{0,16},{8,24},{16,0},{24,8},{32,48},{40,56},{48,32},{56,40},{64,80... | collective-permute-start | bytes 1572872 | tf_op jit(solution)/shard_map/ppermute | solution.py:65
  129.4 3.7 %multiply_convert_fusion.1 = bf16[16,384,384]{2,1,0:T(8,128)(2,1)S(1)} fusion(f32[16,384]{1,0:T(8,128)S(1)} %copy-done.18, pred[384,384]{1,0:T(8,128)(4,1)S(1)} %fusion.19, bf16[384,16,128]{0,2,1:T(8,128)(2,1)S(1)} %bitcast.213, bf16[384,16,128]{2,1,0:T(8,128)(2,1)S(1)} %bitcast.215), kind=kOutput, calls=%fused_computation.1 | convolution fusion | flops 615776256 | bytes 8036352 | tf_op jit(solution)/shard_map/shf,thf->hst/dot_general | solution.py:227
  133.1 4.5 %collective-permute-done.8 = f32[4,256,128]{2,1,0:T(8,128)S(1)} collective-permute-done((f32[4,256,128]{2,1,0:T(8,128)S(1)}, f32[4,256,128]{2,1,0:T(8,128)S(1)}, u32[]{:S(2)}, u32[]{:S(2)}) %collective-permute-start.8) | collective-permute-done | bytes 524320 | tf_op jit(solution)/shard_map/ppermute | solution.py:65
  137.7 5.6 %collective-permute-done.9 = f32[4,256,128]{2,1,0:T(8,128)S(1)} collective-permute-done((f32[4,256,128]{2,1,0:T(8,128)S(1)}, f32[4,256,128]{2,1,0:T(8,128)S(1)}, u32[]{:S(2)}, u32[]{:S(2)}) %collective-permute-start.9) | collective-permute-done | bytes 524320 | tf_op jit(solution)/shard_map/ppermute | solution.py:65
  143.8 1.0 fusion.14
  144.7 1.4 fusion.11
  146.2 2.7 %fusion.16 = f32[16,128,384]{2,1,0:T(8,128)} fusion(bf16[384,16,128]{0,2,1:T(8,128)(2,1)S(1)} %bitcast.197, f32[16,256,128]{2,1,0:T(8,128)S(1)} %bitcast.206), kind=kOutput, calls=%fused_computation.28 | convolution fusion | flops 603979776 | bytes 5767168 | tf_op jit(solution)/shard_map/the,hef->thf/dot_general | solution.py:235
  148.9 2.8 %multiply_reduce_fusion = (f32[384,16]{0,1:T(8,128)S(1)}, bf16[384,16,128]{0,2,1:T(8,128)(2,1)}) fusion(bf16[384,16,128]{0,2,1:T(8,128)(2,1)S(1)} %bitcast.201, f32[16,128,384]{2,1,0:T(8,128)S(1)} %fusion.14, f32[384,16]{0,1:T(8,128)S(1)} %copy-done.15, bf16[16,384,384]{2,1,0:T(8,128)(2,1)S(1)} %multiply_convert_fusion.1, ...), kind=kOutput, calls=%fused_computation.16 | convolution fusion | flops 608692224 | bytes 12632064 | tf_op jit(solution)/shard_map/hst,the->she/dot_general | solution.py:238
  151.6 2.4 %multiply_reduce_fusion.1 = (f32[384,16]{0,1:T(8,128)S(1)}, bf16[384,16,128]{0,2,1:T(8,128)(2,1)}) fusion(bf16[384,16,128]{0,2,1:T(8,128)(2,1)S(1)} %bitcast.199, f32[16,128,384]{2,1,0:T(8,128)S(1)} %fusion.11, f32[384,16]{0,1:T(8,128)S(1)} %copy-done.14, bf16[384,16,128]{0,2,1:T(8,128)(2,1)S(1)} %bitcast.202, ...), kind=kOutput, calls=%fused_computation.17 | convolution fusion | flops 608692224 | bytes 12632064 | tf_op jit(solution)/shard_map/hst,she->the/dot_general | solution.py:244
  154.2 3.6 %collective-permute-start.12 = (f32[16]{0:T(128)S(1)}, f32[16]{0:T(128)S(1)}, u32[]{:S(2)}, u32[]{:S(2)}) collective-permute-start(f32[16]{0:T(128)S(1)} %multiply_reduce_fusion.2), channel_id=1, source_target_pairs={{0,16},{8,24},{16,0},{24,8},{32,48},{40,56},{48,32},{56,40},{64,80... | collective-permute-start | bytes 200 | tf_op jit(solution)/shard_map/ppermute | solution.py:121
  157.9 1.1 collective-permute-start.13
  158.9 7.0 %fusion.8 = bf16[384,16,128]{0,2,1:T(8,128)(2,1)} fusion(f32[16,128,384]{2,1,0:T(8,128)} %fusion.16, bf16[384,16,128]{0,2,1:T(8,128)(2,1)} %bitcast.212, f32[16,384]{1,0:T(8,128)S(1)} %copy-done.18, pred[384,384]{1,0:T(8,128)(4,1)S(1)} %fusion.19, bf16[384,16,128]{0,2,1:T(8,128)(2,1)S(1)} %bitcast.203, bf16[384,16,128]{0,2,1:T(8,128)(2,1)S(1)} %bitcast.200, ...), kind=kOutput, calls=%fused_computation.11 | convolution fusion | flops 1222115328 | bytes 9633792 | tf_op jit(solution)/shard_map/hst,shf->thf/dot_general | solution.py:232
  166.0 2.7 %copy.99 = bf16[1,384,2048]{2,1,0:T(8,128)(2,1)} copy(bf16[1,384,2048]{1,2,0:T(8,128)(2,1)} %bitcast.211) | data formatting | bytes 3145728
  168.8 11.3 %collective-permute-start.15 = (f32[16]{0:T(128)S(1)}, f32[16]{0:T(128)S(1)}, u32[]{:S(2)}, u32[]{:S(2)}) collective-permute-start(f32[16]{0:T(128)S(1)} %fusion.57), channel_id=1, source_target_pairs={{0,64},{8,72},{16,80},{24,88},{32,96},{40,104},{48,112},{56,120},{... | collective-permute-start | bytes 200 | tf_op jit(solution)/shard_map/ppermute | solution.py:121
  180.1 1.4 collective-permute-start.16
  181.6 3.8 %collective-permute-done.16 = f32[16]{0:T(128)S(1)} collective-permute-done((f32[16]{0:T(128)S(1)}, f32[16]{0:T(128)S(1)}, u32[]{:S(2)}, u32[]{:S(2)}) %collective-permute-start.16) | collective-permute-done | bytes 96 | tf_op jit(solution)/shard_map/ppermute | solution.py:121
  185.4 4.7 %collective-permute-start.17 = (f32[16]{0:T(128)S(1)}, f32[16]{0:T(128)S(1)}, u32[]{:S(2)}, u32[]{:S(2)}) collective-permute-start(f32[16]{0:T(128)S(1)} %fusion.54), channel_id=1, source_target_pairs={{0,128},{8,136},{16,144},{24,152},{32,160},{40,168},{48,176},{56,1... | collective-permute-start | bytes 200 | tf_op jit(solution)/shard_map/ppermute | solution.py:121
  190.1 1.6 copy.100
  191.7 1.2 collective-permute-done.17
  193.0 1.0 collective-permute-start.19
  194.0 0.8 collective-permute-start.20
  194.9 1.7 collective-permute-done.19
  197.0 1.2 collective-permute-start.21
  198.2 1.6 copy.101
  199.8 2.3 %collective-permute-done.21 = f32[16]{0:T(128)S(1)} collective-permute-done((f32[16]{0:T(128)S(1)}, f32[16]{0:T(128)S(1)}, u32[]{:S(2)}, u32[]{:S(2)}) %collective-permute-start.21) | collective-permute-done | bytes 96 | tf_op jit(solution)/shard_map/ppermute | solution.py:121
  (145 shorter events, 10.5 us)
Async XLA Ops:
  6.1 2.0 copy-start.16
  26.0 15.5 %collective-permute-start = (f32[4,264,128]{2,1,0:T(8,128)}, f32[4,264,128]{2,1,0:T(8,128)S(1)}, u32[]{:S(2)}, u32[]{:S(2)}) collective-permute-start(f32[4,264,128]{2,1,0:T(8,128)} %get-tuple-element.69), channel_id=1, source_target_pairs={{0,8},{8,16},{16,24},{24,0},{32,40},{40,48},{48,56},{56,32},{64,72... | collective-permute-start | bytes 1622024 | tf_op jit(solution)/shard_map/ppermute | solution.py:65
  27.6 26.8 %collective-permute-start.1 = (f32[4,264,128]{2,1,0:T(8,128)}, f32[4,264,128]{2,1,0:T(8,128)}, u32[]{:S(2)}, u32[]{:S(2)}) collective-permute-start(f32[4,264,128]{2,1,0:T(8,128)} %get-tuple-element.68), channel_id=1, source_target_pairs={{0,16},{8,24},{16,0},{24,8},{32,48},{40,56},{48,32},{56,40},{64,80... | collective-permute-start | bytes 1622024 | tf_op jit(solution)/shard_map/ppermute | solution.py:65
  30.5 23.9 %collective-permute-start.2 = (f32[4,264,128]{2,1,0:T(8,128)}, f32[4,264,128]{2,1,0:T(8,128)}, u32[]{:S(2)}, u32[]{:S(2)}) collective-permute-start(f32[4,264,128]{2,1,0:T(8,128)} %get-tuple-element.67), channel_id=1, source_target_pairs={{0,24},{8,0},{16,8},{24,16},{32,56},{40,32},{48,40},{56,48},{64,88... | collective-permute-start | bytes 1622024 | tf_op jit(solution)/shard_map/ppermute | solution.py:65
  55.8 2.4 %copy-start.4 = (f32[1,4,264,128]{3,2,1,0:T(8,128)}, f32[1,4,264,128]{3,2,1,0:T(8,128)S(1)}, u32[]{:S(2)}) copy-start(f32[1,4,264,128]{3,2,1,0:T(8,128)S(1)} %get-tuple-element.54) | copy-start | bytes 1622020
  55.9 2.4 %copy-start.5 = (f32[1,4,264,128]{3,2,1,0:T(8,128)}, f32[1,4,264,128]{3,2,1,0:T(8,128)S(1)}, u32[]{:S(2)}) copy-start(f32[1,4,264,128]{3,2,1,0:T(8,128)S(1)} %get-tuple-element.51) | copy-start | bytes 1622020
  55.9 2.4 %copy-start.6 = (f32[1,4,264,128]{3,2,1,0:T(8,128)}, f32[1,4,264,128]{3,2,1,0:T(8,128)S(1)}, u32[]{:S(2)}) copy-start(f32[1,4,264,128]{3,2,1,0:T(8,128)S(1)} %get-tuple-element.52) | copy-start | bytes 1622020
  55.9 2.4 %copy-start.7 = (f32[1,4,264,128]{3,2,1,0:T(8,128)}, f32[1,4,264,128]{3,2,1,0:T(8,128)S(1)}, u32[]{:S(2)}) copy-start(f32[1,4,264,128]{3,2,1,0:T(8,128)S(1)} %get-tuple-element.53) | copy-start | bytes 1622020
  56.0 2.2 %copy-start.25 = (f32[4]{0:T(128)}, f32[4]{0:T(128)S(1)}, u32[]{:S(2)}) copy-start(f32[4]{0:T(128)S(1)} %slice_reduce_fusion.8) | copy-start | bytes 52
  56.1 2.1 %copy-start.27 = (f32[4]{0:T(128)}, f32[4]{0:T(128)S(1)}, u32[]{:S(2)}) copy-start(f32[4]{0:T(128)S(1)} %slice_reduce_fusion.9) | copy-start | bytes 52
  56.2 2.0 copy-start.21
  56.4 1.9 copy-start.19
  57.2 1.1 copy-start.29
  57.2 1.1 copy-start.31
  57.2 7.7 %copy-start.17 = (s32[384]{0:T(512)S(1)}, s32[384]{0:T(512)}, u32[]{:S(2)}) copy-start(s32[384]{0:T(512)} %copy-done.16) | copy-start | bytes 4612
  58.3 9.6 %collective-permute-start.5 = (f32[4,136,128]{2,1,0:T(8,128)S(1)}, f32[4,136,128]{2,1,0:T(8,128)S(1)}, u32[]{:S(2)}, u32[]{:S(2)}) collective-permute-start(f32[4,136,128]{2,1,0:T(8,128)S(1)} %get-tuple-element.85), channel_id=1, source_target_pairs={{32,0},{40,8},{48,16},{56,24},{64,32},{72,40},{80,48},{88,56},{96,... | collective-permute-start | bytes 835592 | tf_op jit(solution)/shard_map/ppermute | solution.py:44
  59.6 9.5 %collective-permute-start.3 = (f32[4,136,128]{2,1,0:T(8,128)S(1)}, f32[4,136,128]{2,1,0:T(8,128)S(1)}, u32[]{:S(2)}, u32[]{:S(2)}) collective-permute-start(f32[4,136,128]{2,1,0:T(8,128)S(1)} %get-tuple-element.86), channel_id=1, source_target_pairs={{0,32},{8,40},{16,48},{24,56},{32,64},{40,72},{48,80},{56,88},{64,... | collective-permute-start | bytes 835592 | tf_op jit(solution)/shard_map/ppermute | solution.py:43
  67.9 26.0 %copy-start.9 = (f32[4,136,128]{2,1,0:T(8,128)}, f32[4,136,128]{2,1,0:T(8,128)S(1)}, u32[]{:S(2)}) copy-start(f32[4,136,128]{2,1,0:T(8,128)S(1)} %collective-permute-done.5) | copy-start | bytes 835588
  69.1 0.7 copy-start.10
  70.0 36.5 %copy-start.24 = (s32[384]{0:T(512)S(1)}, s32[384]{0:T(512)}, u32[]{:S(2)}) copy-start(s32[384]{0:T(512)} %select_reduce_fusion) | copy-start | bytes 4612
  70.0 37.1 %copy-start = (bf16[1,384,2048]{2,1,0:T(8,128)(2,1)S(1)}, bf16[1,384,2048]{2,1,0:T(8,128)(2,1)}, u32[]{:S(2)}) copy-start(bf16[1,384,2048]{2,1,0:T(8,128)(2,1)} %query_ref.1) | copy-start | bytes 4718596
  70.0 9.9 %collective-permute-start.4 = (f32[4,136,128]{2,1,0:T(8,128)S(1)}, f32[4,136,128]{2,1,0:T(8,128)S(1)}, u32[]{:S(2)}, u32[]{:S(2)}) collective-permute-start(f32[4,136,128]{2,1,0:T(8,128)S(1)} %pad_maximum_fusion.5), channel_id=1, source_target_pairs={{0,64},{8,72},{16,80},{24,88},{32,96},{40,104},{48,112},{56,120},{... | collective-permute-start | bytes 835592 | tf_op jit(solution)/shard_map/ppermute | solution.py:43
  75.9 17.9 %collective-permute-start.6 = (f32[4,136,128]{2,1,0:T(8,128)S(1)}, f32[4,136,128]{2,1,0:T(8,128)S(1)}, u32[]{:S(2)}, u32[]{:S(2)}) collective-permute-start(f32[4,136,128]{2,1,0:T(8,128)S(1)} %pad_maximum_fusion.6), channel_id=1, source_target_pairs={{64,0},{72,8},{80,16},{88,24},{96,32},{104,40},{112,48},{120,56},{... | collective-permute-start | bytes 835592 | tf_op jit(solution)/shard_map/ppermute | solution.py:44
  79.9 26.6 %copy-start.11 = (f32[4,136,128]{2,1,0:T(8,128)}, f32[4,136,128]{2,1,0:T(8,128)S(1)}, u32[]{:S(2)}) copy-start(f32[4,136,128]{2,1,0:T(8,128)S(1)} %collective-permute-done.4) | copy-start | bytes 835588
  93.8 12.7 %copy-start.12 = (f32[4,136,128]{2,1,0:T(8,128)}, f32[4,136,128]{2,1,0:T(8,128)S(1)}, u32[]{:S(2)}) copy-start(f32[4,136,128]{2,1,0:T(8,128)S(1)} %collective-permute-done.6) | copy-start | bytes 835588
  94.7 22.6 %collective-permute-start.7 = (f32[4,136,128]{2,1,0:T(8,128)}, f32[4,136,128]{2,1,0:T(8,128)}, u32[]{:S(2)}, u32[]{:S(2)}) collective-permute-start(f32[4,136,128]{2,1,0:T(8,128)} %maximum_select_fusion), channel_id=1, source_target_pairs={{0,128},{8,136},{16,144},{24,152},{32,160},{40,168},{48,176},{56,1... | collective-permute-start | bytes 835592 | tf_op jit(solution)/shard_map/ppermute | solution.py:39
  115.6 4.3 %copy-start.22 = (f32[4]{0:T(128)S(1)}, f32[4]{0:T(128)}, u32[]{:S(2)}) copy-start(f32[4]{0:T(128)} %copy-done.21) | copy-start | bytes 52
  115.6 4.3 %copy-start.30 = (f32[4]{0:T(128)S(1)}, f32[4]{0:T(128)}, u32[]{:S(2)}) copy-start(f32[4]{0:T(128)} %copy-done.29) | copy-start | bytes 52
  115.6 5.3 %copy-start.20 = (f32[4]{0:T(128)S(1)}, f32[4]{0:T(128)}, u32[]{:S(2)}) copy-start(f32[4]{0:T(128)} %copy-done.19) | copy-start | bytes 52
  115.6 5.3 %copy-start.33 = (f32[4]{0:T(128)S(1)}, f32[4]{0:T(128)}, u32[]{:S(2)}) copy-start(f32[4]{0:T(128)} %get-tuple-element.87) | copy-start | bytes 52
  118.3 3.7 %copy-start.13 = (f32[4,128,128]{2,1,0:T(8,128)S(1)}, f32[4,128,128]{2,1,0:T(8,128)}, u32[]{:S(2)}) copy-start(f32[4,128,128]{2,1,0:T(8,128)} %get-tuple-element.43) | copy-start | bytes 786436
  118.3 3.7 %copy-start.26 = (f32[4]{0:T(128)S(1)}, f32[4]{0:T(128)}, u32[]{:S(2)}) copy-start(f32[4]{0:T(128)} %copy-done.25) | copy-start | bytes 52
  118.3 3.7 %copy-start.28 = (f32[4]{0:T(128)S(1)}, f32[4]{0:T(128)}, u32[]{:S(2)}) copy-start(f32[4]{0:T(128)} %copy-done.27) | copy-start | bytes 52
  118.3 3.7 %copy-start.32 = (f32[4]{0:T(128)S(1)}, f32[4]{0:T(128)}, u32[]{:S(2)}) copy-start(f32[4]{0:T(128)} %copy-done.31) | copy-start | bytes 52
  118.3 3.7 %copy-start.35 = (f32[4]{0:T(128)S(1)}, f32[4]{0:T(128)}, u32[]{:S(2)}) copy-start(f32[4]{0:T(128)} %get-tuple-element.47) | copy-start | bytes 52
  118.3 3.7 %copy-start.36 = (f32[4]{0:T(128)S(1)}, f32[4]{0:T(128)}, u32[]{:S(2)}) copy-start(f32[4]{0:T(128)} %get-tuple-element.48) | copy-start | bytes 52
  118.3 3.7 %copy-start.37 = (f32[4]{0:T(128)S(1)}, f32[4]{0:T(128)}, u32[]{:S(2)}) copy-start(f32[4]{0:T(128)} %get-tuple-element.88) | copy-start | bytes 52
  123.5 5.9 %copy-start.18 = (f32[16,384]{1,0:T(8,128)S(1)}, f32[16,384]{1,0:T(8,128)}, u32[]{:S(2)}) copy-start(f32[16,384]{1,0:T(8,128)} %get-tuple-element.83) | copy-start | bytes 73732
  123.7 5.7 %copy-start.2 = (bf16[1,384,2048]{1,2,0:T(8,128)(2,1)S(1)}, bf16[1,384,2048]{1,2,0:T(8,128)(2,1)}, u32[]{:S(2)}) copy-start(bf16[1,384,2048]{1,2,0:T(8,128)(2,1)} %copy.106) | copy-start | bytes 4718596
  123.7 5.7 %copy-start.3 = (bf16[48,8,16,128]{3,2,1,0:T(8,128)(2,1)S(1)}, bf16[48,8,16,128]{3,2,1,0:T(8,128)(2,1)}, u32[]{:S(2)}) copy-start(bf16[48,8,16,128]{3,2,1,0:T(8,128)(2,1)} %copy.108) | copy-start | bytes 4718596
  123.8 13.8 %collective-permute-start.8 = (f32[4,256,128]{2,1,0:T(8,128)S(1)}, f32[4,256,128]{2,1,0:T(8,128)S(1)}, u32[]{:S(2)}, u32[]{:S(2)}) collective-permute-start(f32[4,256,128]{2,1,0:T(8,128)S(1)} %get-tuple-element.72), channel_id=1, source_target_pairs={{0,8},{8,16},{16,24},{24,0},{32,40},{40,48},{48,56},{56,32},{64,72... | collective-permute-start | bytes 1572872 | tf_op jit(solution)/shard_map/ppermute | solution.py:65
  125.6 17.6 %collective-permute-start.9 = (f32[4,256,128]{2,1,0:T(8,128)S(1)}, f32[4,256,128]{2,1,0:T(8,128)S(1)}, u32[]{:S(2)}, u32[]{:S(2)}) collective-permute-start(f32[4,256,128]{2,1,0:T(8,128)S(1)} %get-tuple-element.71), channel_id=1, source_target_pairs={{0,16},{8,24},{16,0},{24,8},{32,48},{40,56},{48,32},{56,40},{64,80... | collective-permute-start | bytes 1572872 | tf_op jit(solution)/shard_map/ppermute | solution.py:65
  129.4 13.9 %collective-permute-start.10 = (f32[4,256,128]{2,1,0:T(8,128)S(1)}, f32[4,256,128]{2,1,0:T(8,128)S(1)}, u32[]{:S(2)}, u32[]{:S(2)}) collective-permute-start(f32[4,256,128]{2,1,0:T(8,128)S(1)} %get-tuple-element.70), channel_id=1, source_target_pairs={{0,24},{8,0},{16,8},{24,16},{32,56},{40,32},{48,40},{56,48},{64,88... | collective-permute-start | bytes 1572872 | tf_op jit(solution)/shard_map/ppermute | solution.py:65
  146.2 2.7 %copy-start.15 = (f32[384,16]{0,1:T(8,128)S(1)}, f32[384,16]{0,1:T(8,128)}, u32[]{:S(2)}) copy-start(f32[384,16]{0,1:T(8,128)} %get-tuple-element.82) | copy-start | bytes 73732
  148.8 2.8 %copy-start.14 = (f32[384,16]{0,1:T(8,128)S(1)}, f32[384,16]{0,1:T(8,128)}, u32[]{:S(2)}) copy-start(f32[384,16]{0,1:T(8,128)} %get-tuple-element.81) | copy-start | bytes 73732
  151.6 2.4 %copy-start.23 = (f32[384]{0:T(512)S(1)}, f32[384]{0:T(512)}, u32[]{:S(2)}) copy-start(f32[384]{0:T(512)} %subtract_convert_fusion) | copy-start | bytes 4612
  154.2 14.5 %collective-permute-start.11 = (f32[16]{0:T(128)S(1)}, f32[16]{0:T(128)S(1)}, u32[]{:S(2)}, u32[]{:S(2)}) collective-permute-start(f32[16]{0:T(128)S(1)} %multiply_reduce_fusion.2), channel_id=1, source_target_pairs={{0,8},{8,0},{16,24},{24,16},{32,40},{40,32},{48,56},{56,48},{64,72... | collective-permute-start | bytes 200 | tf_op jit(solution)/shard_map/ppermute | solution.py:121
  154.2 14.4 %collective-permute-start.12 = (f32[16]{0:T(128)S(1)}, f32[16]{0:T(128)S(1)}, u32[]{:S(2)}, u32[]{:S(2)}) collective-permute-start(f32[16]{0:T(128)S(1)} %multiply_reduce_fusion.2), channel_id=1, source_target_pairs={{0,16},{8,24},{16,0},{24,8},{32,48},{40,56},{48,32},{56,40},{64,80... | collective-permute-start | bytes 200 | tf_op jit(solution)/shard_map/ppermute | solution.py:121
  157.9 10.8 %collective-permute-start.13 = (f32[16]{0:T(128)S(1)}, f32[16]{0:T(128)S(1)}, u32[]{:S(2)}, u32[]{:S(2)}) collective-permute-start(f32[16]{0:T(128)S(1)} %multiply_reduce_fusion.2), channel_id=1, source_target_pairs={{0,24},{8,16},{16,8},{24,0},{32,56},{40,48},{48,40},{56,32},{64,88... | collective-permute-start | bytes 200 | tf_op jit(solution)/shard_map/ppermute | solution.py:121
  166.0 24.2 %copy-start.1 = (bf16[384,16,128]{0,2,1:T(8,128)(2,1)S(1)}, bf16[384,16,128]{0,2,1:T(8,128)(2,1)}, u32[]{:S(2)}) copy-start(bf16[384,16,128]{0,2,1:T(8,128)(2,1)} %get-tuple-element.62) | copy-start | bytes 4718596
  168.7 29.5 %copy-start.8 = (bf16[384,16,128]{0,2,1:T(8,128)(2,1)S(1)}, bf16[384,16,128]{0,2,1:T(8,128)(2,1)}, u32[]{:S(2)}) copy-start(bf16[384,16,128]{0,2,1:T(8,128)(2,1)} %fusion.8) | copy-start | bytes 4718596
  168.7 12.8 %collective-permute-start.14 = (f32[16]{0:T(128)S(1)}, f32[16]{0:T(128)S(1)}, u32[]{:S(2)}, u32[]{:S(2)}) collective-permute-start(f32[16]{0:T(128)S(1)} %fusion.57), channel_id=1, source_target_pairs={{0,32},{8,40},{16,48},{24,56},{32,0},{40,8},{48,16},{56,24},{64,96... | collective-permute-start | bytes 200 | tf_op jit(solution)/shard_map/ppermute | solution.py:121
  168.8 12.8 %collective-permute-start.15 = (f32[16]{0:T(128)S(1)}, f32[16]{0:T(128)S(1)}, u32[]{:S(2)}, u32[]{:S(2)}) collective-permute-start(f32[16]{0:T(128)S(1)} %fusion.57), channel_id=1, source_target_pairs={{0,64},{8,72},{16,80},{24,88},{32,96},{40,104},{48,112},{56,120},{... | collective-permute-start | bytes 200 | tf_op jit(solution)/shard_map/ppermute | solution.py:121
  180.1 5.3 %collective-permute-start.16 = (f32[16]{0:T(128)S(1)}, f32[16]{0:T(128)S(1)}, u32[]{:S(2)}, u32[]{:S(2)}) collective-permute-start(f32[16]{0:T(128)S(1)} %fusion.57), channel_id=1, source_target_pairs={{0,96},{8,104},{16,112},{24,120},{32,64},{40,72},{48,80},{56,88},{... | collective-permute-start | bytes 200 | tf_op jit(solution)/shard_map/ppermute | solution.py:121
  185.4 7.5 %collective-permute-start.17 = (f32[16]{0:T(128)S(1)}, f32[16]{0:T(128)S(1)}, u32[]{:S(2)}, u32[]{:S(2)}) collective-permute-start(f32[16]{0:T(128)S(1)} %fusion.54), channel_id=1, source_target_pairs={{0,128},{8,136},{16,144},{24,152},{32,160},{40,168},{48,176},{56,1... | collective-permute-start | bytes 200 | tf_op jit(solution)/shard_map/ppermute | solution.py:121
  191.7 10.4 %copy-start.34 = (f32[16]{0:T(128)S(1)}, f32[16]{0:T(128)}, u32[]{:S(2)}) copy-start(f32[16]{0:T(128)} %param.13) | copy-start | bytes 196
  193.0 1.9 collective-permute-start.18
  193.0 3.6 %collective-permute-start.19 = (f32[16]{0:T(128)S(1)}, f32[16]{0:T(128)S(1)}, u32[]{:S(2)}, u32[]{:S(2)}) collective-permute-start(f32[16]{0:T(128)S(1)} %fusion.51), channel_id=1, source_target_pairs={{0,2},{1,3},{2,0},{3,1},{4,6},{5,7},{6,4},{7,5},{8,10},{9,11},{10,... | collective-permute-start | bytes 200 | tf_op jit(solution)/shard_map/ppermute | solution.py:121
  194.0 3.0 %collective-permute-start.20 = (f32[16]{0:T(128)S(1)}, f32[16]{0:T(128)S(1)}, u32[]{:S(2)}, u32[]{:S(2)}) collective-permute-start(f32[16]{0:T(128)S(1)} %fusion.51), channel_id=1, source_target_pairs={{0,3},{1,2},{2,1},{3,0},{4,7},{5,6},{6,5},{7,4},{8,11},{9,10},{10,... | collective-permute-start | bytes 200 | tf_op jit(solution)/shard_map/ppermute | solution.py:121
  197.0 5.1 %collective-permute-start.21 = (f32[16]{0:T(128)S(1)}, f32[16]{0:T(128)S(1)}, u32[]{:S(2)}, u32[]{:S(2)}) collective-permute-start(f32[16]{0:T(128)S(1)} %fusion.50), channel_id=1, source_target_pairs={{0,4},{1,5},{2,6},{3,7},{4,0},{5,1},{6,2},{7,3},{8,12},{9,13},{10,... | collective-permute-start | bytes 200 | tf_op jit(solution)/shard_map/ppermute | solution.py:121

commit v7 on v5

--- a/solution.py
+++ b/solution.py
@@ -32,6 +32,13 @@
     while shift < count:
         up = [(i, i + shift) for i in range(count - shift)]
         down = [(i + shift, i) for i in range(count - shift)]
+        if 2 * shift >= count:
+            place = lax.axis_index(axis)
+            sent = jnp.where(place < count - shift, fwd, bwd)
+            got = lax.ppermute(sent, axis, up + down)
+            excl = jnp.where(place >= shift, combine(got, excl), excl)
+            rexcl = jnp.where(place < count - shift, combine(got, rexcl), rexcl)
+            break
         got = lax.ppermute(fwd, axis, up)
         rgot = lax.ppermute(bwd, axis, down)
         excl = combine(got, excl)
@@ -58,7 +65,7 @@
     return jnp.stack([lax.select_n((place - j) % group, *got) for j in range(group)])
 
 
-def carried_both(decay, forward_part, backward_part, axis):
+def carried_both(decay, forward_part, backward_part, axis, extra):
     count = lax.axis_size(axis)
     group = 4 if count % 4 == 0 and forward_part.shape[0] % 4 == 0 else 1
     heads, rows, cols = forward_part.shape
@@ -66,6 +73,7 @@
     pad = jnp.broadcast_to(decay[:, None, None], (heads, 8, cols))
     parts = jnp.concatenate([forward_part, backward_part, pad], axis=1)
     mine = row_exchange(parts.reshape(group, share, 2 * rows + 8, cols), axis, group)
+    mine, extra = lax.optimization_barrier((mine, extra))
     own_s = mine[:, :, :rows]
     own_b = mine[:, :, rows : 2 * rows]
     own_a = mine[:, :, 2 * rows, 0]
@@ -102,7 +110,7 @@
         ]
     )
     full = row_exchange(result, axis, group).reshape(heads, 2 * rows, cols)
-    return full[:, :rows], full[:, rows:]
+    return full[:, :rows], full[:, rows:], extra
 
 
 def digit_sum(value, axis, step, radix):
@@ -180,7 +188,13 @@
     back_local = jnp.einsum(
         "she,shf->hef", carry_in[:, :, None] * query_f, grad_f, precision=state_mode
     )
-    state_input, backward_input = carried_both(decay_all, state_local, back_local, "seq")
+    state_input, backward_input, (key_scale, query_scale) = carried_both(
+        decay_all,
+        state_local,
+        back_local,
+        "seq",
+        (position[:, None] * carry_out, position[:, None] * carry_in),
+    )
     weight = weights_of(cum_log, seg_local)
     scores = jnp.einsum("she,the->hst", query_block, key_block, preferred_element_type=jnp.float32)
     grad_scores = jnp.einsum(
@@ -194,20 +208,31 @@
     value_full = value_full + carry_out[:, :, None] * jnp.einsum(
         "the,hef->thf", key_f, backward_input, precision=state_mode
     )
-    query_full = jnp.einsum(
+    query_local = jnp.einsum(
         "hst,the->she", grad_prob, key_block, preferred_element_type=jnp.float32
     )
-    query_full = query_full + carry_in[:, :, None] * jnp.einsum(
+    key_local = jnp.einsum(
+        "hst,she->the", grad_prob, query_block, preferred_element_type=jnp.float32
+    )
+    local_step = jnp.sum(key_f * key_local, axis=2) - jnp.sum(query_f * query_local, axis=2)
+    rate_local = jnp.sum(position[:, None] * local_step, axis=0)
+    key_moment = jnp.einsum(
+        "the,thf->hef", key_scale[:, :, None] * key_f, value_f, precision=state_mode
+    )
+    query_moment = jnp.einsum(
+        "she,shf->hef", query_scale[:, :, None] * query_f, grad_f, precision=state_mode
+    )
+    rate_part = (
+        rate_local
+        + jnp.sum(key_moment * backward_input, axis=(1, 2))
+        - jnp.sum(query_moment * state_input, axis=(1, 2))
+    )
+    query_full = query_local + carry_in[:, :, None] * jnp.einsum(
         "shf,hef->she", grad_f, state_input, precision=state_mode
     )
-    key_full = jnp.einsum(
-        "hst,she->the", grad_prob, query_block, preferred_element_type=jnp.float32
-    )
-    key_full = key_full + carry_out[:, :, None] * jnp.einsum(
+    key_full = key_local + carry_out[:, :, None] * jnp.einsum(
         "thf,hef->the", value_f, backward_input, precision=state_mode
     )
-    inner_step = jnp.sum(key_f * key_full, axis=2) - jnp.sum(query_f * query_full, axis=2)
-    rate_part = jnp.sum(position[:, None] * inner_step, axis=0)
     rate_total = all_sum(rate_part, ("seq", "dp"))
     token_total = row_count * lax.axis_size("seq") * lax.axis_size("dp")
     rate_grad = head_decay_rate * rate_total / math.sqrt(token_total)

time: 196 us -> 220 us (1.12)
  waiting for transfers between devices: 65.9 us -> 86.5 us
  starting transfers between devices: 65.4 us -> 45.8 us
  matrix products: 25.4 us -> 36.6 us
  other arithmetic: 16.6 us -> 24.4 us
  local copies, waits for them, and re-layouts: 19.7 us -> 22.9 us
    ppermute x3 -> x2, starting transfers between devices: 28.3 us -> 11.1 us  [group_scan(): got = lax.ppermute(fwd, axis, up)]
    ppermute x0 -> x1, waiting for transfers between devices: none -> 11.1 us  [group_scan(): got = lax.ppermute(sent, axis, up + down)]
    ppermute x6, waiting for transfers between devices: 35.6 us -> 44.4 us  [row_exchange(): got.append(lax.ppermute(send, axis, pairs))]
    ppermute x3 -> x2, waiting for transfers between devices: 11.4 us -> 16.3 us  [group_scan(): rgot = lax.ppermute(bwd, axis, down)]
    ppermute x0 -> x1, starting transfers between devices: none -> 3.22 us  [group_scan(): got = lax.ppermute(sent, axis, up + down)]
    add x3 -> x4, other arithmetic: 1.42 us -> 4.46 us  [combine(): state = near[:, rows:rows + 1, 0:1] * far[:, :rows] + near[:, :rows]]
    dot_general x0 -> x2, matrix products: none -> 2.98 us  [the longest x1 1.5 us: on_device(): jnp.einsum('the,thf->hef', key_scale[:, :, None] * key_f, value_f, precis...]
    unnamed x42 -> x71, local copies, waits for them, and re-layouts: 14.1 us -> 17.1 us
  transfers between devices with their start and end apart: 23 -> 22, of which waited for: 15 -> 16; matrix products, arithmetic and copies ran while one was open for 11% -> 10% of each run, Pallas kernels for 0% -> 0%
where the time goes in v7:
time: 220 us; the launch traced here: 218 us
  waiting for transfers between devices  86.5 us (39%)
  starting transfers between devices  45.8 us (21%)
  matrix products  36.6 us (17%)
  other arithmetic  24.4 us (11%)
  local copies, waits for them, and re-layouts  22.9 us (10%)
    ppermute x6, waiting for transfers between devices, row_exchange(): got.append(lax.ppermute(send, axis, pairs))  44.4 us
    ppermute x11, starting transfers between devices, digit_sum(): lax.ppermute(value, axis, [(i, i ^ k * step) for i in range(count)])  18.6 us
    unnamed x71, local copies, waits for them, and re-layouts  17.1 us
    ppermute x2, waiting for transfers between devices, group_scan(): rgot = lax.ppermute(bwd, axis, down)  16.3 us
    ppermute x11, waiting for transfers between devices, digit_sum(): lax.ppermute(value, axis, [(i, i ^ k * step) for i in range(count)])  12.2 us
    ppermute x1, waiting for transfers between devices, group_scan(): got = lax.ppermute(sent, axis, up + down)  11.1 us
    ppermute x2, starting transfers between devices, group_scan(): got = lax.ppermute(fwd, axis, up)  11.1 us
    ppermute x6, starting transfers between devices, row_exchange(): got.append(lax.ppermute(send, axis, pairs))  10.3 us
  transfers between devices with their start and end apart: 22, of which 16 were waited for; matrix products, arithmetic and copies ran while one was open for 10% of the time, Pallas kernels for 0%

profile of v7, /device:TPU:6, one launch (start us, length us, event | category | flops | bytes accessed | tf_op | source)
XLA Modules:
  0.0 218.0 jit_solution(3590134945262631699)
XLA Ops:
  0.7 0.9 reduce-window_clone.1
  3.8 1.9 copy.78
  6.9 1.6 copy.98
  8.5 1.6 copy.97
  10.1 1.9 copy.76
  12.0 6.0 %multiply_convert_fusion.1 = bf16[16,384,384]{2,1,0:T(8,128)(2,1)S(1)} fusion(f32[16,384]{1,0:T(8,128)S(1)} %get-tuple-element.84, pred[384,384]{1,0:T(8,128)(4,1)S(1)} %fusion.40, bf16[384,16,128]{2,1,0:T(8,128)(2,1)} %bitcast.207, bf16[384,16,128]{2,1,0:T(8,128)(2,1)} %bitcast.202), kind=kOutput, calls=%fused_computation.1 | convolution fusion | flops 615776256 | bytes 8036352 | tf_op jit(solution)/shard_map/shf,thf->hst/dot_general | solution.py:200
  18.0 3.3 %fusion.11 = (f32[384,16]{0,1:T(8,128)S(1)}, f32[16,384,128]{1,2,0:T(8,128)}) fusion(bf16[384,16,128]{0,2,1:T(8,128)(2,1)S(1)} %bitcast.197, bf16[16,384,384]{2,1,0:T(8,128)(2,1)S(1)} %multiply_convert_fusion.1, bf16[384,16,128]{0,2,1:T(8,128)(2,1)S(1)} %bitcast.191), kind=kOutput, calls=%fused_computation.19 | convolution fusion | flops 606332928 | bytes 11034624 | tf_op jit(solution)/shard_map/hst,the->she/dot_general | solution.py:211
  21.3 3.0 %fusion.8 = (f32[384,16]{0,1:T(8,128)S(1)}, f32[16,384,128]{1,2,0:T(8,128)}) fusion(bf16[384,16,128]{0,2,1:T(8,128)(2,1)S(1)} %bitcast.192, bf16[384,16,128]{0,2,1:T(8,128)(2,1)S(1)} %bitcast.198, bf16[16,384,384]{2,1,0:T(8,128)(2,1)S(1)} %multiply_convert_fusion.1), kind=kOutput, calls=%fused_computation.16 | convolution fusion | flops 606332928 | bytes 11034624 | tf_op jit(solution)/shard_map/hst,she->the/dot_general | solution.py:214
  25.9 1.3 broadcast_multiply_fusion
  27.2 3.9 %fusion.10 = f32[16,128,128]{2,1,0:T(8,128)} fusion(bf16[384,16,128]{0,2,1:T(8,128)(2,1)S(1)} %bitcast.199, f32[384,16]{0,1:T(8,128)S(1)} %get-tuple-element.52, bf16[384,16,128]{2,1,0:T(8,128)(2,1)} %bitcast.203), kind=kOutput, calls=%fused_computation.18 | convolution fusion | flops 605552640 | bytes 4218880 | tf_op jit(solution)/shard_map/she,shf->hef/dot_general | solution.py:188
  31.1 2.4 %fusion.7 = f32[16,128,128]{2,1,0:T(8,128)} fusion(bf16[384,16,128]{0,2,1:T(8,128)(2,1)S(1)} %bitcast.193, f32[384,16]{0,1:T(8,128)S(1)} %get-tuple-element.82, bf16[384,16,128]{2,1,0:T(8,128)(2,1)S(1)} %bitcast.208), kind=kOutput, calls=%fused_computation.15 | convolution fusion | flops 605552640 | bytes 4218880 | tf_op jit(solution)/shard_map/the,thf->hef/dot_general | solution.py:185
  33.5 1.7 pad_maximum_fusion
  35.2 1.4 copy-done.6
  36.6 1.2 dynamic-slice_bitcast_fusion
  37.8 1.6 collective-permute-start
  39.4 2.9 %collective-permute-start.1 = (f32[4,264,128]{2,1,0:T(8,128)}, f32[4,264,128]{2,1,0:T(8,128)}, u32[]{:S(2)}, u32[]{:S(2)}) collective-permute-start(f32[4,264,128]{2,1,0:T(8,128)} %get-tuple-element.70), channel_id=1, source_target_pairs={{0,16},{8,24},{16,0},{24,8},{32,48},{40,56},{48,32},{56,40},{64,80... | collective-permute-start | bytes 1622024 | tf_op jit(solution)/shard_map/ppermute | solution.py:64
  42.3 1.3 collective-permute-start.2
  43.6 9.8 %collective-permute-done = f32[4,264,128]{2,1,0:T(8,128)} collective-permute-done((f32[4,264,128]{2,1,0:T(8,128)}, f32[4,264,128]{2,1,0:T(8,128)}, u32[]{:S(2)}, u32[]{:S(2)}) %collective-permute-start) | collective-permute-done | bytes 540704 | tf_op jit(solution)/shard_map/ppermute | solution.py:64
  53.4 12.8 %collective-permute-done.1 = f32[4,264,128]{2,1,0:T(8,128)} collective-permute-done((f32[4,264,128]{2,1,0:T(8,128)}, f32[4,264,128]{2,1,0:T(8,128)}, u32[]{:S(2)}, u32[]{:S(2)}) %collective-permute-start.1) | collective-permute-done | bytes 540704 | tf_op jit(solution)/shard_map/ppermute | solution.py:64
  66.2 1.8 fusion.42
  68.9 0.9 bitcast_add_fusion.4
  70.0 1.3 collective-permute-start.5
  71.3 4.6 %collective-permute-start.3 = (f32[4,136,128]{2,1,0:T(8,128)S(1)}, f32[4,136,128]{2,1,0:T(8,128)S(1)}, u32[]{:S(2)}, u32[]{:S(2)}) collective-permute-start(f32[4,136,128]{2,1,0:T(8,128)S(1)} %get-tuple-element.86), channel_id=1, source_target_pairs={{0,32},{8,40},{16,48},{24,56},{32,64},{40,72},{48,80},{56,88},{64,... | collective-permute-start | bytes 835592 | tf_op jit(solution)/shard_map/ppermute | solution.py:42
  75.9 3.7 %collective-permute-done.5 = f32[4,136,128]{2,1,0:T(8,128)S(1)} collective-permute-done((f32[4,136,128]{2,1,0:T(8,128)S(1)}, f32[4,136,128]{2,1,0:T(8,128)S(1)}, u32[]{:S(2)}, u32[]{:S(2)}) %collective-permute-start.5) | collective-permute-done | bytes 278560 | tf_op jit(solution)/shard_map/ppermute | solution.py:43
  79.6 1.2 collective-permute-done.3
  83.2 6.5 %collective-permute-start.4 = (f32[4,136,128]{2,1,0:T(8,128)}, f32[4,136,128]{2,1,0:T(8,128)}, u32[]{:S(2)}, u32[]{:S(2)}) collective-permute-start(f32[4,136,128]{2,1,0:T(8,128)} %pad_maximum_fusion.6), channel_id=1, source_target_pairs={{0,64},{8,72},{16,80},{24,88},{32,96},{40,104},{48,112},{56,120},{... | collective-permute-start | bytes 835592 | tf_op jit(solution)/shard_map/ppermute | solution.py:42
  89.7 1.0 pad_maximum_fusion.7
  90.6 1.3 collective-permute-start.6
  92.0 1.2 collective-permute-done.4
  94.0 1.1 multiply_add_fusion.12
  95.2 12.5 %collective-permute-done.6 = f32[4,136,128]{2,1,0:T(8,128)S(1)} collective-permute-done((f32[4,136,128]{2,1,0:T(8,128)S(1)}, f32[4,136,128]{2,1,0:T(8,128)S(1)}, u32[]{:S(2)}, u32[]{:S(2)}) %collective-permute-start.6) | collective-permute-done | bytes 278560 | tf_op jit(solution)/shard_map/ppermute | solution.py:43
  108.4 1.0 multiply_add_fusion.10
  110.2 3.2 %collective-permute-start.7 = (f32[4,136,128]{2,1,0:T(8,128)}, f32[4,136,128]{2,1,0:T(8,128)}, u32[]{:S(2)}, u32[]{:S(2)}) collective-permute-start(f32[4,136,128]{2,1,0:T(8,128)} %maximum_select_fusion), channel_id=1, source_target_pairs={{0,128},{8,136},{16,144},{24,152},{32,160},{40,168},{48,176},{56,1... | collective-permute-start | bytes 835592 | tf_op jit(solution)/shard_map/ppermute | solution.py:38
  115.1 11.1 %collective-permute-done.7 = f32[4,136,128]{2,1,0:T(8,128)} collective-permute-done((f32[4,136,128]{2,1,0:T(8,128)}, f32[4,136,128]{2,1,0:T(8,128)}, u32[]{:S(2)}, u32[]{:S(2)}) %collective-permute-start.7) | collective-permute-done | bytes 278560 | tf_op jit(solution)/shard_map/ppermute | solution.py:38
  127.2 1.5 multiply_add_fusion.9
  128.7 1.2 multiply_add_fusion.4
  130.0 1.2 multiply_add_fusion.1
  131.6 1.3 copy-done.7
  132.9 1.2 dynamic-slice_bitcast_fusion.3
  134.9 3.7 %collective-permute-start.9 = (f32[4,256,128]{2,1,0:T(8,128)}, f32[4,256,128]{2,1,0:T(8,128)}, u32[]{:S(2)}, u32[]{:S(2)}) collective-permute-start(f32[4,256,128]{2,1,0:T(8,128)} %get-tuple-element.73), channel_id=1, source_target_pairs={{0,16},{8,24},{16,0},{24,8},{32,48},{40,56},{48,32},{56,40},{64,80... | collective-permute-start | bytes 1572872 | tf_op jit(solution)/shard_map/ppermute | solution.py:64
  138.6 12.7 %collective-permute-done.8 = f32[4,256,128]{2,1,0:T(8,128)} collective-permute-done((f32[4,256,128]{2,1,0:T(8,128)}, f32[4,256,128]{2,1,0:T(8,128)}, u32[]{:S(2)}, u32[]{:S(2)}) %collective-permute-start.8) | collective-permute-done | bytes 524320 | tf_op jit(solution)/shard_map/ppermute | solution.py:64
  151.4 8.8 %collective-permute-done.9 = f32[4,256,128]{2,1,0:T(8,128)} collective-permute-done((f32[4,256,128]{2,1,0:T(8,128)}, f32[4,256,128]{2,1,0:T(8,128)}, u32[]{:S(2)}, u32[]{:S(2)}) %collective-permute-start.9) | collective-permute-done | bytes 524320 | tf_op jit(solution)/shard_map/ppermute | solution.py:64
  160.5 1.8 fusion.50
  162.5 2.7 %fusion.32 = f32[16,128,384]{2,1,0:T(8,128)} fusion(bf16[384,16,128]{0,2,1:T(8,128)(2,1)S(1)} %bitcast.194, f32[16,256,128]{2,1,0:T(8,128)S(1)} %bitcast.211), kind=kOutput, calls=%fused_computation.47 | convolution fusion | flops 603979776 | bytes 5767168 | tf_op jit(solution)/shard_map/the,hef->thf/dot_general | solution.py:208
  165.3 1.5 fusion.26
  166.8 1.5 fusion.25
  168.3 1.1 collective-permute-start.11
  169.3 3.1 %collective-permute-start.12 = (f32[16]{0:T(128)S(1)}, f32[16]{0:T(128)S(1)}, u32[]{:S(2)}, u32[]{:S(2)}) collective-permute-start(f32[16]{0:T(128)S(1)} %add_subtract_fusion), channel_id=1, source_target_pairs={{0,16},{8,24},{16,0},{24,8},{32,48},{40,56},{48,32},{56,40},{64,80... | collective-permute-start | bytes 200 | tf_op jit(solution)/shard_map/ppermute | solution.py:121
  173.0 2.6 %fusion.18 = bf16[384,16,128]{0,2,1:T(8,128)(2,1)} fusion(f32[16,384,128]{1,2,0:T(8,128)S(1)} %copy-done.5, f32[384,16]{0,1:T(8,128)S(1)} %get-tuple-element.52, f32[16,256,128]{2,1,0:T(8,128)S(1)} %bitcast.214, bf16[384,16,128]{2,1,0:T(8,128)(2,1)S(1)} %bitcast.206), kind=kOutput, calls=%fused_computation.29 | convolution fusion | flops 606339072 | bytes 7364608 | tf_op jit(solution)/shard_map/shf,hef->she/dot_general | solution.py:230
  175.7 2.7 %fusion.16 = bf16[384,16,128]{0,2,1:T(8,128)(2,1)} fusion(f32[16,384,128]{1,2,0:T(8,128)S(1)} %copy-done.4, f32[384,16]{0,1:T(8,128)S(1)} %get-tuple-element.82, bf16[384,16,128]{2,1,0:T(8,128)(2,1)S(1)} %bitcast.210, f32[16,256,128]{2,1,0:T(8,128)S(1)} %bitcast.215), kind=kOutput, calls=%fused_computation.26 | convolution fusion | flops 606339072 | bytes 7364608 | tf_op jit(solution)/shard_map/thf,hef->the/dot_general | solution.py:233
  178.4 7.0 %fusion.14 = bf16[384,16,128]{0,2,1:T(8,128)(2,1)} fusion(f32[16,128,384]{2,1,0:T(8,128)} %fusion.32, f32[16,384]{1,0:T(8,128)S(1)} %get-tuple-element.84, pred[384,384]{1,0:T(8,128)(4,1)S(1)} %copy-done.18, bf16[384,16,128]{0,2,1:T(8,128)(2,1)S(1)} %bitcast.201, bf16[384,16,128]{0,2,1:T(8,128)(2,1)S(1)} %bitcast.196, f32[384,16]{0,1:T(8,128)S(1)} %get-tuple-element.82, ...), kind=kOutput, calls=%fused_computation.23 | convolution fusion | flops 1222115328 | bytes 9633792 | tf_op jit(solution)/shard_map/hst,shf->thf/dot_general | solution.py:205
  185.4 2.7 %copy.89 = bf16[1,384,2048]{2,1,0:T(8,128)(2,1)} copy(bf16[1,384,2048]{1,2,0:T(8,128)(2,1)} %bitcast.219) | data formatting | bytes 3145728
  188.2 7.3 %collective-permute-start.15 = (f32[16]{0:T(128)S(1)}, f32[16]{0:T(128)S(1)}, u32[]{:S(2)}, u32[]{:S(2)}) collective-permute-start(f32[16]{0:T(128)S(1)} %fusion.70), channel_id=1, source_target_pairs={{0,64},{8,72},{16,80},{24,88},{32,96},{40,104},{48,112},{56,120},{... | collective-permute-start | bytes 200 | tf_op jit(solution)/shard_map/ppermute | solution.py:121
  195.6 1.4 collective-permute-start.16
  197.1 3.8 %collective-permute-done.16 = f32[16]{0:T(128)S(1)} collective-permute-done((f32[16]{0:T(128)S(1)}, f32[16]{0:T(128)S(1)}, u32[]{:S(2)}, u32[]{:S(2)}) %collective-permute-start.16) | collective-permute-done | bytes 96 | tf_op jit(solution)/shard_map/ppermute | solution.py:121
  200.9 1.9 collective-permute-start.17
  202.8 1.6 copy.90
  204.4 4.0 %collective-permute-done.17 = f32[16]{0:T(128)S(1)} collective-permute-done((f32[16]{0:T(128)S(1)}, f32[16]{0:T(128)S(1)}, u32[]{:S(2)}, u32[]{:S(2)}) %collective-permute-start.17) | collective-permute-done | bytes 96 | tf_op jit(solution)/shard_map/ppermute | solution.py:121
  208.4 0.9 collective-permute-start.19
  209.4 1.0 collective-permute-start.20
  210.3 1.7 collective-permute-done.19
  212.3 1.3 collective-permute-start.21
  213.6 1.6 copy.91
  215.2 2.3 %collective-permute-done.21 = f32[16]{0:T(128)S(1)} collective-permute-done((f32[16]{0:T(128)S(1)}, f32[16]{0:T(128)S(1)}, u32[]{:S(2)}, u32[]{:S(2)}) %collective-permute-start.21) | collective-permute-done | bytes 96 | tf_op jit(solution)/shard_map/ppermute | solution.py:121
  (128 shorter events, 16.2 us)
Async XLA Ops:
  0.6 5.1 %copy-start.31 = (s32[1,384]{1,0:T(1,128)S(1)}, s32[1,384]{1,0:T(1,128)}, u32[]{:S(2)}) copy-start(s32[1,384]{1,0:T(1,128)} %param.12) | copy-start | bytes 4612
  0.6 5.1 %copy-start.26 = (f32[16]{0:T(128)S(1)}, f32[16]{0:T(128)}, u32[]{:S(2)}) copy-start(f32[16]{0:T(128)} %param.13) | copy-start | bytes 196
  0.7 6.3 %copy-start.10 = (bf16[1,384,2048]{2,1,0:T(8,128)(2,1)S(1)}, bf16[1,384,2048]{2,1,0:T(8,128)(2,1)}, u32[]{:S(2)}) copy-start(bf16[1,384,2048]{2,1,0:T(8,128)(2,1)} %param.9) | copy-start | bytes 4718596
  3.2 8.7 %copy-start.17 = (pred[384,384]{1,0:T(8,128)(4,1)}, pred[384,384]{1,0:T(8,128)(4,1)S(1)}, u32[]{:S(2)}) copy-start(pred[384,384]{1,0:T(8,128)(4,1)S(1)} %fusion.40) | copy-start | bytes 442372
  6.9 1.7 copy-start.11
  27.2 3.9 %copy-start.1 = (bf16[48,8,16,128]{3,2,1,0:T(8,128)(2,1)S(1)}, bf16[48,8,16,128]{3,2,1,0:T(8,128)(2,1)}, u32[]{:S(2)}) copy-start(bf16[48,8,16,128]{3,2,1,0:T(8,128)(2,1)} %copy.98) | copy-start | bytes 4718596
  35.2 1.4 copy-start.6
  37.8 15.6 %collective-permute-start = (f32[4,264,128]{2,1,0:T(8,128)}, f32[4,264,128]{2,1,0:T(8,128)}, u32[]{:S(2)}, u32[]{:S(2)}) collective-permute-start(f32[4,264,128]{2,1,0:T(8,128)} %get-tuple-element.71), channel_id=1, source_target_pairs={{0,8},{8,16},{16,24},{24,0},{32,40},{40,48},{48,56},{56,32},{64,72... | collective-permute-start | bytes 1622024 | tf_op jit(solution)/shard_map/ppermute | solution.py:64
  39.4 26.8 %collective-permute-start.1 = (f32[4,264,128]{2,1,0:T(8,128)}, f32[4,264,128]{2,1,0:T(8,128)}, u32[]{:S(2)}, u32[]{:S(2)}) collective-permute-start(f32[4,264,128]{2,1,0:T(8,128)} %get-tuple-element.70), channel_id=1, source_target_pairs={{0,16},{8,24},{16,0},{24,8},{32,48},{40,56},{48,32},{56,40},{64,80... | collective-permute-start | bytes 1622024 | tf_op jit(solution)/shard_map/ppermute | solution.py:64
  42.3 23.9 %collective-permute-start.2 = (f32[4,264,128]{2,1,0:T(8,128)}, f32[4,264,128]{2,1,0:T(8,128)}, u32[]{:S(2)}, u32[]{:S(2)}) collective-permute-start(f32[4,264,128]{2,1,0:T(8,128)} %get-tuple-element.69), channel_id=1, source_target_pairs={{0,24},{8,0},{16,8},{24,16},{32,56},{40,32},{48,40},{56,48},{64,88... | collective-permute-start | bytes 1622024 | tf_op jit(solution)/shard_map/ppermute | solution.py:64
  68.1 1.9 copy-start.3
  68.9 1.1 copy-start.20
  68.9 1.1 copy-start.22
  70.0 9.6 %collective-permute-start.5 = (f32[4,136,128]{2,1,0:T(8,128)S(1)}, f32[4,136,128]{2,1,0:T(8,128)S(1)}, u32[]{:S(2)}, u32[]{:S(2)}) collective-permute-start(f32[4,136,128]{2,1,0:T(8,128)S(1)} %get-tuple-element.85), channel_id=1, source_target_pairs={{32,0},{40,8},{48,16},{56,24},{64,32},{72,40},{80,48},{88,56},{96,... | collective-permute-start | bytes 835592 | tf_op jit(solution)/shard_map/ppermute | solution.py:43
  71.3 9.5 %collective-permute-start.3 = (f32[4,136,128]{2,1,0:T(8,128)S(1)}, f32[4,136,128]{2,1,0:T(8,128)S(1)}, u32[]{:S(2)}, u32[]{:S(2)}) collective-permute-start(f32[4,136,128]{2,1,0:T(8,128)S(1)} %get-tuple-element.86), channel_id=1, source_target_pairs={{0,32},{8,40},{16,48},{24,56},{32,64},{40,72},{48,80},{56,88},{64,... | collective-permute-start | bytes 835592 | tf_op jit(solution)/shard_map/ppermute | solution.py:42
  79.6 3.5 %copy-start.13 = (f32[4,136,128]{2,1,0:T(8,128)}, f32[4,136,128]{2,1,0:T(8,128)S(1)}, u32[]{:S(2)}) copy-start(f32[4,136,128]{2,1,0:T(8,128)S(1)} %collective-permute-done.5) | copy-start | bytes 835588
  80.8 2.4 %copy-start.14 = (f32[4,136,128]{2,1,0:T(8,128)}, f32[4,136,128]{2,1,0:T(8,128)S(1)}, u32[]{:S(2)}) copy-start(f32[4,136,128]{2,1,0:T(8,128)S(1)} %collective-permute-done.3) | copy-start | bytes 835588
  81.7 0.7 copy-start.9
  83.2 10.1 %collective-permute-start.4 = (f32[4,136,128]{2,1,0:T(8,128)}, f32[4,136,128]{2,1,0:T(8,128)}, u32[]{:S(2)}, u32[]{:S(2)}) collective-permute-start(f32[4,136,128]{2,1,0:T(8,128)} %pad_maximum_fusion.6), channel_id=1, source_target_pairs={{0,64},{8,72},{16,80},{24,88},{32,96},{40,104},{48,112},{56,120},{... | collective-permute-start | bytes 835592 | tf_op jit(solution)/shard_map/ppermute | solution.py:42
  90.6 17.1 %collective-permute-start.6 = (f32[4,136,128]{2,1,0:T(8,128)S(1)}, f32[4,136,128]{2,1,0:T(8,128)S(1)}, u32[]{:S(2)}, u32[]{:S(2)}) collective-permute-start(f32[4,136,128]{2,1,0:T(8,128)S(1)} %pad_maximum_fusion.7), channel_id=1, source_target_pairs={{64,0},{72,8},{80,16},{88,24},{96,32},{104,40},{112,48},{120,56},{... | collective-permute-start | bytes 835592 | tf_op jit(solution)/shard_map/ppermute | solution.py:43
  95.1 33.6 %copy-start.21 = (f32[4]{0:T(128)S(1)}, f32[4]{0:T(128)}, u32[]{:S(2)}) copy-start(f32[4]{0:T(128)} %copy-done.20) | copy-start | bytes 52
  95.1 33.6 %copy-start.25 = (f32[4]{0:T(128)S(1)}, f32[4]{0:T(128)}, u32[]{:S(2)}) copy-start(f32[4]{0:T(128)} %get-tuple-element.88) | copy-start | bytes 52
  107.7 0.7 copy-start.15
  110.2 16.0 %collective-permute-start.7 = (f32[4,136,128]{2,1,0:T(8,128)}, f32[4,136,128]{2,1,0:T(8,128)}, u32[]{:S(2)}, u32[]{:S(2)}) collective-permute-start(f32[4,136,128]{2,1,0:T(8,128)} %maximum_select_fusion), channel_id=1, source_target_pairs={{0,128},{8,136},{16,144},{24,152},{32,160},{40,168},{48,176},{56,1... | collective-permute-start | bytes 835592 | tf_op jit(solution)/shard_map/ppermute | solution.py:38
  127.2 2.7 %copy-start.16 = (f32[4,128,128]{2,1,0:T(8,128)S(1)}, f32[4,128,128]{2,1,0:T(8,128)}, u32[]{:S(2)}) copy-start(f32[4,128,128]{2,1,0:T(8,128)} %get-tuple-element.45) | copy-start | bytes 786436
  127.2 2.7 %copy-start.23 = (f32[4]{0:T(128)S(1)}, f32[4]{0:T(128)}, u32[]{:S(2)}) copy-start(f32[4]{0:T(128)} %copy-done.22) | copy-start | bytes 52
  127.2 2.7 %copy-start.28 = (f32[4]{0:T(128)S(1)}, f32[4]{0:T(128)}, u32[]{:S(2)}) copy-start(f32[4]{0:T(128)} %get-tuple-element.49) | copy-start | bytes 52
  127.2 2.7 %copy-start.29 = (f32[4]{0:T(128)S(1)}, f32[4]{0:T(128)}, u32[]{:S(2)}) copy-start(f32[4]{0:T(128)} %get-tuple-element.50) | copy-start | bytes 52
  127.2 2.7 %copy-start.30 = (f32[4]{0:T(128)S(1)}, f32[4]{0:T(128)}, u32[]{:S(2)}) copy-start(f32[4]{0:T(128)} %get-tuple-element.89) | copy-start | bytes 52
  131.6 1.3 copy-start.7
  134.1 17.2 %collective-permute-start.8 = (f32[4,256,128]{2,1,0:T(8,128)}, f32[4,256,128]{2,1,0:T(8,128)}, u32[]{:S(2)}, u32[]{:S(2)}) collective-permute-start(f32[4,256,128]{2,1,0:T(8,128)} %get-tuple-element.74), channel_id=1, source_target_pairs={{0,8},{8,16},{16,24},{24,0},{32,40},{40,48},{48,56},{56,32},{64,72... | collective-permute-start | bytes 1572872 | tf_op jit(solution)/shard_map/ppermute | solution.py:64
  134.9 25.2 %collective-permute-start.9 = (f32[4,256,128]{2,1,0:T(8,128)}, f32[4,256,128]{2,1,0:T(8,128)}, u32[]{:S(2)}, u32[]{:S(2)}) collective-permute-start(f32[4,256,128]{2,1,0:T(8,128)} %get-tuple-element.73), channel_id=1, source_target_pairs={{0,16},{8,24},{16,0},{24,8},{32,48},{40,56},{48,32},{56,40},{64,80... | collective-permute-start | bytes 1572872 | tf_op jit(solution)/shard_map/ppermute | solution.py:64
  138.6 21.9 %collective-permute-start.10 = (f32[4,256,128]{2,1,0:T(8,128)}, f32[4,256,128]{2,1,0:T(8,128)}, u32[]{:S(2)}, u32[]{:S(2)}) collective-permute-start(f32[4,256,128]{2,1,0:T(8,128)} %get-tuple-element.72), channel_id=1, source_target_pairs={{0,24},{8,0},{16,8},{24,16},{32,56},{40,32},{48,40},{56,48},{64,88... | collective-permute-start | bytes 1572872 | tf_op jit(solution)/shard_map/ppermute | solution.py:64
  162.5 2.7 %copy-start = (bf16[48,8,16,128]{3,2,1,0:T(8,128)(2,1)S(1)}, bf16[48,8,16,128]{3,2,1,0:T(8,128)(2,1)}, u32[]{:S(2)}) copy-start(bf16[48,8,16,128]{3,2,1,0:T(8,128)(2,1)} %copy.97) | copy-start | bytes 4718596
  162.5 2.7 %copy-start.19 = (f32[384,16]{0,1:T(8,128)S(1)}, f32[384,16]{0,1:T(8,128)}, u32[]{:S(2)}) copy-start(f32[384,16]{0,1:T(8,128)} %get-tuple-element.9) | copy-start | bytes 73732
  165.3 1.5 copy-start.2
  166.7 1.5 copy-start.24
  166.7 6.3 %copy-start.5 = (f32[16,384,128]{1,2,0:T(8,128)S(1)}, f32[16,384,128]{1,2,0:T(8,128)}, u32[]{:S(2)}) copy-start(f32[16,384,128]{1,2,0:T(8,128)} %get-tuple-element.99) | copy-start | bytes 9437188
  168.3 19.8 %collective-permute-start.11 = (f32[16]{0:T(128)S(1)}, f32[16]{0:T(128)S(1)}, u32[]{:S(2)}, u32[]{:S(2)}) collective-permute-start(f32[16]{0:T(128)S(1)} %add_subtract_fusion), channel_id=1, source_target_pairs={{0,8},{8,0},{16,24},{24,16},{32,40},{40,32},{48,56},{56,48},{64,72... | collective-permute-start | bytes 200 | tf_op jit(solution)/shard_map/ppermute | solution.py:121
  169.3 18.7 %collective-permute-start.12 = (f32[16]{0:T(128)S(1)}, f32[16]{0:T(128)S(1)}, u32[]{:S(2)}, u32[]{:S(2)}) collective-permute-start(f32[16]{0:T(128)S(1)} %add_subtract_fusion), channel_id=1, source_target_pairs={{0,16},{8,24},{16,0},{24,8},{32,48},{40,56},{48,32},{56,40},{64,80... | collective-permute-start | bytes 200 | tf_op jit(solution)/shard_map/ppermute | solution.py:121
  172.4 15.6 %collective-permute-start.13 = (f32[16]{0:T(128)S(1)}, f32[16]{0:T(128)S(1)}, u32[]{:S(2)}, u32[]{:S(2)}) collective-permute-start(f32[16]{0:T(128)S(1)} %add_subtract_fusion), channel_id=1, source_target_pairs={{0,24},{8,16},{16,8},{24,0},{32,56},{40,48},{48,40},{56,32},{64,88... | collective-permute-start | bytes 200 | tf_op jit(solution)/shard_map/ppermute | solution.py:121
  173.0 2.7 %copy-start.4 = (f32[16,384,128]{1,2,0:T(8,128)S(1)}, f32[16,384,128]{1,2,0:T(8,128)}, u32[]{:S(2)}) copy-start(f32[16,384,128]{1,2,0:T(8,128)} %get-tuple-element.97) | copy-start | bytes 9437188
  175.7 2.7 %copy-start.18 = (pred[384,384]{1,0:T(8,128)(4,1)S(1)}, pred[384,384]{1,0:T(8,128)(4,1)}, u32[]{:S(2)}) copy-start(pred[384,384]{1,0:T(8,128)(4,1)} %copy-done.17) | copy-start | bytes 442372
  185.4 17.4 %copy-start.8 = (bf16[384,16,128]{0,2,1:T(8,128)(2,1)S(1)}, bf16[384,16,128]{0,2,1:T(8,128)(2,1)}, u32[]{:S(2)}) copy-start(bf16[384,16,128]{0,2,1:T(8,128)(2,1)} %fusion.16) | copy-start | bytes 4718596
  188.1 25.5 %copy-start.12 = (bf16[384,16,128]{0,2,1:T(8,128)(2,1)S(1)}, bf16[384,16,128]{0,2,1:T(8,128)(2,1)}, u32[]{:S(2)}) copy-start(bf16[384,16,128]{0,2,1:T(8,128)(2,1)} %fusion.14) | copy-start | bytes 4718596
  188.1 8.8 %collective-permute-start.14 = (f32[16]{0:T(128)S(1)}, f32[16]{0:T(128)S(1)}, u32[]{:S(2)}, u32[]{:S(2)}) collective-permute-start(f32[16]{0:T(128)S(1)} %fusion.70), channel_id=1, source_target_pairs={{0,32},{8,40},{16,48},{24,56},{32,0},{40,8},{48,16},{56,24},{64,96... | collective-permute-start | bytes 200 | tf_op jit(solution)/shard_map/ppermute | solution.py:121
  188.2 8.9 %collective-permute-start.15 = (f32[16]{0:T(128)S(1)}, f32[16]{0:T(128)S(1)}, u32[]{:S(2)}, u32[]{:S(2)}) collective-permute-start(f32[16]{0:T(128)S(1)} %fusion.70), channel_id=1, source_target_pairs={{0,64},{8,72},{16,80},{24,88},{32,96},{40,104},{48,112},{56,120},{... | collective-permute-start | bytes 200 | tf_op jit(solution)/shard_map/ppermute | solution.py:121
  195.6 5.3 %collective-permute-start.16 = (f32[16]{0:T(128)S(1)}, f32[16]{0:T(128)S(1)}, u32[]{:S(2)}, u32[]{:S(2)}) collective-permute-start(f32[16]{0:T(128)S(1)} %fusion.70), channel_id=1, source_target_pairs={{0,96},{8,104},{16,112},{24,120},{32,64},{40,72},{48,80},{56,88},{... | collective-permute-start | bytes 200 | tf_op jit(solution)/shard_map/ppermute | solution.py:121
  200.9 7.5 %collective-permute-start.17 = (f32[16]{0:T(128)S(1)}, f32[16]{0:T(128)S(1)}, u32[]{:S(2)}, u32[]{:S(2)}) collective-permute-start(f32[16]{0:T(128)S(1)} %fusion.67), channel_id=1, source_target_pairs={{0,128},{8,136},{16,144},{24,152},{32,160},{40,168},{48,176},{56,1... | collective-permute-start | bytes 200 | tf_op jit(solution)/shard_map/ppermute | solution.py:121
  204.4 13.0 %copy-start.27 = (f32[16]{0:T(128)S(1)}, f32[16]{0:T(128)}, u32[]{:S(2)}) copy-start(f32[16]{0:T(128)} %param.13) | copy-start | bytes 196
  208.4 1.9 collective-permute-start.18
  208.4 3.6 %collective-permute-start.19 = (f32[16]{0:T(128)S(1)}, f32[16]{0:T(128)S(1)}, u32[]{:S(2)}, u32[]{:S(2)}) collective-permute-start(f32[16]{0:T(128)S(1)} %fusion.64), channel_id=1, source_target_pairs={{0,2},{1,3},{2,0},{3,1},{4,6},{5,7},{6,4},{7,5},{8,10},{9,11},{10,... | collective-permute-start | bytes 200 | tf_op jit(solution)/shard_map/ppermute | solution.py:121
  209.4 3.0 %collective-permute-start.20 = (f32[16]{0:T(128)S(1)}, f32[16]{0:T(128)S(1)}, u32[]{:S(2)}, u32[]{:S(2)}) collective-permute-start(f32[16]{0:T(128)S(1)} %fusion.64), channel_id=1, source_target_pairs={{0,3},{1,2},{2,1},{3,0},{4,7},{5,6},{6,5},{7,4},{8,11},{9,10},{10,... | collective-permute-start | bytes 200 | tf_op jit(solution)/shard_map/ppermute | solution.py:121
  212.3 5.1 %collective-permute-start.21 = (f32[16]{0:T(128)S(1)}, f32[16]{0:T(128)S(1)}, u32[]{:S(2)}, u32[]{:S(2)}) collective-permute-start(f32[16]{0:T(128)S(1)} %fusion.63), channel_id=1, source_target_pairs={{0,4},{1,5},{2,6},{3,7},{4,0},{5,1},{6,2},{7,3},{8,12},{9,13},{10,... | collective-permute-start | bytes 200 | tf_op jit(solution)/shard_map/ppermute | solution.py:121

commit v8 on v7

--- a/solution.py
+++ b/solution.py
@@ -188,13 +188,26 @@
     back_local = jnp.einsum(
         "she,shf->hef", carry_in[:, :, None] * query_f, grad_f, precision=state_mode
     )
-    state_input, backward_input, (key_scale, query_scale) = carried_both(
+    state_input, backward_input, tied = carried_both(
         decay_all,
         state_local,
         back_local,
         "seq",
-        (position[:, None] * carry_out, position[:, None] * carry_in),
-    )
+        (
+            position[:, None] * carry_out,
+            position[:, None] * carry_in,
+            query_block,
+            key_block,
+            value_block,
+            gradient_block,
+            cum_log,
+        ),
+    )
+    key_scale, query_scale, query_block, key_block, value_block, gradient_block, cum_log = tied
+    key_f = key_block.astype(jnp.float32)
+    value_f = value_block.astype(jnp.float32)
+    grad_f = gradient_block.astype(jnp.float32)
+    query_f = query_block.astype(jnp.float32)
     weight = weights_of(cum_log, seg_local)
     scores = jnp.einsum("she,the->hst", query_block, key_block, preferred_element_type=jnp.float32)
     grad_scores = jnp.einsum(

time: 220 us -> 208 us (0.945)
  waiting for transfers between devices: 86.5 us -> 58.2 us
  starting transfers between devices: 45.8 us -> 69.4 us
  other arithmetic: 24.4 us -> 18.3 us
    ppermute x1, starting transfers between devices: 3.22 us -> 18.6 us  [group_scan(): got = lax.ppermute(sent, axis, up + down)]
    ppermute x6, waiting for transfers between devices: 44.4 us -> 33.5 us  [row_exchange(): got.append(lax.ppermute(send, axis, pairs))]
    ppermute x1, waiting for transfers between devices: 11.1 us -> 2.02 us  [group_scan(): got = lax.ppermute(sent, axis, up + down)]
    ppermute x2, waiting for transfers between devices: 16.3 us -> 7.33 us  [group_scan(): rgot = lax.ppermute(bwd, axis, down)]
    ppermute x11, starting transfers between devices: 18.6 us -> 25.4 us  [digit_sum(): lax.ppermute(value, axis, [(i, i ^ k * step) for i in range(count)])]
    dot_general x1, matrix products: 2.65 us -> 5.48 us  [on_device(): jnp.einsum('thf,hef->the', value_f, backward_input, precision=state_mode)]
    dot_general x1, matrix products: 3.89 us -> 1.42 us  [on_device(): jnp.einsum('she,shf->hef', carry_in[:, :, None] * query_f, grad_f, precis...]
    unnamed x71 -> x65, local copies, waits for them, and re-layouts: 17.1 us -> 16.2 us
  transfers between devices with their start and end apart: 22 -> 22, of which waited for: 16 -> 15; matrix products, arithmetic and copies ran while one was open for 10% -> 18% of each run, Pallas kernels for 0% -> 0%
where the time goes in v8:
time: 208 us; the launch traced here: 206 us
  starting transfers between devices  69.4 us (33%)
  waiting for transfers between devices  58.2 us (28%)
  matrix products  37.5 us (18%)
  local copies, waits for them, and re-layouts  20.9 us (10%)
  other arithmetic  18.3 us (9%)
  between operations  2.11 us (1%)
    ppermute x6, waiting for transfers between devices, row_exchange(): got.append(lax.ppermute(send, axis, pairs))  33.5 us
    ppermute x11, starting transfers between devices, digit_sum(): lax.ppermute(value, axis, [(i, i ^ k * step) for i in range(count)])  25.4 us
    ppermute x1, starting transfers between devices, group_scan(): got = lax.ppermute(sent, axis, up + down)  18.6 us
    unnamed x65, local copies, waits for them, and re-layouts  16.2 us
    ppermute x6, starting transfers between devices, row_exchange(): got.append(lax.ppermute(send, axis, pairs))  11.7 us
    ppermute x2, starting transfers between devices, group_scan(): got = lax.ppermute(fwd, axis, up)  11.1 us
    ppermute x11, waiting for transfers between devices, digit_sum(): lax.ppermute(value, axis, [(i, i ^ k * step) for i in range(count)])  11 us
    ppermute x2, waiting for transfers between devices, group_scan(): rgot = lax.ppermute(bwd, axis, down)  7.33 us
  transfers between devices with their start and end apart: 22, of which 15 were waited for; matrix products, arithmetic and copies ran while one was open for 18% of the time, Pallas kernels for 0%

profile of v8, /device:TPU:6, one launch (start us, length us, event | category | flops | bytes accessed | tf_op | source)
XLA Modules:
  0.0 206.5 jit_solution(16529046265864565049)
XLA Ops:
  0.7 0.9 reduce-window_clone.1
  6.4 0.9 reduce-window.24
  7.8 1.9 copy.74
  9.7 1.6 copy.97
  11.2 1.6 copy.98
  12.8 1.9 copy.76
  14.8 3.0 %fusion.20 = f32[16,128,128]{2,1,0:T(8,128)S(1)} fusion(bf16[384,16,128]{0,2,1:T(8,128)(2,1)S(1)} %bitcast.191, bf16[384,16,128]{2,1,0:T(8,128)(2,1)} %bitcast.207, f32[384,16]{0,1:T(8,128)S(1)} %get-tuple-element.64), kind=kOutput, calls=%fused_computation.29 | convolution fusion | flops 605552640 | bytes 4218880 | tf_op jit(solution)/shard_map/the,thf->hef/dot_general | solution.py:185
  17.8 1.4 fusion.17
  19.5 1.3 copy-done.8
  20.8 1.2 dynamic-slice_bitcast_fusion
  22.0 1.6 collective-permute-start
  23.6 2.9 %collective-permute-start.1 = (f32[4,264,128]{2,1,0:T(8,128)}, f32[4,264,128]{2,1,0:T(8,128)}, u32[]{:S(2)}, u32[]{:S(2)}) collective-permute-start(f32[4,264,128]{2,1,0:T(8,128)} %get-tuple-element.82), channel_id=1, source_target_pairs={{0,16},{8,24},{16,0},{24,8},{32,48},{40,56},{48,32},{56,40},{64,80... | collective-permute-start | bytes 1622024 | tf_op jit(solution)/shard_map/ppermute | solution.py:64
  26.5 1.3 collective-permute-start.2
  27.8 9.8 %collective-permute-done = f32[4,264,128]{2,1,0:T(8,128)} collective-permute-done((f32[4,264,128]{2,1,0:T(8,128)}, f32[4,264,128]{2,1,0:T(8,128)}, u32[]{:S(2)}, u32[]{:S(2)}) %collective-permute-start) | collective-permute-done | bytes 540704 | tf_op jit(solution)/shard_map/ppermute | solution.py:64
  37.6 12.8 %collective-permute-done.1 = f32[4,264,128]{2,1,0:T(8,128)} collective-permute-done((f32[4,264,128]{2,1,0:T(8,128)}, f32[4,264,128]{2,1,0:T(8,128)}, u32[]{:S(2)}, u32[]{:S(2)}) %collective-permute-start.1) | collective-permute-done | bytes 540704 | tf_op jit(solution)/shard_map/ppermute | solution.py:64
  50.4 1.8 fusion.46
  53.2 0.9 bitcast_add_fusion.4
  54.2 0.9 pad_maximum_fusion.4
  55.1 4.5 %collective-permute-start.3 = (f32[4,136,128]{2,1,0:T(8,128)}, f32[4,136,128]{2,1,0:T(8,128)}, u32[]{:S(2)}, u32[]{:S(2)}) collective-permute-start(f32[4,136,128]{2,1,0:T(8,128)} %get-tuple-element.96), channel_id=1, source_target_pairs={{0,32},{8,40},{16,48},{24,56},{32,64},{40,72},{48,80},{56,88},{64,... | collective-permute-start | bytes 835592 | tf_op jit(solution)/shard_map/ppermute | solution.py:42
  59.6 1.3 collective-permute-start.5
  61.3 3.0 %collective-permute-done.3 = f32[4,136,128]{2,1,0:T(8,128)} collective-permute-done((f32[4,136,128]{2,1,0:T(8,128)}, f32[4,136,128]{2,1,0:T(8,128)}, u32[]{:S(2)}, u32[]{:S(2)}) %collective-permute-start.3) | collective-permute-done | bytes 278560 | tf_op jit(solution)/shard_map/ppermute | solution.py:42
  64.3 4.8 %collective-permute-done.5 = f32[4,136,128]{2,1,0:T(8,128)} collective-permute-done((f32[4,136,128]{2,1,0:T(8,128)}, f32[4,136,128]{2,1,0:T(8,128)}, u32[]{:S(2)}, u32[]{:S(2)}) %collective-permute-start.5) | collective-permute-done | bytes 278560 | tf_op jit(solution)/shard_map/ppermute | solution.py:43
  69.1 1.3 multiply_add_fusion.11
  71.2 1.3 collective-permute-start.6
  72.5 5.9 %multiply_convert_fusion.1 = bf16[16,384,384]{2,1,0:T(8,128)(2,1)S(1)} fusion(f32[16,384]{1,0:T(8,128)S(1)} %bitcast.223, pred[384,384]{1,0:T(8,128)(4,1)S(1)} %fusion.44, bf16[384,16,128]{2,1,0:T(8,128)(2,1)} %bitcast.208, bf16[384,16,128]{2,1,0:T(8,128)(2,1)S(1)} %bitcast.204), kind=kOutput, calls=%fused_computation.1 | convolution fusion | flops 615776256 | bytes 8036352 | tf_op jit(solution)/shard_map/shf,thf->hst/dot_general | solution.py:213
  78.4 6.5 %collective-permute-start.4 = (f32[4,136,128]{2,1,0:T(8,128)S(1)}, f32[4,136,128]{2,1,0:T(8,128)S(1)}, u32[]{:S(2)}, u32[]{:S(2)}) collective-permute-start(f32[4,136,128]{2,1,0:T(8,128)S(1)} %pad_maximum_fusion.6), channel_id=1, source_target_pairs={{0,64},{8,72},{16,80},{24,88},{32,96},{40,104},{48,112},{56,120},{... | collective-permute-start | bytes 835592 | tf_op jit(solution)/shard_map/ppermute | solution.py:42
  85.1 2.5 %collective-permute-done.6 = f32[4,136,128]{2,1,0:T(8,128)S(1)} collective-permute-done((f32[4,136,128]{2,1,0:T(8,128)S(1)}, f32[4,136,128]{2,1,0:T(8,128)S(1)}, u32[]{:S(2)}, u32[]{:S(2)}) %collective-permute-start.6) | collective-permute-done | bytes 278560 | tf_op jit(solution)/shard_map/ppermute | solution.py:43
  87.7 1.4 collective-permute-done.4
  89.3 18.6 %collective-permute-start.7 = (f32[4,136,128]{2,1,0:T(8,128)S(1)}, f32[4,136,128]{2,1,0:T(8,128)S(1)}, u32[]{:S(2)}, u32[]{:S(2)}) collective-permute-start(f32[4,136,128]{2,1,0:T(8,128)S(1)} %maximum_select_fusion), channel_id=1, source_target_pairs={{0,128},{8,136},{16,144},{24,152},{32,160},{40,168},{48,176},{56,1... | collective-permute-start | bytes 835592 | tf_op jit(solution)/shard_map/ppermute | solution.py:38
  107.9 2.9 %fusion.7 = (f32[384,16]{0,1:T(8,128)S(1)}, f32[16,128,384]{2,1,0:T(8,128)}) fusion(bf16[384,16,128]{0,2,1:T(8,128)(2,1)S(1)} %bitcast.192, bf16[384,16,128]{0,2,1:T(8,128)(2,1)S(1)} %bitcast.198, bf16[16,384,384]{2,1,0:T(8,128)(2,1)S(1)} %multiply_convert_fusion.1), kind=kOutput, calls=%fused_computation.13 | convolution fusion | flops 606332928 | bytes 11034624 | tf_op jit(solution)/shard_map/hst,she->the/dot_general | solution.py:227
  110.8 0.8 slice_reduce_fusion.2
  111.6 0.8 slice_reduce_fusion.4
  112.5 2.0 collective-permute-done.7
  115.5 1.2 multiply_add_fusion.9
  116.8 1.2 multiply_add_fusion.4
  118.1 1.2 multiply_add_fusion.1
  119.7 4.3 %collective-permute-start.10 = (f32[4,256,128]{2,1,0:T(8,128)S(1)}, f32[4,256,128]{2,1,0:T(8,128)S(1)}, u32[]{:S(2)}, u32[]{:S(2)}) collective-permute-start(f32[4,256,128]{2,1,0:T(8,128)S(1)} %get-tuple-element.84), channel_id=1, source_target_pairs={{0,24},{8,0},{16,8},{24,16},{32,56},{40,32},{48,40},{56,48},{64,88... | collective-permute-start | bytes 1572872 | tf_op jit(solution)/shard_map/ppermute | solution.py:64
  124.1 1.6 collective-permute-start.9
  125.6 3.4 %fusion.9 = (f32[384,16]{0,1:T(8,128)S(1)}, f32[16,128,384]{2,1,0:T(8,128)}) fusion(bf16[384,16,128]{0,2,1:T(8,128)(2,1)S(1)} %bitcast.199, bf16[384,16,128]{0,2,1:T(8,128)(2,1)S(1)} %bitcast.193, bf16[16,384,384]{2,1,0:T(8,128)(2,1)S(1)} %multiply_convert_fusion.1), kind=kOutput, calls=%fused_computation.15 | convolution fusion | flops 606332928 | bytes 11034624 | tf_op jit(solution)/shard_map/hst,the->she/dot_general | solution.py:224
  129.1 7.3 %collective-permute-done.10 = f32[4,256,128]{2,1,0:T(8,128)S(1)} collective-permute-done((f32[4,256,128]{2,1,0:T(8,128)S(1)}, f32[4,256,128]{2,1,0:T(8,128)S(1)}, u32[]{:S(2)}, u32[]{:S(2)}) %collective-permute-start.10) | collective-permute-done | bytes 524320 | tf_op jit(solution)/shard_map/ppermute | solution.py:64
  136.4 3.7 %collective-permute-done.8 = f32[4,256,128]{2,1,0:T(8,128)S(1)} collective-permute-done((f32[4,256,128]{2,1,0:T(8,128)S(1)}, f32[4,256,128]{2,1,0:T(8,128)S(1)}, u32[]{:S(2)}, u32[]{:S(2)}) %collective-permute-start.8) | collective-permute-done | bytes 524320 | tf_op jit(solution)/shard_map/ppermute | solution.py:64
  140.6 1.9 copy-done.3
  142.5 1.5 fusion.31
  144.1 1.5 fusion.32
  145.7 1.4 collective-permute-start.12
  147.1 3.2 %collective-permute-start.13 = (f32[16]{0:T(128)S(1)}, f32[16]{0:T(128)S(1)}, u32[]{:S(2)}, u32[]{:S(2)}) collective-permute-start(f32[16]{0:T(128)S(1)} %add_subtract_fusion), channel_id=1, source_target_pairs={{0,24},{8,16},{16,8},{24,0},{32,56},{40,48},{48,40},{56,32},{64,88... | collective-permute-start | bytes 200 | tf_op jit(solution)/shard_map/ppermute | solution.py:121
  150.4 2.8 %fusion.41 = f32[16,128,384]{2,1,0:T(8,128)} fusion(bf16[384,16,128]{0,2,1:T(8,128)(2,1)S(1)} %bitcast.195, f32[16,256,128]{2,1,0:T(8,128)S(1)} %bitcast.213), kind=kOutput, calls=%fused_computation.54 | convolution fusion | flops 603979776 | bytes 5767168 | tf_op jit(solution)/shard_map/the,hef->thf/dot_general | solution.py:221
  153.1 7.0 %fusion.12 = bf16[384,16,128]{0,2,1:T(8,128)(2,1)} fusion(f32[16,128,384]{2,1,0:T(8,128)} %fusion.41, f32[16,384]{1,0:T(8,128)S(1)} %bitcast.224, pred[384,384]{1,0:T(8,128)(4,1)S(1)} %copy-done.17, bf16[384,16,128]{0,2,1:T(8,128)(2,1)S(1)} %bitcast.201, bf16[384,16,128]{0,2,1:T(8,128)(2,1)S(1)} %bitcast.196, f32[384,16]{0,1:T(8,128)S(1)} %get-tuple-element.64, ...), kind=kOutput, calls=%fused_computation.19 | convolution fusion | flops 1222115328 | bytes 9633792 | tf_op jit(solution)/shard_map/hst,shf->thf/dot_general | solution.py:218
  160.2 5.5 %fusion.14 = bf16[384,16,128]{0,2,1:T(8,128)(2,1)} fusion(f32[16,128,384]{2,1,0:T(8,128)} %get-tuple-element.106, f32[384,16]{0,1:T(8,128)S(1)} %get-tuple-element.64, bf16[384,16,128]{2,1,0:T(8,128)(2,1)} %bitcast.209, f32[16,256,128]{2,1,0:T(8,128)} %bitcast.214), kind=kOutput, calls=%fused_computation.22 | convolution fusion | flops 606339072 | bytes 7364608 | tf_op jit(solution)/shard_map/thf,hef->the/dot_general | solution.py:246
  165.7 2.6 %fusion.16 = bf16[384,16,128]{0,2,1:T(8,128)(2,1)} fusion(f32[16,128,384]{2,1,0:T(8,128)S(1)} %copy-done.7, f32[384,16]{0,1:T(8,128)S(1)} %get-tuple-element.94, bf16[384,16,128]{2,1,0:T(8,128)(2,1)S(1)} %bitcast.206, f32[16,256,128]{2,1,0:T(8,128)S(1)} %bitcast.215), kind=kOutput, calls=%fused_computation.25 | convolution fusion | flops 606339072 | bytes 7364608 | tf_op jit(solution)/shard_map/shf,hef->she/dot_general | solution.py:243
  168.3 2.7 %copy.91 = bf16[1,384,2048]{2,1,0:T(8,128)(2,1)} copy(bf16[1,384,2048]{1,2,0:T(8,128)(2,1)} %bitcast.222) | data formatting | bytes 3145728
  171.0 11.3 %collective-permute-start.14 = (f32[16]{0:T(128)S(1)}, f32[16]{0:T(128)S(1)}, u32[]{:S(2)}, u32[]{:S(2)}) collective-permute-start(f32[16]{0:T(128)S(1)} %fusion.74), channel_id=1, source_target_pairs={{0,32},{8,40},{16,48},{24,56},{32,0},{40,8},{48,16},{56,24},{64,96... | collective-permute-start | bytes 200 | tf_op jit(solution)/shard_map/ppermute | solution.py:121
  182.3 1.7 collective-permute-start.15
  184.8 2.0 collective-permute-done.15
  186.8 2.6 %collective-permute-done.16 = f32[16]{0:T(128)S(1)} collective-permute-done((f32[16]{0:T(128)S(1)}, f32[16]{0:T(128)S(1)}, u32[]{:S(2)}, u32[]{:S(2)}) %collective-permute-start.16) | collective-permute-done | bytes 96 | tf_op jit(solution)/shard_map/ppermute | solution.py:121
  189.4 3.8 %collective-permute-start.17 = (f32[16]{0:T(128)S(1)}, f32[16]{0:T(128)S(1)}, u32[]{:S(2)}, u32[]{:S(2)}) collective-permute-start(f32[16]{0:T(128)S(1)} %fusion.71), channel_id=1, source_target_pairs={{0,128},{8,136},{16,144},{24,152},{32,160},{40,168},{48,176},{56,1... | collective-permute-start | bytes 200 | tf_op jit(solution)/shard_map/ppermute | solution.py:121
  193.2 1.6 copy.90
  194.8 2.1 %collective-permute-done.17 = f32[16]{0:T(128)S(1)} collective-permute-done((f32[16]{0:T(128)S(1)}, f32[16]{0:T(128)S(1)}, u32[]{:S(2)}, u32[]{:S(2)}) %collective-permute-start.17) | collective-permute-done | bytes 96 | tf_op jit(solution)/shard_map/ppermute | solution.py:121
  196.9 0.9 collective-permute-start.19
  197.8 1.0 collective-permute-start.20
  198.8 1.7 collective-permute-done.19
  200.8 1.2 collective-permute-start.21
  202.1 1.6 copy.89
  203.7 2.3 %collective-permute-done.21 = f32[16]{0:T(128)S(1)} collective-permute-done((f32[16]{0:T(128)S(1)}, f32[16]{0:T(128)S(1)}, u32[]{:S(2)}, u32[]{:S(2)}) %collective-permute-start.21) | collective-permute-done | bytes 96 | tf_op jit(solution)/shard_map/ppermute | solution.py:121
  (123 shorter events, 11.1 us)
Async XLA Ops:
  0.6 9.0 %copy-start.13 = (bf16[1,384,2048]{2,1,0:T(8,128)(2,1)S(1)}, bf16[1,384,2048]{2,1,0:T(8,128)(2,1)}, u32[]{:S(2)}) copy-start(bf16[1,384,2048]{2,1,0:T(8,128)(2,1)} %param.9) | copy-start | bytes 4718596
  9.6 1.6 copy-start.14
  14.8 3.0 %copy-start = (bf16[48,8,16,128]{3,2,1,0:T(8,128)(2,1)S(1)}, bf16[48,8,16,128]{3,2,1,0:T(8,128)(2,1)}, u32[]{:S(2)}) copy-start(bf16[48,8,16,128]{3,2,1,0:T(8,128)(2,1)} %copy.98) | copy-start | bytes 4718596
  19.5 1.4 copy-start.8
  22.0 15.6 %collective-permute-start = (f32[4,264,128]{2,1,0:T(8,128)}, f32[4,264,128]{2,1,0:T(8,128)}, u32[]{:S(2)}, u32[]{:S(2)}) collective-permute-start(f32[4,264,128]{2,1,0:T(8,128)} %get-tuple-element.83), channel_id=1, source_target_pairs={{0,8},{8,16},{16,24},{24,0},{32,40},{40,48},{48,56},{56,32},{64,72... | collective-permute-start | bytes 1622024 | tf_op jit(solution)/shard_map/ppermute | solution.py:64
  23.6 26.8 %collective-permute-start.1 = (f32[4,264,128]{2,1,0:T(8,128)}, f32[4,264,128]{2,1,0:T(8,128)}, u32[]{:S(2)}, u32[]{:S(2)}) collective-permute-start(f32[4,264,128]{2,1,0:T(8,128)} %get-tuple-element.82), channel_id=1, source_target_pairs={{0,16},{8,24},{16,0},{24,8},{32,48},{40,56},{48,32},{56,40},{64,80... | collective-permute-start | bytes 1622024 | tf_op jit(solution)/shard_map/ppermute | solution.py:64
  26.5 23.9 %collective-permute-start.2 = (f32[4,264,128]{2,1,0:T(8,128)}, f32[4,264,128]{2,1,0:T(8,128)}, u32[]{:S(2)}, u32[]{:S(2)}) collective-permute-start(f32[4,264,128]{2,1,0:T(8,128)} %get-tuple-element.81), channel_id=1, source_target_pairs={{0,24},{8,0},{16,8},{24,16},{32,56},{40,32},{48,40},{56,48},{64,88... | collective-permute-start | bytes 1622024 | tf_op jit(solution)/shard_map/ppermute | solution.py:64
  52.3 2.8 %copy-start.6 = (f32[4,4,264,128]{3,2,1,0:T(8,128)}, f32[4,4,264,128]{3,2,1,0:T(8,128)S(1)}, u32[]{:S(2)}) copy-start(f32[4,4,264,128]{3,2,1,0:T(8,128)S(1)} %pad_maximum_fusion.1) | copy-start | bytes 6488068
  52.4 1.7 copy-start.18
  53.2 0.9 copy-start.20
  53.2 0.9 copy-start.22
  54.1 1.0 copy-start.11
  54.1 5.5 %copy-start.12 = (f32[4,128,128]{2,1,0:T(8,128)}, f32[4,128,128]{2,1,0:T(8,128)S(1)}, u32[]{:S(2)}) copy-start(f32[4,128,128]{2,1,0:T(8,128)S(1)} %get-tuple-element.75) | copy-start | bytes 786436
  55.1 9.2 %collective-permute-start.3 = (f32[4,136,128]{2,1,0:T(8,128)}, f32[4,136,128]{2,1,0:T(8,128)}, u32[]{:S(2)}, u32[]{:S(2)}) collective-permute-start(f32[4,136,128]{2,1,0:T(8,128)} %get-tuple-element.96), channel_id=1, source_target_pairs={{0,32},{8,40},{16,48},{24,56},{32,64},{40,72},{48,80},{56,88},{64,... | collective-permute-start | bytes 835592 | tf_op jit(solution)/shard_map/ppermute | solution.py:42
  59.6 9.4 %collective-permute-start.5 = (f32[4,136,128]{2,1,0:T(8,128)}, f32[4,136,128]{2,1,0:T(8,128)}, u32[]{:S(2)}, u32[]{:S(2)}) collective-permute-start(f32[4,136,128]{2,1,0:T(8,128)} %get-tuple-element.95), channel_id=1, source_target_pairs={{32,0},{40,8},{48,16},{56,24},{64,32},{72,40},{80,48},{88,56},{96,... | collective-permute-start | bytes 835592 | tf_op jit(solution)/shard_map/ppermute | solution.py:43
  61.1 11.4 %copy-start.1 = (bf16[48,8,16,128]{3,2,1,0:T(8,128)(2,1)S(1)}, bf16[48,8,16,128]{3,2,1,0:T(8,128)(2,1)}, u32[]{:S(2)}) copy-start(bf16[48,8,16,128]{3,2,1,0:T(8,128)(2,1)} %copy.98) | copy-start | bytes 4718596
  61.3 17.2 %copy-start.16 = (pred[384,384]{1,0:T(8,128)(4,1)}, pred[384,384]{1,0:T(8,128)(4,1)S(1)}, u32[]{:S(2)}) copy-start(pred[384,384]{1,0:T(8,128)(4,1)S(1)} %fusion.44) | copy-start | bytes 442372
  71.2 16.4 %collective-permute-start.6 = (f32[4,136,128]{2,1,0:T(8,128)S(1)}, f32[4,136,128]{2,1,0:T(8,128)S(1)}, u32[]{:S(2)}, u32[]{:S(2)}) collective-permute-start(f32[4,136,128]{2,1,0:T(8,128)S(1)} %pad_maximum_fusion.7), channel_id=1, source_target_pairs={{64,0},{72,8},{80,16},{88,24},{96,32},{104,40},{112,48},{120,56},{... | collective-permute-start | bytes 835592 | tf_op jit(solution)/shard_map/ppermute | solution.py:43
  78.4 10.7 %collective-permute-start.4 = (f32[4,136,128]{2,1,0:T(8,128)S(1)}, f32[4,136,128]{2,1,0:T(8,128)S(1)}, u32[]{:S(2)}, u32[]{:S(2)}) collective-permute-start(f32[4,136,128]{2,1,0:T(8,128)S(1)} %pad_maximum_fusion.6), channel_id=1, source_target_pairs={{0,64},{8,72},{16,80},{24,88},{32,96},{40,104},{48,112},{56,120},{... | collective-permute-start | bytes 835592 | tf_op jit(solution)/shard_map/ppermute | solution.py:42
  89.3 25.2 %collective-permute-start.7 = (f32[4,136,128]{2,1,0:T(8,128)S(1)}, f32[4,136,128]{2,1,0:T(8,128)S(1)}, u32[]{:S(2)}, u32[]{:S(2)}) collective-permute-start(f32[4,136,128]{2,1,0:T(8,128)S(1)} %maximum_select_fusion), channel_id=1, source_target_pairs={{0,128},{8,136},{16,144},{24,152},{32,160},{40,168},{48,176},{56,1... | collective-permute-start | bytes 835592 | tf_op jit(solution)/shard_map/ppermute | solution.py:38
  110.8 5.9 %copy-start.21 = (f32[4]{0:T(128)S(1)}, f32[4]{0:T(128)}, u32[]{:S(2)}) copy-start(f32[4]{0:T(128)} %copy-done.20) | copy-start | bytes 52
  110.8 5.9 %copy-start.24 = (f32[4]{0:T(128)S(1)}, f32[4]{0:T(128)}, u32[]{:S(2)}) copy-start(f32[4]{0:T(128)} %get-tuple-element.97) | copy-start | bytes 52
  116.7 1.3 copy-start.15
  116.7 1.3 copy-start.19
  116.7 1.3 copy-start.23
  116.7 1.3 copy-start.26
  116.7 1.3 copy-start.27
  116.7 1.3 copy-start.28
  119.7 16.7 %collective-permute-start.10 = (f32[4,256,128]{2,1,0:T(8,128)S(1)}, f32[4,256,128]{2,1,0:T(8,128)S(1)}, u32[]{:S(2)}, u32[]{:S(2)}) collective-permute-start(f32[4,256,128]{2,1,0:T(8,128)S(1)} %get-tuple-element.84), channel_id=1, source_target_pairs={{0,24},{8,0},{16,8},{24,16},{32,56},{40,32},{48,40},{56,48},{64,88... | collective-permute-start | bytes 1572872 | tf_op jit(solution)/shard_map/ppermute | solution.py:64
  124.1 16.0 %collective-permute-start.8 = (f32[4,256,128]{2,1,0:T(8,128)S(1)}, f32[4,256,128]{2,1,0:T(8,128)S(1)}, u32[]{:S(2)}, u32[]{:S(2)}) collective-permute-start(f32[4,256,128]{2,1,0:T(8,128)S(1)} %get-tuple-element.86), channel_id=1, source_target_pairs={{0,8},{8,16},{16,24},{24,0},{32,40},{40,48},{48,56},{56,32},{64,72... | collective-permute-start | bytes 1572872 | tf_op jit(solution)/shard_map/ppermute | solution.py:64
  124.1 16.0 %collective-permute-start.9 = (f32[4,256,128]{2,1,0:T(8,128)S(1)}, f32[4,256,128]{2,1,0:T(8,128)S(1)}, u32[]{:S(2)}, u32[]{:S(2)}) collective-permute-start(f32[4,256,128]{2,1,0:T(8,128)S(1)} %get-tuple-element.85), channel_id=1, source_target_pairs={{0,16},{8,24},{16,0},{24,8},{32,48},{40,56},{48,32},{56,40},{64,80... | collective-permute-start | bytes 1572872 | tf_op jit(solution)/shard_map/ppermute | solution.py:64
  140.4 2.1 %copy-start.3 = (bf16[48,8,16,128]{3,2,1,0:T(8,128)(2,1)S(1)}, bf16[48,8,16,128]{3,2,1,0:T(8,128)(2,1)}, u32[]{:S(2)}) copy-start(bf16[48,8,16,128]{3,2,1,0:T(8,128)(2,1)} %copy.97) | copy-start | bytes 4718596
  140.6 9.8 %copy-start.4 = (f32[4,4,256,128]{3,2,1,0:T(8,128)}, f32[4,4,256,128]{3,2,1,0:T(8,128)S(1)}, u32[]{:S(2)}) copy-start(f32[4,4,256,128]{3,2,1,0:T(8,128)S(1)} %pad_maximum_fusion.3) | copy-start | bytes 6291460
  145.6 7.5 %copy-start.17 = (pred[384,384]{1,0:T(8,128)(4,1)S(1)}, pred[384,384]{1,0:T(8,128)(4,1)}, u32[]{:S(2)}) copy-start(pred[384,384]{1,0:T(8,128)(4,1)} %copy-done.16) | copy-start | bytes 442372
  145.6 25.4 %collective-permute-start.11 = (f32[16]{0:T(128)S(1)}, f32[16]{0:T(128)S(1)}, u32[]{:S(2)}, u32[]{:S(2)}) collective-permute-start(f32[16]{0:T(128)S(1)} %add_subtract_fusion), channel_id=1, source_target_pairs={{0,8},{8,0},{16,24},{24,16},{32,40},{40,32},{48,56},{56,48},{64,72... | collective-permute-start | bytes 200 | tf_op jit(solution)/shard_map/ppermute | solution.py:121
  145.7 25.3 %collective-permute-start.12 = (f32[16]{0:T(128)S(1)}, f32[16]{0:T(128)S(1)}, u32[]{:S(2)}, u32[]{:S(2)}) collective-permute-start(f32[16]{0:T(128)S(1)} %add_subtract_fusion), channel_id=1, source_target_pairs={{0,16},{8,24},{16,0},{24,8},{32,48},{40,56},{48,32},{56,40},{64,80... | collective-permute-start | bytes 200 | tf_op jit(solution)/shard_map/ppermute | solution.py:121
  147.1 23.9 %collective-permute-start.13 = (f32[16]{0:T(128)S(1)}, f32[16]{0:T(128)S(1)}, u32[]{:S(2)}, u32[]{:S(2)}) collective-permute-start(f32[16]{0:T(128)S(1)} %add_subtract_fusion), channel_id=1, source_target_pairs={{0,24},{8,16},{16,8},{24,0},{32,56},{40,48},{48,40},{56,32},{64,88... | collective-permute-start | bytes 200 | tf_op jit(solution)/shard_map/ppermute | solution.py:121
  160.2 5.5 %copy-start.2 = (bf16[48,8,16,128]{3,2,1,0:T(8,128)(2,1)S(1)}, bf16[48,8,16,128]{3,2,1,0:T(8,128)(2,1)}, u32[]{:S(2)}) copy-start(bf16[48,8,16,128]{3,2,1,0:T(8,128)(2,1)} %copy.98) | copy-start | bytes 4718596
  160.2 5.5 %copy-start.5 = (f32[4,4,256,128]{3,2,1,0:T(8,128)S(1)}, f32[4,4,256,128]{3,2,1,0:T(8,128)}, u32[]{:S(2)}) copy-start(f32[4,4,256,128]{3,2,1,0:T(8,128)} %copy-done.4) | copy-start | bytes 6291460
  160.2 5.5 %copy-start.7 = (f32[16,128,384]{2,1,0:T(8,128)S(1)}, f32[16,128,384]{2,1,0:T(8,128)}, u32[]{:S(2)}) copy-start(f32[16,128,384]{2,1,0:T(8,128)} %get-tuple-element.108) | copy-start | bytes 9437188
  168.3 24.9 %copy-start.10 = (bf16[384,16,128]{0,2,1:T(8,128)(2,1)S(1)}, bf16[384,16,128]{0,2,1:T(8,128)(2,1)}, u32[]{:S(2)}) copy-start(bf16[384,16,128]{0,2,1:T(8,128)(2,1)} %fusion.14) | copy-start | bytes 4718596
  171.0 31.1 %copy-start.9 = (bf16[384,16,128]{0,2,1:T(8,128)(2,1)S(1)}, bf16[384,16,128]{0,2,1:T(8,128)(2,1)}, u32[]{:S(2)}) copy-start(bf16[384,16,128]{0,2,1:T(8,128)(2,1)} %fusion.16) | copy-start | bytes 4718596
  171.0 13.8 %collective-permute-start.14 = (f32[16]{0:T(128)S(1)}, f32[16]{0:T(128)S(1)}, u32[]{:S(2)}, u32[]{:S(2)}) collective-permute-start(f32[16]{0:T(128)S(1)} %fusion.74), channel_id=1, source_target_pairs={{0,32},{8,40},{16,48},{24,56},{32,0},{40,8},{48,16},{56,24},{64,96... | collective-permute-start | bytes 200 | tf_op jit(solution)/shard_map/ppermute | solution.py:121
  182.3 4.4 %collective-permute-start.15 = (f32[16]{0:T(128)S(1)}, f32[16]{0:T(128)S(1)}, u32[]{:S(2)}, u32[]{:S(2)}) collective-permute-start(f32[16]{0:T(128)S(1)} %fusion.74), channel_id=1, source_target_pairs={{0,64},{8,72},{16,80},{24,88},{32,96},{40,104},{48,112},{56,120},{... | collective-permute-start | bytes 200 | tf_op jit(solution)/shard_map/ppermute | solution.py:121
  184.0 5.3 %collective-permute-start.16 = (f32[16]{0:T(128)S(1)}, f32[16]{0:T(128)S(1)}, u32[]{:S(2)}, u32[]{:S(2)}) collective-permute-start(f32[16]{0:T(128)S(1)} %fusion.74), channel_id=1, source_target_pairs={{0,96},{8,104},{16,112},{24,120},{32,64},{40,72},{48,80},{56,88},{... | collective-permute-start | bytes 200 | tf_op jit(solution)/shard_map/ppermute | solution.py:121
  189.4 7.5 %collective-permute-start.17 = (f32[16]{0:T(128)S(1)}, f32[16]{0:T(128)S(1)}, u32[]{:S(2)}, u32[]{:S(2)}) collective-permute-start(f32[16]{0:T(128)S(1)} %fusion.71), channel_id=1, source_target_pairs={{0,128},{8,136},{16,144},{24,152},{32,160},{40,168},{48,176},{56,1... | collective-permute-start | bytes 200 | tf_op jit(solution)/shard_map/ppermute | solution.py:121
  194.8 11.2 %copy-start.25 = (f32[16]{0:T(128)S(1)}, f32[16]{0:T(128)}, u32[]{:S(2)}) copy-start(f32[16]{0:T(128)} %param.13) | copy-start | bytes 196
  196.9 1.9 collective-permute-start.18
  196.9 3.6 %collective-permute-start.19 = (f32[16]{0:T(128)S(1)}, f32[16]{0:T(128)S(1)}, u32[]{:S(2)}, u32[]{:S(2)}) collective-permute-start(f32[16]{0:T(128)S(1)} %fusion.68), channel_id=1, source_target_pairs={{0,2},{1,3},{2,0},{3,1},{4,6},{5,7},{6,4},{7,5},{8,10},{9,11},{10,... | collective-permute-start | bytes 200 | tf_op jit(solution)/shard_map/ppermute | solution.py:121
  197.8 3.0 %collective-permute-start.20 = (f32[16]{0:T(128)S(1)}, f32[16]{0:T(128)S(1)}, u32[]{:S(2)}, u32[]{:S(2)}) collective-permute-start(f32[16]{0:T(128)S(1)} %fusion.68), channel_id=1, source_target_pairs={{0,3},{1,2},{2,1},{3,0},{4,7},{5,6},{6,5},{7,4},{8,11},{9,10},{10,... | collective-permute-start | bytes 200 | tf_op jit(solution)/shard_map/ppermute | solution.py:121
  200.8 5.1 %collective-permute-start.21 = (f32[16]{0:T(128)S(1)}, f32[16]{0:T(128)S(1)}, u32[]{:S(2)}, u32[]{:S(2)}) collective-permute-start(f32[16]{0:T(128)S(1)} %fusion.67), channel_id=1, source_target_pairs={{0,4},{1,5},{2,6},{3,7},{4,0},{5,1},{6,2},{7,3},{8,12},{9,13},{10,... | collective-permute-start | bytes 200 | tf_op jit(solution)/shard_map/ppermute | solution.py:121

commit v9 on v8

--- a/solution.py
+++ b/solution.py
@@ -73,7 +73,6 @@
     pad = jnp.broadcast_to(decay[:, None, None], (heads, 8, cols))
     parts = jnp.concatenate([forward_part, backward_part, pad], axis=1)
     mine = row_exchange(parts.reshape(group, share, 2 * rows + 8, cols), axis, group)
-    mine, extra = lax.optimization_barrier((mine, extra))
     own_s = mine[:, :, :rows]
     own_b = mine[:, :, rows : 2 * rows]
     own_a = mine[:, :, 2 * rows, 0]
@@ -95,8 +94,7 @@
     before, after = group_scan(
         packed(total_a, total), packed(total_a, rtotal), axis, group
     )
-    before = before[:, :rows]
-    after = after[:, :rows]
+    before, after, extra = lax.optimization_barrier((before[:, :rows], after[:, :rows], extra))
     result = jnp.stack(
         [
             jnp.concatenate(

time: 208 us -> 199 us (0.957)
  starting transfers between devices: 69.4 us -> 57.1 us
  waiting for transfers between devices: 58.2 us -> 64.1 us
    ppermute x1, starting transfers between devices: 18.6 us -> 9.56 us  [group_scan(): got = lax.ppermute(sent, axis, up + down)]
    ppermute x2, waiting for transfers between devices: 7.33 us -> 13.1 us  [group_scan(): rgot = lax.ppermute(bwd, axis, down)]
    ppermute x1, waiting for transfers between devices: 2.02 us -> 5.94 us  [group_scan(): got = lax.ppermute(sent, axis, up + down)]
    ppermute x11, starting transfers between devices: 25.4 us -> 22 us  [digit_sum(): lax.ppermute(value, axis, [(i, i ^ k * step) for i in range(count)])]
    ppermute x11, waiting for transfers between devices: 11 us -> 7.57 us  [digit_sum(): lax.ppermute(value, axis, [(i, i ^ k * step) for i in range(count)])]
    unnamed x65 -> x67, local copies, waits for them, and re-layouts: 16.2 us -> 14.9 us
  transfers between devices with their start and end apart: 22 -> 22, of which waited for: 15 -> 14; matrix products, arithmetic and copies ran while one was open for 18% -> 19% of each run, Pallas kernels for 0% -> 0%
where the time goes in v9:
time: 199 us; the launch traced here: 198 us
  waiting for transfers between devices  64.1 us (32%)
  starting transfers between devices  57.1 us (29%)
  matrix products  35.7 us (18%)
  local copies, waits for them, and re-layouts  20.1 us (10%)
  other arithmetic  19 us (10%)
    ppermute x6, waiting for transfers between devices, row_exchange(): got.append(lax.ppermute(send, axis, pairs))  34.2 us
    ppermute x11, starting transfers between devices, digit_sum(): lax.ppermute(value, axis, [(i, i ^ k * step) for i in range(count)])  22 us
    unnamed x67, local copies, waits for them, and re-layouts  14.9 us
    ppermute x2, waiting for transfers between devices, group_scan(): rgot = lax.ppermute(bwd, axis, down)  13.1 us
    ppermute x6, starting transfers between devices, row_exchange(): got.append(lax.ppermute(send, axis, pairs))  12 us
    ppermute x2, starting transfers between devices, group_scan(): got = lax.ppermute(fwd, axis, up)  11.1 us
    ppermute x1, starting transfers between devices, group_scan(): got = lax.ppermute(sent, axis, up + down)  9.56 us
    ppermute x11, waiting for transfers between devices, digit_sum(): lax.ppermute(value, axis, [(i, i ^ k * step) for i in range(count)])  7.57 us
  transfers between devices with their start and end apart: 22, of which 14 were waited for; matrix products, arithmetic and copies ran while one was open for 19% of the time, Pallas kernels for 0%

profile of v9, /device:TPU:6, one launch (start us, length us, event | category | flops | bytes accessed | tf_op | source)
XLA Modules:
  0.0 197.9 jit_solution(12982701068807935383)
XLA Ops:
  0.7 0.9 reduce-window_clone.1
  6.4 0.9 reduce-window.24
  7.8 1.9 copy.74
  9.7 1.6 copy.97
  11.2 1.6 copy.98
  12.8 1.9 copy.76
  14.8 3.0 %fusion.20 = f32[16,128,128]{2,1,0:T(8,128)S(1)} fusion(bf16[384,16,128]{0,2,1:T(8,128)(2,1)S(1)} %bitcast.207, bf16[384,16,128]{2,1,0:T(8,128)(2,1)} %bitcast.223, f32[384,16]{0,1:T(8,128)S(1)} %get-tuple-element.43), kind=kOutput, calls=%fused_computation.29 | convolution fusion | flops 605552640 | bytes 4218880 | tf_op jit(solution)/shard_map/the,thf->hef/dot_general | solution.py:183
  17.8 1.4 fusion.17
  19.5 1.3 copy-done.7
  20.8 1.2 dynamic-slice_bitcast_fusion
  22.0 1.6 collective-permute-start
  23.6 2.9 %collective-permute-start.1 = (f32[4,264,128]{2,1,0:T(8,128)}, f32[4,264,128]{2,1,0:T(8,128)}, u32[]{:S(2)}, u32[]{:S(2)}) collective-permute-start(f32[4,264,128]{2,1,0:T(8,128)} %get-tuple-element.72), channel_id=1, source_target_pairs={{0,16},{8,24},{16,0},{24,8},{32,48},{40,56},{48,32},{56,40},{64,80... | collective-permute-start | bytes 1622024 | tf_op jit(solution)/shard_map/ppermute | solution.py:64
  26.5 1.3 collective-permute-start.2
  27.8 9.8 %collective-permute-done = f32[4,264,128]{2,1,0:T(8,128)} collective-permute-done((f32[4,264,128]{2,1,0:T(8,128)}, f32[4,264,128]{2,1,0:T(8,128)}, u32[]{:S(2)}, u32[]{:S(2)}) %collective-permute-start) | collective-permute-done | bytes 540704 | tf_op jit(solution)/shard_map/ppermute | solution.py:64
  37.6 12.8 %collective-permute-done.1 = f32[4,264,128]{2,1,0:T(8,128)} collective-permute-done((f32[4,264,128]{2,1,0:T(8,128)}, f32[4,264,128]{2,1,0:T(8,128)}, u32[]{:S(2)}, u32[]{:S(2)}) %collective-permute-start.1) | collective-permute-done | bytes 540704 | tf_op jit(solution)/shard_map/ppermute | solution.py:64
  50.4 1.8 fusion.48
  52.7 0.8 fusion.85
  53.5 1.0 fusion.66
  54.6 0.9 pad_maximum_fusion.3
  55.5 4.5 %collective-permute-start.3 = (f32[4,136,128]{2,1,0:T(8,128)}, f32[4,136,128]{2,1,0:T(8,128)}, u32[]{:S(2)}, u32[]{:S(2)}) collective-permute-start(f32[4,136,128]{2,1,0:T(8,128)} %get-tuple-element.90), channel_id=1, source_target_pairs={{0,32},{8,40},{16,48},{24,56},{32,64},{40,72},{48,80},{56,88},{64,... | collective-permute-start | bytes 835592 | tf_op jit(solution)/shard_map/ppermute | solution.py:42
  60.1 1.3 collective-permute-start.5
  61.4 3.3 %collective-permute-done.3 = f32[4,136,128]{2,1,0:T(8,128)} collective-permute-done((f32[4,136,128]{2,1,0:T(8,128)}, f32[4,136,128]{2,1,0:T(8,128)}, u32[]{:S(2)}, u32[]{:S(2)}) %collective-permute-start.3) | collective-permute-done | bytes 278560 | tf_op jit(solution)/shard_map/ppermute | solution.py:42
  64.7 4.8 %collective-permute-done.5 = f32[4,136,128]{2,1,0:T(8,128)} collective-permute-done((f32[4,136,128]{2,1,0:T(8,128)}, f32[4,136,128]{2,1,0:T(8,128)}, u32[]{:S(2)}, u32[]{:S(2)}) %collective-permute-start.5) | collective-permute-done | bytes 278560 | tf_op jit(solution)/shard_map/ppermute | solution.py:43
  69.5 1.2 multiply_add_fusion.11
  70.8 0.8 slice_multiply_fusion.4
  71.6 1.3 collective-permute-start.6
  72.9 6.5 %collective-permute-start.4 = (f32[4,136,128]{2,1,0:T(8,128)S(1)}, f32[4,136,128]{2,1,0:T(8,128)S(1)}, u32[]{:S(2)}, u32[]{:S(2)}) collective-permute-start(f32[4,136,128]{2,1,0:T(8,128)S(1)} %pad_maximum_fusion.5), channel_id=1, source_target_pairs={{0,64},{8,72},{16,80},{24,88},{32,96},{40,104},{48,112},{56,120},{... | collective-permute-start | bytes 835592 | tf_op jit(solution)/shard_map/ppermute | solution.py:42
  79.7 8.3 %collective-permute-done.6 = f32[4,136,128]{2,1,0:T(8,128)S(1)} collective-permute-done((f32[4,136,128]{2,1,0:T(8,128)S(1)}, f32[4,136,128]{2,1,0:T(8,128)S(1)}, u32[]{:S(2)}, u32[]{:S(2)}) %collective-permute-start.6) | collective-permute-done | bytes 278560 | tf_op jit(solution)/shard_map/ppermute | solution.py:43
  89.6 9.6 %collective-permute-start.7 = (f32[4,136,128]{2,1,0:T(8,128)}, f32[4,136,128]{2,1,0:T(8,128)}, u32[]{:S(2)}, u32[]{:S(2)}) collective-permute-start(f32[4,136,128]{2,1,0:T(8,128)} %maximum_select_fusion), channel_id=1, source_target_pairs={{0,128},{8,136},{16,144},{24,152},{32,160},{40,168},{48,176},{56,1... | collective-permute-start | bytes 835592 | tf_op jit(solution)/shard_map/ppermute | solution.py:38
  99.1 0.8 fusion.44
  99.9 0.9 slice_reduce_fusion.2
  100.8 0.8 slice_reduce_fusion.4
  101.6 5.9 %collective-permute-done.7 = f32[4,136,128]{2,1,0:T(8,128)} collective-permute-done((f32[4,136,128]{2,1,0:T(8,128)}, f32[4,136,128]{2,1,0:T(8,128)}, u32[]{:S(2)}, u32[]{:S(2)}) %collective-permute-start.7) | collective-permute-done | bytes 278560 | tf_op jit(solution)/shard_map/ppermute | solution.py:38
  107.6 0.8 slice_multiply_fusion
  108.6 1.3 multiply_add_fusion.7
  110.0 1.5 multiply_add_fusion.2
  112.1 4.4 %collective-permute-start.10 = (f32[4,256,128]{2,1,0:T(8,128)S(1)}, f32[4,256,128]{2,1,0:T(8,128)S(1)}, u32[]{:S(2)}, u32[]{:S(2)}) collective-permute-start(f32[4,256,128]{2,1,0:T(8,128)S(1)} %get-tuple-element.74), channel_id=1, source_target_pairs={{0,24},{8,0},{16,8},{24,16},{32,56},{40,32},{48,40},{56,48},{64,88... | collective-permute-start | bytes 1572872 | tf_op jit(solution)/shard_map/ppermute | solution.py:64
  116.5 1.7 collective-permute-start.9
  118.2 4.0 %multiply_convert_fusion.1 = bf16[16,384,384]{2,1,0:T(8,128)(2,1)S(1)} fusion(f32[16,384]{1,0:T(8,128)S(1)} %bitcast.239, pred[384,384]{1,0:T(8,128)(4,1)S(1)} %copy-done.20, bf16[384,16,128]{2,1,0:T(8,128)(2,1)S(1)} %bitcast.225, bf16[384,16,128]{2,1,0:T(8,128)(2,1)S(1)} %bitcast.220), kind=kOutput, calls=%fused_computation.1 | convolution fusion | flops 615776256 | bytes 8036352 | tf_op jit(solution)/shard_map/shf,thf->hst/dot_general | solution.py:211
  122.2 3.0 %fusion.7 = (f32[384,16]{0,1:T(8,128)S(1)}, f32[16,128,384]{2,1,0:T(8,128)}) fusion(bf16[384,16,128]{0,2,1:T(8,128)(2,1)S(1)} %bitcast.208, bf16[384,16,128]{0,2,1:T(8,128)(2,1)S(1)} %bitcast.214, bf16[16,384,384]{2,1,0:T(8,128)(2,1)S(1)} %multiply_convert_fusion.1), kind=kOutput, calls=%fused_computation.13 | convolution fusion | flops 606332928 | bytes 11034624 | tf_op jit(solution)/shard_map/hst,she->the/dot_general | solution.py:225
  125.2 3.3 %fusion.9 = (f32[384,16]{0,1:T(8,128)S(1)}, f32[16,128,384]{2,1,0:T(8,128)}) fusion(bf16[384,16,128]{0,2,1:T(8,128)(2,1)S(1)} %bitcast.215, bf16[384,16,128]{0,2,1:T(8,128)(2,1)S(1)} %bitcast.209, bf16[16,384,384]{2,1,0:T(8,128)(2,1)S(1)} %multiply_convert_fusion.1), kind=kOutput, calls=%fused_computation.15 | convolution fusion | flops 606332928 | bytes 11034624 | tf_op jit(solution)/shard_map/hst,the->she/dot_general | solution.py:222
  128.7 8.2 %collective-permute-done.10 = f32[4,256,128]{2,1,0:T(8,128)S(1)} collective-permute-done((f32[4,256,128]{2,1,0:T(8,128)S(1)}, f32[4,256,128]{2,1,0:T(8,128)S(1)}, u32[]{:S(2)}, u32[]{:S(2)}) %collective-permute-start.10) | collective-permute-done | bytes 524320 | tf_op jit(solution)/shard_map/ppermute | solution.py:64
  136.9 3.4 %collective-permute-done.8 = f32[4,256,128]{2,1,0:T(8,128)S(1)} collective-permute-done((f32[4,256,128]{2,1,0:T(8,128)S(1)}, f32[4,256,128]{2,1,0:T(8,128)S(1)}, u32[]{:S(2)}, u32[]{:S(2)}) %collective-permute-start.8) | collective-permute-done | bytes 524320 | tf_op jit(solution)/shard_map/ppermute | solution.py:64
  140.8 1.5 fusion.31
  142.4 1.5 fusion.32
  144.0 1.7 collective-permute-start.12
  145.7 3.0 %collective-permute-start.13 = (f32[16]{0:T(128)S(1)}, f32[16]{0:T(128)S(1)}, u32[]{:S(2)}, u32[]{:S(2)}) collective-permute-start(f32[16]{0:T(128)S(1)} %add_subtract_fusion), channel_id=1, source_target_pairs={{0,24},{8,16},{16,8},{24,0},{32,56},{40,48},{48,40},{56,32},{64,88... | collective-permute-start | bytes 200 | tf_op jit(solution)/shard_map/ppermute | solution.py:119
  148.7 2.8 %fusion.41 = f32[16,128,384]{2,1,0:T(8,128)} fusion(bf16[384,16,128]{0,2,1:T(8,128)(2,1)S(1)} %bitcast.211, f32[16,256,128]{2,1,0:T(8,128)S(1)} %bitcast.229), kind=kOutput, calls=%fused_computation.53 | convolution fusion | flops 603979776 | bytes 5767168 | tf_op jit(solution)/shard_map/the,hef->thf/dot_general | solution.py:219
  151.4 7.0 %fusion.12 = bf16[384,16,128]{0,2,1:T(8,128)(2,1)} fusion(f32[16,128,384]{2,1,0:T(8,128)} %fusion.41, f32[16,384]{1,0:T(8,128)S(1)} %bitcast.240, pred[384,384]{1,0:T(8,128)(4,1)S(1)} %copy-done.20, bf16[384,16,128]{0,2,1:T(8,128)(2,1)S(1)} %bitcast.217, bf16[384,16,128]{0,2,1:T(8,128)(2,1)S(1)} %bitcast.212, f32[384,16]{0,1:T(8,128)S(1)} %get-tuple-element.43, ...), kind=kOutput, calls=%fused_computation.19 | convolution fusion | flops 1222115328 | bytes 9633792 | tf_op jit(solution)/shard_map/hst,shf->thf/dot_general | solution.py:216
  158.5 5.5 %fusion.14 = bf16[384,16,128]{0,2,1:T(8,128)(2,1)} fusion(f32[16,128,384]{2,1,0:T(8,128)} %get-tuple-element.101, f32[384,16]{0,1:T(8,128)S(1)} %get-tuple-element.43, bf16[384,16,128]{2,1,0:T(8,128)(2,1)} %bitcast.224, f32[16,256,128]{2,1,0:T(8,128)} %bitcast.230), kind=kOutput, calls=%fused_computation.22 | convolution fusion | flops 606339072 | bytes 7364608 | tf_op jit(solution)/shard_map/thf,hef->the/dot_general | solution.py:244
  164.0 2.6 %fusion.16 = bf16[384,16,128]{0,2,1:T(8,128)(2,1)} fusion(f32[16,128,384]{2,1,0:T(8,128)S(1)} %copy-done.6, f32[384,16]{0,1:T(8,128)S(1)} %get-tuple-element.88, bf16[384,16,128]{2,1,0:T(8,128)(2,1)S(1)} %bitcast.222, f32[16,256,128]{2,1,0:T(8,128)S(1)} %bitcast.231), kind=kOutput, calls=%fused_computation.25 | convolution fusion | flops 606339072 | bytes 7364608 | tf_op jit(solution)/shard_map/shf,hef->she/dot_general | solution.py:241
  166.6 2.7 %copy.91 = bf16[1,384,2048]{2,1,0:T(8,128)(2,1)} copy(bf16[1,384,2048]{1,2,0:T(8,128)(2,1)} %bitcast.238) | data formatting | bytes 3145728
  169.3 6.1 %collective-permute-start.14 = (f32[16]{0:T(128)S(1)}, f32[16]{0:T(128)S(1)}, u32[]{:S(2)}, u32[]{:S(2)}) collective-permute-start(f32[16]{0:T(128)S(1)} %fusion.82), channel_id=1, source_target_pairs={{0,32},{8,40},{16,48},{24,56},{32,0},{40,8},{48,16},{56,24},{64,96... | collective-permute-start | bytes 200 | tf_op jit(solution)/shard_map/ppermute | solution.py:119
  175.5 2.5 %collective-permute-start.16 = (f32[16]{0:T(128)S(1)}, f32[16]{0:T(128)S(1)}, u32[]{:S(2)}, u32[]{:S(2)}) collective-permute-start(f32[16]{0:T(128)S(1)} %fusion.82), channel_id=1, source_target_pairs={{0,96},{8,104},{16,112},{24,120},{32,64},{40,72},{48,80},{56,88},{... | collective-permute-start | bytes 200 | tf_op jit(solution)/shard_map/ppermute | solution.py:119
  178.0 2.0 collective-permute-done.15
  179.9 0.9 collective-permute-done.16
  180.8 5.5 %collective-permute-start.17 = (f32[16]{0:T(128)S(1)}, f32[16]{0:T(128)S(1)}, u32[]{:S(2)}, u32[]{:S(2)}) collective-permute-start(f32[16]{0:T(128)S(1)} %fusion.79), channel_id=1, source_target_pairs={{0,128},{8,136},{16,144},{24,152},{32,160},{40,168},{48,176},{56,1... | collective-permute-start | bytes 200 | tf_op jit(solution)/shard_map/ppermute | solution.py:119
  186.3 1.6 copy.90
  188.4 0.9 collective-permute-start.19
  189.3 1.0 collective-permute-start.20
  190.3 1.7 collective-permute-done.19
  192.3 1.2 collective-permute-start.21
  193.5 1.6 copy.89
  195.1 2.3 %collective-permute-done.21 = f32[16]{0:T(128)S(1)} collective-permute-done((f32[16]{0:T(128)S(1)}, f32[16]{0:T(128)S(1)}, u32[]{:S(2)}, u32[]{:S(2)}) %collective-permute-start.21) | collective-permute-done | bytes 96 | tf_op jit(solution)/shard_map/ppermute | solution.py:119
  (129 shorter events, 10.0 us)
Async XLA Ops:
  0.6 9.0 %copy-start.15 = (bf16[1,384,2048]{2,1,0:T(8,128)(2,1)S(1)}, bf16[1,384,2048]{2,1,0:T(8,128)(2,1)}, u32[]{:S(2)}) copy-start(bf16[1,384,2048]{2,1,0:T(8,128)(2,1)} %param.9) | copy-start | bytes 4718596
  9.6 1.6 copy-start.16
  14.8 3.0 %copy-start = (bf16[48,8,16,128]{3,2,1,0:T(8,128)(2,1)S(1)}, bf16[48,8,16,128]{3,2,1,0:T(8,128)(2,1)}, u32[]{:S(2)}) copy-start(bf16[48,8,16,128]{3,2,1,0:T(8,128)(2,1)} %copy.98) | copy-start | bytes 4718596
  19.5 1.4 copy-start.7
  22.0 15.6 %collective-permute-start = (f32[4,264,128]{2,1,0:T(8,128)}, f32[4,264,128]{2,1,0:T(8,128)}, u32[]{:S(2)}, u32[]{:S(2)}) collective-permute-start(f32[4,264,128]{2,1,0:T(8,128)} %get-tuple-element.73), channel_id=1, source_target_pairs={{0,8},{8,16},{16,24},{24,0},{32,40},{40,48},{48,56},{56,32},{64,72... | collective-permute-start | bytes 1622024 | tf_op jit(solution)/shard_map/ppermute | solution.py:64
  23.6 26.8 %collective-permute-start.1 = (f32[4,264,128]{2,1,0:T(8,128)}, f32[4,264,128]{2,1,0:T(8,128)}, u32[]{:S(2)}, u32[]{:S(2)}) collective-permute-start(f32[4,264,128]{2,1,0:T(8,128)} %get-tuple-element.72), channel_id=1, source_target_pairs={{0,16},{8,24},{16,0},{24,8},{32,48},{40,56},{48,32},{56,40},{64,80... | collective-permute-start | bytes 1622024 | tf_op jit(solution)/shard_map/ppermute | solution.py:64
  26.5 23.9 %collective-permute-start.2 = (f32[4,264,128]{2,1,0:T(8,128)}, f32[4,264,128]{2,1,0:T(8,128)}, u32[]{:S(2)}, u32[]{:S(2)}) collective-permute-start(f32[4,264,128]{2,1,0:T(8,128)} %get-tuple-element.71), channel_id=1, source_target_pairs={{0,24},{8,0},{16,8},{24,16},{32,56},{40,32},{48,40},{56,48},{64,88... | collective-permute-start | bytes 1622024 | tf_op jit(solution)/shard_map/ppermute | solution.py:64
  52.2 3.3 %copy-start.10 = (f32[1,4,264,128]{3,2,1,0:T(8,128)}, f32[1,4,264,128]{3,2,1,0:T(8,128)S(1)}, u32[]{:S(2)}) copy-start(f32[1,4,264,128]{3,2,1,0:T(8,128)S(1)} %get-tuple-element.61) | copy-start | bytes 1622020
  52.2 3.3 %copy-start.11 = (f32[1,4,264,128]{3,2,1,0:T(8,128)}, f32[1,4,264,128]{3,2,1,0:T(8,128)S(1)}, u32[]{:S(2)}) copy-start(f32[1,4,264,128]{3,2,1,0:T(8,128)S(1)} %get-tuple-element.62) | copy-start | bytes 1622020
  52.2 3.3 %copy-start.12 = (f32[1,4,264,128]{3,2,1,0:T(8,128)}, f32[1,4,264,128]{3,2,1,0:T(8,128)S(1)}, u32[]{:S(2)}) copy-start(f32[1,4,264,128]{3,2,1,0:T(8,128)S(1)} %get-tuple-element.63) | copy-start | bytes 1622020
  52.2 3.3 %copy-start.13 = (f32[1,4,264,128]{3,2,1,0:T(8,128)}, f32[1,4,264,128]{3,2,1,0:T(8,128)S(1)}, u32[]{:S(2)}) copy-start(f32[1,4,264,128]{3,2,1,0:T(8,128)S(1)} %get-tuple-element.64) | copy-start | bytes 1622020
  52.3 2.2 %copy-start.21 = (f32[4]{0:T(128)}, f32[4]{0:T(128)S(1)}, u32[]{:S(2)}) copy-start(f32[4]{0:T(128)S(1)} %slice_reduce_fusion.10) | copy-start | bytes 52
  52.4 2.1 %copy-start.23 = (f32[4]{0:T(128)}, f32[4]{0:T(128)S(1)}, u32[]{:S(2)}) copy-start(f32[4]{0:T(128)S(1)} %slice_reduce_fusion.11) | copy-start | bytes 52
  52.6 2.0 copy-start.24
  52.7 1.9 copy-start.25
  53.5 2.0 %copy-start.26 = (f32[4]{0:T(128)}, f32[4]{0:T(128)S(1)}, u32[]{:S(2)}) copy-start(f32[4]{0:T(128)S(1)} %get-tuple-element.91) | copy-start | bytes 52
  53.5 2.0 %copy-start.27 = (f32[4]{0:T(128)}, f32[4]{0:T(128)S(1)}, u32[]{:S(2)}) copy-start(f32[4]{0:T(128)S(1)} %get-tuple-element.94) | copy-start | bytes 52
  53.5 2.0 %copy-start.28 = (f32[4]{0:T(128)}, f32[4]{0:T(128)S(1)}, u32[]{:S(2)}) copy-start(f32[4]{0:T(128)S(1)} %get-tuple-element.95) | copy-start | bytes 52
  54.5 1.0 copy-start.14
  55.5 9.2 %collective-permute-start.3 = (f32[4,136,128]{2,1,0:T(8,128)}, f32[4,136,128]{2,1,0:T(8,128)}, u32[]{:S(2)}, u32[]{:S(2)}) collective-permute-start(f32[4,136,128]{2,1,0:T(8,128)} %get-tuple-element.90), channel_id=1, source_target_pairs={{0,32},{8,40},{16,48},{24,56},{32,64},{40,72},{48,80},{56,88},{64,... | collective-permute-start | bytes 835592 | tf_op jit(solution)/shard_map/ppermute | solution.py:42
  60.1 9.4 %collective-permute-start.5 = (f32[4,136,128]{2,1,0:T(8,128)}, f32[4,136,128]{2,1,0:T(8,128)}, u32[]{:S(2)}, u32[]{:S(2)}) collective-permute-start(f32[4,136,128]{2,1,0:T(8,128)} %get-tuple-element.89), channel_id=1, source_target_pairs={{32,0},{40,8},{48,16},{56,24},{64,32},{72,40},{80,48},{88,56},{96,... | collective-permute-start | bytes 835592 | tf_op jit(solution)/shard_map/ppermute | solution.py:43
  71.6 16.4 %collective-permute-start.6 = (f32[4,136,128]{2,1,0:T(8,128)S(1)}, f32[4,136,128]{2,1,0:T(8,128)S(1)}, u32[]{:S(2)}, u32[]{:S(2)}) collective-permute-start(f32[4,136,128]{2,1,0:T(8,128)S(1)} %pad_maximum_fusion.6), channel_id=1, source_target_pairs={{64,0},{72,8},{80,16},{88,24},{96,32},{104,40},{112,48},{120,56},{... | collective-permute-start | bytes 835592 | tf_op jit(solution)/shard_map/ppermute | solution.py:43
  72.9 15.2 %collective-permute-start.4 = (f32[4,136,128]{2,1,0:T(8,128)S(1)}, f32[4,136,128]{2,1,0:T(8,128)S(1)}, u32[]{:S(2)}, u32[]{:S(2)}) collective-permute-start(f32[4,136,128]{2,1,0:T(8,128)S(1)} %pad_maximum_fusion.5), channel_id=1, source_target_pairs={{0,64},{8,72},{16,80},{24,88},{32,96},{40,104},{48,112},{56,120},{... | collective-permute-start | bytes 835592 | tf_op jit(solution)/shard_map/ppermute | solution.py:42
  88.1 0.7 copy-start.17
  89.6 18.0 %collective-permute-start.7 = (f32[4,136,128]{2,1,0:T(8,128)}, f32[4,136,128]{2,1,0:T(8,128)}, u32[]{:S(2)}, u32[]{:S(2)}) collective-permute-start(f32[4,136,128]{2,1,0:T(8,128)} %maximum_select_fusion), channel_id=1, source_target_pairs={{0,128},{8,136},{16,144},{24,152},{32,160},{40,168},{48,176},{56,1... | collective-permute-start | bytes 835592 | tf_op jit(solution)/shard_map/ppermute | solution.py:38
  99.9 10.1 %copy-start.22 = (f32[4]{0:T(128)S(1)}, f32[4]{0:T(128)}, u32[]{:S(2)}) copy-start(f32[4]{0:T(128)} %copy-done.21) | copy-start | bytes 52
  99.9 10.1 %copy-start.18 = (f32[4,128,128]{2,1,0:T(8,128)S(1)}, f32[4,128,128]{2,1,0:T(8,128)}, u32[]{:S(2)}) copy-start(f32[4,128,128]{2,1,0:T(8,128)} %get-tuple-element.53) | copy-start | bytes 786436
  99.9 10.1 %copy-start.19 = (f32[4,128,128]{2,1,0:T(8,128)S(1)}, f32[4,128,128]{2,1,0:T(8,128)}, u32[]{:S(2)}) copy-start(f32[4,128,128]{2,1,0:T(8,128)} %get-tuple-element.70) | copy-start | bytes 786436
  111.7 6.5 %copy-start.20 = (pred[384,384]{1,0:T(8,128)(4,1)S(1)}, pred[384,384]{1,0:T(8,128)(4,1)}, u32[]{:S(2)}) copy-start(pred[384,384]{1,0:T(8,128)(4,1)} %fusion.44) | copy-start | bytes 442372
  111.9 6.3 %copy-start.1 = (bf16[48,8,16,128]{3,2,1,0:T(8,128)(2,1)S(1)}, bf16[48,8,16,128]{3,2,1,0:T(8,128)(2,1)}, u32[]{:S(2)}) copy-start(bf16[48,8,16,128]{3,2,1,0:T(8,128)(2,1)} %copy.98) | copy-start | bytes 4718596
  111.9 6.3 %copy-start.3 = (bf16[48,8,16,128]{3,2,1,0:T(8,128)(2,1)S(1)}, bf16[48,8,16,128]{3,2,1,0:T(8,128)(2,1)}, u32[]{:S(2)}) copy-start(bf16[48,8,16,128]{3,2,1,0:T(8,128)(2,1)} %copy.97) | copy-start | bytes 4718596
  112.1 24.8 %collective-permute-start.10 = (f32[4,256,128]{2,1,0:T(8,128)S(1)}, f32[4,256,128]{2,1,0:T(8,128)S(1)}, u32[]{:S(2)}, u32[]{:S(2)}) collective-permute-start(f32[4,256,128]{2,1,0:T(8,128)S(1)} %get-tuple-element.74), channel_id=1, source_target_pairs={{0,24},{8,0},{16,8},{24,16},{32,56},{40,32},{48,40},{56,48},{64,88... | collective-permute-start | bytes 1572872 | tf_op jit(solution)/shard_map/ppermute | solution.py:64
  116.5 23.8 %collective-permute-start.8 = (f32[4,256,128]{2,1,0:T(8,128)S(1)}, f32[4,256,128]{2,1,0:T(8,128)S(1)}, u32[]{:S(2)}, u32[]{:S(2)}) collective-permute-start(f32[4,256,128]{2,1,0:T(8,128)S(1)} %get-tuple-element.76), channel_id=1, source_target_pairs={{0,8},{8,16},{16,24},{24,0},{32,40},{40,48},{48,56},{56,32},{64,72... | collective-permute-start | bytes 1572872 | tf_op jit(solution)/shard_map/ppermute | solution.py:64
  116.5 23.8 %collective-permute-start.9 = (f32[4,256,128]{2,1,0:T(8,128)S(1)}, f32[4,256,128]{2,1,0:T(8,128)S(1)}, u32[]{:S(2)}, u32[]{:S(2)}) collective-permute-start(f32[4,256,128]{2,1,0:T(8,128)S(1)} %get-tuple-element.75), channel_id=1, source_target_pairs={{0,16},{8,24},{16,0},{24,8},{32,48},{40,56},{48,32},{56,40},{64,80... | collective-permute-start | bytes 1572872 | tf_op jit(solution)/shard_map/ppermute | solution.py:64
  140.8 7.8 %copy-start.4 = (f32[4,4,256,128]{3,2,1,0:T(8,128)}, f32[4,4,256,128]{3,2,1,0:T(8,128)S(1)}, u32[]{:S(2)}) copy-start(f32[4,4,256,128]{3,2,1,0:T(8,128)S(1)} %pad_maximum_fusion.2) | copy-start | bytes 6291460
  143.9 25.4 %collective-permute-start.11 = (f32[16]{0:T(128)S(1)}, f32[16]{0:T(128)S(1)}, u32[]{:S(2)}, u32[]{:S(2)}) collective-permute-start(f32[16]{0:T(128)S(1)} %add_subtract_fusion), channel_id=1, source_target_pairs={{0,8},{8,0},{16,24},{24,16},{32,40},{40,32},{48,56},{56,48},{64,72... | collective-permute-start | bytes 200 | tf_op jit(solution)/shard_map/ppermute | solution.py:119
  144.0 25.3 %collective-permute-start.12 = (f32[16]{0:T(128)S(1)}, f32[16]{0:T(128)S(1)}, u32[]{:S(2)}, u32[]{:S(2)}) collective-permute-start(f32[16]{0:T(128)S(1)} %add_subtract_fusion), channel_id=1, source_target_pairs={{0,16},{8,24},{16,0},{24,8},{32,48},{40,56},{48,32},{56,40},{64,80... | collective-permute-start | bytes 200 | tf_op jit(solution)/shard_map/ppermute | solution.py:119
  145.7 23.6 %collective-permute-start.13 = (f32[16]{0:T(128)S(1)}, f32[16]{0:T(128)S(1)}, u32[]{:S(2)}, u32[]{:S(2)}) collective-permute-start(f32[16]{0:T(128)S(1)} %add_subtract_fusion), channel_id=1, source_target_pairs={{0,24},{8,16},{16,8},{24,0},{32,56},{40,48},{48,40},{56,32},{64,88... | collective-permute-start | bytes 200 | tf_op jit(solution)/shard_map/ppermute | solution.py:119
  158.5 5.5 %copy-start.2 = (bf16[48,8,16,128]{3,2,1,0:T(8,128)(2,1)S(1)}, bf16[48,8,16,128]{3,2,1,0:T(8,128)(2,1)}, u32[]{:S(2)}) copy-start(bf16[48,8,16,128]{3,2,1,0:T(8,128)(2,1)} %copy.98) | copy-start | bytes 4718596
  158.5 5.5 %copy-start.5 = (f32[4,4,256,128]{3,2,1,0:T(8,128)S(1)}, f32[4,4,256,128]{3,2,1,0:T(8,128)}, u32[]{:S(2)}) copy-start(f32[4,4,256,128]{3,2,1,0:T(8,128)} %copy-done.4) | copy-start | bytes 6291460
  158.5 5.5 %copy-start.6 = (f32[16,128,384]{2,1,0:T(8,128)S(1)}, f32[16,128,384]{2,1,0:T(8,128)}, u32[]{:S(2)}) copy-start(f32[16,128,384]{2,1,0:T(8,128)} %get-tuple-element.103) | copy-start | bytes 9437188
  166.6 19.7 %copy-start.9 = (bf16[384,16,128]{0,2,1:T(8,128)(2,1)S(1)}, bf16[384,16,128]{0,2,1:T(8,128)(2,1)}, u32[]{:S(2)}) copy-start(bf16[384,16,128]{0,2,1:T(8,128)(2,1)} %fusion.14) | copy-start | bytes 4718596
  169.3 24.2 %copy-start.8 = (bf16[384,16,128]{0,2,1:T(8,128)(2,1)S(1)}, bf16[384,16,128]{0,2,1:T(8,128)(2,1)}, u32[]{:S(2)}) copy-start(bf16[384,16,128]{0,2,1:T(8,128)(2,1)} %fusion.16) | copy-start | bytes 4718596
  169.3 8.6 %collective-permute-start.14 = (f32[16]{0:T(128)S(1)}, f32[16]{0:T(128)S(1)}, u32[]{:S(2)}, u32[]{:S(2)}) collective-permute-start(f32[16]{0:T(128)S(1)} %fusion.82), channel_id=1, source_target_pairs={{0,32},{8,40},{16,48},{24,56},{32,0},{40,8},{48,16},{56,24},{64,96... | collective-permute-start | bytes 200 | tf_op jit(solution)/shard_map/ppermute | solution.py:119
  175.5 4.4 %collective-permute-start.15 = (f32[16]{0:T(128)S(1)}, f32[16]{0:T(128)S(1)}, u32[]{:S(2)}, u32[]{:S(2)}) collective-permute-start(f32[16]{0:T(128)S(1)} %fusion.82), channel_id=1, source_target_pairs={{0,64},{8,72},{16,80},{24,88},{32,96},{40,104},{48,112},{56,120},{... | collective-permute-start | bytes 200 | tf_op jit(solution)/shard_map/ppermute | solution.py:119
  175.5 5.3 %collective-permute-start.16 = (f32[16]{0:T(128)S(1)}, f32[16]{0:T(128)S(1)}, u32[]{:S(2)}, u32[]{:S(2)}) collective-permute-start(f32[16]{0:T(128)S(1)} %fusion.82), channel_id=1, source_target_pairs={{0,96},{8,104},{16,112},{24,120},{32,64},{40,72},{48,80},{56,88},{... | collective-permute-start | bytes 200 | tf_op jit(solution)/shard_map/ppermute | solution.py:119
  180.8 7.5 %collective-permute-start.17 = (f32[16]{0:T(128)S(1)}, f32[16]{0:T(128)S(1)}, u32[]{:S(2)}, u32[]{:S(2)}) collective-permute-start(f32[16]{0:T(128)S(1)} %fusion.79), channel_id=1, source_target_pairs={{0,128},{8,136},{16,144},{24,152},{32,160},{40,168},{48,176},{56,1... | collective-permute-start | bytes 200 | tf_op jit(solution)/shard_map/ppermute | solution.py:119
  188.0 9.4 %copy-start.29 = (f32[16]{0:T(128)S(1)}, f32[16]{0:T(128)}, u32[]{:S(2)}) copy-start(f32[16]{0:T(128)} %param.13) | copy-start | bytes 196
  188.4 1.9 collective-permute-start.18
  188.4 3.6 %collective-permute-start.19 = (f32[16]{0:T(128)S(1)}, f32[16]{0:T(128)S(1)}, u32[]{:S(2)}, u32[]{:S(2)}) collective-permute-start(f32[16]{0:T(128)S(1)} %fusion.76), channel_id=1, source_target_pairs={{0,2},{1,3},{2,0},{3,1},{4,6},{5,7},{6,4},{7,5},{8,10},{9,11},{10,... | collective-permute-start | bytes 200 | tf_op jit(solution)/shard_map/ppermute | solution.py:119
  189.3 3.0 %collective-permute-start.20 = (f32[16]{0:T(128)S(1)}, f32[16]{0:T(128)S(1)}, u32[]{:S(2)}, u32[]{:S(2)}) collective-permute-start(f32[16]{0:T(128)S(1)} %fusion.76), channel_id=1, source_target_pairs={{0,3},{1,2},{2,1},{3,0},{4,7},{5,6},{6,5},{7,4},{8,11},{9,10},{10,... | collective-permute-start | bytes 200 | tf_op jit(solution)/shard_map/ppermute | solution.py:119
  192.3 5.1 %collective-permute-start.21 = (f32[16]{0:T(128)S(1)}, f32[16]{0:T(128)S(1)}, u32[]{:S(2)}, u32[]{:S(2)}) collective-permute-start(f32[16]{0:T(128)S(1)} %fusion.75), channel_id=1, source_target_pairs={{0,4},{1,5},{2,6},{3,7},{4,0},{5,1},{6,2},{7,3},{8,12},{9,13},{10,... | collective-permute-start | bytes 200 | tf_op jit(solution)/shard_map/ppermute | solution.py:119

commit v10 on v9

--- a/solution.py
+++ b/solution.py
@@ -213,17 +213,17 @@
     )
     attn_prob = (weight * scores).astype(jnp.bfloat16)
     grad_prob = (weight * grad_scores).astype(jnp.bfloat16)
-    value_full = jnp.einsum(
-        "hst,shf->thf", attn_prob, gradient_block, preferred_element_type=jnp.float32
-    )
-    value_full = value_full + carry_out[:, :, None] * jnp.einsum(
-        "the,hef->thf", key_f, backward_input, precision=state_mode
-    )
     query_local = jnp.einsum(
         "hst,the->she", grad_prob, key_block, preferred_element_type=jnp.float32
     )
     key_local = jnp.einsum(
         "hst,she->the", grad_prob, query_block, preferred_element_type=jnp.float32
+    )
+    value_local = jnp.einsum(
+        "hst,shf->thf", attn_prob, gradient_block, preferred_element_type=jnp.float32
+    )
+    query_local, key_local, value_local = lax.optimization_barrier(
+        (query_local, key_local, value_local)
     )
     local_step = jnp.sum(key_f * key_local, axis=2) - jnp.sum(query_f * query_local, axis=2)
     rate_local = jnp.sum(position[:, None] * local_step, axis=0)
@@ -243,6 +243,9 @@
     )
     key_full = key_local + carry_out[:, :, None] * jnp.einsum(
         "thf,hef->the", value_f, backward_input, precision=state_mode
+    )
+    value_full = value_local + carry_out[:, :, None] * jnp.einsum(
+        "the,hef->thf", key_f, backward_input, precision=state_mode
     )
     rate_total = all_sum(rate_part, ("seq", "dp"))
     token_total = row_count * lax.axis_size("seq") * lax.axis_size("dp")

time: 199 us -> 213 us (1.070)
  waiting for transfers between devices: 64.1 us -> 83.8 us
  starting transfers between devices: 57.1 us -> 51.8 us
  matrix products: 35.7 us -> 31.3 us
  local copies, waits for them, and re-layouts: 20.1 us -> 22.9 us
    ppermute x6, waiting for transfers between devices: 34.2 us -> 47.6 us  [row_exchange(): got.append(lax.ppermute(send, axis, pairs))]
    ppermute x6, starting transfers between devices: 12 us -> 6.74 us  [row_exchange(): got.append(lax.ppermute(send, axis, pairs))]
    ppermute x2, waiting for transfers between devices: 13.1 us -> 18.1 us  [group_scan(): rgot = lax.ppermute(bwd, axis, down)]
    dot_general x1, matrix products: 5.48 us -> 2.75 us  [on_device(): jnp.einsum('thf,hef->the', value_f, backward_input, precision=state_mode)]
    unnamed x67 -> x83, local copies, waits for them, and re-layouts: 14.9 us -> 17.6 us
  transfers between devices with their start and end apart: 22 -> 22, of which waited for: 14 -> 16; matrix products, arithmetic and copies ran while one was open for 19% -> 5% of each run, Pallas kernels for 0% -> 0%
where the time goes in v10:
time: 213 us; the launch traced here: 212 us
  waiting for transfers between devices  83.8 us (39%)
  starting transfers between devices  51.8 us (24%)
  matrix products  31.3 us (15%)
  local copies, waits for them, and re-layouts  22.9 us (11%)
  other arithmetic  20.6 us (10%)
    ppermute x6, waiting for transfers between devices, row_exchange(): got.append(lax.ppermute(send, axis, pairs))  47.6 us
    ppermute x11, starting transfers between devices, digit_sum(): lax.ppermute(value, axis, [(i, i ^ k * step) for i in range(count)])  20.5 us
    ppermute x2, waiting for transfers between devices, group_scan(): rgot = lax.ppermute(bwd, axis, down)  18.1 us
    unnamed x83, local copies, waits for them, and re-layouts  17.6 us
    ppermute x2, starting transfers between devices, group_scan(): got = lax.ppermute(fwd, axis, up)  11 us
    ppermute x1, starting transfers between devices, group_scan(): got = lax.ppermute(sent, axis, up + down)  11 us
    ppermute x11, waiting for transfers between devices, digit_sum(): lax.ppermute(value, axis, [(i, i ^ k * step) for i in range(count)])  8.18 us
    ppermute x6, starting transfers between devices, row_exchange(): got.append(lax.ppermute(send, axis, pairs))  6.74 us
  transfers between devices with their start and end apart: 22, of which 16 were waited for; matrix products, arithmetic and copies ran while one was open for 5% of the time, Pallas kernels for 0%

profile of v10, /device:TPU:6, one launch (start us, length us, event | category | flops | bytes accessed | tf_op | source)
XLA Modules:
  0.0 212.5 jit_solution(1105941314224283246)
XLA Ops:
  0.7 0.8 reduce-window_clone.1
  6.3 0.9 reduce-window.24
  7.6 1.9 copy.76
  9.5 1.9 copy.74
  11.4 3.1 %copy.97 = bf16[48,8,16,128]{3,2,1,0:T(8,128)(2,1)} copy(bf16[48,8,16,128]{3,1,2,0:T(8,128)(2,1)} %bitcast.235) | data formatting | bytes 3145728
  14.5 1.6 copy.98
  16.2 2.9 %fusion.20 = f32[16,128,128]{2,1,0:T(8,128)S(1)} fusion(bf16[384,16,128]{0,2,1:T(8,128)(2,1)S(1)} %bitcast.205, bf16[384,16,128]{2,1,0:T(8,128)(2,1)} %bitcast.221, f32[384,16]{0,1:T(8,128)S(1)} %get-tuple-element.49), kind=kOutput, calls=%fused_computation.29 | convolution fusion | flops 605552640 | bytes 4218880 | tf_op jit(solution)/shard_map/the,thf->hef/dot_general | solution.py:183
  19.2 1.4 fusion.17
  20.8 1.3 copy-done.6
  22.2 1.2 dynamic-slice_bitcast_fusion
  23.4 3.0 %collective-permute-start.2 = (f32[4,264,128]{2,1,0:T(8,128)}, f32[4,264,128]{2,1,0:T(8,128)}, u32[]{:S(2)}, u32[]{:S(2)}) collective-permute-start(f32[4,264,128]{2,1,0:T(8,128)} %get-tuple-element.77), channel_id=1, source_target_pairs={{0,24},{8,0},{16,8},{24,16},{32,56},{40,32},{48,40},{56,48},{64,88... | collective-permute-start | bytes 1622024 | tf_op jit(solution)/shard_map/ppermute | solution.py:64
  27.0 1.0 collective-permute-start
  28.0 21.8 %collective-permute-done.2 = f32[4,264,128]{2,1,0:T(8,128)} collective-permute-done((f32[4,264,128]{2,1,0:T(8,128)}, f32[4,264,128]{2,1,0:T(8,128)}, u32[]{:S(2)}, u32[]{:S(2)}) %collective-permute-start.2) | collective-permute-done | bytes 540704 | tf_op jit(solution)/shard_map/ppermute | solution.py:64
  49.9 3.7 %collective-permute-done = f32[4,264,128]{2,1,0:T(8,128)} collective-permute-done((f32[4,264,128]{2,1,0:T(8,128)}, f32[4,264,128]{2,1,0:T(8,128)}, u32[]{:S(2)}, u32[]{:S(2)}) %collective-permute-start) | collective-permute-done | bytes 540704 | tf_op jit(solution)/shard_map/ppermute | solution.py:64
  53.6 1.8 fusion.48
  56.6 1.0 fusion.66
  57.7 0.8 pad_maximum_fusion.3
  58.6 1.3 collective-permute-start.5
  59.9 5.3 %collective-permute-start.3 = (f32[4,136,128]{2,1,0:T(8,128)}, f32[4,136,128]{2,1,0:T(8,128)}, u32[]{:S(2)}, u32[]{:S(2)}) collective-permute-start(f32[4,136,128]{2,1,0:T(8,128)} %get-tuple-element.96), channel_id=1, source_target_pairs={{0,32},{8,40},{16,48},{24,56},{32,64},{40,72},{48,80},{56,88},{64,... | collective-permute-start | bytes 835592 | tf_op jit(solution)/shard_map/ppermute | solution.py:42
  65.2 4.4 %collective-permute-done.5 = f32[4,136,128]{2,1,0:T(8,128)} collective-permute-done((f32[4,136,128]{2,1,0:T(8,128)}, f32[4,136,128]{2,1,0:T(8,128)}, u32[]{:S(2)}, u32[]{:S(2)}) %collective-permute-start.5) | collective-permute-done | bytes 278560 | tf_op jit(solution)/shard_map/ppermute | solution.py:43
  69.6 1.2 collective-permute-done.3
  70.8 1.2 multiply_add_fusion.11
  72.0 0.8 slice_multiply_fusion.4
  72.9 5.8 %collective-permute-start.4 = (f32[4,136,128]{2,1,0:T(8,128)S(1)}, f32[4,136,128]{2,1,0:T(8,128)S(1)}, u32[]{:S(2)}, u32[]{:S(2)}) collective-permute-start(f32[4,136,128]{2,1,0:T(8,128)S(1)} %pad_maximum_fusion.5), channel_id=1, source_target_pairs={{0,64},{8,72},{16,80},{24,88},{32,96},{40,104},{48,112},{56,120},{... | collective-permute-start | bytes 835592 | tf_op jit(solution)/shard_map/ppermute | solution.py:42
  78.7 1.3 collective-permute-start.6
  80.2 3.6 %collective-permute-done.4 = f32[4,136,128]{2,1,0:T(8,128)S(1)} collective-permute-done((f32[4,136,128]{2,1,0:T(8,128)S(1)}, f32[4,136,128]{2,1,0:T(8,128)S(1)}, u32[]{:S(2)}, u32[]{:S(2)}) %collective-permute-start.4) | collective-permute-done | bytes 278560 | tf_op jit(solution)/shard_map/ppermute | solution.py:42
  83.9 13.7 %collective-permute-done.6 = f32[4,136,128]{2,1,0:T(8,128)S(1)} collective-permute-done((f32[4,136,128]{2,1,0:T(8,128)S(1)}, f32[4,136,128]{2,1,0:T(8,128)S(1)}, u32[]{:S(2)}, u32[]{:S(2)}) %collective-permute-start.6) | collective-permute-done | bytes 278560 | tf_op jit(solution)/shard_map/ppermute | solution.py:43
  99.0 11.0 %collective-permute-start.7 = (f32[4,136,128]{2,1,0:T(8,128)}, f32[4,136,128]{2,1,0:T(8,128)}, u32[]{:S(2)}, u32[]{:S(2)}) collective-permute-start(f32[4,136,128]{2,1,0:T(8,128)} %maximum_select_fusion), channel_id=1, source_target_pairs={{0,128},{8,136},{16,144},{24,152},{32,160},{40,168},{48,176},{56,1... | collective-permute-start | bytes 835592 | tf_op jit(solution)/shard_map/ppermute | solution.py:38
  110.0 0.8 fusion.44
  110.8 1.0 slice_reduce_fusion.2
  111.8 0.8 slice_reduce_fusion.4
  112.6 5.1 %collective-permute-done.7 = f32[4,136,128]{2,1,0:T(8,128)} collective-permute-done((f32[4,136,128]{2,1,0:T(8,128)}, f32[4,136,128]{2,1,0:T(8,128)}, u32[]{:S(2)}, u32[]{:S(2)}) %collective-permute-start.7) | collective-permute-done | bytes 278560 | tf_op jit(solution)/shard_map/ppermute | solution.py:38
  118.8 1.4 multiply_add_fusion.7
  120.9 5.2 %multiply_convert_fusion.1 = bf16[16,384,384]{2,1,0:T(8,128)(2,1)} fusion(f32[16,384]{1,0:T(8,128)S(1)} %bitcast.237, pred[384,384]{1,0:T(8,128)(4,1)S(1)} %copy-done.19, bf16[384,16,128]{2,1,0:T(8,128)(2,1)S(1)} %bitcast.222, bf16[384,16,128]{2,1,0:T(8,128)(2,1)S(1)} %bitcast.218), kind=kOutput, calls=%fused_computation.1 | convolution fusion | flops 615776256 | bytes 8036352 | tf_op jit(solution)/shard_map/shf,thf->hst/dot_general | solution.py:211
  126.1 6.6 %fusion.23 = f32[384,16,128]{0,2,1:T(8,128)} fusion(f32[16,384]{1,0:T(8,128)S(1)} %bitcast.238, pred[384,384]{1,0:T(8,128)(4,1)} %fusion.44, bf16[384,16,128]{0,2,1:T(8,128)(2,1)S(1)} %bitcast.212, bf16[384,16,128]{0,2,1:T(8,128)(2,1)S(1)} %bitcast.206, bf16[384,16,128]{2,1,0:T(8,128)(2,1)} %bitcast.216), kind=kOutput, calls=%fused_computation.35 | convolution fusion | flops 1219756032 | bytes 8036352 | tf_op jit(solution)/shard_map/hst,shf->thf/dot_general | solution.py:222
  132.7 3.7 %convolution_bitcast_fusion = f32[384,16,128]{0,2,1:T(8,128)S(1)} fusion(bf16[384,16,128]{0,2,1:T(8,128)(2,1)S(1)} %bitcast.213, bf16[16,384,384]{2,1,0:T(8,128)(2,1)} %multiply_convert_fusion.1), kind=kOutput, calls=%fused_computation.36 | convolution fusion | flops 603979776 | bytes 9437184 | tf_op jit(solution)/shard_map/hst,she->the/dot_general | solution.py:219
  136.6 1.6 convolution_bitcast_fusion.1
  138.3 1.5 multiply_add_fusion.2
  140.3 1.2 collective-permute-start.10
  142.4 1.2 fusion.7
  143.7 11.5 %collective-permute-done.10 = f32[4,256,128]{2,1,0:T(8,128)S(1)} collective-permute-done((f32[4,256,128]{2,1,0:T(8,128)S(1)}, f32[4,256,128]{2,1,0:T(8,128)S(1)}, u32[]{:S(2)}, u32[]{:S(2)}) %collective-permute-start.10) | collective-permute-done | bytes 524320 | tf_op jit(solution)/shard_map/ppermute | solution.py:64
  155.2 2.6 %collective-permute-done.9 = f32[4,256,128]{2,1,0:T(8,128)S(1)} collective-permute-done((f32[4,256,128]{2,1,0:T(8,128)S(1)}, f32[4,256,128]{2,1,0:T(8,128)S(1)}, u32[]{:S(2)}, u32[]{:S(2)}) %collective-permute-start.9) | collective-permute-done | bytes 524320 | tf_op jit(solution)/shard_map/ppermute | solution.py:64
  157.8 8.0 %collective-permute-done.8 = f32[4,256,128]{2,1,0:T(8,128)S(1)} collective-permute-done((f32[4,256,128]{2,1,0:T(8,128)S(1)}, f32[4,256,128]{2,1,0:T(8,128)S(1)}, u32[]{:S(2)}, u32[]{:S(2)}) %collective-permute-start.8) | collective-permute-done | bytes 524320 | tf_op jit(solution)/shard_map/ppermute | solution.py:64
  166.3 1.2 copy-done.3
  167.5 2.8 %fusion.16 = bf16[384,16,128]{0,2,1:T(8,128)(2,1)} fusion(f32[384,16,128]{0,2,1:T(8,128)S(1)} %convolution_bitcast_fusion.1, f32[384,16]{0,1:T(8,128)S(1)} %get-tuple-element.94, bf16[384,16,128]{2,1,0:T(8,128)(2,1)S(1)} %bitcast.219, f32[16,256,128]{2,1,0:T(8,128)S(1)} %bitcast.225), kind=kOutput, calls=%fused_computation.25 | convolution fusion | flops 606339072 | bytes 7364608 | tf_op jit(solution)/shard_map/shf,hef->she/dot_general | solution.py:241
  170.3 2.7 %fusion.14 = bf16[384,16,128]{0,2,1:T(8,128)(2,1)} fusion(f32[384,16,128]{0,2,1:T(8,128)S(1)} %convolution_bitcast_fusion, f32[384,16]{0,1:T(8,128)S(1)} %get-tuple-element.49, bf16[384,16,128]{2,1,0:T(8,128)(2,1)S(1)} %bitcast.223, f32[16,256,128]{2,1,0:T(8,128)S(1)} %bitcast.226), kind=kOutput, calls=%fused_computation.22 | convolution fusion | flops 606339072 | bytes 7364608 | tf_op jit(solution)/shard_map/thf,hef->the/dot_general | solution.py:244
  173.0 1.5 fusion.32
  174.5 1.5 fusion.33
  176.0 1.1 collective-permute-start.13
  177.3 2.8 %collective-permute-start.11 = (f32[16]{0:T(128)S(1)}, f32[16]{0:T(128)S(1)}, u32[]{:S(2)}, u32[]{:S(2)}) collective-permute-start(f32[16]{0:T(128)S(1)} %add_subtract_fusion), channel_id=1, source_target_pairs={{0,8},{8,0},{16,24},{24,16},{32,40},{40,32},{48,56},{56,48},{64,72... | collective-permute-start | bytes 200 | tf_op jit(solution)/shard_map/ppermute | solution.py:119
  180.2 1.4 fusion.12
  181.5 2.6 %copy.90 = bf16[1,384,2048]{2,1,0:T(8,128)(2,1)} copy(bf16[1,384,2048]{1,2,0:T(8,128)(2,1)} %bitcast.234) | data formatting | bytes 3145728
  184.3 7.8 %collective-permute-start.15 = (f32[16]{0:T(128)S(1)}, f32[16]{0:T(128)S(1)}, u32[]{:S(2)}, u32[]{:S(2)}) collective-permute-start(f32[16]{0:T(128)S(1)} %fusion.82), channel_id=1, source_target_pairs={{0,64},{8,72},{16,80},{24,88},{32,96},{40,104},{48,112},{56,120},{... | collective-permute-start | bytes 200 | tf_op jit(solution)/shard_map/ppermute | solution.py:119
  192.5 1.0 collective-permute-done.15
  193.6 2.0 collective-permute-done.14
  195.6 4.6 %collective-permute-start.17 = (f32[16]{0:T(128)S(1)}, f32[16]{0:T(128)S(1)}, u32[]{:S(2)}, u32[]{:S(2)}) collective-permute-start(f32[16]{0:T(128)S(1)} %fusion.79), channel_id=1, source_target_pairs={{0,128},{8,136},{16,144},{24,152},{32,160},{40,168},{48,176},{56,1... | collective-permute-start | bytes 200 | tf_op jit(solution)/shard_map/ppermute | solution.py:119
  200.2 1.6 copy.91
  201.9 1.3 collective-permute-done.17
  203.2 0.9 collective-permute-start.19
  204.1 0.9 collective-permute-start.18
  205.0 1.1 collective-permute-done.20
  206.8 1.5 collective-permute-start.21
  208.3 1.6 copy.89
  209.9 2.0 collective-permute-done.21
  (146 shorter events, 14.6 us)
Async XLA Ops:
  11.4 3.1 %copy-start.15 = (bf16[1,384,2048]{2,1,0:T(8,128)(2,1)S(1)}, bf16[1,384,2048]{2,1,0:T(8,128)(2,1)}, u32[]{:S(2)}) copy-start(bf16[1,384,2048]{2,1,0:T(8,128)(2,1)} %param.10) | copy-start | bytes 4718596
  16.2 3.0 %copy-start.1 = (bf16[48,8,16,128]{3,2,1,0:T(8,128)(2,1)S(1)}, bf16[48,8,16,128]{3,2,1,0:T(8,128)(2,1)}, u32[]{:S(2)}) copy-start(bf16[48,8,16,128]{3,2,1,0:T(8,128)(2,1)} %copy.98) | copy-start | bytes 4718596
  20.8 1.4 copy-start.6
  23.4 26.4 %collective-permute-start.2 = (f32[4,264,128]{2,1,0:T(8,128)}, f32[4,264,128]{2,1,0:T(8,128)}, u32[]{:S(2)}, u32[]{:S(2)}) collective-permute-start(f32[4,264,128]{2,1,0:T(8,128)} %get-tuple-element.77), channel_id=1, source_target_pairs={{0,24},{8,0},{16,8},{24,16},{32,56},{40,32},{48,40},{56,48},{64,88... | collective-permute-start | bytes 1622024 | tf_op jit(solution)/shard_map/ppermute | solution.py:64
  26.4 23.4 %collective-permute-start.1 = (f32[4,264,128]{2,1,0:T(8,128)}, f32[4,264,128]{2,1,0:T(8,128)}, u32[]{:S(2)}, u32[]{:S(2)}) collective-permute-start(f32[4,264,128]{2,1,0:T(8,128)} %get-tuple-element.78), channel_id=1, source_target_pairs={{0,16},{8,24},{16,0},{24,8},{32,48},{40,56},{48,32},{56,40},{64,80... | collective-permute-start | bytes 1622024 | tf_op jit(solution)/shard_map/ppermute | solution.py:64
  27.0 26.5 %collective-permute-start = (f32[4,264,128]{2,1,0:T(8,128)}, f32[4,264,128]{2,1,0:T(8,128)}, u32[]{:S(2)}, u32[]{:S(2)}) collective-permute-start(f32[4,264,128]{2,1,0:T(8,128)} %get-tuple-element.79), channel_id=1, source_target_pairs={{0,8},{8,16},{16,24},{24,0},{32,40},{40,48},{48,56},{56,32},{64,72... | collective-permute-start | bytes 1622024 | tf_op jit(solution)/shard_map/ppermute | solution.py:64
  55.3 3.3 %copy-start.8 = (f32[1,4,264,128]{3,2,1,0:T(8,128)}, f32[1,4,264,128]{3,2,1,0:T(8,128)S(1)}, u32[]{:S(2)}) copy-start(f32[1,4,264,128]{3,2,1,0:T(8,128)S(1)} %get-tuple-element.67) | copy-start | bytes 1622020
  55.3 3.3 %copy-start.9 = (f32[1,4,264,128]{3,2,1,0:T(8,128)}, f32[1,4,264,128]{3,2,1,0:T(8,128)S(1)}, u32[]{:S(2)}) copy-start(f32[1,4,264,128]{3,2,1,0:T(8,128)S(1)} %get-tuple-element.68) | copy-start | bytes 1622020
  55.3 3.3 %copy-start.10 = (f32[1,4,264,128]{3,2,1,0:T(8,128)}, f32[1,4,264,128]{3,2,1,0:T(8,128)S(1)}, u32[]{:S(2)}) copy-start(f32[1,4,264,128]{3,2,1,0:T(8,128)S(1)} %get-tuple-element.69) | copy-start | bytes 1622020
  55.4 3.2 %copy-start.11 = (f32[1,4,264,128]{3,2,1,0:T(8,128)}, f32[1,4,264,128]{3,2,1,0:T(8,128)S(1)}, u32[]{:S(2)}) copy-start(f32[1,4,264,128]{3,2,1,0:T(8,128)S(1)} %get-tuple-element.70) | copy-start | bytes 1622020
  55.5 2.2 %copy-start.20 = (f32[4]{0:T(128)}, f32[4]{0:T(128)S(1)}, u32[]{:S(2)}) copy-start(f32[4]{0:T(128)S(1)} %slice_reduce_fusion.10) | copy-start | bytes 52
  55.6 2.1 copy-start.22
  55.7 1.9 copy-start.24
  55.8 1.8 copy-start.26
  56.6 2.0 copy-start.28
  56.6 2.0 copy-start.29
  56.6 2.0 copy-start.31
  57.7 1.0 copy-start.14
  58.6 11.0 %collective-permute-start.5 = (f32[4,136,128]{2,1,0:T(8,128)}, f32[4,136,128]{2,1,0:T(8,128)}, u32[]{:S(2)}, u32[]{:S(2)}) collective-permute-start(f32[4,136,128]{2,1,0:T(8,128)} %get-tuple-element.95), channel_id=1, source_target_pairs={{32,0},{40,8},{48,16},{56,24},{64,32},{72,40},{80,48},{88,56},{96,... | collective-permute-start | bytes 835592 | tf_op jit(solution)/shard_map/ppermute | solution.py:43
  59.9 10.9 %collective-permute-start.3 = (f32[4,136,128]{2,1,0:T(8,128)}, f32[4,136,128]{2,1,0:T(8,128)}, u32[]{:S(2)}, u32[]{:S(2)}) collective-permute-start(f32[4,136,128]{2,1,0:T(8,128)} %get-tuple-element.96), channel_id=1, source_target_pairs={{0,32},{8,40},{16,48},{24,56},{32,64},{40,72},{48,80},{56,88},{64,... | collective-permute-start | bytes 835592 | tf_op jit(solution)/shard_map/ppermute | solution.py:42
  72.9 10.9 %collective-permute-start.4 = (f32[4,136,128]{2,1,0:T(8,128)S(1)}, f32[4,136,128]{2,1,0:T(8,128)S(1)}, u32[]{:S(2)}, u32[]{:S(2)}) collective-permute-start(f32[4,136,128]{2,1,0:T(8,128)S(1)} %pad_maximum_fusion.5), channel_id=1, source_target_pairs={{0,64},{8,72},{16,80},{24,88},{32,96},{40,104},{48,112},{56,120},{... | collective-permute-start | bytes 835592 | tf_op jit(solution)/shard_map/ppermute | solution.py:42
  78.7 18.9 %collective-permute-start.6 = (f32[4,136,128]{2,1,0:T(8,128)S(1)}, f32[4,136,128]{2,1,0:T(8,128)S(1)}, u32[]{:S(2)}, u32[]{:S(2)}) collective-permute-start(f32[4,136,128]{2,1,0:T(8,128)S(1)} %pad_maximum_fusion.6), channel_id=1, source_target_pairs={{64,0},{72,8},{80,16},{88,24},{96,32},{104,40},{112,48},{120,56},{... | collective-permute-start | bytes 835592 | tf_op jit(solution)/shard_map/ppermute | solution.py:43
  97.6 0.7 copy-start.16
  99.0 18.8 %collective-permute-start.7 = (f32[4,136,128]{2,1,0:T(8,128)}, f32[4,136,128]{2,1,0:T(8,128)}, u32[]{:S(2)}, u32[]{:S(2)}) collective-permute-start(f32[4,136,128]{2,1,0:T(8,128)} %maximum_select_fusion), channel_id=1, source_target_pairs={{0,128},{8,136},{16,144},{24,152},{32,160},{40,168},{48,176},{56,1... | collective-permute-start | bytes 835592 | tf_op jit(solution)/shard_map/ppermute | solution.py:38
  110.8 10.1 %copy-start.2 = (bf16[48,8,16,128]{3,2,1,0:T(8,128)(2,1)S(1)}, bf16[48,8,16,128]{3,2,1,0:T(8,128)(2,1)}, u32[]{:S(2)}) copy-start(bf16[48,8,16,128]{3,2,1,0:T(8,128)(2,1)} %copy.98) | copy-start | bytes 4718596
  110.8 10.1 %copy-start.4 = (bf16[48,8,16,128]{3,2,1,0:T(8,128)(2,1)S(1)}, bf16[48,8,16,128]{3,2,1,0:T(8,128)(2,1)}, u32[]{:S(2)}) copy-start(bf16[48,8,16,128]{3,2,1,0:T(8,128)(2,1)} %copy.97) | copy-start | bytes 4718596
  110.8 10.1 %copy-start.19 = (pred[384,384]{1,0:T(8,128)(4,1)S(1)}, pred[384,384]{1,0:T(8,128)(4,1)}, u32[]{:S(2)}) copy-start(pred[384,384]{1,0:T(8,128)(4,1)} %fusion.44) | copy-start | bytes 442372
  132.7 3.8 %copy-start = (bf16[16,384,384]{2,1,0:T(8,128)(2,1)S(1)}, bf16[16,384,384]{2,1,0:T(8,128)(2,1)}, u32[]{:S(2)}) copy-start(bf16[16,384,384]{2,1,0:T(8,128)(2,1)} %multiply_convert_fusion.1) | copy-start | bytes 14155780
  136.5 1.7 copy-start.13
  136.5 1.7 copy-start.17
  136.5 1.7 copy-start.18
  136.5 1.7 copy-start.21
  136.5 1.7 copy-start.23
  136.5 1.7 copy-start.25
  136.5 1.7 copy-start.27
  136.5 1.7 copy-start.30
  136.5 1.7 copy-start.32
  136.5 1.7 copy-start.33
  136.5 1.7 copy-start.34
  136.6 1.7 copy-start.35
  136.6 1.7 copy-start.36
  140.3 14.9 %collective-permute-start.10 = (f32[4,256,128]{2,1,0:T(8,128)S(1)}, f32[4,256,128]{2,1,0:T(8,128)S(1)}, u32[]{:S(2)}, u32[]{:S(2)}) collective-permute-start(f32[4,256,128]{2,1,0:T(8,128)S(1)} %get-tuple-element.80), channel_id=1, source_target_pairs={{0,24},{8,0},{16,8},{24,16},{32,56},{40,32},{48,40},{56,48},{64,88... | collective-permute-start | bytes 1572872 | tf_op jit(solution)/shard_map/ppermute | solution.py:64
  141.4 16.4 %collective-permute-start.9 = (f32[4,256,128]{2,1,0:T(8,128)S(1)}, f32[4,256,128]{2,1,0:T(8,128)S(1)}, u32[]{:S(2)}, u32[]{:S(2)}) collective-permute-start(f32[4,256,128]{2,1,0:T(8,128)S(1)} %get-tuple-element.81), channel_id=1, source_target_pairs={{0,16},{8,24},{16,0},{24,8},{32,48},{40,56},{48,32},{56,40},{64,80... | collective-permute-start | bytes 1572872 | tf_op jit(solution)/shard_map/ppermute | solution.py:64
  142.1 23.7 %collective-permute-start.8 = (f32[4,256,128]{2,1,0:T(8,128)S(1)}, f32[4,256,128]{2,1,0:T(8,128)S(1)}, u32[]{:S(2)}, u32[]{:S(2)}) collective-permute-start(f32[4,256,128]{2,1,0:T(8,128)S(1)} %get-tuple-element.82), channel_id=1, source_target_pairs={{0,8},{8,16},{16,24},{24,0},{32,40},{40,48},{48,56},{56,32},{64,72... | collective-permute-start | bytes 1572872 | tf_op jit(solution)/shard_map/ppermute | solution.py:64
  166.1 1.4 copy-start.3
  167.5 2.8 %copy-start.5 = (bf16[48,8,16,128]{3,2,1,0:T(8,128)(2,1)S(1)}, bf16[48,8,16,128]{3,2,1,0:T(8,128)(2,1)}, u32[]{:S(2)}) copy-start(bf16[48,8,16,128]{3,2,1,0:T(8,128)(2,1)} %copy.97) | copy-start | bytes 4718596
  174.5 5.7 %copy-start.12 = (f32[384,16,128]{0,2,1:T(8,128)S(1)}, f32[384,16,128]{0,2,1:T(8,128)}, u32[]{:S(2)}) copy-start(f32[384,16,128]{0,2,1:T(8,128)} %fusion.23) | copy-start | bytes 9437188
  176.0 8.1 %collective-permute-start.13 = (f32[16]{0:T(128)S(1)}, f32[16]{0:T(128)S(1)}, u32[]{:S(2)}, u32[]{:S(2)}) collective-permute-start(f32[16]{0:T(128)S(1)} %add_subtract_fusion), channel_id=1, source_target_pairs={{0,24},{8,16},{16,8},{24,0},{32,56},{40,48},{48,40},{56,32},{64,88... | collective-permute-start | bytes 200 | tf_op jit(solution)/shard_map/ppermute | solution.py:119
  177.2 7.0 %collective-permute-start.12 = (f32[16]{0:T(128)S(1)}, f32[16]{0:T(128)S(1)}, u32[]{:S(2)}, u32[]{:S(2)}) collective-permute-start(f32[16]{0:T(128)S(1)} %add_subtract_fusion), channel_id=1, source_target_pairs={{0,16},{8,24},{16,0},{24,8},{32,48},{40,56},{48,32},{56,40},{64,80... | collective-permute-start | bytes 200 | tf_op jit(solution)/shard_map/ppermute | solution.py:119
  177.3 6.8 %collective-permute-start.11 = (f32[16]{0:T(128)S(1)}, f32[16]{0:T(128)S(1)}, u32[]{:S(2)}, u32[]{:S(2)}) collective-permute-start(f32[16]{0:T(128)S(1)} %add_subtract_fusion), channel_id=1, source_target_pairs={{0,8},{8,0},{16,24},{24,16},{32,40},{40,32},{48,56},{56,48},{64,72... | collective-permute-start | bytes 200 | tf_op jit(solution)/shard_map/ppermute | solution.py:119
  184.1 24.2 %copy-start.7 = (bf16[384,16,128]{0,2,1:T(8,128)(2,1)S(1)}, bf16[384,16,128]{0,2,1:T(8,128)(2,1)}, u32[]{:S(2)}) copy-start(bf16[384,16,128]{0,2,1:T(8,128)(2,1)} %fusion.16) | copy-start | bytes 4718596
  184.2 8.4 %collective-permute-start.16 = (f32[16]{0:T(128)S(1)}, f32[16]{0:T(128)S(1)}, u32[]{:S(2)}, u32[]{:S(2)}) collective-permute-start(f32[16]{0:T(128)S(1)} %fusion.82), channel_id=1, source_target_pairs={{0,96},{8,104},{16,112},{24,120},{32,64},{40,72},{48,80},{56,88},{... | collective-permute-start | bytes 200 | tf_op jit(solution)/shard_map/ppermute | solution.py:119
  184.3 9.3 %collective-permute-start.15 = (f32[16]{0:T(128)S(1)}, f32[16]{0:T(128)S(1)}, u32[]{:S(2)}, u32[]{:S(2)}) collective-permute-start(f32[16]{0:T(128)S(1)} %fusion.82), channel_id=1, source_target_pairs={{0,64},{8,72},{16,80},{24,88},{32,96},{40,104},{48,112},{56,120},{... | collective-permute-start | bytes 200 | tf_op jit(solution)/shard_map/ppermute | solution.py:119
  192.1 3.5 %collective-permute-start.14 = (f32[16]{0:T(128)S(1)}, f32[16]{0:T(128)S(1)}, u32[]{:S(2)}, u32[]{:S(2)}) collective-permute-start(f32[16]{0:T(128)S(1)} %fusion.82), channel_id=1, source_target_pairs={{0,32},{8,40},{16,48},{24,56},{32,0},{40,8},{48,16},{56,24},{64,96... | collective-permute-start | bytes 200 | tf_op jit(solution)/shard_map/ppermute | solution.py:119
  195.6 7.5 %collective-permute-start.17 = (f32[16]{0:T(128)S(1)}, f32[16]{0:T(128)S(1)}, u32[]{:S(2)}, u32[]{:S(2)}) collective-permute-start(f32[16]{0:T(128)S(1)} %fusion.79), channel_id=1, source_target_pairs={{0,128},{8,136},{16,144},{24,152},{32,160},{40,168},{48,176},{56,1... | collective-permute-start | bytes 200 | tf_op jit(solution)/shard_map/ppermute | solution.py:119
  201.8 10.1 %copy-start.37 = (f32[16]{0:T(128)S(1)}, f32[16]{0:T(128)}, u32[]{:S(2)}) copy-start(f32[16]{0:T(128)} %param.13) | copy-start | bytes 196
  203.2 3.0 %collective-permute-start.20 = (f32[16]{0:T(128)S(1)}, f32[16]{0:T(128)S(1)}, u32[]{:S(2)}, u32[]{:S(2)}) collective-permute-start(f32[16]{0:T(128)S(1)} %fusion.76), channel_id=1, source_target_pairs={{0,3},{1,2},{2,1},{3,0},{4,7},{5,6},{6,5},{7,4},{8,11},{9,10},{10,... | collective-permute-start | bytes 200 | tf_op jit(solution)/shard_map/ppermute | solution.py:119
  203.2 3.6 %collective-permute-start.19 = (f32[16]{0:T(128)S(1)}, f32[16]{0:T(128)S(1)}, u32[]{:S(2)}, u32[]{:S(2)}) collective-permute-start(f32[16]{0:T(128)S(1)} %fusion.76), channel_id=1, source_target_pairs={{0,2},{1,3},{2,0},{3,1},{4,6},{5,7},{6,4},{7,5},{8,10},{9,11},{10,... | collective-permute-start | bytes 200 | tf_op jit(solution)/shard_map/ppermute | solution.py:119
  204.1 2.7 %collective-permute-start.18 = (f32[16]{0:T(128)S(1)}, f32[16]{0:T(128)S(1)}, u32[]{:S(2)}, u32[]{:S(2)}) collective-permute-start(f32[16]{0:T(128)S(1)} %fusion.76), channel_id=1, source_target_pairs={{0,1},{1,0},{2,3},{3,2},{4,5},{5,4},{6,7},{7,6},{8,9},{9,8},{10,11... | collective-permute-start | bytes 200 | tf_op jit(solution)/shard_map/ppermute | solution.py:119
  206.8 5.1 %collective-permute-start.21 = (f32[16]{0:T(128)S(1)}, f32[16]{0:T(128)S(1)}, u32[]{:S(2)}, u32[]{:S(2)}) collective-permute-start(f32[16]{0:T(128)S(1)} %fusion.75), channel_id=1, source_target_pairs={{0,4},{1,5},{2,6},{3,7},{4,0},{5,1},{6,2},{7,3},{8,12},{9,13},{10,... | collective-permute-start | bytes 200 | tf_op jit(solution)/shard_map/ppermute | solution.py:119

commit v11 on v5

--- a/solution.py
+++ b/solution.py
@@ -32,6 +32,13 @@
     while shift < count:
         up = [(i, i + shift) for i in range(count - shift)]
         down = [(i + shift, i) for i in range(count - shift)]
+        if 2 * shift >= count:
+            place = lax.axis_index(axis)
+            sent = jnp.where(place < count - shift, fwd, bwd)
+            got = lax.ppermute(sent, axis, up + down)
+            excl = jnp.where(place >= shift, combine(got, excl), excl)
+            rexcl = jnp.where(place < count - shift, combine(got, rexcl), rexcl)
+            break
         got = lax.ppermute(fwd, axis, up)
         rgot = lax.ppermute(bwd, axis, down)
         excl = combine(got, excl)

time: 196 us -> 202 us (1.031)
  waiting for transfers between devices: 65.9 us -> 76.3 us
  starting transfers between devices: 65.4 us -> 57.8 us
  other arithmetic: 16.6 us -> 18.7 us
    ppermute x3 -> x2, starting transfers between devices: 28.3 us -> 11 us  [group_scan(): got = lax.ppermute(fwd, axis, up)]
    ppermute x0 -> x1, starting transfers between devices: none -> 11 us  [group_scan(): got = lax.ppermute(sent, axis, up + down)]
    ppermute x0 -> x1, waiting for transfers between devices: none -> 8.71 us  [group_scan(): got = lax.ppermute(sent, axis, up + down)]
    ppermute x3 -> x2, waiting for transfers between devices: 11.4 us -> 16.2 us  [group_scan(): rgot = lax.ppermute(bwd, axis, down)]
    ppermute x11, waiting for transfers between devices: 14.1 us -> 9.58 us  [digit_sum(): lax.ppermute(value, axis, [(i, i ^ k * step) for i in range(count)])]
    ppermute x6, waiting for transfers between devices: 35.6 us -> 38.2 us  [row_exchange(): got.append(lax.ppermute(send, axis, pairs))]
    ppermute x3 -> x2, waiting for transfers between devices: 4.74 us -> 3.66 us  [group_scan(): got = lax.ppermute(fwd, axis, up)]
    unnamed x42 -> x44, local copies, waits for them, and re-layouts: 14.1 us -> 14.1 us
  transfers between devices with their start and end apart: 23 -> 22, of which waited for: 15 -> 15; matrix products, arithmetic and copies ran while one was open for 11% -> 10% of each run, Pallas kernels for 0% -> 0%
where the time goes in v11:
time: 202 us; the launch traced here: 201 us
  waiting for transfers between devices  76.3 us (38%)
  starting transfers between devices  57.8 us (29%)
  matrix products  25.4 us (13%)
  local copies, waits for them, and re-layouts  20.8 us (10%)
  other arithmetic  18.7 us (9%)
    ppermute x6, waiting for transfers between devices, row_exchange(): got.append(lax.ppermute(send, axis, pairs))  38.2 us
    ppermute x11, starting transfers between devices, digit_sum(): lax.ppermute(value, axis, [(i, i ^ k * step) for i in range(count)])  21.7 us
    ppermute x2, waiting for transfers between devices, group_scan(): rgot = lax.ppermute(bwd, axis, down)  16.2 us
    unnamed x44, local copies, waits for them, and re-layouts  14.1 us
    ppermute x6, starting transfers between devices, row_exchange(): got.append(lax.ppermute(send, axis, pairs))  11.4 us
    ppermute x1, starting transfers between devices, group_scan(): got = lax.ppermute(sent, axis, up + down)  11 us
    ppermute x2, starting transfers between devices, group_scan(): got = lax.ppermute(fwd, axis, up)  11 us
    ppermute x11, waiting for transfers between devices, digit_sum(): lax.ppermute(value, axis, [(i, i ^ k * step) for i in range(count)])  9.58 us
  transfers between devices with their start and end apart: 22, of which 15 were waited for; matrix products, arithmetic and copies ran while one was open for 10% of the time, Pallas kernels for 0%

profile of v11, /device:TPU:6, one launch (start us, length us, event | category | flops | bytes accessed | tf_op | source)
XLA Modules:
  0.0 200.9 jit_solution(13506498769190654800)
XLA Ops:
  0.7 0.9 reduce-window_clone.1
  4.9 1.9 copy.87
  6.8 1.6 copy.103
  8.5 0.9 reduce-window.24
  9.8 1.9 copy.85
  11.7 3.0 %copy.105 = bf16[48,8,16,128]{3,2,1,0:T(8,128)(2,1)} copy(bf16[48,8,16,128]{3,1,2,0:T(8,128)(2,1)} %bitcast.221) | data formatting | bytes 3145728
  14.8 2.9 %fusion.9 = f32[16,128,128]{2,1,0:T(8,128)S(1)} fusion(bf16[384,16,128]{0,2,1:T(8,128)(2,1)} %bitcast.207, bf16[384,16,128]{0,2,1:T(8,128)(2,1)S(1)} %bitcast.203, f32[384,16]{0,1:T(8,128)S(1)} %get-tuple-element.78), kind=kOutput, calls=%fused_computation.15 | convolution fusion | flops 605552640 | bytes 4218880 | tf_op jit(solution)/shard_map/she,shf->hef/dot_general | solution.py:187
  17.8 1.4 fusion.7
  19.4 1.3 copy-done.3
  20.8 1.2 dynamic-slice_bitcast_fusion
  22.0 1.6 collective-permute-start
  23.6 2.9 %collective-permute-start.1 = (f32[4,264,128]{2,1,0:T(8,128)}, f32[4,264,128]{2,1,0:T(8,128)}, u32[]{:S(2)}, u32[]{:S(2)}) collective-permute-start(f32[4,264,128]{2,1,0:T(8,128)} %get-tuple-element.62), channel_id=1, source_target_pairs={{0,16},{8,24},{16,0},{24,8},{32,48},{40,56},{48,32},{56,40},{64,80... | collective-permute-start | bytes 1622024 | tf_op jit(solution)/shard_map/ppermute | solution.py:64
  26.5 1.3 collective-permute-start.2
  27.8 9.8 %collective-permute-done = f32[4,264,128]{2,1,0:T(8,128)} collective-permute-done((f32[4,264,128]{2,1,0:T(8,128)}, f32[4,264,128]{2,1,0:T(8,128)}, u32[]{:S(2)}, u32[]{:S(2)}) %collective-permute-start) | collective-permute-done | bytes 540704 | tf_op jit(solution)/shard_map/ppermute | solution.py:64
  37.6 12.8 %collective-permute-done.1 = f32[4,264,128]{2,1,0:T(8,128)} collective-permute-done((f32[4,264,128]{2,1,0:T(8,128)}, f32[4,264,128]{2,1,0:T(8,128)}, u32[]{:S(2)}, u32[]{:S(2)}) %collective-permute-start.1) | collective-permute-done | bytes 540704 | tf_op jit(solution)/shard_map/ppermute | solution.py:64
  50.4 1.8 fusion.28
  52.7 1.0 fusion.49
  53.7 0.9 pad_maximum_fusion.3
  54.6 1.3 collective-permute-start.5
  56.0 5.3 %collective-permute-start.3 = (f32[4,136,128]{2,1,0:T(8,128)}, f32[4,136,128]{2,1,0:T(8,128)}, u32[]{:S(2)}, u32[]{:S(2)}) collective-permute-start(f32[4,136,128]{2,1,0:T(8,128)} %get-tuple-element.80), channel_id=1, source_target_pairs={{0,32},{8,40},{16,48},{24,56},{32,64},{40,72},{48,80},{56,88},{64,... | collective-permute-start | bytes 835592 | tf_op jit(solution)/shard_map/ppermute | solution.py:42
  62.1 2.5 %collective-permute-done.5 = f32[4,136,128]{2,1,0:T(8,128)} collective-permute-done((f32[4,136,128]{2,1,0:T(8,128)}, f32[4,136,128]{2,1,0:T(8,128)}, u32[]{:S(2)}, u32[]{:S(2)}) %collective-permute-start.5) | collective-permute-done | bytes 278560 | tf_op jit(solution)/shard_map/ppermute | solution.py:43
  64.6 1.2 collective-permute-done.3
  65.8 0.8 slice_multiply_fusion.4
  66.6 1.3 multiply_add_fusion.11
  67.9 5.8 %collective-permute-start.4 = (f32[4,136,128]{2,1,0:T(8,128)S(1)}, f32[4,136,128]{2,1,0:T(8,128)S(1)}, u32[]{:S(2)}, u32[]{:S(2)}) collective-permute-start(f32[4,136,128]{2,1,0:T(8,128)S(1)} %pad_maximum_fusion.5), channel_id=1, source_target_pairs={{0,64},{8,72},{16,80},{24,88},{32,96},{40,104},{48,112},{56,120},{... | collective-permute-start | bytes 835592 | tf_op jit(solution)/shard_map/ppermute | solution.py:42
  73.7 1.3 collective-permute-start.6
  75.2 2.5 %collective-permute-done.4 = f32[4,136,128]{2,1,0:T(8,128)S(1)} collective-permute-done((f32[4,136,128]{2,1,0:T(8,128)S(1)}, f32[4,136,128]{2,1,0:T(8,128)S(1)}, u32[]{:S(2)}, u32[]{:S(2)}) %collective-permute-start.4) | collective-permute-done | bytes 278560 | tf_op jit(solution)/shard_map/ppermute | solution.py:42
  77.8 13.7 %collective-permute-done.6 = f32[4,136,128]{2,1,0:T(8,128)S(1)} collective-permute-done((f32[4,136,128]{2,1,0:T(8,128)S(1)}, f32[4,136,128]{2,1,0:T(8,128)S(1)}, u32[]{:S(2)}, u32[]{:S(2)}) %collective-permute-start.6) | collective-permute-done | bytes 278560 | tf_op jit(solution)/shard_map/ppermute | solution.py:43
  92.4 11.0 %collective-permute-start.7 = (f32[4,136,128]{2,1,0:T(8,128)}, f32[4,136,128]{2,1,0:T(8,128)}, u32[]{:S(2)}, u32[]{:S(2)}) collective-permute-start(f32[4,136,128]{2,1,0:T(8,128)} %maximum_select_fusion), channel_id=1, source_target_pairs={{0,128},{8,136},{16,144},{24,152},{32,160},{40,168},{48,176},{56,1... | collective-permute-start | bytes 835592 | tf_op jit(solution)/shard_map/ppermute | solution.py:38
  103.4 0.8 slice_reduce_fusion.4
  104.2 0.8 slice_reduce_fusion.2
  105.1 8.7 %collective-permute-done.7 = f32[4,136,128]{2,1,0:T(8,128)} collective-permute-done((f32[4,136,128]{2,1,0:T(8,128)}, f32[4,136,128]{2,1,0:T(8,128)}, u32[]{:S(2)}, u32[]{:S(2)}) %collective-permute-start.7) | collective-permute-done | bytes 278560 | tf_op jit(solution)/shard_map/ppermute | solution.py:38
  113.8 0.8 slice_multiply_fusion.1
  114.8 1.5 multiply_add_fusion.9
  116.3 1.1 multiply_add_fusion.4
  117.4 1.1 multiply_add_fusion.5
  118.4 1.2 multiply_add_fusion.2
  120.2 1.6 collective-permute-start.8
  121.8 1.5 collective-permute-start.9
  123.2 2.5 %collective-permute-start.10 = (f32[4,256,128]{2,1,0:T(8,128)S(1)}, f32[4,256,128]{2,1,0:T(8,128)S(1)}, u32[]{:S(2)}, u32[]{:S(2)}) collective-permute-start(f32[4,256,128]{2,1,0:T(8,128)S(1)} %get-tuple-element.64), channel_id=1, source_target_pairs={{0,24},{8,0},{16,8},{24,16},{32,56},{40,32},{48,40},{56,48},{64,88... | collective-permute-start | bytes 1572872 | tf_op jit(solution)/shard_map/ppermute | solution.py:64
  125.7 3.7 %multiply_convert_fusion.1 = bf16[16,384,384]{2,1,0:T(8,128)(2,1)S(1)} fusion(f32[16,384]{1,0:T(8,128)S(1)} %get-tuple-element.75, pred[384,384]{1,0:T(8,128)(4,1)S(1)} %copy-done.16, bf16[384,16,128]{0,2,1:T(8,128)(2,1)S(1)} %bitcast.209, bf16[384,16,128]{2,1,0:T(8,128)(2,1)S(1)} %bitcast.212), kind=kOutput, calls=%fused_computation.1 | convolution fusion | flops 615776256 | bytes 8036352 | tf_op jit(solution)/shard_map/shf,thf->hst/dot_general | solution.py:193
  129.5 4.3 %collective-permute-done.8 = f32[4,256,128]{2,1,0:T(8,128)S(1)} collective-permute-done((f32[4,256,128]{2,1,0:T(8,128)S(1)}, f32[4,256,128]{2,1,0:T(8,128)S(1)}, u32[]{:S(2)}, u32[]{:S(2)}) %collective-permute-start.8) | collective-permute-done | bytes 524320 | tf_op jit(solution)/shard_map/ppermute | solution.py:64
  133.7 11.4 %collective-permute-done.9 = f32[4,256,128]{2,1,0:T(8,128)S(1)} collective-permute-done((f32[4,256,128]{2,1,0:T(8,128)S(1)}, f32[4,256,128]{2,1,0:T(8,128)S(1)}, u32[]{:S(2)}, u32[]{:S(2)}) %collective-permute-start.9) | collective-permute-done | bytes 524320 | tf_op jit(solution)/shard_map/ppermute | solution.py:64
  145.5 1.0 fusion.21
  146.5 1.4 fusion.17
  148.0 2.7 %fusion.23 = f32[16,128,384]{2,1,0:T(8,128)} fusion(bf16[384,16,128]{0,2,1:T(8,128)(2,1)S(1)} %bitcast.199, f32[16,256,128]{2,1,0:T(8,128)S(1)} %bitcast.216), kind=kOutput, calls=%fused_computation.35 | convolution fusion | flops 603979776 | bytes 5767168 | tf_op jit(solution)/shard_map/the,hef->thf/dot_general | solution.py:201
  150.7 2.7 %fusion.10 = (f32[384,16]{0,1:T(8,128)S(1)}, bf16[384,16,128]{0,2,1:T(8,128)(2,1)}) fusion(bf16[384,16,128]{0,2,1:T(8,128)(2,1)S(1)} %bitcast.204, f32[16,128,384]{2,1,0:T(8,128)S(1)} %fusion.21, f32[384,16]{0,1:T(8,128)S(1)} %get-tuple-element.78, bf16[16,384,384]{2,1,0:T(8,128)(2,1)S(1)} %multiply_convert_fusion.1, bf16[384,16,128]{0,2,1:T(8,128)(2,1)S(1)} %bitcast.200), kind=kOutput, calls=%fused_computation.16 | convolution fusion | flops 608692224 | bytes 12632064 | tf_op jit(solution)/shard_map/hst,the->she/dot_general | solution.py:204
  153.4 2.4 %fusion.8 = (f32[384,16]{0,1:T(8,128)S(1)}, bf16[384,16,128]{0,2,1:T(8,128)(2,1)}) fusion(bf16[384,16,128]{0,2,1:T(8,128)(2,1)S(1)} %bitcast.201, f32[16,128,384]{2,1,0:T(8,128)S(1)} %fusion.17, f32[384,16]{0,1:T(8,128)S(1)} %get-tuple-element.77, bf16[384,16,128]{0,2,1:T(8,128)(2,1)S(1)} %bitcast.205, bf16[16,384,384]{2,1,0:T(8,128)(2,1)S(1)} %multiply_convert_fusion.1), kind=kOutput, calls=%fused_computation.14 | convolution fusion | flops 608692224 | bytes 12632064 | tf_op jit(solution)/shard_map/hst,she->the/dot_general | solution.py:210
  156.0 3.6 %collective-permute-start.12 = (f32[16]{0:T(128)S(1)}, f32[16]{0:T(128)S(1)}, u32[]{:S(2)}, u32[]{:S(2)}) collective-permute-start(f32[16]{0:T(128)S(1)} %multiply_reduce_fusion), channel_id=1, source_target_pairs={{0,16},{8,24},{16,0},{24,8},{32,48},{40,56},{48,32},{56,40},{64,80... | collective-permute-start | bytes 200 | tf_op jit(solution)/shard_map/ppermute | solution.py:120
  159.7 1.1 collective-permute-start.13
  160.7 7.1 %fusion.12 = bf16[384,16,128]{0,2,1:T(8,128)(2,1)} fusion(f32[16,128,384]{2,1,0:T(8,128)} %fusion.23, bf16[384,16,128]{0,2,1:T(8,128)(2,1)} %bitcast.208, f32[16,384]{1,0:T(8,128)S(1)} %get-tuple-element.75, pred[384,384]{1,0:T(8,128)(4,1)S(1)} %copy-done.16, bf16[384,16,128]{0,2,1:T(8,128)(2,1)S(1)} %bitcast.206, bf16[384,16,128]{0,2,1:T(8,128)(2,1)S(1)} %bitcast.202, ...), kind=kOutput, calls=%fused_computation.19 | convolution fusion | flops 1222115328 | bytes 9633792 | tf_op jit(solution)/shard_map/hst,shf->thf/dot_general | solution.py:198
  167.8 2.7 %copy.96 = bf16[1,384,2048]{2,1,0:T(8,128)(2,1)} copy(bf16[1,384,2048]{1,2,0:T(8,128)(2,1)} %bitcast.220) | data formatting | bytes 3145728
  170.6 7.8 %collective-permute-start.15 = (f32[16]{0:T(128)S(1)}, f32[16]{0:T(128)S(1)}, u32[]{:S(2)}, u32[]{:S(2)}) collective-permute-start(f32[16]{0:T(128)S(1)} %fusion.64), channel_id=1, source_target_pairs={{0,64},{8,72},{16,80},{24,88},{32,96},{40,104},{48,112},{56,120},{... | collective-permute-start | bytes 200 | tf_op jit(solution)/shard_map/ppermute | solution.py:120
  178.5 1.4 collective-permute-start.16
  180.0 3.8 %collective-permute-done.16 = f32[16]{0:T(128)S(1)} collective-permute-done((f32[16]{0:T(128)S(1)}, f32[16]{0:T(128)S(1)}, u32[]{:S(2)}, u32[]{:S(2)}) %collective-permute-start.16) | collective-permute-done | bytes 96 | tf_op jit(solution)/shard_map/ppermute | solution.py:120
  183.8 4.6 %collective-permute-start.17 = (f32[16]{0:T(128)S(1)}, f32[16]{0:T(128)S(1)}, u32[]{:S(2)}, u32[]{:S(2)}) collective-permute-start(f32[16]{0:T(128)S(1)} %fusion.61), channel_id=1, source_target_pairs={{0,128},{8,136},{16,144},{24,152},{32,160},{40,168},{48,176},{56,1... | collective-permute-start | bytes 200 | tf_op jit(solution)/shard_map/ppermute | solution.py:120
  188.4 1.6 copy.97
  190.0 1.3 collective-permute-done.17
  191.3 0.9 collective-permute-start.19
  192.3 1.0 collective-permute-start.20
  193.2 1.7 collective-permute-done.19
  195.2 1.2 collective-permute-start.21
  196.5 1.6 copy.98
  198.1 2.3 %collective-permute-done.21 = f32[16]{0:T(128)S(1)} collective-permute-done((f32[16]{0:T(128)S(1)}, f32[16]{0:T(128)S(1)}, u32[]{:S(2)}, u32[]{:S(2)}) %collective-permute-start.21) | collective-permute-done | bytes 96 | tf_op jit(solution)/shard_map/ppermute | solution.py:120
  (104 shorter events, 8.5 us)
Async XLA Ops:
  0.6 6.2 %copy-start.11 = (bf16[1,384,2048]{2,1,0:T(8,128)(2,1)S(1)}, bf16[1,384,2048]{2,1,0:T(8,128)(2,1)}, u32[]{:S(2)}) copy-start(bf16[1,384,2048]{2,1,0:T(8,128)(2,1)} %param.10) | copy-start | bytes 4718596
  6.8 1.6 copy-start.18
  6.8 1.6 copy-start.17
  14.8 2.9 %copy-start.1 = (bf16[48,8,16,128]{3,2,1,0:T(8,128)(2,1)S(1)}, bf16[48,8,16,128]{3,2,1,0:T(8,128)(2,1)}, u32[]{:S(2)}) copy-start(bf16[48,8,16,128]{3,2,1,0:T(8,128)(2,1)} %copy.105) | copy-start | bytes 4718596
  19.4 1.4 copy-start.3
  22.0 15.6 %collective-permute-start = (f32[4,264,128]{2,1,0:T(8,128)}, f32[4,264,128]{2,1,0:T(8,128)}, u32[]{:S(2)}, u32[]{:S(2)}) collective-permute-start(f32[4,264,128]{2,1,0:T(8,128)} %get-tuple-element.63), channel_id=1, source_target_pairs={{0,8},{8,16},{16,24},{24,0},{32,40},{40,48},{48,56},{56,32},{64,72... | collective-permute-start | bytes 1622024 | tf_op jit(solution)/shard_map/ppermute | solution.py:64
  23.6 26.8 %collective-permute-start.1 = (f32[4,264,128]{2,1,0:T(8,128)}, f32[4,264,128]{2,1,0:T(8,128)}, u32[]{:S(2)}, u32[]{:S(2)}) collective-permute-start(f32[4,264,128]{2,1,0:T(8,128)} %get-tuple-element.62), channel_id=1, source_target_pairs={{0,16},{8,24},{16,0},{24,8},{32,48},{40,56},{48,32},{56,40},{64,80... | collective-permute-start | bytes 1622024 | tf_op jit(solution)/shard_map/ppermute | solution.py:64
  26.5 23.9 %collective-permute-start.2 = (f32[4,264,128]{2,1,0:T(8,128)}, f32[4,264,128]{2,1,0:T(8,128)}, u32[]{:S(2)}, u32[]{:S(2)}) collective-permute-start(f32[4,264,128]{2,1,0:T(8,128)} %get-tuple-element.61), channel_id=1, source_target_pairs={{0,24},{8,0},{16,8},{24,16},{32,56},{40,32},{48,40},{56,48},{64,88... | collective-permute-start | bytes 1622024 | tf_op jit(solution)/shard_map/ppermute | solution.py:64
  52.1 2.5 %copy-start.5 = (f32[1,4,264,128]{3,2,1,0:T(8,128)}, f32[1,4,264,128]{3,2,1,0:T(8,128)S(1)}, u32[]{:S(2)}) copy-start(f32[1,4,264,128]{3,2,1,0:T(8,128)S(1)} %get-tuple-element.50) | copy-start | bytes 1622020
  52.1 2.5 %copy-start.6 = (f32[1,4,264,128]{3,2,1,0:T(8,128)}, f32[1,4,264,128]{3,2,1,0:T(8,128)S(1)}, u32[]{:S(2)}) copy-start(f32[1,4,264,128]{3,2,1,0:T(8,128)S(1)} %get-tuple-element.47) | copy-start | bytes 1622020
  52.2 2.5 %copy-start.7 = (f32[1,4,264,128]{3,2,1,0:T(8,128)}, f32[1,4,264,128]{3,2,1,0:T(8,128)S(1)}, u32[]{:S(2)}) copy-start(f32[1,4,264,128]{3,2,1,0:T(8,128)S(1)} %get-tuple-element.48) | copy-start | bytes 1622020
  52.2 2.5 %copy-start.8 = (f32[1,4,264,128]{3,2,1,0:T(8,128)}, f32[1,4,264,128]{3,2,1,0:T(8,128)S(1)}, u32[]{:S(2)}) copy-start(f32[1,4,264,128]{3,2,1,0:T(8,128)S(1)} %get-tuple-element.49) | copy-start | bytes 1622020
  53.6 1.0 copy-start.9
  53.6 2.3 %copy-start.10 = (f32[4,128,128]{2,1,0:T(8,128)}, f32[4,128,128]{2,1,0:T(8,128)S(1)}, u32[]{:S(2)}) copy-start(f32[4,128,128]{2,1,0:T(8,128)S(1)} %get-tuple-element.59) | copy-start | bytes 786436
  54.6 9.9 %collective-permute-start.5 = (f32[4,136,128]{2,1,0:T(8,128)}, f32[4,136,128]{2,1,0:T(8,128)}, u32[]{:S(2)}, u32[]{:S(2)}) collective-permute-start(f32[4,136,128]{2,1,0:T(8,128)} %get-tuple-element.79), channel_id=1, source_target_pairs={{32,0},{40,8},{48,16},{56,24},{64,32},{72,40},{80,48},{88,56},{96,... | collective-permute-start | bytes 835592 | tf_op jit(solution)/shard_map/ppermute | solution.py:43
  56.0 9.8 %collective-permute-start.3 = (f32[4,136,128]{2,1,0:T(8,128)}, f32[4,136,128]{2,1,0:T(8,128)}, u32[]{:S(2)}, u32[]{:S(2)}) collective-permute-start(f32[4,136,128]{2,1,0:T(8,128)} %get-tuple-element.80), channel_id=1, source_target_pairs={{0,32},{8,40},{16,48},{24,56},{32,64},{40,72},{48,80},{56,88},{64,... | collective-permute-start | bytes 835592 | tf_op jit(solution)/shard_map/ppermute | solution.py:42
  67.9 9.8 %collective-permute-start.4 = (f32[4,136,128]{2,1,0:T(8,128)S(1)}, f32[4,136,128]{2,1,0:T(8,128)S(1)}, u32[]{:S(2)}, u32[]{:S(2)}) collective-permute-start(f32[4,136,128]{2,1,0:T(8,128)S(1)} %pad_maximum_fusion.5), channel_id=1, source_target_pairs={{0,64},{8,72},{16,80},{24,88},{32,96},{40,104},{48,112},{56,120},{... | collective-permute-start | bytes 835592 | tf_op jit(solution)/shard_map/ppermute | solution.py:42
  73.7 17.8 %collective-permute-start.6 = (f32[4,136,128]{2,1,0:T(8,128)S(1)}, f32[4,136,128]{2,1,0:T(8,128)S(1)}, u32[]{:S(2)}, u32[]{:S(2)}) collective-permute-start(f32[4,136,128]{2,1,0:T(8,128)S(1)} %pad_maximum_fusion.6), channel_id=1, source_target_pairs={{64,0},{72,8},{80,16},{88,24},{96,32},{104,40},{112,48},{120,56},{... | collective-permute-start | bytes 835592 | tf_op jit(solution)/shard_map/ppermute | solution.py:43
  77.7 13.9 %copy-start.13 = (f32[4,136,128]{2,1,0:T(8,128)}, f32[4,136,128]{2,1,0:T(8,128)S(1)}, u32[]{:S(2)}) copy-start(f32[4,136,128]{2,1,0:T(8,128)S(1)} %collective-permute-done.4) | copy-start | bytes 835588
  91.5 0.9 copy-start.14
  92.4 21.4 %collective-permute-start.7 = (f32[4,136,128]{2,1,0:T(8,128)}, f32[4,136,128]{2,1,0:T(8,128)}, u32[]{:S(2)}, u32[]{:S(2)}) collective-permute-start(f32[4,136,128]{2,1,0:T(8,128)} %maximum_select_fusion), channel_id=1, source_target_pairs={{0,128},{8,136},{16,144},{24,152},{32,160},{40,168},{48,176},{56,1... | collective-permute-start | bytes 835592 | tf_op jit(solution)/shard_map/ppermute | solution.py:38
  114.8 3.6 %copy-start.15 = (f32[4,128,128]{2,1,0:T(8,128)S(1)}, f32[4,128,128]{2,1,0:T(8,128)}, u32[]{:S(2)}) copy-start(f32[4,128,128]{2,1,0:T(8,128)} %get-tuple-element.39) | copy-start | bytes 786436
  119.8 5.9 %copy-start.16 = (pred[384,384]{1,0:T(8,128)(4,1)S(1)}, pred[384,384]{1,0:T(8,128)(4,1)}, u32[]{:S(2)}) copy-start(pred[384,384]{1,0:T(8,128)(4,1)} %fusion.26) | copy-start | bytes 442372
  120.0 5.7 %copy-start = (bf16[1,384,2048]{1,2,0:T(8,128)(2,1)S(1)}, bf16[1,384,2048]{1,2,0:T(8,128)(2,1)}, u32[]{:S(2)}) copy-start(bf16[1,384,2048]{1,2,0:T(8,128)(2,1)} %copy.103) | copy-start | bytes 4718596
  120.0 5.7 %copy-start.2 = (bf16[48,8,16,128]{3,2,1,0:T(8,128)(2,1)S(1)}, bf16[48,8,16,128]{3,2,1,0:T(8,128)(2,1)}, u32[]{:S(2)}) copy-start(bf16[48,8,16,128]{3,2,1,0:T(8,128)(2,1)} %copy.105) | copy-start | bytes 4718596
  120.2 13.6 %collective-permute-start.8 = (f32[4,256,128]{2,1,0:T(8,128)S(1)}, f32[4,256,128]{2,1,0:T(8,128)S(1)}, u32[]{:S(2)}, u32[]{:S(2)}) collective-permute-start(f32[4,256,128]{2,1,0:T(8,128)S(1)} %get-tuple-element.66), channel_id=1, source_target_pairs={{0,8},{8,16},{16,24},{24,0},{32,40},{40,48},{48,56},{56,32},{64,72... | collective-permute-start | bytes 1572872 | tf_op jit(solution)/shard_map/ppermute | solution.py:64
  121.8 23.3 %collective-permute-start.9 = (f32[4,256,128]{2,1,0:T(8,128)S(1)}, f32[4,256,128]{2,1,0:T(8,128)S(1)}, u32[]{:S(2)}, u32[]{:S(2)}) collective-permute-start(f32[4,256,128]{2,1,0:T(8,128)S(1)} %get-tuple-element.65), channel_id=1, source_target_pairs={{0,16},{8,24},{16,0},{24,8},{32,48},{40,56},{48,32},{56,40},{64,80... | collective-permute-start | bytes 1572872 | tf_op jit(solution)/shard_map/ppermute | solution.py:64
  123.2 21.9 %collective-permute-start.10 = (f32[4,256,128]{2,1,0:T(8,128)S(1)}, f32[4,256,128]{2,1,0:T(8,128)S(1)}, u32[]{:S(2)}, u32[]{:S(2)}) collective-permute-start(f32[4,256,128]{2,1,0:T(8,128)S(1)} %get-tuple-element.64), channel_id=1, source_target_pairs={{0,24},{8,0},{16,8},{24,16},{32,56},{40,32},{48,40},{56,48},{64,88... | collective-permute-start | bytes 1572872 | tf_op jit(solution)/shard_map/ppermute | solution.py:64
  156.0 14.5 %collective-permute-start.11 = (f32[16]{0:T(128)S(1)}, f32[16]{0:T(128)S(1)}, u32[]{:S(2)}, u32[]{:S(2)}) collective-permute-start(f32[16]{0:T(128)S(1)} %multiply_reduce_fusion), channel_id=1, source_target_pairs={{0,8},{8,0},{16,24},{24,16},{32,40},{40,32},{48,56},{56,48},{64,72... | collective-permute-start | bytes 200 | tf_op jit(solution)/shard_map/ppermute | solution.py:120
  156.0 14.5 %collective-permute-start.12 = (f32[16]{0:T(128)S(1)}, f32[16]{0:T(128)S(1)}, u32[]{:S(2)}, u32[]{:S(2)}) collective-permute-start(f32[16]{0:T(128)S(1)} %multiply_reduce_fusion), channel_id=1, source_target_pairs={{0,16},{8,24},{16,0},{24,8},{32,48},{40,56},{48,32},{56,40},{64,80... | collective-permute-start | bytes 200 | tf_op jit(solution)/shard_map/ppermute | solution.py:120
  159.7 10.8 %collective-permute-start.13 = (f32[16]{0:T(128)S(1)}, f32[16]{0:T(128)S(1)}, u32[]{:S(2)}, u32[]{:S(2)}) collective-permute-start(f32[16]{0:T(128)S(1)} %multiply_reduce_fusion), channel_id=1, source_target_pairs={{0,24},{8,16},{16,8},{24,0},{32,56},{40,48},{48,40},{56,32},{64,88... | collective-permute-start | bytes 200 | tf_op jit(solution)/shard_map/ppermute | solution.py:120
  167.8 20.6 %copy-start.4 = (bf16[384,16,128]{0,2,1:T(8,128)(2,1)S(1)}, bf16[384,16,128]{0,2,1:T(8,128)(2,1)}, u32[]{:S(2)}) copy-start(bf16[384,16,128]{0,2,1:T(8,128)(2,1)} %get-tuple-element.58) | copy-start | bytes 4718596
  170.5 26.0 %copy-start.12 = (bf16[384,16,128]{0,2,1:T(8,128)(2,1)S(1)}, bf16[384,16,128]{0,2,1:T(8,128)(2,1)}, u32[]{:S(2)}) copy-start(bf16[384,16,128]{0,2,1:T(8,128)(2,1)} %fusion.12) | copy-start | bytes 4718596
  170.5 9.3 %collective-permute-start.14 = (f32[16]{0:T(128)S(1)}, f32[16]{0:T(128)S(1)}, u32[]{:S(2)}, u32[]{:S(2)}) collective-permute-start(f32[16]{0:T(128)S(1)} %fusion.64), channel_id=1, source_target_pairs={{0,32},{8,40},{16,48},{24,56},{32,0},{40,8},{48,16},{56,24},{64,96... | collective-permute-start | bytes 200 | tf_op jit(solution)/shard_map/ppermute | solution.py:120
  170.6 9.3 %collective-permute-start.15 = (f32[16]{0:T(128)S(1)}, f32[16]{0:T(128)S(1)}, u32[]{:S(2)}, u32[]{:S(2)}) collective-permute-start(f32[16]{0:T(128)S(1)} %fusion.64), channel_id=1, source_target_pairs={{0,64},{8,72},{16,80},{24,88},{32,96},{40,104},{48,112},{56,120},{... | collective-permute-start | bytes 200 | tf_op jit(solution)/shard_map/ppermute | solution.py:120
  178.5 5.3 %collective-permute-start.16 = (f32[16]{0:T(128)S(1)}, f32[16]{0:T(128)S(1)}, u32[]{:S(2)}, u32[]{:S(2)}) collective-permute-start(f32[16]{0:T(128)S(1)} %fusion.64), channel_id=1, source_target_pairs={{0,96},{8,104},{16,112},{24,120},{32,64},{40,72},{48,80},{56,88},{... | collective-permute-start | bytes 200 | tf_op jit(solution)/shard_map/ppermute | solution.py:120
  183.8 7.5 %collective-permute-start.17 = (f32[16]{0:T(128)S(1)}, f32[16]{0:T(128)S(1)}, u32[]{:S(2)}, u32[]{:S(2)}) collective-permute-start(f32[16]{0:T(128)S(1)} %fusion.61), channel_id=1, source_target_pairs={{0,128},{8,136},{16,144},{24,152},{32,160},{40,168},{48,176},{56,1... | collective-permute-start | bytes 200 | tf_op jit(solution)/shard_map/ppermute | solution.py:120
  191.3 1.9 collective-permute-start.18
  191.3 3.6 %collective-permute-start.19 = (f32[16]{0:T(128)S(1)}, f32[16]{0:T(128)S(1)}, u32[]{:S(2)}, u32[]{:S(2)}) collective-permute-start(f32[16]{0:T(128)S(1)} %fusion.58), channel_id=1, source_target_pairs={{0,2},{1,3},{2,0},{3,1},{4,6},{5,7},{6,4},{7,5},{8,10},{9,11},{10,... | collective-permute-start | bytes 200 | tf_op jit(solution)/shard_map/ppermute | solution.py:120
  192.3 3.0 %collective-permute-start.20 = (f32[16]{0:T(128)S(1)}, f32[16]{0:T(128)S(1)}, u32[]{:S(2)}, u32[]{:S(2)}) collective-permute-start(f32[16]{0:T(128)S(1)} %fusion.58), channel_id=1, source_target_pairs={{0,3},{1,2},{2,1},{3,0},{4,7},{5,6},{6,5},{7,4},{8,11},{9,10},{10,... | collective-permute-start | bytes 200 | tf_op jit(solution)/shard_map/ppermute | solution.py:120
  195.2 5.1 %collective-permute-start.21 = (f32[16]{0:T(128)S(1)}, f32[16]{0:T(128)S(1)}, u32[]{:S(2)}, u32[]{:S(2)}) collective-permute-start(f32[16]{0:T(128)S(1)} %fusion.57), channel_id=1, source_target_pairs={{0,4},{1,5},{2,6},{3,7},{4,0},{5,1},{6,2},{7,3},{8,12},{9,13},{10,... | collective-permute-start | bytes 200 | tf_op jit(solution)/shard_map/ppermute | solution.py:120

commit v12 on v5

--- a/solution.py
+++ b/solution.py
@@ -105,12 +105,11 @@
     return full[:, :rows], full[:, rows:]
 
 
-def digit_sum(value, axis, step, radix):
-    count = lax.axis_size(axis)
-    digit = (lax.axis_index(axis) // step) % radix
+def digit_sum(value, axes, count, step, radix):
+    digit = (lax.axis_index(axes) // step) % radix
     got = [value]
     for k in range(1, radix):
-        got.append(lax.ppermute(value, axis, [(i, i ^ (k * step)) for i in range(count)]))
+        got.append(lax.ppermute(value, axes, [(i, i ^ (k * step)) for i in range(count)]))
     total = lax.select_n(digit, *got)
     for m in range(1, radix):
         total = total + lax.select_n(digit ^ m, *got)
@@ -118,13 +117,12 @@
 
 
 def all_sum(value, axes):
-    for axis in axes:
-        count = lax.axis_size(axis)
-        step = 1
-        while step < count:
-            radix = 4 if count % (step * 4) == 0 else 2
-            value = digit_sum(value, axis, step, radix)
-            step *= radix
+    count = math.prod(lax.axis_size(axis) for axis in axes)
+    step = 1
+    while step < count:
+        radix = 4 if count % (step * 4) == 0 else 2
+        value = digit_sum(value, axes, count, step, radix)
+        step *= radix
     return value
 
 

time: 196 us -> 203 us (1.036)
  starting transfers between devices: 65.4 us -> 70.4 us
    ppermute x11 -> x12, starting transfers between devices: 20.7 us -> 25.7 us  [digit_sum(): lax.ppermute(value, axes, [(i, i ^ k * step) for i in range(count)])]
    unnamed x42 -> x38, local copies, waits for them, and re-layouts: 14.1 us -> 15.9 us
    ppermute x11 -> x12, waiting for transfers between devices: 14.1 us -> 12.8 us  [digit_sum(): lax.ppermute(value, axes, [(i, i ^ k * step) for i in range(count)])]
  transfers between devices with their start and end apart: 23 -> 24, of which waited for: 15 -> 15; matrix products, arithmetic and copies ran while one was open for 11% -> 12% of each run, Pallas kernels for 0% -> 0%
where the time goes in v12:
time: 203 us; the launch traced here: 200 us
  starting transfers between devices  70.4 us (35%)
  waiting for transfers between devices  64.5 us (32%)
  matrix products  25.4 us (13%)
  local copies, waits for them, and re-layouts  21.5 us (11%)
  other arithmetic  16.6 us (8%)
  between operations  2.09 us (1%)
    ppermute x6, waiting for transfers between devices, row_exchange(): got.append(lax.ppermute(send, axis, pairs))  35.6 us
    ppermute x3, starting transfers between devices, group_scan(): got = lax.ppermute(fwd, axis, up)  28.4 us
    ppermute x12, starting transfers between devices, digit_sum(): lax.ppermute(value, axes, [(i, i ^ k * step) for i in range(count)])  25.7 us
    unnamed x38, local copies, waits for them, and re-layouts  15.9 us
    ppermute x12, waiting for transfers between devices, digit_sum(): lax.ppermute(value, axes, [(i, i ^ k * step) for i in range(count)])  12.8 us
    ppermute x6, starting transfers between devices, row_exchange(): got.append(lax.ppermute(send, axis, pairs))  12.4 us
    ppermute x3, waiting for transfers between devices, group_scan(): rgot = lax.ppermute(bwd, axis, down)  11.3 us
    dot_general x1, matrix products, on_device(): jnp.einsum('hst,shf->thf', attn_prob, gradient_block, preferred_element_t...  7 us
  transfers between devices with their start and end apart: 24, of which 15 were waited for; matrix products, arithmetic and copies ran while one was open for 12% of the time, Pallas kernels for 0%

profile of v12, /device:TPU:6, one launch (start us, length us, event | category | flops | bytes accessed | tf_op | source)
XLA Modules:
  0.0 200.4 jit_solution(15494255107808506140)
XLA Ops:
  0.7 0.9 reduce-window_clone.1
  1.6 0.7 subtract_bitcast_fusion
  4.2 0.7 broadcast_compare_fusion
  4.9 1.9 copy.87
  6.8 1.6 copy.103
  8.5 0.9 reduce-window.24
  9.8 1.9 copy.85
  11.7 3.0 %copy.105 = bf16[48,8,16,128]{3,2,1,0:T(8,128)(2,1)} copy(bf16[48,8,16,128]{3,1,2,0:T(8,128)(2,1)} %bitcast.221) | data formatting | bytes 3145728
  14.8 2.9 %fusion.9 = f32[16,128,128]{2,1,0:T(8,128)S(1)} fusion(bf16[384,16,128]{0,2,1:T(8,128)(2,1)} %bitcast.207, bf16[384,16,128]{0,2,1:T(8,128)(2,1)S(1)} %bitcast.203, f32[384,16]{0,1:T(8,128)S(1)} %get-tuple-element.74), kind=kOutput, calls=%fused_computation.15 | convolution fusion | flops 605552640 | bytes 4218880 | tf_op jit(solution)/shard_map/she,shf->hef/dot_general | solution.py:178
  17.8 1.4 fusion.7
  19.4 1.3 copy-done.3
  20.8 1.2 dynamic-slice_bitcast_fusion
  22.0 1.6 collective-permute-start
  23.6 2.9 %collective-permute-start.1 = (f32[4,264,128]{2,1,0:T(8,128)}, f32[4,264,128]{2,1,0:T(8,128)}, u32[]{:S(2)}, u32[]{:S(2)}) collective-permute-start(f32[4,264,128]{2,1,0:T(8,128)} %get-tuple-element.54), channel_id=1, source_target_pairs={{0,16},{8,24},{16,0},{24,8},{32,48},{40,56},{48,32},{56,40},{64,80... | collective-permute-start | bytes 1622024 | tf_op jit(solution)/shard_map/ppermute | solution.py:57
  26.5 1.3 collective-permute-start.2
  27.9 9.7 %collective-permute-done = f32[4,264,128]{2,1,0:T(8,128)} collective-permute-done((f32[4,264,128]{2,1,0:T(8,128)}, f32[4,264,128]{2,1,0:T(8,128)}, u32[]{:S(2)}, u32[]{:S(2)}) %collective-permute-start) | collective-permute-done | bytes 540704 | tf_op jit(solution)/shard_map/ppermute | solution.py:57
  37.6 12.8 %collective-permute-done.1 = f32[4,264,128]{2,1,0:T(8,128)} collective-permute-done((f32[4,264,128]{2,1,0:T(8,128)}, f32[4,264,128]{2,1,0:T(8,128)}, u32[]{:S(2)}, u32[]{:S(2)}) %collective-permute-start.1) | collective-permute-done | bytes 540704 | tf_op jit(solution)/shard_map/ppermute | solution.py:57
  50.4 1.8 fusion.28
  52.4 1.1 fusion.49
  53.6 0.9 pad_maximum_fusion.4
  54.6 1.3 collective-permute-start.6
  56.3 4.6 %collective-permute-start.3 = (f32[4,136,128]{2,1,0:T(8,128)}, f32[4,136,128]{2,1,0:T(8,128)S(1)}, u32[]{:S(2)}, u32[]{:S(2)}) collective-permute-start(f32[4,136,128]{2,1,0:T(8,128)} %get-tuple-element.75), channel_id=1, source_target_pairs={{0,32},{8,40},{16,48},{24,56},{32,64},{40,72},{48,80},{56,88},{64,... | collective-permute-start | bytes 835592 | tf_op jit(solution)/shard_map/ppermute | solution.py:35
  60.8 3.7 %collective-permute-done.6 = f32[4,136,128]{2,1,0:T(8,128)} collective-permute-done((f32[4,136,128]{2,1,0:T(8,128)}, f32[4,136,128]{2,1,0:T(8,128)}, u32[]{:S(2)}, u32[]{:S(2)}) %collective-permute-start.6) | collective-permute-done | bytes 278560 | tf_op jit(solution)/shard_map/ppermute | solution.py:36
  64.5 0.8 fusion.78
  65.4 0.6 collective-permute-done.3
  66.1 1.2 multiply_add_fusion.9
  67.4 5.7 %collective-permute-start.4 = (f32[4,136,128]{2,1,0:T(8,128)S(1)}, f32[4,136,128]{2,1,0:T(8,128)S(1)}, u32[]{:S(2)}, u32[]{:S(2)}) collective-permute-start(f32[4,136,128]{2,1,0:T(8,128)S(1)} %pad_maximum_fusion.5), channel_id=1, source_target_pairs={{0,64},{8,72},{16,80},{24,88},{32,96},{40,104},{48,112},{56,120},{... | collective-permute-start | bytes 835592 | tf_op jit(solution)/shard_map/ppermute | solution.py:35
  73.2 1.3 collective-permute-start.7
  74.5 0.8 slice_reduce_fusion.2
  75.4 1.8 collective-permute-done.4
  77.4 18.2 %collective-permute-start.5 = (f32[4,136,128]{2,1,0:T(8,128)S(1)}, f32[4,136,128]{2,1,0:T(8,128)S(1)}, u32[]{:S(2)}, u32[]{:S(2)}) collective-permute-start(f32[4,136,128]{2,1,0:T(8,128)S(1)} %pad_maximum_fusion.6), channel_id=1, source_target_pairs={{0,128},{8,136},{16,144},{24,152},{32,160},{40,168},{48,176},{56,1... | collective-permute-start | bytes 835592 | tf_op jit(solution)/shard_map/ppermute | solution.py:35
  95.7 1.3 collective-permute-start.8
  97.2 2.3 %collective-permute-done.5 = f32[4,136,128]{2,1,0:T(8,128)S(1)} collective-permute-done((f32[4,136,128]{2,1,0:T(8,128)S(1)}, f32[4,136,128]{2,1,0:T(8,128)S(1)}, u32[]{:S(2)}, u32[]{:S(2)}) %collective-permute-start.5) | collective-permute-done | bytes 278560 | tf_op jit(solution)/shard_map/ppermute | solution.py:35
  99.6 1.1 multiply_add_fusion.4
  100.7 1.1 multiply_add_fusion.2
  101.8 7.6 %collective-permute-done.8 = f32[4,136,128]{2,1,0:T(8,128)S(1)} collective-permute-done((f32[4,136,128]{2,1,0:T(8,128)S(1)}, f32[4,136,128]{2,1,0:T(8,128)S(1)}, u32[]{:S(2)}, u32[]{:S(2)}) %collective-permute-start.8) | collective-permute-done | bytes 278560 | tf_op jit(solution)/shard_map/ppermute | solution.py:36
  109.4 1.2 multiply_add_fusion.5
  110.6 1.1 multiply_add_fusion.3
  112.2 1.8 collective-permute-start.9
  113.9 4.9 %collective-permute-start.10 = (f32[4,256,128]{2,1,0:T(8,128)S(1)}, f32[4,256,128]{2,1,0:T(8,128)S(1)}, u32[]{:S(2)}, u32[]{:S(2)}) collective-permute-start(f32[4,256,128]{2,1,0:T(8,128)S(1)} %get-tuple-element.57), channel_id=1, source_target_pairs={{0,16},{8,24},{16,0},{24,8},{32,48},{40,56},{48,32},{56,40},{64,80... | collective-permute-start | bytes 1572872 | tf_op jit(solution)/shard_map/ppermute | solution.py:57
  118.8 3.7 %multiply_convert_fusion.1 = bf16[16,384,384]{2,1,0:T(8,128)(2,1)S(1)} fusion(f32[16,384]{1,0:T(8,128)S(1)} %get-tuple-element.71, pred[384,384]{1,0:T(8,128)(4,1)S(1)} %fusion.26, bf16[384,16,128]{0,2,1:T(8,128)(2,1)S(1)} %bitcast.209, bf16[384,16,128]{2,1,0:T(8,128)(2,1)S(1)} %bitcast.212), kind=kOutput, calls=%fused_computation.1 | convolution fusion | flops 615776256 | bytes 8036352 | tf_op jit(solution)/shard_map/shf,thf->hst/dot_general | solution.py:184
  122.5 7.5 %collective-permute-done.9 = f32[4,256,128]{2,1,0:T(8,128)S(1)} collective-permute-done((f32[4,256,128]{2,1,0:T(8,128)S(1)}, f32[4,256,128]{2,1,0:T(8,128)S(1)}, u32[]{:S(2)}, u32[]{:S(2)}) %collective-permute-start.9) | collective-permute-done | bytes 524320 | tf_op jit(solution)/shard_map/ppermute | solution.py:57
  130.1 5.6 %collective-permute-done.10 = f32[4,256,128]{2,1,0:T(8,128)S(1)} collective-permute-done((f32[4,256,128]{2,1,0:T(8,128)S(1)}, f32[4,256,128]{2,1,0:T(8,128)S(1)}, u32[]{:S(2)}, u32[]{:S(2)}) %collective-permute-start.10) | collective-permute-done | bytes 524320 | tf_op jit(solution)/shard_map/ppermute | solution.py:57
  136.1 1.0 fusion.21
  137.1 1.4 fusion.17
  138.6 2.7 %fusion.23 = f32[16,128,384]{2,1,0:T(8,128)} fusion(bf16[384,16,128]{0,2,1:T(8,128)(2,1)S(1)} %bitcast.199, f32[16,256,128]{2,1,0:T(8,128)S(1)} %bitcast.216), kind=kOutput, calls=%fused_computation.35 | convolution fusion | flops 603979776 | bytes 5767168 | tf_op jit(solution)/shard_map/the,hef->thf/dot_general | solution.py:192
  141.3 2.7 %fusion.10 = (f32[384,16]{0,1:T(8,128)S(1)}, bf16[384,16,128]{0,2,1:T(8,128)(2,1)}) fusion(bf16[384,16,128]{0,2,1:T(8,128)(2,1)S(1)} %bitcast.204, f32[16,128,384]{2,1,0:T(8,128)S(1)} %fusion.21, f32[384,16]{0,1:T(8,128)S(1)} %get-tuple-element.74, bf16[16,384,384]{2,1,0:T(8,128)(2,1)S(1)} %multiply_convert_fusion.1, bf16[384,16,128]{0,2,1:T(8,128)(2,1)S(1)} %bitcast.200), kind=kOutput, calls=%fused_computation.16 | convolution fusion | flops 608692224 | bytes 12632064 | tf_op jit(solution)/shard_map/hst,the->she/dot_general | solution.py:195
  144.0 2.4 %fusion.8 = (f32[384,16]{0,1:T(8,128)S(1)}, bf16[384,16,128]{0,2,1:T(8,128)(2,1)}) fusion(bf16[384,16,128]{0,2,1:T(8,128)(2,1)S(1)} %bitcast.201, f32[16,128,384]{2,1,0:T(8,128)S(1)} %fusion.17, f32[384,16]{0,1:T(8,128)S(1)} %get-tuple-element.73, bf16[384,16,128]{0,2,1:T(8,128)(2,1)S(1)} %bitcast.205, bf16[16,384,384]{2,1,0:T(8,128)(2,1)S(1)} %multiply_convert_fusion.1), kind=kOutput, calls=%fused_computation.14 | convolution fusion | flops 608692224 | bytes 12632064 | tf_op jit(solution)/shard_map/hst,she->the/dot_general | solution.py:201
  146.7 0.9 collective-permute-start.13
  147.6 0.9 collective-permute-start.14
  148.5 2.6 %copy.96 = bf16[1,384,2048]{2,1,0:T(8,128)(2,1)} copy(bf16[1,384,2048]{1,2,0:T(8,128)(2,1)} %bitcast.219) | data formatting | bytes 3145728
  151.1 2.6 %copy.97 = bf16[1,384,2048]{2,1,0:T(8,128)(2,1)} copy(bf16[1,384,2048]{1,2,0:T(8,128)(2,1)} %bitcast.220) | data formatting | bytes 3145728
  153.7 7.0 %fusion.12 = bf16[384,16,128]{0,2,1:T(8,128)(2,1)} fusion(f32[16,128,384]{2,1,0:T(8,128)} %fusion.23, bf16[384,16,128]{0,2,1:T(8,128)(2,1)} %bitcast.208, f32[16,384]{1,0:T(8,128)S(1)} %get-tuple-element.71, pred[384,384]{1,0:T(8,128)(4,1)S(1)} %copy-done.13, bf16[384,16,128]{0,2,1:T(8,128)(2,1)S(1)} %bitcast.206, bf16[384,16,128]{0,2,1:T(8,128)(2,1)S(1)} %bitcast.202, ...), kind=kOutput, calls=%fused_computation.19 | convolution fusion | flops 1222115328 | bytes 9633792 | tf_op jit(solution)/shard_map/hst,shf->thf/dot_general | solution.py:189
  160.7 2.6 %copy.98 = bf16[1,384,2048]{2,1,0:T(8,128)(2,1)} copy(bf16[1,384,2048]{1,2,0:T(8,128)(2,1)} %bitcast.222) | data formatting | bytes 3145728
  163.3 1.5 collective-permute-start.15
  165.1 3.3 %collective-permute-start.17 = (f32[16]{0:T(128)S(1)}, f32[16]{0:T(128)S(1)}, u32[]{:S(2)}, u32[]{:S(2)}) collective-permute-start(f32[16]{0:T(128)S(1)} %fusion.66), channel_id=1, source_target_pairs={{0,12},{1,13},{2,14},{3,15},{4,8},{5,9},{6,10},{7,11},{8,4},{9,5},... | collective-permute-start | bytes 200 | tf_op jit(solution)/shard_map/ppermute | solution.py:112
  168.5 2.6 %collective-permute-done.17 = f32[16]{0:T(128)S(1)} collective-permute-done((f32[16]{0:T(128)S(1)}, f32[16]{0:T(128)S(1)}, u32[]{:S(2)}, u32[]{:S(2)}) %collective-permute-start.17) | collective-permute-done | bytes 96 | tf_op jit(solution)/shard_map/ppermute | solution.py:112
  171.1 3.4 %collective-permute-start.18 = (f32[16]{0:T(128)S(1)}, f32[16]{0:T(128)S(1)}, u32[]{:S(2)}, u32[]{:S(2)}) collective-permute-start(f32[16]{0:T(128)S(1)} %fusion.63), channel_id=1, source_target_pairs={{0,16},{1,17},{2,18},{3,19},{4,20},{5,21},{6,22},{7,23},{8,24},{9,... | collective-permute-start | bytes 200 | tf_op jit(solution)/shard_map/ppermute | solution.py:112
  174.5 3.1 %collective-permute-start.19 = (f32[16]{0:T(128)S(1)}, f32[16]{0:T(128)S(1)}, u32[]{:S(2)}, u32[]{:S(2)}) collective-permute-start(f32[16]{0:T(128)S(1)} %fusion.63), channel_id=1, source_target_pairs={{0,32},{1,33},{2,34},{3,35},{4,36},{5,37},{6,38},{7,39},{8,40},{9,... | collective-permute-start | bytes 200 | tf_op jit(solution)/shard_map/ppermute | solution.py:112
  177.8 1.3 collective-permute-done.19
  179.1 4.4 %collective-permute-done.20 = f32[16]{0:T(128)S(1)} collective-permute-done((f32[16]{0:T(128)S(1)}, f32[16]{0:T(128)S(1)}, u32[]{:S(2)}, u32[]{:S(2)}) %collective-permute-start.20) | collective-permute-done | bytes 96 | tf_op jit(solution)/shard_map/ppermute | solution.py:112
  183.9 11.5 %collective-permute-start.23 = (f32[16]{0:T(128)S(1)}, f32[16]{0:T(128)S(1)}, u32[]{:S(2)}, u32[]{:S(2)}) collective-permute-start(f32[16]{0:T(128)S(1)} %fusion.60), channel_id=1, source_target_pairs={{0,192},{1,193},{2,194},{3,195},{4,196},{5,197},{6,198},{7,199},{8... | collective-permute-start | bytes 200 | tf_op jit(solution)/shard_map/ppermute | solution.py:112
  195.4 1.5 collective-permute-done.23
  196.9 2.9 %collective-permute-done.21 = f32[16]{0:T(128)S(1)} collective-permute-done((f32[16]{0:T(128)S(1)}, f32[16]{0:T(128)S(1)}, u32[]{:S(2)}, u32[]{:S(2)}) %collective-permute-start.21) | collective-permute-done | bytes 96 | tf_op jit(solution)/shard_map/ppermute | solution.py:112
  (100 shorter events, 6.3 us)
Async XLA Ops:
  0.6 6.2 %copy-start.10 = (bf16[1,384,2048]{2,1,0:T(8,128)(2,1)S(1)}, bf16[1,384,2048]{2,1,0:T(8,128)(2,1)}, u32[]{:S(2)}) copy-start(bf16[1,384,2048]{2,1,0:T(8,128)(2,1)} %param.10) | copy-start | bytes 4718596
  6.8 1.6 copy-start.15
  6.8 1.6 copy-start.14
  14.8 2.9 %copy-start.1 = (bf16[48,8,16,128]{3,2,1,0:T(8,128)(2,1)S(1)}, bf16[48,8,16,128]{3,2,1,0:T(8,128)(2,1)}, u32[]{:S(2)}) copy-start(bf16[48,8,16,128]{3,2,1,0:T(8,128)(2,1)} %copy.105) | copy-start | bytes 4718596
  19.4 1.4 copy-start.3
  22.0 15.6 %collective-permute-start = (f32[4,264,128]{2,1,0:T(8,128)}, f32[4,264,128]{2,1,0:T(8,128)}, u32[]{:S(2)}, u32[]{:S(2)}) collective-permute-start(f32[4,264,128]{2,1,0:T(8,128)} %get-tuple-element.55), channel_id=1, source_target_pairs={{0,8},{8,16},{16,24},{24,0},{32,40},{40,48},{48,56},{56,32},{64,72... | collective-permute-start | bytes 1622024 | tf_op jit(solution)/shard_map/ppermute | solution.py:57
  23.6 26.8 %collective-permute-start.1 = (f32[4,264,128]{2,1,0:T(8,128)}, f32[4,264,128]{2,1,0:T(8,128)}, u32[]{:S(2)}, u32[]{:S(2)}) collective-permute-start(f32[4,264,128]{2,1,0:T(8,128)} %get-tuple-element.54), channel_id=1, source_target_pairs={{0,16},{8,24},{16,0},{24,8},{32,48},{40,56},{48,32},{56,40},{64,80... | collective-permute-start | bytes 1622024 | tf_op jit(solution)/shard_map/ppermute | solution.py:57
  26.5 23.9 %collective-permute-start.2 = (f32[4,264,128]{2,1,0:T(8,128)}, f32[4,264,128]{2,1,0:T(8,128)}, u32[]{:S(2)}, u32[]{:S(2)}) collective-permute-start(f32[4,264,128]{2,1,0:T(8,128)} %get-tuple-element.53), channel_id=1, source_target_pairs={{0,24},{8,0},{16,8},{24,16},{32,56},{40,32},{48,40},{56,48},{64,88... | collective-permute-start | bytes 1622024 | tf_op jit(solution)/shard_map/ppermute | solution.py:57
  52.1 2.4 %copy-start.4 = (f32[1,4,264,128]{3,2,1,0:T(8,128)}, f32[1,4,264,128]{3,2,1,0:T(8,128)S(1)}, u32[]{:S(2)}) copy-start(f32[1,4,264,128]{3,2,1,0:T(8,128)S(1)} %get-tuple-element.40) | copy-start | bytes 1622020
  52.1 2.4 %copy-start.5 = (f32[1,4,264,128]{3,2,1,0:T(8,128)}, f32[1,4,264,128]{3,2,1,0:T(8,128)S(1)}, u32[]{:S(2)}) copy-start(f32[1,4,264,128]{3,2,1,0:T(8,128)S(1)} %get-tuple-element.42) | copy-start | bytes 1622020
  52.2 2.4 %copy-start.6 = (f32[1,4,264,128]{3,2,1,0:T(8,128)}, f32[1,4,264,128]{3,2,1,0:T(8,128)S(1)}, u32[]{:S(2)}) copy-start(f32[1,4,264,128]{3,2,1,0:T(8,128)S(1)} %get-tuple-element.41) | copy-start | bytes 1622020
  52.2 2.4 %copy-start.7 = (f32[1,4,264,128]{3,2,1,0:T(8,128)}, f32[1,4,264,128]{3,2,1,0:T(8,128)S(1)}, u32[]{:S(2)}) copy-start(f32[1,4,264,128]{3,2,1,0:T(8,128)S(1)} %get-tuple-element.39) | copy-start | bytes 1622020
  53.5 1.0 copy-start.8
  53.5 2.4 %copy-start.9 = (f32[4,128,128]{2,1,0:T(8,128)}, f32[4,128,128]{2,1,0:T(8,128)S(1)}, u32[]{:S(2)}) copy-start(f32[4,128,128]{2,1,0:T(8,128)S(1)} %get-tuple-element.51) | copy-start | bytes 786436
  54.6 9.9 %collective-permute-start.6 = (f32[4,136,128]{2,1,0:T(8,128)}, f32[4,136,128]{2,1,0:T(8,128)}, u32[]{:S(2)}, u32[]{:S(2)}) collective-permute-start(f32[4,136,128]{2,1,0:T(8,128)} %get-tuple-element.76), channel_id=1, source_target_pairs={{32,0},{40,8},{48,16},{56,24},{64,32},{72,40},{80,48},{88,56},{96,... | collective-permute-start | bytes 835592 | tf_op jit(solution)/shard_map/ppermute | solution.py:36
  56.2 62.6 %copy-start.12 = (pred[384,384]{1,0:T(8,128)(4,1)}, pred[384,384]{1,0:T(8,128)(4,1)S(1)}, u32[]{:S(2)}) copy-start(pred[384,384]{1,0:T(8,128)(4,1)S(1)} %fusion.26) | copy-start | bytes 442372
  56.3 9.8 %collective-permute-start.3 = (f32[4,136,128]{2,1,0:T(8,128)}, f32[4,136,128]{2,1,0:T(8,128)S(1)}, u32[]{:S(2)}, u32[]{:S(2)}) collective-permute-start(f32[4,136,128]{2,1,0:T(8,128)} %get-tuple-element.75), channel_id=1, source_target_pairs={{0,32},{8,40},{16,48},{24,56},{32,64},{40,72},{48,80},{56,88},{64,... | collective-permute-start | bytes 835592 | tf_op jit(solution)/shard_map/ppermute | solution.py:35
  67.4 9.8 %collective-permute-start.4 = (f32[4,136,128]{2,1,0:T(8,128)S(1)}, f32[4,136,128]{2,1,0:T(8,128)S(1)}, u32[]{:S(2)}, u32[]{:S(2)}) collective-permute-start(f32[4,136,128]{2,1,0:T(8,128)S(1)} %pad_maximum_fusion.5), channel_id=1, source_target_pairs={{0,64},{8,72},{16,80},{24,88},{32,96},{40,104},{48,112},{56,120},{... | collective-permute-start | bytes 835592 | tf_op jit(solution)/shard_map/ppermute | solution.py:35
  73.2 22.3 %collective-permute-start.7 = (f32[4,136,128]{2,1,0:T(8,128)S(1)}, f32[4,136,128]{2,1,0:T(8,128)S(1)}, u32[]{:S(2)}, u32[]{:S(2)}) collective-permute-start(f32[4,136,128]{2,1,0:T(8,128)S(1)} %pad_maximum_fusion.7), channel_id=1, source_target_pairs={{64,0},{72,8},{80,16},{88,24},{96,32},{104,40},{112,48},{120,56},{... | collective-permute-start | bytes 835592 | tf_op jit(solution)/shard_map/ppermute | solution.py:36
  75.4 25.2 %copy-start.11 = (f32[4,128,128]{2,1,0:T(8,128)S(1)}, f32[4,128,128]{2,1,0:T(8,128)}, u32[]{:S(2)}) copy-start(f32[4,128,128]{2,1,0:T(8,128)} %get-tuple-element.31) | copy-start | bytes 786436
  77.4 22.2 %collective-permute-start.5 = (f32[4,136,128]{2,1,0:T(8,128)S(1)}, f32[4,136,128]{2,1,0:T(8,128)S(1)}, u32[]{:S(2)}, u32[]{:S(2)}) collective-permute-start(f32[4,136,128]{2,1,0:T(8,128)S(1)} %pad_maximum_fusion.6), channel_id=1, source_target_pairs={{0,128},{8,136},{16,144},{24,152},{32,160},{40,168},{48,176},{56,1... | collective-permute-start | bytes 835592 | tf_op jit(solution)/shard_map/ppermute | solution.py:35
  95.7 13.7 %collective-permute-start.8 = (f32[4,136,128]{2,1,0:T(8,128)S(1)}, f32[4,136,128]{2,1,0:T(8,128)S(1)}, u32[]{:S(2)}, u32[]{:S(2)}) collective-permute-start(f32[4,136,128]{2,1,0:T(8,128)S(1)} %pad_maximum_fusion.8), channel_id=1, source_target_pairs={{128,0},{136,8},{144,16},{152,24},{160,32},{168,40},{176,48},{184,... | collective-permute-start | bytes 835592 | tf_op jit(solution)/shard_map/ppermute | solution.py:36
  112.0 6.8 %copy-start = (bf16[1,384,2048]{1,2,0:T(8,128)(2,1)S(1)}, bf16[1,384,2048]{1,2,0:T(8,128)(2,1)}, u32[]{:S(2)}) copy-start(bf16[1,384,2048]{1,2,0:T(8,128)(2,1)} %copy.103) | copy-start | bytes 4718596
  112.0 6.8 %copy-start.2 = (bf16[48,8,16,128]{3,2,1,0:T(8,128)(2,1)S(1)}, bf16[48,8,16,128]{3,2,1,0:T(8,128)(2,1)}, u32[]{:S(2)}) copy-start(bf16[48,8,16,128]{3,2,1,0:T(8,128)(2,1)} %copy.105) | copy-start | bytes 4718596
  112.2 17.9 %collective-permute-start.9 = (f32[4,256,128]{2,1,0:T(8,128)S(1)}, f32[4,256,128]{2,1,0:T(8,128)S(1)}, u32[]{:S(2)}, u32[]{:S(2)}) collective-permute-start(f32[4,256,128]{2,1,0:T(8,128)S(1)} %get-tuple-element.58), channel_id=1, source_target_pairs={{0,8},{8,16},{16,24},{24,0},{32,40},{40,48},{48,56},{56,32},{64,72... | collective-permute-start | bytes 1572872 | tf_op jit(solution)/shard_map/ppermute | solution.py:57
  113.9 21.8 %collective-permute-start.10 = (f32[4,256,128]{2,1,0:T(8,128)S(1)}, f32[4,256,128]{2,1,0:T(8,128)S(1)}, u32[]{:S(2)}, u32[]{:S(2)}) collective-permute-start(f32[4,256,128]{2,1,0:T(8,128)S(1)} %get-tuple-element.57), channel_id=1, source_target_pairs={{0,16},{8,24},{16,0},{24,8},{32,48},{40,56},{48,32},{56,40},{64,80... | collective-permute-start | bytes 1572872 | tf_op jit(solution)/shard_map/ppermute | solution.py:57
  118.8 16.9 %collective-permute-start.11 = (f32[4,256,128]{2,1,0:T(8,128)S(1)}, f32[4,256,128]{2,1,0:T(8,128)S(1)}, u32[]{:S(2)}, u32[]{:S(2)}) collective-permute-start(f32[4,256,128]{2,1,0:T(8,128)S(1)} %get-tuple-element.56), channel_id=1, source_target_pairs={{0,24},{8,0},{16,8},{24,16},{32,56},{40,32},{48,40},{56,48},{64,88... | collective-permute-start | bytes 1572872 | tf_op jit(solution)/shard_map/ppermute | solution.py:57
  146.6 16.7 %collective-permute-start.12 = (f32[16]{0:T(128)S(1)}, f32[16]{0:T(128)S(1)}, u32[]{:S(2)}, u32[]{:S(2)}) collective-permute-start(f32[16]{0:T(128)S(1)} %multiply_reduce_fusion), channel_id=1, source_target_pairs={{0,1},{1,0},{2,3},{3,2},{4,5},{5,4},{6,7},{7,6},{8,9},{9,8},{10,11... | collective-permute-start | bytes 200 | tf_op jit(solution)/shard_map/ppermute | solution.py:112
  146.7 16.6 %collective-permute-start.13 = (f32[16]{0:T(128)S(1)}, f32[16]{0:T(128)S(1)}, u32[]{:S(2)}, u32[]{:S(2)}) collective-permute-start(f32[16]{0:T(128)S(1)} %multiply_reduce_fusion), channel_id=1, source_target_pairs={{0,2},{1,3},{2,0},{3,1},{4,6},{5,7},{6,4},{7,5},{8,10},{9,11},{10,... | collective-permute-start | bytes 200 | tf_op jit(solution)/shard_map/ppermute | solution.py:112
  147.6 15.7 %collective-permute-start.14 = (f32[16]{0:T(128)S(1)}, f32[16]{0:T(128)S(1)}, u32[]{:S(2)}, u32[]{:S(2)}) collective-permute-start(f32[16]{0:T(128)S(1)} %multiply_reduce_fusion), channel_id=1, source_target_pairs={{0,3},{1,2},{2,1},{3,0},{4,7},{5,6},{6,5},{7,4},{8,11},{9,10},{10,... | collective-permute-start | bytes 200 | tf_op jit(solution)/shard_map/ppermute | solution.py:112
  151.1 2.6 %copy-start.13 = (pred[384,384]{1,0:T(8,128)(4,1)S(1)}, pred[384,384]{1,0:T(8,128)(4,1)}, u32[]{:S(2)}) copy-start(pred[384,384]{1,0:T(8,128)(4,1)} %copy-done.12) | copy-start | bytes 442372
  163.3 5.1 %collective-permute-start.15 = (f32[16]{0:T(128)S(1)}, f32[16]{0:T(128)S(1)}, u32[]{:S(2)}, u32[]{:S(2)}) collective-permute-start(f32[16]{0:T(128)S(1)} %fusion.66), channel_id=1, source_target_pairs={{0,4},{1,5},{2,6},{3,7},{4,0},{5,1},{6,2},{7,3},{8,12},{9,13},{10,... | collective-permute-start | bytes 200 | tf_op jit(solution)/shard_map/ppermute | solution.py:112
  164.9 3.6 %collective-permute-start.16 = (f32[16]{0:T(128)S(1)}, f32[16]{0:T(128)S(1)}, u32[]{:S(2)}, u32[]{:S(2)}) collective-permute-start(f32[16]{0:T(128)S(1)} %fusion.66), channel_id=1, source_target_pairs={{0,8},{1,9},{2,10},{3,11},{4,12},{5,13},{6,14},{7,15},{8,0},{9,1},... | collective-permute-start | bytes 200 | tf_op jit(solution)/shard_map/ppermute | solution.py:112
  165.1 5.9 %collective-permute-start.17 = (f32[16]{0:T(128)S(1)}, f32[16]{0:T(128)S(1)}, u32[]{:S(2)}, u32[]{:S(2)}) collective-permute-start(f32[16]{0:T(128)S(1)} %fusion.66), channel_id=1, source_target_pairs={{0,12},{1,13},{2,14},{3,15},{4,8},{5,9},{6,10},{7,11},{8,4},{9,5},... | collective-permute-start | bytes 200 | tf_op jit(solution)/shard_map/ppermute | solution.py:112
  171.1 6.8 %collective-permute-start.18 = (f32[16]{0:T(128)S(1)}, f32[16]{0:T(128)S(1)}, u32[]{:S(2)}, u32[]{:S(2)}) collective-permute-start(f32[16]{0:T(128)S(1)} %fusion.63), channel_id=1, source_target_pairs={{0,16},{1,17},{2,18},{3,19},{4,20},{5,21},{6,22},{7,23},{8,24},{9,... | collective-permute-start | bytes 200 | tf_op jit(solution)/shard_map/ppermute | solution.py:112
  174.5 4.6 %collective-permute-start.19 = (f32[16]{0:T(128)S(1)}, f32[16]{0:T(128)S(1)}, u32[]{:S(2)}, u32[]{:S(2)}) collective-permute-start(f32[16]{0:T(128)S(1)} %fusion.63), channel_id=1, source_target_pairs={{0,32},{1,33},{2,34},{3,35},{4,36},{5,37},{6,38},{7,39},{8,40},{9,... | collective-permute-start | bytes 200 | tf_op jit(solution)/shard_map/ppermute | solution.py:112
  177.6 5.9 %collective-permute-start.20 = (f32[16]{0:T(128)S(1)}, f32[16]{0:T(128)S(1)}, u32[]{:S(2)}, u32[]{:S(2)}) collective-permute-start(f32[16]{0:T(128)S(1)} %fusion.63), channel_id=1, source_target_pairs={{0,48},{1,49},{2,50},{3,51},{4,52},{5,53},{6,54},{7,55},{8,56},{9,... | collective-permute-start | bytes 200 | tf_op jit(solution)/shard_map/ppermute | solution.py:112
  183.5 11.9 %collective-permute-start.22 = (f32[16]{0:T(128)S(1)}, f32[16]{0:T(128)S(1)}, u32[]{:S(2)}, u32[]{:S(2)}) collective-permute-start(f32[16]{0:T(128)S(1)} %fusion.60), channel_id=1, source_target_pairs={{0,128},{1,129},{2,130},{3,131},{4,132},{5,133},{6,134},{7,135},{8... | collective-permute-start | bytes 200 | tf_op jit(solution)/shard_map/ppermute | solution.py:112
  183.9 13.1 %collective-permute-start.23 = (f32[16]{0:T(128)S(1)}, f32[16]{0:T(128)S(1)}, u32[]{:S(2)}, u32[]{:S(2)}) collective-permute-start(f32[16]{0:T(128)S(1)} %fusion.60), channel_id=1, source_target_pairs={{0,192},{1,193},{2,194},{3,195},{4,196},{5,197},{6,198},{7,199},{8... | collective-permute-start | bytes 200 | tf_op jit(solution)/shard_map/ppermute | solution.py:112
  195.4 4.4 %collective-permute-start.21 = (f32[16]{0:T(128)S(1)}, f32[16]{0:T(128)S(1)}, u32[]{:S(2)}, u32[]{:S(2)}) collective-permute-start(f32[16]{0:T(128)S(1)} %fusion.60), channel_id=1, source_target_pairs={{0,64},{1,65},{2,66},{3,67},{4,68},{5,69},{6,70},{7,71},{8,72},{9,... | collective-permute-start | bytes 200 | tf_op jit(solution)/shard_map/ppermute | solution.py:112

commit v13 on v5

--- a/solution.py
+++ b/solution.py
@@ -46,15 +46,28 @@
 def row_exchange(parts, axis, group):
     count = lax.axis_size(axis)
     place = lax.axis_index(axis) % group
-    got = [lax.dynamic_index_in_dim(parts, place, 0, False)]
-    for step in range(1, group):
-        pairs = [
+
+    def ring(step):
+        return [
             (base + j, base + (j + step) % group)
             for base in range(0, count, group)
             for j in range(group)
         ]
-        send = lax.dynamic_index_in_dim(parts, (place + step) % group, 0, False)
-        got.append(lax.ppermute(send, axis, pairs))
+
+    def piece(step):
+        return lax.dynamic_index_in_dim(parts, (place + step) % group, 0, False)
+
+    got = [lax.dynamic_index_in_dim(parts, place, 0, False)]
+    if group != 4 or parts.shape[1] % 2:
+        got += [lax.ppermute(piece(step), axis, ring(step)) for step in range(1, group)]
+    else:
+        half = parts.shape[1] // 2
+        far = piece(2)
+        near = lax.ppermute(far[:half], axis, ring(2))
+        first = lax.ppermute(piece(1), axis, ring(1))
+        back = lax.ppermute(jnp.concatenate([piece(3), far[half:]], axis=0), axis, ring(3))
+        relay = lax.ppermute(back[parts.shape[1] :], axis, ring(3))
+        got += [first, jnp.concatenate([near, relay], axis=0), back[: parts.shape[1]]]
     return jnp.stack([lax.select_n((place - j) % group, *got) for j in range(group)])
 
 

time: 196 us -> 209 us (1.066)
  local copies, waits for them, and re-layouts: 19.7 us -> 25.7 us
  waiting for transfers between devices: 65.9 us -> 71.5 us
  other arithmetic: 16.6 us -> 14.1 us
    ppermute x6 -> x8, starting transfers between devices: 12.4 us -> 18 us  [the longest x2 6.7 us: row_exchange(): lax.ppermute(jnp.concatenate([piece(3), far[half:]], axis=0), axis, ring(3))]
    ppermute x6 -> x8, waiting for transfers between devices: 35.6 us -> 40.2 us  [the longest x2 29.9 us: row_exchange(): lax.ppermute(jnp.concatenate([piece(3), far[half:]], axis=0), axis, ring(3))]
    ppermute x3, waiting for transfers between devices: 4.74 us -> 8.89 us  [group_scan(): got = lax.ppermute(fwd, axis, up)]
    another operation x3 -> x5, other arithmetic: 2.17 us -> 6.17 us  [row_exchange(): jnp.stack([lax.select_n((place - j) % group, *got) for j in range(group)])]
    unnamed x42 -> x44, local copies, waits for them, and re-layouts: 14.1 us -> 17.5 us
    ppermute x3, waiting for transfers between devices: 11.4 us -> 8.36 us  [group_scan(): rgot = lax.ppermute(bwd, axis, down)]
  transfers between devices with their start and end apart: 23 -> 25, of which waited for: 15 -> 16; matrix products, arithmetic and copies ran while one was open for 11% -> 12% of each run, Pallas kernels for 0% -> 0%
where the time goes in v13:
time: 209 us; the launch traced here: 207 us
  waiting for transfers between devices  71.5 us (34%)
  starting transfers between devices  67.2 us (32%)
  matrix products  26.9 us (13%)
  local copies, waits for them, and re-layouts  25.7 us (12%)
  other arithmetic  14.1 us (7%)
    ppermute x2, waiting for transfers between devices, row_exchange(): lax.ppermute(jnp.concatenate([piece(3), far[half:]], axis=0), axis, ring(3))  29.9 us
    ppermute x3, starting transfers between devices, group_scan(): got = lax.ppermute(fwd, axis, up)  26.5 us
    ppermute x11, starting transfers between devices, digit_sum(): lax.ppermute(value, axis, [(i, i ^ k * step) for i in range(count)])  18.9 us
    unnamed x44, local copies, waits for them, and re-layouts  17.5 us
    ppermute x11, waiting for transfers between devices, digit_sum(): lax.ppermute(value, axis, [(i, i ^ k * step) for i in range(count)])  14.1 us
    ppermute x2, waiting for transfers between devices, row_exchange(): relay = lax.ppermute(back[parts.shape[1]:], axis, ring(3))  9.64 us
    ppermute x3, waiting for transfers between devices, group_scan(): got = lax.ppermute(fwd, axis, up)  8.89 us
    ppermute x3, waiting for transfers between devices, group_scan(): rgot = lax.ppermute(bwd, axis, down)  8.36 us
  transfers between devices with their start and end apart: 25, of which 16 were waited for; matrix products, arithmetic and copies ran while one was open for 12% of the time, Pallas kernels for 0%

profile of v13, /device:TPU:6, one launch (start us, length us, event | category | flops | bytes accessed | tf_op | source)
XLA Modules:
  0.0 207.5 jit_solution(7289188792562523693)
XLA Ops:
  0.7 0.9 reduce-window_clone.1
  4.9 1.9 copy.115
  6.8 1.6 copy.131
  9.8 1.9 copy.113
  11.7 3.0 %copy.133 = bf16[48,8,16,128]{3,2,1,0:T(8,128)(2,1)} copy(bf16[48,8,16,128]{3,1,2,0:T(8,128)(2,1)} %bitcast.229) | data formatting | bytes 3145728
  14.8 2.9 %fusion.9 = f32[16,128,128]{2,1,0:T(8,128)S(1)} fusion(bf16[384,16,128]{0,2,1:T(8,128)(2,1)} %bitcast.213, bf16[384,16,128]{0,2,1:T(8,128)(2,1)S(1)} %bitcast.207, f32[384,16]{0,1:T(8,128)S(1)} %get-tuple-element.78), kind=kOutput, calls=%fused_computation.15 | convolution fusion | flops 605552640 | bytes 4218880 | tf_op jit(solution)/shard_map/she,shf->hef/dot_general | solution.py:193
  17.8 1.4 fusion.7
  19.4 1.0 dynamic-slice_bitcast_fusion
  21.0 3.0 %collective-permute-start.2 = (f32[6,264,128]{2,1,0:T(8,128)S(1)}, f32[6,264,128]{2,1,0:T(8,128)S(1)}, u32[]{:S(2)}, u32[]{:S(2)}) collective-permute-start(f32[6,264,128]{2,1,0:T(8,128)S(1)} %pad_maximum_fusion.3), channel_id=1, source_target_pairs={{0,24},{8,0},{16,8},{24,16},{32,56},{40,32},{48,40},{56,48},{64,88... | collective-permute-start | bytes 2433032 | tf_op jit(solution)/shard_map/ppermute | solution.py:68
  24.0 2.2 %collective-permute-start.1 = (f32[2,264,128]{2,1,0:T(8,128)S(1)}, f32[2,264,128]{2,1,0:T(8,128)}, u32[]{:S(2)}, u32[]{:S(2)}) collective-permute-start(f32[2,264,128]{2,1,0:T(8,128)S(1)} %get-tuple-element.58), channel_id=1, source_target_pairs={{0,16},{8,24},{16,0},{24,8},{32,48},{40,56},{48,32},{56,40},{64,80... | collective-permute-start | bytes 811016 | tf_op jit(solution)/shard_map/ppermute | solution.py:66
  26.2 20.9 %collective-permute-done.2 = f32[6,264,128]{2,1,0:T(8,128)S(1)} collective-permute-done((f32[6,264,128]{2,1,0:T(8,128)S(1)}, f32[6,264,128]{2,1,0:T(8,128)S(1)}, u32[]{:S(2)}, u32[]{:S(2)}) %collective-permute-start.2) | collective-permute-done | bytes 811040 | tf_op jit(solution)/shard_map/ppermute | solution.py:68
  47.1 0.9 copy-done.8
  48.7 3.7 %collective-permute-start.3 = (f32[2,264,128]{2,1,0:T(8,128)}, f32[2,264,128]{2,1,0:T(8,128)}, u32[]{:S(2)}, u32[]{:S(2)}) collective-permute-start(f32[2,264,128]{2,1,0:T(8,128)} %slice.251), channel_id=1, source_target_pairs={{0,24},{8,0},{16,8},{24,16},{32,56},{40,32},{48,40},{56,48},{64,88... | collective-permute-start | bytes 811016 | tf_op jit(solution)/shard_map/ppermute | solution.py:69
  52.4 1.0 constant_dynamic-update-slice_fusion.1
  53.4 3.8 %collective-permute-done.3 = f32[2,264,128]{2,1,0:T(8,128)} collective-permute-done((f32[2,264,128]{2,1,0:T(8,128)}, f32[2,264,128]{2,1,0:T(8,128)}, u32[]{:S(2)}, u32[]{:S(2)}) %collective-permute-start.3) | collective-permute-done | bytes 270368 | tf_op jit(solution)/shard_map/ppermute | solution.py:69
  57.1 1.0 constant_dynamic-update-slice_fusion
  58.1 1.6 fusion.28
  59.8 1.4 fusion.30
  61.7 1.3 collective-permute-start.7
  63.1 4.6 %collective-permute-start.4 = (f32[4,136,128]{2,1,0:T(8,128)S(1)}, f32[4,136,128]{2,1,0:T(8,128)S(1)}, u32[]{:S(2)}, u32[]{:S(2)}) collective-permute-start(f32[4,136,128]{2,1,0:T(8,128)S(1)} %get-tuple-element.79), channel_id=1, source_target_pairs={{0,32},{8,40},{16,48},{24,56},{32,64},{40,72},{48,80},{56,88},{64,... | collective-permute-start | bytes 835592 | tf_op jit(solution)/shard_map/ppermute | solution.py:35
  67.7 2.4 %collective-permute-done.7 = f32[4,136,128]{2,1,0:T(8,128)S(1)} collective-permute-done((f32[4,136,128]{2,1,0:T(8,128)S(1)}, f32[4,136,128]{2,1,0:T(8,128)S(1)}, u32[]{:S(2)}, u32[]{:S(2)}) %collective-permute-start.7) | collective-permute-done | bytes 278560 | tf_op jit(solution)/shard_map/ppermute | solution.py:36
  70.3 1.4 collective-permute-done.4
  72.0 5.8 %collective-permute-start.5 = (f32[4,136,128]{2,1,0:T(8,128)S(1)}, f32[4,136,128]{2,1,0:T(8,128)S(1)}, u32[]{:S(2)}, u32[]{:S(2)}) collective-permute-start(f32[4,136,128]{2,1,0:T(8,128)S(1)} %pad_maximum_fusion.7), channel_id=1, source_target_pairs={{0,64},{8,72},{16,80},{24,88},{32,96},{40,104},{48,112},{56,120},{... | collective-permute-start | bytes 835592 | tf_op jit(solution)/shard_map/ppermute | solution.py:35
  77.9 1.3 collective-permute-start.8
  79.4 2.4 %collective-permute-done.5 = f32[4,136,128]{2,1,0:T(8,128)S(1)} collective-permute-done((f32[4,136,128]{2,1,0:T(8,128)S(1)}, f32[4,136,128]{2,1,0:T(8,128)S(1)}, u32[]{:S(2)}, u32[]{:S(2)}) %collective-permute-start.5) | collective-permute-done | bytes 278560 | tf_op jit(solution)/shard_map/ppermute | solution.py:35
  82.0 16.2 %collective-permute-start.6 = (f32[4,136,128]{2,1,0:T(8,128)S(1)}, f32[4,136,128]{2,1,0:T(8,128)S(1)}, u32[]{:S(2)}, u32[]{:S(2)}) collective-permute-start(f32[4,136,128]{2,1,0:T(8,128)S(1)} %pad_maximum_fusion.8), channel_id=1, source_target_pairs={{0,128},{8,136},{16,144},{24,152},{32,160},{40,168},{48,176},{56,1... | collective-permute-start | bytes 835592 | tf_op jit(solution)/shard_map/ppermute | solution.py:35
  98.3 1.3 collective-permute-start.9
  99.8 5.0 %collective-permute-done.6 = f32[4,136,128]{2,1,0:T(8,128)S(1)} collective-permute-done((f32[4,136,128]{2,1,0:T(8,128)S(1)}, f32[4,136,128]{2,1,0:T(8,128)S(1)}, u32[]{:S(2)}, u32[]{:S(2)}) %collective-permute-start.6) | collective-permute-done | bytes 278560 | tf_op jit(solution)/shard_map/ppermute | solution.py:35
  105.1 5.9 %collective-permute-done.9 = f32[4,136,128]{2,1,0:T(8,128)S(1)} collective-permute-done((f32[4,136,128]{2,1,0:T(8,128)S(1)}, f32[4,136,128]{2,1,0:T(8,128)S(1)}, u32[]{:S(2)}, u32[]{:S(2)}) %collective-permute-start.9) | collective-permute-done | bytes 278560 | tf_op jit(solution)/shard_map/ppermute | solution.py:36
  111.7 0.9 dynamic-slice_bitcast_fusion.2
  112.7 0.9 pad_maximum_fusion.4
  113.6 3.7 %collective-permute-start.12 = (f32[6,256,128]{2,1,0:T(8,128)}, f32[6,256,128]{2,1,0:T(8,128)}, u32[]{:S(2)}, u32[]{:S(2)}) collective-permute-start(f32[6,256,128]{2,1,0:T(8,128)} %pad_maximum_fusion.4), channel_id=1, source_target_pairs={{0,24},{8,0},{16,8},{24,16},{32,56},{40,32},{48,40},{56,48},{64,88... | collective-permute-start | bytes 2359304 | tf_op jit(solution)/shard_map/ppermute | solution.py:68
  117.3 5.1 %multiply_convert_fusion.1 = bf16[16,384,384]{2,1,0:T(8,128)(2,1)} fusion(f32[16,384]{1,0:T(8,128)S(1)} %get-tuple-element.75, pred[384,384]{1,0:T(8,128)(4,1)S(1)} %fusion.26, bf16[384,16,128]{0,2,1:T(8,128)(2,1)S(1)} %bitcast.215, bf16[384,16,128]{2,1,0:T(8,128)(2,1)S(1)} %bitcast.218), kind=kOutput, calls=%fused_computation.1 | convolution fusion | flops 615776256 | bytes 8036352 | tf_op jit(solution)/shard_map/shf,thf->hst/dot_general | solution.py:199
  122.4 2.2 %collective-permute-start.10 = (f32[4,256,128]{2,1,0:T(8,128)}, f32[4,256,128]{2,1,0:T(8,128)}, u32[]{:S(2)}, u32[]{:S(2)}) collective-permute-start(f32[4,256,128]{2,1,0:T(8,128)} %get-tuple-element.60), channel_id=1, source_target_pairs={{0,8},{8,16},{16,24},{24,0},{32,40},{40,48},{48,56},{56,32},{64,72... | collective-permute-start | bytes 1572872 | tf_op jit(solution)/shard_map/ppermute | solution.py:67
  124.6 0.9 collective-permute-start.11
  125.7 8.9 %collective-permute-done.12 = f32[6,256,128]{2,1,0:T(8,128)} collective-permute-done((f32[6,256,128]{2,1,0:T(8,128)}, f32[6,256,128]{2,1,0:T(8,128)}, u32[]{:S(2)}, u32[]{:S(2)}) %collective-permute-start.12) | collective-permute-done | bytes 786464 | tf_op jit(solution)/shard_map/ppermute | solution.py:68
  134.6 1.0 slice.283
  135.6 2.4 %collective-permute-start.13 = (f32[2,256,128]{2,1,0:T(8,128)S(1)}, f32[2,256,128]{2,1,0:T(8,128)S(1)}, u32[]{:S(2)}, u32[]{:S(2)}) collective-permute-start(f32[2,256,128]{2,1,0:T(8,128)S(1)} %slice.283), channel_id=1, source_target_pairs={{0,24},{8,0},{16,8},{24,16},{32,56},{40,32},{48,40},{56,48},{64,88... | collective-permute-start | bytes 786440 | tf_op jit(solution)/shard_map/ppermute | solution.py:69
  138.7 1.0 constant_dynamic-update-slice_fusion.3
  139.7 5.9 %collective-permute-done.13 = f32[2,256,128]{2,1,0:T(8,128)S(1)} collective-permute-done((f32[2,256,128]{2,1,0:T(8,128)S(1)}, f32[2,256,128]{2,1,0:T(8,128)S(1)}, u32[]{:S(2)}, u32[]{:S(2)}) %collective-permute-start.13) | collective-permute-done | bytes 262176 | tf_op jit(solution)/shard_map/ppermute | solution.py:69
  145.6 1.6 fusion.36
  147.1 1.5 fusion.38
  148.8 1.2 copy-done.1
  150.0 1.0 fusion.21
  151.5 1.4 fusion.17
  152.9 2.7 %fusion.23 = f32[16,128,384]{2,1,0:T(8,128)} fusion(bf16[384,16,128]{0,2,1:T(8,128)(2,1)S(1)} %bitcast.203, f32[16,256,128]{2,1,0:T(8,128)S(1)} %bitcast.222), kind=kOutput, calls=%fused_computation.35 | convolution fusion | flops 603979776 | bytes 5767168 | tf_op jit(solution)/shard_map/the,hef->thf/dot_general | solution.py:207
  155.6 2.8 %fusion.10 = (f32[384,16]{0,1:T(8,128)S(1)}, bf16[384,16,128]{0,2,1:T(8,128)(2,1)}) fusion(bf16[384,16,128]{0,2,1:T(8,128)(2,1)S(1)} %bitcast.208, f32[16,128,384]{2,1,0:T(8,128)S(1)} %fusion.21, f32[384,16]{0,1:T(8,128)S(1)} %get-tuple-element.78, bf16[16,384,384]{2,1,0:T(8,128)(2,1)S(1)} %bitcast.212, bf16[384,16,128]{0,2,1:T(8,128)(2,1)S(1)} %bitcast.204), kind=kOutput, calls=%fused_computation.16 | convolution fusion | flops 608692224 | bytes 12632064 | tf_op jit(solution)/shard_map/hst,the->she/dot_general | solution.py:210
  158.4 2.4 %fusion.8 = (f32[384,16]{0,1:T(8,128)S(1)}, bf16[384,16,128]{0,2,1:T(8,128)(2,1)}) fusion(bf16[384,16,128]{0,2,1:T(8,128)(2,1)S(1)} %bitcast.205, f32[16,128,384]{2,1,0:T(8,128)S(1)} %fusion.17, f32[384,16]{0,1:T(8,128)S(1)} %get-tuple-element.77, bf16[384,16,128]{0,2,1:T(8,128)(2,1)S(1)} %bitcast.209, bf16[16,384,384]{2,1,0:T(8,128)(2,1)S(1)} %bitcast.212), kind=kOutput, calls=%fused_computation.14 | convolution fusion | flops 608692224 | bytes 12632064 | tf_op jit(solution)/shard_map/hst,she->the/dot_general | solution.py:216
  160.9 1.9 collective-permute-start.14
  162.9 2.8 %collective-permute-start.16 = (f32[16]{0:T(128)S(1)}, f32[16]{0:T(128)S(1)}, u32[]{:S(2)}, u32[]{:S(2)}) collective-permute-start(f32[16]{0:T(128)S(1)} %multiply_reduce_fusion), channel_id=1, source_target_pairs={{0,24},{8,16},{16,8},{24,0},{32,56},{40,48},{48,40},{56,32},{64,88... | collective-permute-start | bytes 200 | tf_op jit(solution)/shard_map/ppermute | solution.py:126
  165.7 7.0 %fusion.12 = bf16[384,16,128]{0,2,1:T(8,128)(2,1)} fusion(f32[16,128,384]{2,1,0:T(8,128)} %fusion.23, bf16[384,16,128]{0,2,1:T(8,128)(2,1)} %bitcast.214, f32[16,384]{1,0:T(8,128)S(1)} %get-tuple-element.75, pred[384,384]{1,0:T(8,128)(4,1)S(1)} %copy-done.13, bf16[384,16,128]{0,2,1:T(8,128)(2,1)S(1)} %bitcast.210, bf16[384,16,128]{0,2,1:T(8,128)(2,1)S(1)} %bitcast.206, ...), kind=kOutput, calls=%fused_computation.19 | convolution fusion | flops 1222115328 | bytes 9633792 | tf_op jit(solution)/shard_map/hst,shf->thf/dot_general | solution.py:204
  172.8 2.7 %copy.124 = bf16[1,384,2048]{2,1,0:T(8,128)(2,1)} copy(bf16[1,384,2048]{1,2,0:T(8,128)(2,1)} %bitcast.228) | data formatting | bytes 3145728
  175.5 5.7 %collective-permute-start.17 = (f32[16]{0:T(128)S(1)}, f32[16]{0:T(128)S(1)}, u32[]{:S(2)}, u32[]{:S(2)}) collective-permute-start(f32[16]{0:T(128)S(1)} %fusion.66), channel_id=1, source_target_pairs={{0,32},{8,40},{16,48},{24,56},{32,0},{40,8},{48,16},{56,24},{64,96... | collective-permute-start | bytes 200 | tf_op jit(solution)/shard_map/ppermute | solution.py:126
  181.1 3.9 %collective-permute-start.18 = (f32[16]{0:T(128)S(1)}, f32[16]{0:T(128)S(1)}, u32[]{:S(2)}, u32[]{:S(2)}) collective-permute-start(f32[16]{0:T(128)S(1)} %fusion.66), channel_id=1, source_target_pairs={{0,64},{8,72},{16,80},{24,88},{32,96},{40,104},{48,112},{56,120},{... | collective-permute-start | bytes 200 | tf_op jit(solution)/shard_map/ppermute | solution.py:126
  185.0 1.4 collective-permute-start.19
  186.6 3.8 %collective-permute-done.19 = f32[16]{0:T(128)S(1)} collective-permute-done((f32[16]{0:T(128)S(1)}, f32[16]{0:T(128)S(1)}, u32[]{:S(2)}, u32[]{:S(2)}) %collective-permute-start.19) | collective-permute-done | bytes 96 | tf_op jit(solution)/shard_map/ppermute | solution.py:126
  190.5 1.6 copy.125
  192.1 5.8 %collective-permute-done.20 = f32[16]{0:T(128)S(1)} collective-permute-done((f32[16]{0:T(128)S(1)}, f32[16]{0:T(128)S(1)}, u32[]{:S(2)}, u32[]{:S(2)}) %collective-permute-start.20) | collective-permute-done | bytes 96 | tf_op jit(solution)/shard_map/ppermute | solution.py:126
  197.9 0.9 collective-permute-start.22
  198.8 1.0 collective-permute-start.23
  199.8 1.7 collective-permute-done.22
  201.8 1.2 collective-permute-start.24
  203.0 1.6 copy.126
  204.6 2.3 %collective-permute-done.24 = f32[16]{0:T(128)S(1)} collective-permute-done((f32[16]{0:T(128)S(1)}, f32[16]{0:T(128)S(1)}, u32[]{:S(2)}, u32[]{:S(2)}) %collective-permute-start.24) | collective-permute-done | bytes 96 | tf_op jit(solution)/shard_map/ppermute | solution.py:126
  (120 shorter events, 11.1 us)
Async XLA Ops:
  0.6 6.2 %copy-start.10 = (bf16[1,384,2048]{2,1,0:T(8,128)(2,1)S(1)}, bf16[1,384,2048]{2,1,0:T(8,128)(2,1)}, u32[]{:S(2)}) copy-start(bf16[1,384,2048]{2,1,0:T(8,128)(2,1)} %param.10) | copy-start | bytes 4718596
  6.8 1.6 copy-start.15
  6.8 1.6 copy-start.14
  14.8 2.9 %copy-start.2 = (bf16[48,8,16,128]{3,2,1,0:T(8,128)(2,1)S(1)}, bf16[48,8,16,128]{3,2,1,0:T(8,128)(2,1)}, u32[]{:S(2)}) copy-start(bf16[48,8,16,128]{3,2,1,0:T(8,128)(2,1)} %copy.133) | copy-start | bytes 4718596
  19.4 1.5 copy-start.5
  21.0 26.2 %collective-permute-start.2 = (f32[6,264,128]{2,1,0:T(8,128)S(1)}, f32[6,264,128]{2,1,0:T(8,128)S(1)}, u32[]{:S(2)}, u32[]{:S(2)}) collective-permute-start(f32[6,264,128]{2,1,0:T(8,128)S(1)} %pad_maximum_fusion.3), channel_id=1, source_target_pairs={{0,24},{8,0},{16,8},{24,16},{32,56},{40,32},{48,40},{56,48},{64,88... | collective-permute-start | bytes 2433032 | tf_op jit(solution)/shard_map/ppermute | solution.py:68
  24.0 34.1 %collective-permute-start = (f32[4,264,128]{2,1,0:T(8,128)}, f32[4,264,128]{2,1,0:T(8,128)}, u32[]{:S(2)}, u32[]{:S(2)}) collective-permute-start(f32[4,264,128]{2,1,0:T(8,128)} %get-tuple-element.56), channel_id=1, source_target_pairs={{0,8},{8,16},{16,24},{24,0},{32,40},{40,48},{48,56},{56,32},{64,72... | collective-permute-start | bytes 1622024 | tf_op jit(solution)/shard_map/ppermute | solution.py:67
  24.0 28.4 %collective-permute-start.1 = (f32[2,264,128]{2,1,0:T(8,128)S(1)}, f32[2,264,128]{2,1,0:T(8,128)}, u32[]{:S(2)}, u32[]{:S(2)}) collective-permute-start(f32[2,264,128]{2,1,0:T(8,128)S(1)} %get-tuple-element.58), channel_id=1, source_target_pairs={{0,16},{8,24},{16,0},{24,8},{32,48},{40,56},{48,32},{56,40},{64,80... | collective-permute-start | bytes 811016 | tf_op jit(solution)/shard_map/ppermute | solution.py:66
  47.1 0.9 copy-start.8
  48.7 8.4 %collective-permute-start.3 = (f32[2,264,128]{2,1,0:T(8,128)}, f32[2,264,128]{2,1,0:T(8,128)}, u32[]{:S(2)}, u32[]{:S(2)}) collective-permute-start(f32[2,264,128]{2,1,0:T(8,128)} %slice.251), channel_id=1, source_target_pairs={{0,24},{8,0},{16,8},{24,16},{32,56},{40,32},{48,40},{56,48},{64,88... | collective-permute-start | bytes 811016 | tf_op jit(solution)/shard_map/ppermute | solution.py:69
  53.3 6.4 %copy-start.9 = (f32[6,264,128]{2,1,0:T(8,128)S(1)}, f32[6,264,128]{2,1,0:T(8,128)}, u32[]{:S(2)}) copy-start(f32[6,264,128]{2,1,0:T(8,128)} %copy-done.8) | copy-start | bytes 2433028
  61.7 8.4 %collective-permute-start.7 = (f32[4,136,128]{2,1,0:T(8,128)S(1)}, f32[4,136,128]{2,1,0:T(8,128)S(1)}, u32[]{:S(2)}, u32[]{:S(2)}) collective-permute-start(f32[4,136,128]{2,1,0:T(8,128)S(1)} %get-tuple-element.80), channel_id=1, source_target_pairs={{32,0},{40,8},{48,16},{56,24},{64,32},{72,40},{80,48},{88,56},{96,... | collective-permute-start | bytes 835592 | tf_op jit(solution)/shard_map/ppermute | solution.py:36
  63.1 54.2 %copy-start.12 = (pred[384,384]{1,0:T(8,128)(4,1)}, pred[384,384]{1,0:T(8,128)(4,1)S(1)}, u32[]{:S(2)}) copy-start(pred[384,384]{1,0:T(8,128)(4,1)S(1)} %fusion.26) | copy-start | bytes 442372
  63.1 8.6 %collective-permute-start.4 = (f32[4,136,128]{2,1,0:T(8,128)S(1)}, f32[4,136,128]{2,1,0:T(8,128)S(1)}, u32[]{:S(2)}, u32[]{:S(2)}) collective-permute-start(f32[4,136,128]{2,1,0:T(8,128)S(1)} %get-tuple-element.79), channel_id=1, source_target_pairs={{0,32},{8,40},{16,48},{24,56},{32,64},{40,72},{48,80},{56,88},{64,... | collective-permute-start | bytes 835592 | tf_op jit(solution)/shard_map/ppermute | solution.py:35
  72.0 9.8 %collective-permute-start.5 = (f32[4,136,128]{2,1,0:T(8,128)S(1)}, f32[4,136,128]{2,1,0:T(8,128)S(1)}, u32[]{:S(2)}, u32[]{:S(2)}) collective-permute-start(f32[4,136,128]{2,1,0:T(8,128)S(1)} %pad_maximum_fusion.7), channel_id=1, source_target_pairs={{0,64},{8,72},{16,80},{24,88},{32,96},{40,104},{48,112},{56,120},{... | collective-permute-start | bytes 835592 | tf_op jit(solution)/shard_map/ppermute | solution.py:35
  77.9 20.3 %collective-permute-start.8 = (f32[4,136,128]{2,1,0:T(8,128)S(1)}, f32[4,136,128]{2,1,0:T(8,128)S(1)}, u32[]{:S(2)}, u32[]{:S(2)}) collective-permute-start(f32[4,136,128]{2,1,0:T(8,128)S(1)} %pad_maximum_fusion.9), channel_id=1, source_target_pairs={{64,0},{72,8},{80,16},{88,24},{96,32},{104,40},{112,48},{120,56},{... | collective-permute-start | bytes 835592 | tf_op jit(solution)/shard_map/ppermute | solution.py:36
  82.0 22.9 %collective-permute-start.6 = (f32[4,136,128]{2,1,0:T(8,128)S(1)}, f32[4,136,128]{2,1,0:T(8,128)S(1)}, u32[]{:S(2)}, u32[]{:S(2)}) collective-permute-start(f32[4,136,128]{2,1,0:T(8,128)S(1)} %pad_maximum_fusion.8), channel_id=1, source_target_pairs={{0,128},{8,136},{16,144},{24,152},{32,160},{40,168},{48,176},{56,1... | collective-permute-start | bytes 835592 | tf_op jit(solution)/shard_map/ppermute | solution.py:35
  98.3 12.8 %collective-permute-start.9 = (f32[4,136,128]{2,1,0:T(8,128)S(1)}, f32[4,136,128]{2,1,0:T(8,128)S(1)}, u32[]{:S(2)}, u32[]{:S(2)}) collective-permute-start(f32[4,136,128]{2,1,0:T(8,128)S(1)} %pad_maximum_fusion.10), channel_id=1, source_target_pairs={{128,0},{136,8},{144,16},{152,24},{160,32},{168,40},{176,48},{184,... | collective-permute-start | bytes 835592 | tf_op jit(solution)/shard_map/ppermute | solution.py:36
  111.7 1.9 copy-start.6
  111.7 5.6 %copy-start = (bf16[1,384,2048]{1,2,0:T(8,128)(2,1)S(1)}, bf16[1,384,2048]{1,2,0:T(8,128)(2,1)}, u32[]{:S(2)}) copy-start(bf16[1,384,2048]{1,2,0:T(8,128)(2,1)} %copy.131) | copy-start | bytes 4718596
  111.7 5.6 %copy-start.3 = (bf16[48,8,16,128]{3,2,1,0:T(8,128)(2,1)S(1)}, bf16[48,8,16,128]{3,2,1,0:T(8,128)(2,1)}, u32[]{:S(2)}) copy-start(bf16[48,8,16,128]{3,2,1,0:T(8,128)(2,1)} %copy.133) | copy-start | bytes 4718596
  113.6 21.0 %collective-permute-start.12 = (f32[6,256,128]{2,1,0:T(8,128)}, f32[6,256,128]{2,1,0:T(8,128)}, u32[]{:S(2)}, u32[]{:S(2)}) collective-permute-start(f32[6,256,128]{2,1,0:T(8,128)} %pad_maximum_fusion.4), channel_id=1, source_target_pairs={{0,24},{8,0},{16,8},{24,16},{32,56},{40,32},{48,40},{56,48},{64,88... | collective-permute-start | bytes 2359304 | tf_op jit(solution)/shard_map/ppermute | solution.py:68
  122.4 23.1 %collective-permute-start.10 = (f32[4,256,128]{2,1,0:T(8,128)}, f32[4,256,128]{2,1,0:T(8,128)}, u32[]{:S(2)}, u32[]{:S(2)}) collective-permute-start(f32[4,256,128]{2,1,0:T(8,128)} %get-tuple-element.60), channel_id=1, source_target_pairs={{0,8},{8,16},{16,24},{24,0},{32,40},{40,48},{48,56},{56,32},{64,72... | collective-permute-start | bytes 1572872 | tf_op jit(solution)/shard_map/ppermute | solution.py:67
  124.6 14.1 %collective-permute-start.11 = (f32[2,256,128]{2,1,0:T(8,128)S(1)}, f32[2,256,128]{2,1,0:T(8,128)}, u32[]{:S(2)}, u32[]{:S(2)}) collective-permute-start(f32[2,256,128]{2,1,0:T(8,128)S(1)} %get-tuple-element.62), channel_id=1, source_target_pairs={{0,16},{8,24},{16,0},{24,8},{32,48},{40,56},{48,32},{56,40},{64,80... | collective-permute-start | bytes 786440 | tf_op jit(solution)/shard_map/ppermute | solution.py:66
  135.6 9.9 %collective-permute-start.13 = (f32[2,256,128]{2,1,0:T(8,128)S(1)}, f32[2,256,128]{2,1,0:T(8,128)S(1)}, u32[]{:S(2)}, u32[]{:S(2)}) collective-permute-start(f32[2,256,128]{2,1,0:T(8,128)S(1)} %slice.283), channel_id=1, source_target_pairs={{0,24},{8,0},{16,8},{24,16},{32,56},{40,32},{48,40},{56,48},{64,88... | collective-permute-start | bytes 786440 | tf_op jit(solution)/shard_map/ppermute | solution.py:69
  148.6 1.4 copy-start.1
  150.0 1.4 copy-start.4
  150.0 5.6 %slice-start = ((s8[4718592]{0:T(1024)(128)(4,1)}), s8[4194304]{0:T(1024)(128)(4,1)S(1)}, s32[]{:S(2)}) async-start(s8[4718592]{0:T(1024)(128)(4,1)} %bitcast.211), calls=%async_computation | async-start | bytes 8388608
  151.4 4.2 %slice-start.1 = ((s8[4718592]{0:T(1024)(128)(4,1)}), s8[524288]{0:T(1024)(128)(4,1)S(1)}, s32[]{:S(2)}) async-start(s8[4718592]{0:T(1024)(128)(4,1)} %bitcast.211), calls=%async_computation.1 | async-start | bytes 1048576
  158.4 7.3 %copy-start.13 = (pred[384,384]{1,0:T(8,128)(4,1)S(1)}, pred[384,384]{1,0:T(8,128)(4,1)}, u32[]{:S(2)}) copy-start(pred[384,384]{1,0:T(8,128)(4,1)} %copy-done.12) | copy-start | bytes 442372
  160.9 14.5 %collective-permute-start.14 = (f32[16]{0:T(128)S(1)}, f32[16]{0:T(128)S(1)}, u32[]{:S(2)}, u32[]{:S(2)}) collective-permute-start(f32[16]{0:T(128)S(1)} %multiply_reduce_fusion), channel_id=1, source_target_pairs={{0,8},{8,0},{16,24},{24,16},{32,40},{40,32},{48,56},{56,48},{64,72... | collective-permute-start | bytes 200 | tf_op jit(solution)/shard_map/ppermute | solution.py:126
  162.9 12.6 %collective-permute-start.15 = (f32[16]{0:T(128)S(1)}, f32[16]{0:T(128)S(1)}, u32[]{:S(2)}, u32[]{:S(2)}) collective-permute-start(f32[16]{0:T(128)S(1)} %multiply_reduce_fusion), channel_id=1, source_target_pairs={{0,16},{8,24},{16,0},{24,8},{32,48},{40,56},{48,32},{56,40},{64,80... | collective-permute-start | bytes 200 | tf_op jit(solution)/shard_map/ppermute | solution.py:126
  162.9 12.6 %collective-permute-start.16 = (f32[16]{0:T(128)S(1)}, f32[16]{0:T(128)S(1)}, u32[]{:S(2)}, u32[]{:S(2)}) collective-permute-start(f32[16]{0:T(128)S(1)} %multiply_reduce_fusion), channel_id=1, source_target_pairs={{0,24},{8,16},{16,8},{24,0},{32,56},{40,48},{48,40},{56,32},{64,88... | collective-permute-start | bytes 200 | tf_op jit(solution)/shard_map/ppermute | solution.py:126
  172.7 17.7 %copy-start.7 = (bf16[384,16,128]{0,2,1:T(8,128)(2,1)S(1)}, bf16[384,16,128]{0,2,1:T(8,128)(2,1)}, u32[]{:S(2)}) copy-start(bf16[384,16,128]{0,2,1:T(8,128)(2,1)} %get-tuple-element.52) | copy-start | bytes 4718596
  175.4 27.6 %copy-start.11 = (bf16[384,16,128]{0,2,1:T(8,128)(2,1)S(1)}, bf16[384,16,128]{0,2,1:T(8,128)(2,1)}, u32[]{:S(2)}) copy-start(bf16[384,16,128]{0,2,1:T(8,128)(2,1)} %fusion.12) | copy-start | bytes 4718596
  175.5 10.9 %collective-permute-start.17 = (f32[16]{0:T(128)S(1)}, f32[16]{0:T(128)S(1)}, u32[]{:S(2)}, u32[]{:S(2)}) collective-permute-start(f32[16]{0:T(128)S(1)} %fusion.66), channel_id=1, source_target_pairs={{0,32},{8,40},{16,48},{24,56},{32,0},{40,8},{48,16},{56,24},{64,96... | collective-permute-start | bytes 200 | tf_op jit(solution)/shard_map/ppermute | solution.py:126
  181.1 5.4 %collective-permute-start.18 = (f32[16]{0:T(128)S(1)}, f32[16]{0:T(128)S(1)}, u32[]{:S(2)}, u32[]{:S(2)}) collective-permute-start(f32[16]{0:T(128)S(1)} %fusion.66), channel_id=1, source_target_pairs={{0,64},{8,72},{16,80},{24,88},{32,96},{40,104},{48,112},{56,120},{... | collective-permute-start | bytes 200 | tf_op jit(solution)/shard_map/ppermute | solution.py:126
  185.0 5.3 %collective-permute-start.19 = (f32[16]{0:T(128)S(1)}, f32[16]{0:T(128)S(1)}, u32[]{:S(2)}, u32[]{:S(2)}) collective-permute-start(f32[16]{0:T(128)S(1)} %fusion.66), channel_id=1, source_target_pairs={{0,96},{8,104},{16,112},{24,120},{32,64},{40,72},{48,80},{56,88},{... | collective-permute-start | bytes 200 | tf_op jit(solution)/shard_map/ppermute | solution.py:126
  190.4 7.5 %collective-permute-start.20 = (f32[16]{0:T(128)S(1)}, f32[16]{0:T(128)S(1)}, u32[]{:S(2)}, u32[]{:S(2)}) collective-permute-start(f32[16]{0:T(128)S(1)} %fusion.63), channel_id=1, source_target_pairs={{0,128},{8,136},{16,144},{24,152},{32,160},{40,168},{48,176},{56,1... | collective-permute-start | bytes 200 | tf_op jit(solution)/shard_map/ppermute | solution.py:126
  197.9 1.9 collective-permute-start.21
  197.9 3.6 %collective-permute-start.22 = (f32[16]{0:T(128)S(1)}, f32[16]{0:T(128)S(1)}, u32[]{:S(2)}, u32[]{:S(2)}) collective-permute-start(f32[16]{0:T(128)S(1)} %fusion.60), channel_id=1, source_target_pairs={{0,2},{1,3},{2,0},{3,1},{4,6},{5,7},{6,4},{7,5},{8,10},{9,11},{10,... | collective-permute-start | bytes 200 | tf_op jit(solution)/shard_map/ppermute | solution.py:126
  198.8 3.0 %collective-permute-start.23 = (f32[16]{0:T(128)S(1)}, f32[16]{0:T(128)S(1)}, u32[]{:S(2)}, u32[]{:S(2)}) collective-permute-start(f32[16]{0:T(128)S(1)} %fusion.60), channel_id=1, source_target_pairs={{0,3},{1,2},{2,1},{3,0},{4,7},{5,6},{6,5},{7,4},{8,11},{9,10},{10,... | collective-permute-start | bytes 200 | tf_op jit(solution)/shard_map/ppermute | solution.py:126
  201.8 5.1 %collective-permute-start.24 = (f32[16]{0:T(128)S(1)}, f32[16]{0:T(128)S(1)}, u32[]{:S(2)}, u32[]{:S(2)}) collective-permute-start(f32[16]{0:T(128)S(1)} %fusion.59), channel_id=1, source_target_pairs={{0,4},{1,5},{2,6},{3,7},{4,0},{5,1},{6,2},{7,3},{8,12},{9,13},{10,... | collective-permute-start | bytes 200 | tf_op jit(solution)/shard_map/ppermute | solution.py:126

commit v14 on v5

--- a/solution.py
+++ b/solution.py
@@ -208,7 +208,7 @@
     )
     inner_step = jnp.sum(key_f * key_full, axis=2) - jnp.sum(query_f * query_full, axis=2)
     rate_part = jnp.sum(position[:, None] * inner_step, axis=0)
-    rate_total = all_sum(rate_part, ("seq", "dp"))
+    rate_total = all_sum(rate_part, ("dp", "seq"))
     token_total = row_count * lax.axis_size("seq") * lax.axis_size("dp")
     rate_grad = head_decay_rate * rate_total / math.sqrt(token_total)
     out_shape = (1, row_count, HEADS * HEAD_DIM)

time: 196 us -> 197 us (level)
  no operation moved by 1% of the time
where the time goes in v14:
time: 197 us
  waiting for transfers between devices  67.2 us (34%)
  starting transfers between devices  65.7 us (33%)
  matrix products  25.4 us (13%)
  local copies, waits for them, and re-layouts  19.7 us (10%)
  other arithmetic  16.6 us (8%)
  between operations  2.1 us (1%)
    ppermute x6, waiting for transfers between devices, row_exchange(): got.append(lax.ppermute(send, axis, pairs))  35.6 us
    ppermute x3, starting transfers between devices, group_scan(): got = lax.ppermute(fwd, axis, up)  28.3 us
    ppermute x11, starting transfers between devices, digit_sum(): lax.ppermute(value, axis, [(i, i ^ k * step) for i in range(count)])  21 us
    ppermute x11, waiting for transfers between devices, digit_sum(): lax.ppermute(value, axis, [(i, i ^ k * step) for i in range(count)])  15.5 us
    unnamed x42, local copies, waits for them, and re-layouts  14.1 us
    ppermute x6, starting transfers between devices, row_exchange(): got.append(lax.ppermute(send, axis, pairs))  12.4 us
    ppermute x3, waiting for transfers between devices, group_scan(): rgot = lax.ppermute(bwd, axis, down)  11.4 us
    dot_general x1, matrix products, on_device(): jnp.einsum('hst,shf->thf', attn_prob, gradient_block, preferred_element_t...  7.06 us
  transfers between devices with their start and end apart: 23, of which 15 were waited for; matrix products, arithmetic and copies ran while one was open for 11% of the time, Pallas kernels for 0%

profile of v14, /device:TPU:6, one launch (start us, length us, event | category | flops | bytes accessed | tf_op | source)
XLA Modules:
  0.0 196.7 jit_solution(8596268811315379976)
XLA Ops:
  0.7 0.9 reduce-window_clone.1
  1.6 0.7 subtract_bitcast_fusion
  4.2 0.7 broadcast_compare_fusion
  4.9 1.9 copy.87
  6.8 1.6 copy.103
  8.5 0.9 reduce-window.24
  9.8 1.9 copy.85
  11.7 3.0 %copy.105 = bf16[48,8,16,128]{3,2,1,0:T(8,128)(2,1)} copy(bf16[48,8,16,128]{3,1,2,0:T(8,128)(2,1)} %bitcast.221) | data formatting | bytes 3145728
  14.8 2.9 %fusion.9 = f32[16,128,128]{2,1,0:T(8,128)S(1)} fusion(bf16[384,16,128]{0,2,1:T(8,128)(2,1)} %bitcast.207, bf16[384,16,128]{0,2,1:T(8,128)(2,1)S(1)} %bitcast.203, f32[384,16]{0,1:T(8,128)S(1)} %get-tuple-element.74), kind=kOutput, calls=%fused_computation.15 | convolution fusion | flops 605552640 | bytes 4218880 | tf_op jit(solution)/shard_map/she,shf->hef/dot_general | solution.py:180
  17.8 1.4 fusion.7
  19.4 1.3 copy-done.3
  20.8 1.2 dynamic-slice_bitcast_fusion
  22.0 1.6 collective-permute-start
  23.6 2.9 %collective-permute-start.1 = (f32[4,264,128]{2,1,0:T(8,128)}, f32[4,264,128]{2,1,0:T(8,128)}, u32[]{:S(2)}, u32[]{:S(2)}) collective-permute-start(f32[4,264,128]{2,1,0:T(8,128)} %get-tuple-element.54), channel_id=1, source_target_pairs={{0,16},{8,24},{16,0},{24,8},{32,48},{40,56},{48,32},{56,40},{64,80... | collective-permute-start | bytes 1622024 | tf_op jit(solution)/shard_map/ppermute | solution.py:57
  26.5 1.3 collective-permute-start.2
  27.9 9.7 %collective-permute-done = f32[4,264,128]{2,1,0:T(8,128)} collective-permute-done((f32[4,264,128]{2,1,0:T(8,128)}, f32[4,264,128]{2,1,0:T(8,128)}, u32[]{:S(2)}, u32[]{:S(2)}) %collective-permute-start) | collective-permute-done | bytes 540704 | tf_op jit(solution)/shard_map/ppermute | solution.py:57
  37.6 12.8 %collective-permute-done.1 = f32[4,264,128]{2,1,0:T(8,128)} collective-permute-done((f32[4,264,128]{2,1,0:T(8,128)}, f32[4,264,128]{2,1,0:T(8,128)}, u32[]{:S(2)}, u32[]{:S(2)}) %collective-permute-start.1) | collective-permute-done | bytes 540704 | tf_op jit(solution)/shard_map/ppermute | solution.py:57
  50.4 1.8 fusion.28
  52.4 1.1 fusion.49
  53.6 0.9 pad_maximum_fusion.4
  54.6 1.3 collective-permute-start.6
  56.3 4.6 %collective-permute-start.3 = (f32[4,136,128]{2,1,0:T(8,128)}, f32[4,136,128]{2,1,0:T(8,128)S(1)}, u32[]{:S(2)}, u32[]{:S(2)}) collective-permute-start(f32[4,136,128]{2,1,0:T(8,128)} %get-tuple-element.75), channel_id=1, source_target_pairs={{0,32},{8,40},{16,48},{24,56},{32,64},{40,72},{48,80},{56,88},{64,... | collective-permute-start | bytes 835592 | tf_op jit(solution)/shard_map/ppermute | solution.py:35
  60.8 3.7 %collective-permute-done.6 = f32[4,136,128]{2,1,0:T(8,128)} collective-permute-done((f32[4,136,128]{2,1,0:T(8,128)}, f32[4,136,128]{2,1,0:T(8,128)}, u32[]{:S(2)}, u32[]{:S(2)}) %collective-permute-start.6) | collective-permute-done | bytes 278560 | tf_op jit(solution)/shard_map/ppermute | solution.py:36
  64.5 0.8 fusion.79
  65.4 0.6 collective-permute-done.3
  66.0 1.2 multiply_add_fusion.9
  67.4 5.6 %collective-permute-start.4 = (f32[4,136,128]{2,1,0:T(8,128)S(1)}, f32[4,136,128]{2,1,0:T(8,128)S(1)}, u32[]{:S(2)}, u32[]{:S(2)}) collective-permute-start(f32[4,136,128]{2,1,0:T(8,128)S(1)} %pad_maximum_fusion.5), channel_id=1, source_target_pairs={{0,64},{8,72},{16,80},{24,88},{32,96},{40,104},{48,112},{56,120},{... | collective-permute-start | bytes 835592 | tf_op jit(solution)/shard_map/ppermute | solution.py:35
  73.2 1.3 collective-permute-start.7
  74.5 0.8 slice_reduce_fusion.2
  75.4 1.8 collective-permute-done.4
  77.3 18.1 %collective-permute-start.5 = (f32[4,136,128]{2,1,0:T(8,128)S(1)}, f32[4,136,128]{2,1,0:T(8,128)S(1)}, u32[]{:S(2)}, u32[]{:S(2)}) collective-permute-start(f32[4,136,128]{2,1,0:T(8,128)S(1)} %pad_maximum_fusion.6), channel_id=1, source_target_pairs={{0,128},{8,136},{16,144},{24,152},{32,160},{40,168},{48,176},{56,1... | collective-permute-start | bytes 835592 | tf_op jit(solution)/shard_map/ppermute | solution.py:35
  95.6 1.3 collective-permute-start.8
  97.2 2.3 %collective-permute-done.5 = f32[4,136,128]{2,1,0:T(8,128)S(1)} collective-permute-done((f32[4,136,128]{2,1,0:T(8,128)S(1)}, f32[4,136,128]{2,1,0:T(8,128)S(1)}, u32[]{:S(2)}, u32[]{:S(2)}) %collective-permute-start.5) | collective-permute-done | bytes 278560 | tf_op jit(solution)/shard_map/ppermute | solution.py:35
  99.5 1.1 multiply_add_fusion.4
  100.6 1.1 multiply_add_fusion.2
  101.7 7.7 %collective-permute-done.8 = f32[4,136,128]{2,1,0:T(8,128)S(1)} collective-permute-done((f32[4,136,128]{2,1,0:T(8,128)S(1)}, f32[4,136,128]{2,1,0:T(8,128)S(1)}, u32[]{:S(2)}, u32[]{:S(2)}) %collective-permute-start.8) | collective-permute-done | bytes 278560 | tf_op jit(solution)/shard_map/ppermute | solution.py:36
  109.4 1.2 multiply_add_fusion.5
  110.6 1.1 multiply_add_fusion.3
  112.2 1.7 collective-permute-start.9
  113.9 4.9 %collective-permute-start.10 = (f32[4,256,128]{2,1,0:T(8,128)S(1)}, f32[4,256,128]{2,1,0:T(8,128)S(1)}, u32[]{:S(2)}, u32[]{:S(2)}) collective-permute-start(f32[4,256,128]{2,1,0:T(8,128)S(1)} %get-tuple-element.57), channel_id=1, source_target_pairs={{0,16},{8,24},{16,0},{24,8},{32,48},{40,56},{48,32},{56,40},{64,80... | collective-permute-start | bytes 1572872 | tf_op jit(solution)/shard_map/ppermute | solution.py:57
  118.8 3.7 %multiply_convert_fusion.1 = bf16[16,384,384]{2,1,0:T(8,128)(2,1)S(1)} fusion(f32[16,384]{1,0:T(8,128)S(1)} %get-tuple-element.71, pred[384,384]{1,0:T(8,128)(4,1)S(1)} %fusion.26, bf16[384,16,128]{0,2,1:T(8,128)(2,1)S(1)} %bitcast.209, bf16[384,16,128]{2,1,0:T(8,128)(2,1)S(1)} %bitcast.212), kind=kOutput, calls=%fused_computation.1 | convolution fusion | flops 615776256 | bytes 8036352 | tf_op jit(solution)/shard_map/shf,thf->hst/dot_general | solution.py:186
  122.5 7.5 %collective-permute-done.9 = f32[4,256,128]{2,1,0:T(8,128)S(1)} collective-permute-done((f32[4,256,128]{2,1,0:T(8,128)S(1)}, f32[4,256,128]{2,1,0:T(8,128)S(1)}, u32[]{:S(2)}, u32[]{:S(2)}) %collective-permute-start.9) | collective-permute-done | bytes 524320 | tf_op jit(solution)/shard_map/ppermute | solution.py:57
  130.1 5.6 %collective-permute-done.10 = f32[4,256,128]{2,1,0:T(8,128)S(1)} collective-permute-done((f32[4,256,128]{2,1,0:T(8,128)S(1)}, f32[4,256,128]{2,1,0:T(8,128)S(1)}, u32[]{:S(2)}, u32[]{:S(2)}) %collective-permute-start.10) | collective-permute-done | bytes 524320 | tf_op jit(solution)/shard_map/ppermute | solution.py:57
  136.1 1.0 fusion.21
  137.1 1.4 fusion.17
  138.6 2.7 %fusion.23 = f32[16,128,384]{2,1,0:T(8,128)} fusion(bf16[384,16,128]{0,2,1:T(8,128)(2,1)S(1)} %bitcast.199, f32[16,256,128]{2,1,0:T(8,128)S(1)} %bitcast.216), kind=kOutput, calls=%fused_computation.35 | convolution fusion | flops 603979776 | bytes 5767168 | tf_op jit(solution)/shard_map/the,hef->thf/dot_general | solution.py:194
  141.3 2.8 %fusion.10 = (f32[384,16]{0,1:T(8,128)S(1)}, bf16[384,16,128]{0,2,1:T(8,128)(2,1)}) fusion(bf16[384,16,128]{0,2,1:T(8,128)(2,1)S(1)} %bitcast.204, f32[16,128,384]{2,1,0:T(8,128)S(1)} %fusion.21, f32[384,16]{0,1:T(8,128)S(1)} %get-tuple-element.74, bf16[16,384,384]{2,1,0:T(8,128)(2,1)S(1)} %multiply_convert_fusion.1, bf16[384,16,128]{0,2,1:T(8,128)(2,1)S(1)} %bitcast.200), kind=kOutput, calls=%fused_computation.16 | convolution fusion | flops 608692224 | bytes 12632064 | tf_op jit(solution)/shard_map/hst,the->she/dot_general | solution.py:197
  144.0 2.4 %fusion.8 = (f32[384,16]{0,1:T(8,128)S(1)}, bf16[384,16,128]{0,2,1:T(8,128)(2,1)}) fusion(bf16[384,16,128]{0,2,1:T(8,128)(2,1)S(1)} %bitcast.201, f32[16,128,384]{2,1,0:T(8,128)S(1)} %fusion.17, f32[384,16]{0,1:T(8,128)S(1)} %get-tuple-element.73, bf16[384,16,128]{0,2,1:T(8,128)(2,1)S(1)} %bitcast.205, bf16[16,384,384]{2,1,0:T(8,128)(2,1)S(1)} %multiply_convert_fusion.1), kind=kOutput, calls=%fused_computation.14 | convolution fusion | flops 608692224 | bytes 12632064 | tf_op jit(solution)/shard_map/hst,she->the/dot_general | solution.py:203
  146.7 0.9 collective-permute-start.13
  147.6 0.9 collective-permute-start.14
  148.5 7.1 %fusion.12 = bf16[384,16,128]{0,2,1:T(8,128)(2,1)} fusion(f32[16,128,384]{2,1,0:T(8,128)} %fusion.23, bf16[384,16,128]{0,2,1:T(8,128)(2,1)} %bitcast.208, f32[16,384]{1,0:T(8,128)S(1)} %get-tuple-element.71, pred[384,384]{1,0:T(8,128)(4,1)S(1)} %copy-done.15, bf16[384,16,128]{0,2,1:T(8,128)(2,1)S(1)} %bitcast.206, bf16[384,16,128]{0,2,1:T(8,128)(2,1)S(1)} %bitcast.202, ...), kind=kOutput, calls=%fused_computation.19 | convolution fusion | flops 1222115328 | bytes 9633792 | tf_op jit(solution)/shard_map/hst,shf->thf/dot_general | solution.py:191
  155.6 2.7 %copy.96 = bf16[1,384,2048]{2,1,0:T(8,128)(2,1)} copy(bf16[1,384,2048]{1,2,0:T(8,128)(2,1)} %bitcast.220) | data formatting | bytes 3145728
  158.3 1.5 collective-permute-start.15
  159.8 1.6 copy.97
  161.5 2.0 %collective-permute-done.15 = f32[16]{0:T(128)S(1)} collective-permute-done((f32[16]{0:T(128)S(1)}, f32[16]{0:T(128)S(1)}, u32[]{:S(2)}, u32[]{:S(2)}) %collective-permute-start.15) | collective-permute-done | bytes 96 | tf_op jit(solution)/shard_map/ppermute | solution.py:113
  163.8 3.3 %collective-permute-start.17 = (f32[16]{0:T(128)S(1)}, f32[16]{0:T(128)S(1)}, u32[]{:S(2)}, u32[]{:S(2)}) collective-permute-start(f32[16]{0:T(128)S(1)} %fusion.63), channel_id=1, source_target_pairs={{0,16},{8,24},{16,0},{24,8},{32,48},{40,56},{48,32},{56,40},{64,80... | collective-permute-start | bytes 200 | tf_op jit(solution)/shard_map/ppermute | solution.py:113
  167.1 1.1 collective-permute-start.18
  168.8 3.1 %collective-permute-done.18 = f32[16]{0:T(128)S(1)} collective-permute-done((f32[16]{0:T(128)S(1)}, f32[16]{0:T(128)S(1)}, u32[]{:S(2)}, u32[]{:S(2)}) %collective-permute-start.18) | collective-permute-done | bytes 96 | tf_op jit(solution)/shard_map/ppermute | solution.py:113
  171.9 3.1 %collective-permute-start.19 = (f32[16]{0:T(128)S(1)}, f32[16]{0:T(128)S(1)}, u32[]{:S(2)}, u32[]{:S(2)}) collective-permute-start(f32[16]{0:T(128)S(1)} %fusion.62), channel_id=1, source_target_pairs={{0,32},{8,40},{16,48},{24,56},{32,0},{40,8},{48,16},{56,24},{64,96... | collective-permute-start | bytes 200 | tf_op jit(solution)/shard_map/ppermute | solution.py:113
  175.0 8.3 %collective-permute-start.20 = (f32[16]{0:T(128)S(1)}, f32[16]{0:T(128)S(1)}, u32[]{:S(2)}, u32[]{:S(2)}) collective-permute-start(f32[16]{0:T(128)S(1)} %fusion.62), channel_id=1, source_target_pairs={{0,64},{8,72},{16,80},{24,88},{32,96},{40,104},{48,112},{56,120},{... | collective-permute-start | bytes 200 | tf_op jit(solution)/shard_map/ppermute | solution.py:113
  183.3 1.4 collective-permute-start.21
  184.8 3.8 %collective-permute-done.21 = f32[16]{0:T(128)S(1)} collective-permute-done((f32[16]{0:T(128)S(1)}, f32[16]{0:T(128)S(1)}, u32[]{:S(2)}, u32[]{:S(2)}) %collective-permute-start.21) | collective-permute-done | bytes 96 | tf_op jit(solution)/shard_map/ppermute | solution.py:113
  188.8 1.6 copy.98
  190.4 5.8 %collective-permute-done.22 = f32[16]{0:T(128)S(1)} collective-permute-done((f32[16]{0:T(128)S(1)}, f32[16]{0:T(128)S(1)}, u32[]{:S(2)}, u32[]{:S(2)}) %collective-permute-start.22) | collective-permute-done | bytes 96 | tf_op jit(solution)/shard_map/ppermute | solution.py:113
  (103 shorter events, 6.5 us)
Async XLA Ops:
  0.6 6.2 %copy-start.11 = (bf16[1,384,2048]{2,1,0:T(8,128)(2,1)S(1)}, bf16[1,384,2048]{2,1,0:T(8,128)(2,1)}, u32[]{:S(2)}) copy-start(bf16[1,384,2048]{2,1,0:T(8,128)(2,1)} %param.10) | copy-start | bytes 4718596
  6.8 1.6 copy-start.17
  6.8 1.6 copy-start.16
  14.8 2.9 %copy-start.1 = (bf16[48,8,16,128]{3,2,1,0:T(8,128)(2,1)S(1)}, bf16[48,8,16,128]{3,2,1,0:T(8,128)(2,1)}, u32[]{:S(2)}) copy-start(bf16[48,8,16,128]{3,2,1,0:T(8,128)(2,1)} %copy.105) | copy-start | bytes 4718596
  19.4 1.4 copy-start.3
  22.0 15.6 %collective-permute-start = (f32[4,264,128]{2,1,0:T(8,128)}, f32[4,264,128]{2,1,0:T(8,128)}, u32[]{:S(2)}, u32[]{:S(2)}) collective-permute-start(f32[4,264,128]{2,1,0:T(8,128)} %get-tuple-element.55), channel_id=1, source_target_pairs={{0,8},{8,16},{16,24},{24,0},{32,40},{40,48},{48,56},{56,32},{64,72... | collective-permute-start | bytes 1622024 | tf_op jit(solution)/shard_map/ppermute | solution.py:57
  23.6 26.8 %collective-permute-start.1 = (f32[4,264,128]{2,1,0:T(8,128)}, f32[4,264,128]{2,1,0:T(8,128)}, u32[]{:S(2)}, u32[]{:S(2)}) collective-permute-start(f32[4,264,128]{2,1,0:T(8,128)} %get-tuple-element.54), channel_id=1, source_target_pairs={{0,16},{8,24},{16,0},{24,8},{32,48},{40,56},{48,32},{56,40},{64,80... | collective-permute-start | bytes 1622024 | tf_op jit(solution)/shard_map/ppermute | solution.py:57
  26.5 23.9 %collective-permute-start.2 = (f32[4,264,128]{2,1,0:T(8,128)}, f32[4,264,128]{2,1,0:T(8,128)}, u32[]{:S(2)}, u32[]{:S(2)}) collective-permute-start(f32[4,264,128]{2,1,0:T(8,128)} %get-tuple-element.53), channel_id=1, source_target_pairs={{0,24},{8,0},{16,8},{24,16},{32,56},{40,32},{48,40},{56,48},{64,88... | collective-permute-start | bytes 1622024 | tf_op jit(solution)/shard_map/ppermute | solution.py:57
  52.1 2.4 %copy-start.5 = (f32[1,4,264,128]{3,2,1,0:T(8,128)}, f32[1,4,264,128]{3,2,1,0:T(8,128)S(1)}, u32[]{:S(2)}) copy-start(f32[1,4,264,128]{3,2,1,0:T(8,128)S(1)} %get-tuple-element.40) | copy-start | bytes 1622020
  52.1 2.4 %copy-start.6 = (f32[1,4,264,128]{3,2,1,0:T(8,128)}, f32[1,4,264,128]{3,2,1,0:T(8,128)S(1)}, u32[]{:S(2)}) copy-start(f32[1,4,264,128]{3,2,1,0:T(8,128)S(1)} %get-tuple-element.42) | copy-start | bytes 1622020
  52.2 2.4 %copy-start.7 = (f32[1,4,264,128]{3,2,1,0:T(8,128)}, f32[1,4,264,128]{3,2,1,0:T(8,128)S(1)}, u32[]{:S(2)}) copy-start(f32[1,4,264,128]{3,2,1,0:T(8,128)S(1)} %get-tuple-element.41) | copy-start | bytes 1622020
  52.2 2.4 %copy-start.8 = (f32[1,4,264,128]{3,2,1,0:T(8,128)}, f32[1,4,264,128]{3,2,1,0:T(8,128)S(1)}, u32[]{:S(2)}) copy-start(f32[1,4,264,128]{3,2,1,0:T(8,128)S(1)} %get-tuple-element.39) | copy-start | bytes 1622020
  53.5 1.0 copy-start.9
  53.5 2.4 %copy-start.10 = (f32[4,128,128]{2,1,0:T(8,128)}, f32[4,128,128]{2,1,0:T(8,128)S(1)}, u32[]{:S(2)}) copy-start(f32[4,128,128]{2,1,0:T(8,128)S(1)} %get-tuple-element.51) | copy-start | bytes 786436
  54.6 9.9 %collective-permute-start.6 = (f32[4,136,128]{2,1,0:T(8,128)}, f32[4,136,128]{2,1,0:T(8,128)}, u32[]{:S(2)}, u32[]{:S(2)}) collective-permute-start(f32[4,136,128]{2,1,0:T(8,128)} %get-tuple-element.76), channel_id=1, source_target_pairs={{32,0},{40,8},{48,16},{56,24},{64,32},{72,40},{80,48},{88,56},{96,... | collective-permute-start | bytes 835592 | tf_op jit(solution)/shard_map/ppermute | solution.py:36
  56.2 62.6 %copy-start.14 = (pred[384,384]{1,0:T(8,128)(4,1)}, pred[384,384]{1,0:T(8,128)(4,1)S(1)}, u32[]{:S(2)}) copy-start(pred[384,384]{1,0:T(8,128)(4,1)S(1)} %fusion.26) | copy-start | bytes 442372
  56.3 9.8 %collective-permute-start.3 = (f32[4,136,128]{2,1,0:T(8,128)}, f32[4,136,128]{2,1,0:T(8,128)S(1)}, u32[]{:S(2)}, u32[]{:S(2)}) collective-permute-start(f32[4,136,128]{2,1,0:T(8,128)} %get-tuple-element.75), channel_id=1, source_target_pairs={{0,32},{8,40},{16,48},{24,56},{32,64},{40,72},{48,80},{56,88},{64,... | collective-permute-start | bytes 835592 | tf_op jit(solution)/shard_map/ppermute | solution.py:35
  67.4 9.8 %collective-permute-start.4 = (f32[4,136,128]{2,1,0:T(8,128)S(1)}, f32[4,136,128]{2,1,0:T(8,128)S(1)}, u32[]{:S(2)}, u32[]{:S(2)}) collective-permute-start(f32[4,136,128]{2,1,0:T(8,128)S(1)} %pad_maximum_fusion.5), channel_id=1, source_target_pairs={{0,64},{8,72},{16,80},{24,88},{32,96},{40,104},{48,112},{56,120},{... | collective-permute-start | bytes 835592 | tf_op jit(solution)/shard_map/ppermute | solution.py:35
  73.2 22.3 %collective-permute-start.7 = (f32[4,136,128]{2,1,0:T(8,128)S(1)}, f32[4,136,128]{2,1,0:T(8,128)S(1)}, u32[]{:S(2)}, u32[]{:S(2)}) collective-permute-start(f32[4,136,128]{2,1,0:T(8,128)S(1)} %pad_maximum_fusion.7), channel_id=1, source_target_pairs={{64,0},{72,8},{80,16},{88,24},{96,32},{104,40},{112,48},{120,56},{... | collective-permute-start | bytes 835592 | tf_op jit(solution)/shard_map/ppermute | solution.py:36
  75.4 25.2 %copy-start.13 = (f32[4,128,128]{2,1,0:T(8,128)S(1)}, f32[4,128,128]{2,1,0:T(8,128)}, u32[]{:S(2)}) copy-start(f32[4,128,128]{2,1,0:T(8,128)} %get-tuple-element.31) | copy-start | bytes 786436
  77.3 22.2 %collective-permute-start.5 = (f32[4,136,128]{2,1,0:T(8,128)S(1)}, f32[4,136,128]{2,1,0:T(8,128)S(1)}, u32[]{:S(2)}, u32[]{:S(2)}) collective-permute-start(f32[4,136,128]{2,1,0:T(8,128)S(1)} %pad_maximum_fusion.6), channel_id=1, source_target_pairs={{0,128},{8,136},{16,144},{24,152},{32,160},{40,168},{48,176},{56,1... | collective-permute-start | bytes 835592 | tf_op jit(solution)/shard_map/ppermute | solution.py:35
  95.6 13.8 %collective-permute-start.8 = (f32[4,136,128]{2,1,0:T(8,128)S(1)}, f32[4,136,128]{2,1,0:T(8,128)S(1)}, u32[]{:S(2)}, u32[]{:S(2)}) collective-permute-start(f32[4,136,128]{2,1,0:T(8,128)S(1)} %pad_maximum_fusion.8), channel_id=1, source_target_pairs={{128,0},{136,8},{144,16},{152,24},{160,32},{168,40},{176,48},{184,... | collective-permute-start | bytes 835592 | tf_op jit(solution)/shard_map/ppermute | solution.py:36
  112.0 6.8 %copy-start = (bf16[1,384,2048]{1,2,0:T(8,128)(2,1)S(1)}, bf16[1,384,2048]{1,2,0:T(8,128)(2,1)}, u32[]{:S(2)}) copy-start(bf16[1,384,2048]{1,2,0:T(8,128)(2,1)} %copy.103) | copy-start | bytes 4718596
  112.0 6.8 %copy-start.2 = (bf16[48,8,16,128]{3,2,1,0:T(8,128)(2,1)S(1)}, bf16[48,8,16,128]{3,2,1,0:T(8,128)(2,1)}, u32[]{:S(2)}) copy-start(bf16[48,8,16,128]{3,2,1,0:T(8,128)(2,1)} %copy.105) | copy-start | bytes 4718596
  112.2 17.9 %collective-permute-start.9 = (f32[4,256,128]{2,1,0:T(8,128)S(1)}, f32[4,256,128]{2,1,0:T(8,128)S(1)}, u32[]{:S(2)}, u32[]{:S(2)}) collective-permute-start(f32[4,256,128]{2,1,0:T(8,128)S(1)} %get-tuple-element.58), channel_id=1, source_target_pairs={{0,8},{8,16},{16,24},{24,0},{32,40},{40,48},{48,56},{56,32},{64,72... | collective-permute-start | bytes 1572872 | tf_op jit(solution)/shard_map/ppermute | solution.py:57
  113.9 21.8 %collective-permute-start.10 = (f32[4,256,128]{2,1,0:T(8,128)S(1)}, f32[4,256,128]{2,1,0:T(8,128)S(1)}, u32[]{:S(2)}, u32[]{:S(2)}) collective-permute-start(f32[4,256,128]{2,1,0:T(8,128)S(1)} %get-tuple-element.57), channel_id=1, source_target_pairs={{0,16},{8,24},{16,0},{24,8},{32,48},{40,56},{48,32},{56,40},{64,80... | collective-permute-start | bytes 1572872 | tf_op jit(solution)/shard_map/ppermute | solution.py:57
  118.8 16.9 %collective-permute-start.11 = (f32[4,256,128]{2,1,0:T(8,128)S(1)}, f32[4,256,128]{2,1,0:T(8,128)S(1)}, u32[]{:S(2)}, u32[]{:S(2)}) collective-permute-start(f32[4,256,128]{2,1,0:T(8,128)S(1)} %get-tuple-element.56), channel_id=1, source_target_pairs={{0,24},{8,0},{16,8},{24,16},{32,56},{40,32},{48,40},{56,48},{64,88... | collective-permute-start | bytes 1572872 | tf_op jit(solution)/shard_map/ppermute | solution.py:57
  144.0 4.5 %copy-start.15 = (pred[384,384]{1,0:T(8,128)(4,1)S(1)}, pred[384,384]{1,0:T(8,128)(4,1)}, u32[]{:S(2)}) copy-start(pred[384,384]{1,0:T(8,128)(4,1)} %copy-done.14) | copy-start | bytes 442372
  146.6 11.7 %collective-permute-start.12 = (f32[16]{0:T(128)S(1)}, f32[16]{0:T(128)S(1)}, u32[]{:S(2)}, u32[]{:S(2)}) collective-permute-start(f32[16]{0:T(128)S(1)} %multiply_reduce_fusion), channel_id=1, source_target_pairs={{0,1},{1,0},{2,3},{3,2},{4,5},{5,4},{6,7},{7,6},{8,9},{9,8},{10,11... | collective-permute-start | bytes 200 | tf_op jit(solution)/shard_map/ppermute | solution.py:113
  146.7 11.6 %collective-permute-start.13 = (f32[16]{0:T(128)S(1)}, f32[16]{0:T(128)S(1)}, u32[]{:S(2)}, u32[]{:S(2)}) collective-permute-start(f32[16]{0:T(128)S(1)} %multiply_reduce_fusion), channel_id=1, source_target_pairs={{0,2},{1,3},{2,0},{3,1},{4,6},{5,7},{6,4},{7,5},{8,10},{9,11},{10,... | collective-permute-start | bytes 200 | tf_op jit(solution)/shard_map/ppermute | solution.py:113
  147.6 10.7 %collective-permute-start.14 = (f32[16]{0:T(128)S(1)}, f32[16]{0:T(128)S(1)}, u32[]{:S(2)}, u32[]{:S(2)}) collective-permute-start(f32[16]{0:T(128)S(1)} %multiply_reduce_fusion), channel_id=1, source_target_pairs={{0,3},{1,2},{2,1},{3,0},{4,7},{5,6},{6,5},{7,4},{8,11},{9,10},{10,... | collective-permute-start | bytes 200 | tf_op jit(solution)/shard_map/ppermute | solution.py:113
  155.6 4.2 %copy-start.4 = (bf16[384,16,128]{0,2,1:T(8,128)(2,1)S(1)}, bf16[384,16,128]{0,2,1:T(8,128)(2,1)}, u32[]{:S(2)}) copy-start(bf16[384,16,128]{0,2,1:T(8,128)(2,1)} %get-tuple-element.50) | copy-start | bytes 4718596
  158.3 30.5 %copy-start.12 = (bf16[384,16,128]{0,2,1:T(8,128)(2,1)S(1)}, bf16[384,16,128]{0,2,1:T(8,128)(2,1)}, u32[]{:S(2)}) copy-start(bf16[384,16,128]{0,2,1:T(8,128)(2,1)} %fusion.12) | copy-start | bytes 4718596
  158.3 5.1 %collective-permute-start.15 = (f32[16]{0:T(128)S(1)}, f32[16]{0:T(128)S(1)}, u32[]{:S(2)}, u32[]{:S(2)}) collective-permute-start(f32[16]{0:T(128)S(1)} %fusion.66), channel_id=1, source_target_pairs={{0,4},{1,5},{2,6},{3,7},{4,0},{5,1},{6,2},{7,3},{8,12},{9,13},{10,... | collective-permute-start | bytes 200 | tf_op jit(solution)/shard_map/ppermute | solution.py:113
  163.5 4.7 %collective-permute-start.16 = (f32[16]{0:T(128)S(1)}, f32[16]{0:T(128)S(1)}, u32[]{:S(2)}, u32[]{:S(2)}) collective-permute-start(f32[16]{0:T(128)S(1)} %fusion.63), channel_id=1, source_target_pairs={{0,8},{8,0},{16,24},{24,16},{32,40},{40,32},{48,56},{56,48},{64,72... | collective-permute-start | bytes 200 | tf_op jit(solution)/shard_map/ppermute | solution.py:113
  163.8 5.0 %collective-permute-start.17 = (f32[16]{0:T(128)S(1)}, f32[16]{0:T(128)S(1)}, u32[]{:S(2)}, u32[]{:S(2)}) collective-permute-start(f32[16]{0:T(128)S(1)} %fusion.63), channel_id=1, source_target_pairs={{0,16},{8,24},{16,0},{24,8},{32,48},{40,56},{48,32},{56,40},{64,80... | collective-permute-start | bytes 200 | tf_op jit(solution)/shard_map/ppermute | solution.py:113
  167.1 4.8 %collective-permute-start.18 = (f32[16]{0:T(128)S(1)}, f32[16]{0:T(128)S(1)}, u32[]{:S(2)}, u32[]{:S(2)}) collective-permute-start(f32[16]{0:T(128)S(1)} %fusion.63), channel_id=1, source_target_pairs={{0,24},{8,16},{16,8},{24,0},{32,56},{40,48},{48,40},{56,32},{64,88... | collective-permute-start | bytes 200 | tf_op jit(solution)/shard_map/ppermute | solution.py:113
  171.9 12.8 %collective-permute-start.19 = (f32[16]{0:T(128)S(1)}, f32[16]{0:T(128)S(1)}, u32[]{:S(2)}, u32[]{:S(2)}) collective-permute-start(f32[16]{0:T(128)S(1)} %fusion.62), channel_id=1, source_target_pairs={{0,32},{8,40},{16,48},{24,56},{32,0},{40,8},{48,16},{56,24},{64,96... | collective-permute-start | bytes 200 | tf_op jit(solution)/shard_map/ppermute | solution.py:113
  175.0 9.8 %collective-permute-start.20 = (f32[16]{0:T(128)S(1)}, f32[16]{0:T(128)S(1)}, u32[]{:S(2)}, u32[]{:S(2)}) collective-permute-start(f32[16]{0:T(128)S(1)} %fusion.62), channel_id=1, source_target_pairs={{0,64},{8,72},{16,80},{24,88},{32,96},{40,104},{48,112},{56,120},{... | collective-permute-start | bytes 200 | tf_op jit(solution)/shard_map/ppermute | solution.py:113
  183.3 5.3 %collective-permute-start.21 = (f32[16]{0:T(128)S(1)}, f32[16]{0:T(128)S(1)}, u32[]{:S(2)}, u32[]{:S(2)}) collective-permute-start(f32[16]{0:T(128)S(1)} %fusion.62), channel_id=1, source_target_pairs={{0,96},{8,104},{16,112},{24,120},{32,64},{40,72},{48,80},{56,88},{... | collective-permute-start | bytes 200 | tf_op jit(solution)/shard_map/ppermute | solution.py:113
  188.6 7.5 %collective-permute-start.22 = (f32[16]{0:T(128)S(1)}, f32[16]{0:T(128)S(1)}, u32[]{:S(2)}, u32[]{:S(2)}) collective-permute-start(f32[16]{0:T(128)S(1)} %fusion.59), channel_id=1, source_target_pairs={{0,128},{8,136},{16,144},{24,152},{32,160},{40,168},{48,176},{56,1... | collective-permute-start | bytes 200 | tf_op jit(solution)/shard_map/ppermute | solution.py:113

commit v15 on v5

--- a/solution.py
+++ b/solution.py
@@ -122,7 +122,7 @@
         count = lax.axis_size(axis)
         step = 1
         while step < count:
-            radix = 4 if count % (step * 4) == 0 else 2
+            radix = count if count <= 8 else (4 if count % (step * 4) == 0 else 2)
             value = digit_sum(value, axis, step, radix)
             step *= radix
     return value

time: 196 us -> 200 us (1.020)
  starting transfers between devices: 65.4 us -> 70.7 us
  waiting for transfers between devices: 65.9 us -> 63 us
    ppermute x11 -> x14, starting transfers between devices: 20.7 us -> 26.1 us  [digit_sum(): lax.ppermute(value, axis, [(i, i ^ k * step) for i in range(count)])]
    ppermute x11 -> x14, waiting for transfers between devices: 14.1 us -> 11.2 us  [digit_sum(): lax.ppermute(value, axis, [(i, i ^ k * step) for i in range(count)])]
    unnamed x42 -> x40, local copies, waits for them, and re-layouts: 14.1 us -> 15 us
  transfers between devices with their start and end apart: 23 -> 26, of which waited for: 15 -> 13; matrix products, arithmetic and copies ran while one was open for 11% -> 11% of each run, Pallas kernels for 0% -> 0%
where the time goes in v15:
time: 200 us; the launch traced here: 199 us
  starting transfers between devices  70.7 us (35%)
  waiting for transfers between devices  63 us (32%)
  matrix products  25.4 us (13%)
  local copies, waits for them, and re-layouts  20.6 us (10%)
  other arithmetic  16.6 us (8%)
  between operations  2.16 us (1%)
    ppermute x6, waiting for transfers between devices, row_exchange(): got.append(lax.ppermute(send, axis, pairs))  35.6 us
    ppermute x3, starting transfers between devices, group_scan(): got = lax.ppermute(fwd, axis, up)  28.3 us
    ppermute x14, starting transfers between devices, digit_sum(): lax.ppermute(value, axis, [(i, i ^ k * step) for i in range(count)])  26.1 us
    unnamed x40, local copies, waits for them, and re-layouts  15 us
    ppermute x6, starting transfers between devices, row_exchange(): got.append(lax.ppermute(send, axis, pairs))  12.4 us
    ppermute x3, waiting for transfers between devices, group_scan(): rgot = lax.ppermute(bwd, axis, down)  11.4 us
    ppermute x14, waiting for transfers between devices, digit_sum(): lax.ppermute(value, axis, [(i, i ^ k * step) for i in range(count)])  11.2 us
    dot_general x1, matrix products, on_device(): jnp.einsum('hst,shf->thf', attn_prob, gradient_block, preferred_element_t...  7.06 us
  transfers between devices with their start and end apart: 26, of which 13 were waited for; matrix products, arithmetic and copies ran while one was open for 11% of the time, Pallas kernels for 0%

profile of v15, /device:TPU:6, one launch (start us, length us, event | category | flops | bytes accessed | tf_op | source)
XLA Modules:
  0.0 198.6 jit_solution(14090957539293686355)
XLA Ops:
  0.7 0.9 reduce-window_clone.1
  1.6 0.7 subtract_bitcast_fusion
  3.0 0.6 slice.169
  4.2 0.7 broadcast_compare_fusion
  4.9 1.9 copy.87
  6.8 1.6 copy.103
  8.5 0.9 reduce-window.24
  9.8 1.9 copy.85
  11.7 3.0 %copy.105 = bf16[48,8,16,128]{3,2,1,0:T(8,128)(2,1)} copy(bf16[48,8,16,128]{3,1,2,0:T(8,128)(2,1)} %bitcast.221) | data formatting | bytes 3145728
  14.8 2.9 %fusion.9 = f32[16,128,128]{2,1,0:T(8,128)S(1)} fusion(bf16[384,16,128]{0,2,1:T(8,128)(2,1)} %bitcast.207, bf16[384,16,128]{0,2,1:T(8,128)(2,1)S(1)} %bitcast.203, f32[384,16]{0,1:T(8,128)S(1)} %get-tuple-element.74), kind=kOutput, calls=%fused_computation.15 | convolution fusion | flops 605552640 | bytes 4218880 | tf_op jit(solution)/shard_map/she,shf->hef/dot_general | solution.py:180
  17.8 1.4 fusion.7
  19.4 1.3 copy-done.3
  20.8 1.2 dynamic-slice_bitcast_fusion
  22.0 1.6 collective-permute-start
  23.6 2.9 %collective-permute-start.1 = (f32[4,264,128]{2,1,0:T(8,128)}, f32[4,264,128]{2,1,0:T(8,128)}, u32[]{:S(2)}, u32[]{:S(2)}) collective-permute-start(f32[4,264,128]{2,1,0:T(8,128)} %get-tuple-element.54), channel_id=1, source_target_pairs={{0,16},{8,24},{16,0},{24,8},{32,48},{40,56},{48,32},{56,40},{64,80... | collective-permute-start | bytes 1622024 | tf_op jit(solution)/shard_map/ppermute | solution.py:57
  26.5 1.3 collective-permute-start.2
  27.9 9.7 %collective-permute-done = f32[4,264,128]{2,1,0:T(8,128)} collective-permute-done((f32[4,264,128]{2,1,0:T(8,128)}, f32[4,264,128]{2,1,0:T(8,128)}, u32[]{:S(2)}, u32[]{:S(2)}) %collective-permute-start) | collective-permute-done | bytes 540704 | tf_op jit(solution)/shard_map/ppermute | solution.py:57
  37.6 12.8 %collective-permute-done.1 = f32[4,264,128]{2,1,0:T(8,128)} collective-permute-done((f32[4,264,128]{2,1,0:T(8,128)}, f32[4,264,128]{2,1,0:T(8,128)}, u32[]{:S(2)}, u32[]{:S(2)}) %collective-permute-start.1) | collective-permute-done | bytes 540704 | tf_op jit(solution)/shard_map/ppermute | solution.py:57
  50.4 1.8 fusion.28
  52.4 1.1 fusion.49
  53.6 0.9 pad_maximum_fusion.4
  54.6 1.3 collective-permute-start.6
  56.3 4.6 %collective-permute-start.3 = (f32[4,136,128]{2,1,0:T(8,128)}, f32[4,136,128]{2,1,0:T(8,128)S(1)}, u32[]{:S(2)}, u32[]{:S(2)}) collective-permute-start(f32[4,136,128]{2,1,0:T(8,128)} %get-tuple-element.75), channel_id=1, source_target_pairs={{0,32},{8,40},{16,48},{24,56},{32,64},{40,72},{48,80},{56,88},{64,... | collective-permute-start | bytes 835592 | tf_op jit(solution)/shard_map/ppermute | solution.py:35
  60.9 3.6 %collective-permute-done.6 = f32[4,136,128]{2,1,0:T(8,128)} collective-permute-done((f32[4,136,128]{2,1,0:T(8,128)}, f32[4,136,128]{2,1,0:T(8,128)}, u32[]{:S(2)}, u32[]{:S(2)}) %collective-permute-start.6) | collective-permute-done | bytes 278560 | tf_op jit(solution)/shard_map/ppermute | solution.py:36
  64.5 0.8 fusion.82
  65.4 0.7 collective-permute-done.3
  66.1 1.2 multiply_add_fusion.9
  67.5 5.6 %collective-permute-start.4 = (f32[4,136,128]{2,1,0:T(8,128)S(1)}, f32[4,136,128]{2,1,0:T(8,128)S(1)}, u32[]{:S(2)}, u32[]{:S(2)}) collective-permute-start(f32[4,136,128]{2,1,0:T(8,128)S(1)} %pad_maximum_fusion.5), channel_id=1, source_target_pairs={{0,64},{8,72},{16,80},{24,88},{32,96},{40,104},{48,112},{56,120},{... | collective-permute-start | bytes 835592 | tf_op jit(solution)/shard_map/ppermute | solution.py:35
  73.3 1.3 collective-permute-start.7
  74.5 0.8 slice_reduce_fusion.2
  75.5 1.8 collective-permute-done.4
  77.4 18.1 %collective-permute-start.5 = (f32[4,136,128]{2,1,0:T(8,128)S(1)}, f32[4,136,128]{2,1,0:T(8,128)S(1)}, u32[]{:S(2)}, u32[]{:S(2)}) collective-permute-start(f32[4,136,128]{2,1,0:T(8,128)S(1)} %pad_maximum_fusion.6), channel_id=1, source_target_pairs={{0,128},{8,136},{16,144},{24,152},{32,160},{40,168},{48,176},{56,1... | collective-permute-start | bytes 835592 | tf_op jit(solution)/shard_map/ppermute | solution.py:35
  95.7 1.3 collective-permute-start.8
  97.2 2.3 %collective-permute-done.5 = f32[4,136,128]{2,1,0:T(8,128)S(1)} collective-permute-done((f32[4,136,128]{2,1,0:T(8,128)S(1)}, f32[4,136,128]{2,1,0:T(8,128)S(1)}, u32[]{:S(2)}, u32[]{:S(2)}) %collective-permute-start.5) | collective-permute-done | bytes 278560 | tf_op jit(solution)/shard_map/ppermute | solution.py:35
  99.5 1.1 multiply_add_fusion.4
  100.6 1.1 multiply_add_fusion.2
  101.7 7.8 %collective-permute-done.8 = f32[4,136,128]{2,1,0:T(8,128)S(1)} collective-permute-done((f32[4,136,128]{2,1,0:T(8,128)S(1)}, f32[4,136,128]{2,1,0:T(8,128)S(1)}, u32[]{:S(2)}, u32[]{:S(2)}) %collective-permute-start.8) | collective-permute-done | bytes 278560 | tf_op jit(solution)/shard_map/ppermute | solution.py:36
  109.5 1.2 multiply_add_fusion.5
  110.7 1.1 multiply_add_fusion.3
  112.3 1.7 collective-permute-start.9
  114.0 4.9 %collective-permute-start.10 = (f32[4,256,128]{2,1,0:T(8,128)S(1)}, f32[4,256,128]{2,1,0:T(8,128)S(1)}, u32[]{:S(2)}, u32[]{:S(2)}) collective-permute-start(f32[4,256,128]{2,1,0:T(8,128)S(1)} %get-tuple-element.57), channel_id=1, source_target_pairs={{0,16},{8,24},{16,0},{24,8},{32,48},{40,56},{48,32},{56,40},{64,80... | collective-permute-start | bytes 1572872 | tf_op jit(solution)/shard_map/ppermute | solution.py:57
  118.9 3.7 %multiply_convert_fusion.1 = bf16[16,384,384]{2,1,0:T(8,128)(2,1)S(1)} fusion(f32[16,384]{1,0:T(8,128)S(1)} %get-tuple-element.71, pred[384,384]{1,0:T(8,128)(4,1)S(1)} %fusion.26, bf16[384,16,128]{0,2,1:T(8,128)(2,1)S(1)} %bitcast.209, bf16[384,16,128]{2,1,0:T(8,128)(2,1)S(1)} %bitcast.212), kind=kOutput, calls=%fused_computation.1 | convolution fusion | flops 615776256 | bytes 8036352 | tf_op jit(solution)/shard_map/shf,thf->hst/dot_general | solution.py:186
  122.6 7.5 %collective-permute-done.9 = f32[4,256,128]{2,1,0:T(8,128)S(1)} collective-permute-done((f32[4,256,128]{2,1,0:T(8,128)S(1)}, f32[4,256,128]{2,1,0:T(8,128)S(1)}, u32[]{:S(2)}, u32[]{:S(2)}) %collective-permute-start.9) | collective-permute-done | bytes 524320 | tf_op jit(solution)/shard_map/ppermute | solution.py:57
  130.1 5.6 %collective-permute-done.10 = f32[4,256,128]{2,1,0:T(8,128)S(1)} collective-permute-done((f32[4,256,128]{2,1,0:T(8,128)S(1)}, f32[4,256,128]{2,1,0:T(8,128)S(1)}, u32[]{:S(2)}, u32[]{:S(2)}) %collective-permute-start.10) | collective-permute-done | bytes 524320 | tf_op jit(solution)/shard_map/ppermute | solution.py:57
  136.2 1.0 fusion.21
  137.2 1.4 fusion.17
  138.6 2.7 %fusion.23 = f32[16,128,384]{2,1,0:T(8,128)} fusion(bf16[384,16,128]{0,2,1:T(8,128)(2,1)S(1)} %bitcast.199, f32[16,256,128]{2,1,0:T(8,128)S(1)} %bitcast.216), kind=kOutput, calls=%fused_computation.35 | convolution fusion | flops 603979776 | bytes 5767168 | tf_op jit(solution)/shard_map/the,hef->thf/dot_general | solution.py:194
  141.4 2.7 %fusion.10 = (f32[384,16]{0,1:T(8,128)S(1)}, bf16[384,16,128]{0,2,1:T(8,128)(2,1)}) fusion(bf16[384,16,128]{0,2,1:T(8,128)(2,1)S(1)} %bitcast.204, f32[16,128,384]{2,1,0:T(8,128)S(1)} %fusion.21, f32[384,16]{0,1:T(8,128)S(1)} %get-tuple-element.74, bf16[16,384,384]{2,1,0:T(8,128)(2,1)S(1)} %multiply_convert_fusion.1, bf16[384,16,128]{0,2,1:T(8,128)(2,1)S(1)} %bitcast.200), kind=kOutput, calls=%fused_computation.16 | convolution fusion | flops 608692224 | bytes 12632064 | tf_op jit(solution)/shard_map/hst,the->she/dot_general | solution.py:197
  144.1 2.4 %fusion.8 = (f32[384,16]{0,1:T(8,128)S(1)}, bf16[384,16,128]{0,2,1:T(8,128)(2,1)}) fusion(bf16[384,16,128]{0,2,1:T(8,128)(2,1)S(1)} %bitcast.201, f32[16,128,384]{2,1,0:T(8,128)S(1)} %fusion.17, f32[384,16]{0,1:T(8,128)S(1)} %get-tuple-element.73, bf16[384,16,128]{0,2,1:T(8,128)(2,1)S(1)} %bitcast.205, bf16[16,384,384]{2,1,0:T(8,128)(2,1)S(1)} %multiply_convert_fusion.1), kind=kOutput, calls=%fused_computation.14 | convolution fusion | flops 608692224 | bytes 12632064 | tf_op jit(solution)/shard_map/hst,she->the/dot_general | solution.py:203
  147.0 3.3 %collective-permute-start.13 = (f32[16]{0:T(128)S(1)}, f32[16]{0:T(128)S(1)}, u32[]{:S(2)}, u32[]{:S(2)}) collective-permute-start(f32[16]{0:T(128)S(1)} %multiply_reduce_fusion), channel_id=1, source_target_pairs={{0,16},{8,24},{16,0},{24,8},{32,48},{40,56},{48,32},{56,40},{64,80... | collective-permute-start | bytes 200 | tf_op jit(solution)/shard_map/ppermute | solution.py:113
  150.3 1.1 collective-permute-start.14
  151.4 2.6 %copy.96 = bf16[1,384,2048]{2,1,0:T(8,128)(2,1)} copy(bf16[1,384,2048]{1,2,0:T(8,128)(2,1)} %bitcast.220) | data formatting | bytes 3145728
  154.0 7.1 %fusion.12 = bf16[384,16,128]{0,2,1:T(8,128)(2,1)} fusion(f32[16,128,384]{2,1,0:T(8,128)} %fusion.23, bf16[384,16,128]{0,2,1:T(8,128)(2,1)} %bitcast.208, f32[16,384]{1,0:T(8,128)S(1)} %get-tuple-element.71, pred[384,384]{1,0:T(8,128)(4,1)S(1)} %copy-done.14, bf16[384,16,128]{0,2,1:T(8,128)(2,1)S(1)} %bitcast.206, bf16[384,16,128]{0,2,1:T(8,128)(2,1)S(1)} %bitcast.202, ...), kind=kOutput, calls=%fused_computation.19 | convolution fusion | flops 1222115328 | bytes 9633792 | tf_op jit(solution)/shard_map/hst,shf->thf/dot_general | solution.py:191
  161.1 2.7 %copy.97 = bf16[1,384,2048]{2,1,0:T(8,128)(2,1)} copy(bf16[1,384,2048]{1,2,0:T(8,128)(2,1)} %bitcast.219) | data formatting | bytes 3145728
  163.8 2.8 %collective-permute-start.15 = (f32[16]{0:T(128)S(1)}, f32[16]{0:T(128)S(1)}, u32[]{:S(2)}, u32[]{:S(2)}) collective-permute-start(f32[16]{0:T(128)S(1)} %fusion.64), channel_id=1, source_target_pairs={{0,32},{8,40},{16,48},{24,56},{32,0},{40,8},{48,16},{56,24},{64,96... | collective-permute-start | bytes 200 | tf_op jit(solution)/shard_map/ppermute | solution.py:113
  166.6 8.7 %collective-permute-start.16 = (f32[16]{0:T(128)S(1)}, f32[16]{0:T(128)S(1)}, u32[]{:S(2)}, u32[]{:S(2)}) collective-permute-start(f32[16]{0:T(128)S(1)} %fusion.64), channel_id=1, source_target_pairs={{0,64},{8,72},{16,80},{24,88},{32,96},{40,104},{48,112},{56,120},{... | collective-permute-start | bytes 200 | tf_op jit(solution)/shard_map/ppermute | solution.py:113
  175.3 1.4 collective-permute-start.17
  176.9 3.8 %collective-permute-done.17 = f32[16]{0:T(128)S(1)} collective-permute-done((f32[16]{0:T(128)S(1)}, f32[16]{0:T(128)S(1)}, u32[]{:S(2)}, u32[]{:S(2)}) %collective-permute-start.17) | collective-permute-done | bytes 96 | tf_op jit(solution)/shard_map/ppermute | solution.py:113
  180.8 1.6 copy.98
  182.4 5.8 %collective-permute-done.18 = f32[16]{0:T(128)S(1)} collective-permute-done((f32[16]{0:T(128)S(1)}, f32[16]{0:T(128)S(1)}, u32[]{:S(2)}, u32[]{:S(2)}) %collective-permute-start.18) | collective-permute-done | bytes 96 | tf_op jit(solution)/shard_map/ppermute | solution.py:113
  188.7 2.5 %collective-permute-start.22 = (f32[16]{0:T(128)S(1)}, f32[16]{0:T(128)S(1)}, u32[]{:S(2)}, u32[]{:S(2)}) collective-permute-start(f32[16]{0:T(128)S(1)} %fusion.58), channel_id=1, source_target_pairs={{0,4},{1,5},{2,6},{3,7},{4,0},{5,1},{6,2},{7,3},{8,12},{9,13},{10,... | collective-permute-start | bytes 200 | tf_op jit(solution)/shard_map/ppermute | solution.py:113
  191.2 3.3 %collective-permute-start.23 = (f32[16]{0:T(128)S(1)}, f32[16]{0:T(128)S(1)}, u32[]{:S(2)}, u32[]{:S(2)}) collective-permute-start(f32[16]{0:T(128)S(1)} %fusion.58), channel_id=1, source_target_pairs={{0,5},{1,4},{2,7},{3,6},{4,1},{5,0},{6,3},{7,2},{8,13},{9,12},{10,... | collective-permute-start | bytes 200 | tf_op jit(solution)/shard_map/ppermute | solution.py:113
  194.5 2.1 %collective-permute-start.19 = (f32[16]{0:T(128)S(1)}, f32[16]{0:T(128)S(1)}, u32[]{:S(2)}, u32[]{:S(2)}) collective-permute-start(f32[16]{0:T(128)S(1)} %fusion.58), channel_id=1, source_target_pairs={{0,1},{1,0},{2,3},{3,2},{4,5},{5,4},{6,7},{7,6},{8,9},{9,8},{10,11... | collective-permute-start | bytes 200 | tf_op jit(solution)/shard_map/ppermute | solution.py:113
  196.6 1.4 collective-permute-done.20
  (106 shorter events, 5.9 us)
Async XLA Ops:
  0.6 6.2 %copy-start.10 = (bf16[1,384,2048]{2,1,0:T(8,128)(2,1)S(1)}, bf16[1,384,2048]{2,1,0:T(8,128)(2,1)}, u32[]{:S(2)}) copy-start(bf16[1,384,2048]{2,1,0:T(8,128)(2,1)} %param.10) | copy-start | bytes 4718596
  6.8 1.6 copy-start.16
  6.8 1.6 copy-start.15
  14.8 2.9 %copy-start.1 = (bf16[48,8,16,128]{3,2,1,0:T(8,128)(2,1)S(1)}, bf16[48,8,16,128]{3,2,1,0:T(8,128)(2,1)}, u32[]{:S(2)}) copy-start(bf16[48,8,16,128]{3,2,1,0:T(8,128)(2,1)} %copy.105) | copy-start | bytes 4718596
  19.4 1.4 copy-start.3
  22.0 15.6 %collective-permute-start = (f32[4,264,128]{2,1,0:T(8,128)}, f32[4,264,128]{2,1,0:T(8,128)}, u32[]{:S(2)}, u32[]{:S(2)}) collective-permute-start(f32[4,264,128]{2,1,0:T(8,128)} %get-tuple-element.55), channel_id=1, source_target_pairs={{0,8},{8,16},{16,24},{24,0},{32,40},{40,48},{48,56},{56,32},{64,72... | collective-permute-start | bytes 1622024 | tf_op jit(solution)/shard_map/ppermute | solution.py:57
  23.6 26.8 %collective-permute-start.1 = (f32[4,264,128]{2,1,0:T(8,128)}, f32[4,264,128]{2,1,0:T(8,128)}, u32[]{:S(2)}, u32[]{:S(2)}) collective-permute-start(f32[4,264,128]{2,1,0:T(8,128)} %get-tuple-element.54), channel_id=1, source_target_pairs={{0,16},{8,24},{16,0},{24,8},{32,48},{40,56},{48,32},{56,40},{64,80... | collective-permute-start | bytes 1622024 | tf_op jit(solution)/shard_map/ppermute | solution.py:57
  26.5 23.9 %collective-permute-start.2 = (f32[4,264,128]{2,1,0:T(8,128)}, f32[4,264,128]{2,1,0:T(8,128)}, u32[]{:S(2)}, u32[]{:S(2)}) collective-permute-start(f32[4,264,128]{2,1,0:T(8,128)} %get-tuple-element.53), channel_id=1, source_target_pairs={{0,24},{8,0},{16,8},{24,16},{32,56},{40,32},{48,40},{56,48},{64,88... | collective-permute-start | bytes 1622024 | tf_op jit(solution)/shard_map/ppermute | solution.py:57
  52.1 2.4 %copy-start.4 = (f32[1,4,264,128]{3,2,1,0:T(8,128)}, f32[1,4,264,128]{3,2,1,0:T(8,128)S(1)}, u32[]{:S(2)}) copy-start(f32[1,4,264,128]{3,2,1,0:T(8,128)S(1)} %get-tuple-element.40) | copy-start | bytes 1622020
  52.1 2.4 %copy-start.5 = (f32[1,4,264,128]{3,2,1,0:T(8,128)}, f32[1,4,264,128]{3,2,1,0:T(8,128)S(1)}, u32[]{:S(2)}) copy-start(f32[1,4,264,128]{3,2,1,0:T(8,128)S(1)} %get-tuple-element.42) | copy-start | bytes 1622020
  52.2 2.4 %copy-start.6 = (f32[1,4,264,128]{3,2,1,0:T(8,128)}, f32[1,4,264,128]{3,2,1,0:T(8,128)S(1)}, u32[]{:S(2)}) copy-start(f32[1,4,264,128]{3,2,1,0:T(8,128)S(1)} %get-tuple-element.41) | copy-start | bytes 1622020
  52.2 2.4 %copy-start.7 = (f32[1,4,264,128]{3,2,1,0:T(8,128)}, f32[1,4,264,128]{3,2,1,0:T(8,128)S(1)}, u32[]{:S(2)}) copy-start(f32[1,4,264,128]{3,2,1,0:T(8,128)S(1)} %get-tuple-element.39) | copy-start | bytes 1622020
  53.5 1.0 copy-start.8
  53.5 2.4 %copy-start.9 = (f32[4,128,128]{2,1,0:T(8,128)}, f32[4,128,128]{2,1,0:T(8,128)S(1)}, u32[]{:S(2)}) copy-start(f32[4,128,128]{2,1,0:T(8,128)S(1)} %get-tuple-element.51) | copy-start | bytes 786436
  54.6 9.9 %collective-permute-start.6 = (f32[4,136,128]{2,1,0:T(8,128)}, f32[4,136,128]{2,1,0:T(8,128)}, u32[]{:S(2)}, u32[]{:S(2)}) collective-permute-start(f32[4,136,128]{2,1,0:T(8,128)} %get-tuple-element.76), channel_id=1, source_target_pairs={{32,0},{40,8},{48,16},{56,24},{64,32},{72,40},{80,48},{88,56},{96,... | collective-permute-start | bytes 835592 | tf_op jit(solution)/shard_map/ppermute | solution.py:36
  56.3 62.6 %copy-start.13 = (pred[384,384]{1,0:T(8,128)(4,1)}, pred[384,384]{1,0:T(8,128)(4,1)S(1)}, u32[]{:S(2)}) copy-start(pred[384,384]{1,0:T(8,128)(4,1)S(1)} %fusion.26) | copy-start | bytes 442372
  56.3 9.8 %collective-permute-start.3 = (f32[4,136,128]{2,1,0:T(8,128)}, f32[4,136,128]{2,1,0:T(8,128)S(1)}, u32[]{:S(2)}, u32[]{:S(2)}) collective-permute-start(f32[4,136,128]{2,1,0:T(8,128)} %get-tuple-element.75), channel_id=1, source_target_pairs={{0,32},{8,40},{16,48},{24,56},{32,64},{40,72},{48,80},{56,88},{64,... | collective-permute-start | bytes 835592 | tf_op jit(solution)/shard_map/ppermute | solution.py:35
  67.5 9.8 %collective-permute-start.4 = (f32[4,136,128]{2,1,0:T(8,128)S(1)}, f32[4,136,128]{2,1,0:T(8,128)S(1)}, u32[]{:S(2)}, u32[]{:S(2)}) collective-permute-start(f32[4,136,128]{2,1,0:T(8,128)S(1)} %pad_maximum_fusion.5), channel_id=1, source_target_pairs={{0,64},{8,72},{16,80},{24,88},{32,96},{40,104},{48,112},{56,120},{... | collective-permute-start | bytes 835592 | tf_op jit(solution)/shard_map/ppermute | solution.py:35
  73.3 22.2 %collective-permute-start.7 = (f32[4,136,128]{2,1,0:T(8,128)S(1)}, f32[4,136,128]{2,1,0:T(8,128)S(1)}, u32[]{:S(2)}, u32[]{:S(2)}) collective-permute-start(f32[4,136,128]{2,1,0:T(8,128)S(1)} %pad_maximum_fusion.7), channel_id=1, source_target_pairs={{64,0},{72,8},{80,16},{88,24},{96,32},{104,40},{112,48},{120,56},{... | collective-permute-start | bytes 835592 | tf_op jit(solution)/shard_map/ppermute | solution.py:36
  75.5 25.1 %copy-start.12 = (f32[4,128,128]{2,1,0:T(8,128)S(1)}, f32[4,128,128]{2,1,0:T(8,128)}, u32[]{:S(2)}) copy-start(f32[4,128,128]{2,1,0:T(8,128)} %get-tuple-element.31) | copy-start | bytes 786436
  77.4 22.1 %collective-permute-start.5 = (f32[4,136,128]{2,1,0:T(8,128)S(1)}, f32[4,136,128]{2,1,0:T(8,128)S(1)}, u32[]{:S(2)}, u32[]{:S(2)}) collective-permute-start(f32[4,136,128]{2,1,0:T(8,128)S(1)} %pad_maximum_fusion.6), channel_id=1, source_target_pairs={{0,128},{8,136},{16,144},{24,152},{32,160},{40,168},{48,176},{56,1... | collective-permute-start | bytes 835592 | tf_op jit(solution)/shard_map/ppermute | solution.py:35
  95.7 13.8 %collective-permute-start.8 = (f32[4,136,128]{2,1,0:T(8,128)S(1)}, f32[4,136,128]{2,1,0:T(8,128)S(1)}, u32[]{:S(2)}, u32[]{:S(2)}) collective-permute-start(f32[4,136,128]{2,1,0:T(8,128)S(1)} %pad_maximum_fusion.8), channel_id=1, source_target_pairs={{128,0},{136,8},{144,16},{152,24},{160,32},{168,40},{176,48},{184,... | collective-permute-start | bytes 835592 | tf_op jit(solution)/shard_map/ppermute | solution.py:36
  112.1 6.8 %copy-start = (bf16[1,384,2048]{1,2,0:T(8,128)(2,1)S(1)}, bf16[1,384,2048]{1,2,0:T(8,128)(2,1)}, u32[]{:S(2)}) copy-start(bf16[1,384,2048]{1,2,0:T(8,128)(2,1)} %copy.103) | copy-start | bytes 4718596
  112.1 6.8 %copy-start.2 = (bf16[48,8,16,128]{3,2,1,0:T(8,128)(2,1)S(1)}, bf16[48,8,16,128]{3,2,1,0:T(8,128)(2,1)}, u32[]{:S(2)}) copy-start(bf16[48,8,16,128]{3,2,1,0:T(8,128)(2,1)} %copy.105) | copy-start | bytes 4718596
  112.3 17.9 %collective-permute-start.9 = (f32[4,256,128]{2,1,0:T(8,128)S(1)}, f32[4,256,128]{2,1,0:T(8,128)S(1)}, u32[]{:S(2)}, u32[]{:S(2)}) collective-permute-start(f32[4,256,128]{2,1,0:T(8,128)S(1)} %get-tuple-element.58), channel_id=1, source_target_pairs={{0,8},{8,16},{16,24},{24,0},{32,40},{40,48},{48,56},{56,32},{64,72... | collective-permute-start | bytes 1572872 | tf_op jit(solution)/shard_map/ppermute | solution.py:57
  114.0 21.8 %collective-permute-start.10 = (f32[4,256,128]{2,1,0:T(8,128)S(1)}, f32[4,256,128]{2,1,0:T(8,128)S(1)}, u32[]{:S(2)}, u32[]{:S(2)}) collective-permute-start(f32[4,256,128]{2,1,0:T(8,128)S(1)} %get-tuple-element.57), channel_id=1, source_target_pairs={{0,16},{8,24},{16,0},{24,8},{32,48},{40,56},{48,32},{56,40},{64,80... | collective-permute-start | bytes 1572872 | tf_op jit(solution)/shard_map/ppermute | solution.py:57
  118.9 16.9 %collective-permute-start.11 = (f32[4,256,128]{2,1,0:T(8,128)S(1)}, f32[4,256,128]{2,1,0:T(8,128)S(1)}, u32[]{:S(2)}, u32[]{:S(2)}) collective-permute-start(f32[4,256,128]{2,1,0:T(8,128)S(1)} %get-tuple-element.56), channel_id=1, source_target_pairs={{0,24},{8,0},{16,8},{24,16},{32,56},{40,32},{48,40},{56,48},{64,88... | collective-permute-start | bytes 1572872 | tf_op jit(solution)/shard_map/ppermute | solution.py:57
  146.5 7.5 %copy-start.14 = (pred[384,384]{1,0:T(8,128)(4,1)S(1)}, pred[384,384]{1,0:T(8,128)(4,1)}, u32[]{:S(2)}) copy-start(pred[384,384]{1,0:T(8,128)(4,1)} %copy-done.13) | copy-start | bytes 442372
  146.6 17.1 %collective-permute-start.12 = (f32[16]{0:T(128)S(1)}, f32[16]{0:T(128)S(1)}, u32[]{:S(2)}, u32[]{:S(2)}) collective-permute-start(f32[16]{0:T(128)S(1)} %multiply_reduce_fusion), channel_id=1, source_target_pairs={{0,8},{8,0},{16,24},{24,16},{32,40},{40,32},{48,56},{56,48},{64,72... | collective-permute-start | bytes 200 | tf_op jit(solution)/shard_map/ppermute | solution.py:113
  147.0 16.7 %collective-permute-start.13 = (f32[16]{0:T(128)S(1)}, f32[16]{0:T(128)S(1)}, u32[]{:S(2)}, u32[]{:S(2)}) collective-permute-start(f32[16]{0:T(128)S(1)} %multiply_reduce_fusion), channel_id=1, source_target_pairs={{0,16},{8,24},{16,0},{24,8},{32,48},{40,56},{48,32},{56,40},{64,80... | collective-permute-start | bytes 200 | tf_op jit(solution)/shard_map/ppermute | solution.py:113
  150.3 13.4 %collective-permute-start.14 = (f32[16]{0:T(128)S(1)}, f32[16]{0:T(128)S(1)}, u32[]{:S(2)}, u32[]{:S(2)}) collective-permute-start(f32[16]{0:T(128)S(1)} %multiply_reduce_fusion), channel_id=1, source_target_pairs={{0,24},{8,16},{16,8},{24,0},{32,56},{40,48},{48,40},{56,32},{64,88... | collective-permute-start | bytes 200 | tf_op jit(solution)/shard_map/ppermute | solution.py:113
  161.1 19.7 %copy-start.11 = (bf16[384,16,128]{0,2,1:T(8,128)(2,1)S(1)}, bf16[384,16,128]{0,2,1:T(8,128)(2,1)}, u32[]{:S(2)}) copy-start(bf16[384,16,128]{0,2,1:T(8,128)(2,1)} %fusion.12) | copy-start | bytes 4718596
  163.8 12.9 %collective-permute-start.15 = (f32[16]{0:T(128)S(1)}, f32[16]{0:T(128)S(1)}, u32[]{:S(2)}, u32[]{:S(2)}) collective-permute-start(f32[16]{0:T(128)S(1)} %fusion.64), channel_id=1, source_target_pairs={{0,32},{8,40},{16,48},{24,56},{32,0},{40,8},{48,16},{56,24},{64,96... | collective-permute-start | bytes 200 | tf_op jit(solution)/shard_map/ppermute | solution.py:113
  166.6 10.2 %collective-permute-start.16 = (f32[16]{0:T(128)S(1)}, f32[16]{0:T(128)S(1)}, u32[]{:S(2)}, u32[]{:S(2)}) collective-permute-start(f32[16]{0:T(128)S(1)} %fusion.64), channel_id=1, source_target_pairs={{0,64},{8,72},{16,80},{24,88},{32,96},{40,104},{48,112},{56,120},{... | collective-permute-start | bytes 200 | tf_op jit(solution)/shard_map/ppermute | solution.py:113
  175.3 5.3 %collective-permute-start.17 = (f32[16]{0:T(128)S(1)}, f32[16]{0:T(128)S(1)}, u32[]{:S(2)}, u32[]{:S(2)}) collective-permute-start(f32[16]{0:T(128)S(1)} %fusion.64), channel_id=1, source_target_pairs={{0,96},{8,104},{16,112},{24,120},{32,64},{40,72},{48,80},{56,88},{... | collective-permute-start | bytes 200 | tf_op jit(solution)/shard_map/ppermute | solution.py:113
  180.7 7.5 %collective-permute-start.18 = (f32[16]{0:T(128)S(1)}, f32[16]{0:T(128)S(1)}, u32[]{:S(2)}, u32[]{:S(2)}) collective-permute-start(f32[16]{0:T(128)S(1)} %fusion.61), channel_id=1, source_target_pairs={{0,128},{8,136},{16,144},{24,152},{32,160},{40,168},{48,176},{56,1... | collective-permute-start | bytes 200 | tf_op jit(solution)/shard_map/ppermute | solution.py:113
  188.2 6.2 %collective-permute-start.24 = (f32[16]{0:T(128)S(1)}, f32[16]{0:T(128)S(1)}, u32[]{:S(2)}, u32[]{:S(2)}) collective-permute-start(f32[16]{0:T(128)S(1)} %fusion.58), channel_id=1, source_target_pairs={{0,6},{1,7},{2,4},{3,5},{4,2},{5,3},{6,0},{7,1},{8,14},{9,15},{10,... | collective-permute-start | bytes 200 | tf_op jit(solution)/shard_map/ppermute | solution.py:113
  188.7 5.8 %collective-permute-start.25 = (f32[16]{0:T(128)S(1)}, f32[16]{0:T(128)S(1)}, u32[]{:S(2)}, u32[]{:S(2)}) collective-permute-start(f32[16]{0:T(128)S(1)} %fusion.58), channel_id=1, source_target_pairs={{0,7},{1,6},{2,5},{3,4},{4,3},{5,2},{6,1},{7,0},{8,15},{9,14},{10,... | collective-permute-start | bytes 200 | tf_op jit(solution)/shard_map/ppermute | solution.py:113
  188.7 7.9 %collective-permute-start.22 = (f32[16]{0:T(128)S(1)}, f32[16]{0:T(128)S(1)}, u32[]{:S(2)}, u32[]{:S(2)}) collective-permute-start(f32[16]{0:T(128)S(1)} %fusion.58), channel_id=1, source_target_pairs={{0,4},{1,5},{2,6},{3,7},{4,0},{5,1},{6,2},{7,3},{8,12},{9,13},{10,... | collective-permute-start | bytes 200 | tf_op jit(solution)/shard_map/ppermute | solution.py:113
  191.2 5.4 %collective-permute-start.23 = (f32[16]{0:T(128)S(1)}, f32[16]{0:T(128)S(1)}, u32[]{:S(2)}, u32[]{:S(2)}) collective-permute-start(f32[16]{0:T(128)S(1)} %fusion.58), channel_id=1, source_target_pairs={{0,5},{1,4},{2,7},{3,6},{4,1},{5,0},{6,3},{7,2},{8,13},{9,12},{10,... | collective-permute-start | bytes 200 | tf_op jit(solution)/shard_map/ppermute | solution.py:113
  194.4 3.5 %collective-permute-start.20 = (f32[16]{0:T(128)S(1)}, f32[16]{0:T(128)S(1)}, u32[]{:S(2)}, u32[]{:S(2)}) collective-permute-start(f32[16]{0:T(128)S(1)} %fusion.58), channel_id=1, source_target_pairs={{0,2},{1,3},{2,0},{3,1},{4,6},{5,7},{6,4},{7,5},{8,10},{9,11},{10,... | collective-permute-start | bytes 200 | tf_op jit(solution)/shard_map/ppermute | solution.py:113
  194.5 3.5 %collective-permute-start.21 = (f32[16]{0:T(128)S(1)}, f32[16]{0:T(128)S(1)}, u32[]{:S(2)}, u32[]{:S(2)}) collective-permute-start(f32[16]{0:T(128)S(1)} %fusion.58), channel_id=1, source_target_pairs={{0,3},{1,2},{2,1},{3,0},{4,7},{5,6},{6,5},{7,4},{8,11},{9,10},{10,... | collective-permute-start | bytes 200 | tf_op jit(solution)/shard_map/ppermute | solution.py:113
  194.5 3.5 %collective-permute-start.19 = (f32[16]{0:T(128)S(1)}, f32[16]{0:T(128)S(1)}, u32[]{:S(2)}, u32[]{:S(2)}) collective-permute-start(f32[16]{0:T(128)S(1)} %fusion.58), channel_id=1, source_target_pairs={{0,1},{1,0},{2,3},{3,2},{4,5},{5,4},{6,7},{7,6},{8,9},{9,8},{10,11... | collective-permute-start | bytes 200 | tf_op jit(solution)/shard_map/ppermute | solution.py:113

commit v16 on v5

--- a/solution.py
+++ b/solution.py
@@ -74,7 +74,12 @@
     for j in range(1, group):
         excl.append(own_a[j - 1][:, None, None] * excl[j - 1] + own_s[j - 1])
         excl_a.append(excl_a[j - 1] * own_a[j - 1])
-    total = own_a[group - 1][:, None, None] * excl[group - 1] + own_s[group - 1]
+    total = own_s[group - 1]
+    for j in range(group - 1):
+        scale = own_a[j + 1]
+        for k in range(j + 2, group):
+            scale = scale * own_a[k]
+        total = total + scale[:, None, None] * own_s[j]
     total_a = excl_a[group - 1] * own_a[group - 1]
     later = [None] * group
     later_a = [None] * group
@@ -83,7 +88,12 @@
     for j in range(group - 2, -1, -1):
         later[j] = own_b[j + 1] + own_a[j + 1][:, None, None] * later[j + 1]
         later_a[j] = own_a[j + 1] * later_a[j + 1]
-    rtotal = own_b[0] + own_a[0][:, None, None] * later[0]
+    rtotal = own_b[0]
+    for j in range(1, group):
+        scale = own_a[0]
+        for k in range(1, j):
+            scale = scale * own_a[k]
+        rtotal = rtotal + scale[:, None, None] * own_b[j]
     before, after = group_scan(
         packed(total_a, total), packed(total_a, rtotal), axis, group
     )

time: 196 us -> 196 us (level)
  other arithmetic: 16.6 us -> 12.6 us
  waiting for transfers between devices: 65.9 us -> 67.9 us
    ppermute x3, waiting for transfers between devices: 11.4 us -> 13.5 us  [group_scan(): rgot = lax.ppermute(bwd, axis, down)]
    unnamed x42 -> x46, local copies, waits for them, and re-layouts: 14.1 us -> 15.2 us
  transfers between devices with their start and end apart: 23 -> 23, of which waited for: 15 -> 15; matrix products, arithmetic and copies ran while one was open for 11% -> 10% of each run, Pallas kernels for 0% -> 0%
where the time goes in v16:
time: 196 us; the launch traced here: 194 us
  waiting for transfers between devices  67.9 us (35%)
  starting transfers between devices  65.5 us (33%)
  matrix products  25.4 us (13%)
  local copies, waits for them, and re-layouts  20.8 us (11%)
  other arithmetic  12.6 us (6%)
  between operations  2.1 us (1%)
    ppermute x6, waiting for transfers between devices, row_exchange(): got.append(lax.ppermute(send, axis, pairs))  35.6 us
    ppermute x3, starting transfers between devices, group_scan(): got = lax.ppermute(fwd, axis, up)  28.5 us
    ppermute x11, starting transfers between devices, digit_sum(): lax.ppermute(value, axis, [(i, i ^ k * step) for i in range(count)])  20.7 us
    unnamed x46, local copies, waits for them, and re-layouts  15.2 us
    ppermute x11, waiting for transfers between devices, digit_sum(): lax.ppermute(value, axis, [(i, i ^ k * step) for i in range(count)])  14.1 us
    ppermute x3, waiting for transfers between devices, group_scan(): rgot = lax.ppermute(bwd, axis, down)  13.5 us
    ppermute x6, starting transfers between devices, row_exchange(): got.append(lax.ppermute(send, axis, pairs))  12.4 us
    dot_general x1, matrix products, on_device(): jnp.einsum('hst,shf->thf', attn_prob, gradient_block, preferred_element_t...  7.06 us
  transfers between devices with their start and end apart: 23, of which 15 were waited for; matrix products, arithmetic and copies ran while one was open for 10% of the time, Pallas kernels for 0%

profile of v16, /device:TPU:6, one launch (start us, length us, event | category | flops | bytes accessed | tf_op | source)
XLA Modules:
  0.0 194.3 jit_solution(8575535046376377354)
XLA Ops:
  0.7 0.9 reduce-window_clone.1
  1.6 0.7 subtract_bitcast_fusion
  3.0 0.6 slice.185
  4.2 0.7 broadcast_compare_fusion
  4.9 1.9 copy.87
  6.8 1.6 copy.103
  8.5 0.9 reduce-window.24
  9.8 1.9 copy.85
  11.7 3.0 %copy.105 = bf16[48,8,16,128]{3,2,1,0:T(8,128)(2,1)} copy(bf16[48,8,16,128]{3,1,2,0:T(8,128)(2,1)} %bitcast.245) | data formatting | bytes 3145728
  14.8 2.9 %fusion.9 = f32[16,128,128]{2,1,0:T(8,128)S(1)} fusion(bf16[384,16,128]{0,2,1:T(8,128)(2,1)} %bitcast.231, bf16[384,16,128]{0,2,1:T(8,128)(2,1)S(1)} %bitcast.227, f32[384,16]{0,1:T(8,128)S(1)} %get-tuple-element.72), kind=kOutput, calls=%fused_computation.15 | convolution fusion | flops 605552640 | bytes 4218880 | tf_op jit(solution)/shard_map/she,shf->hef/dot_general | solution.py:190
  17.8 1.4 fusion.7
  19.4 1.3 copy-done.3
  20.8 1.2 dynamic-slice_bitcast_fusion
  22.0 1.6 collective-permute-start
  23.6 2.9 %collective-permute-start.1 = (f32[4,264,128]{2,1,0:T(8,128)}, f32[4,264,128]{2,1,0:T(8,128)}, u32[]{:S(2)}, u32[]{:S(2)}) collective-permute-start(f32[4,264,128]{2,1,0:T(8,128)} %get-tuple-element.50), channel_id=1, source_target_pairs={{0,16},{8,24},{16,0},{24,8},{32,48},{40,56},{48,32},{56,40},{64,80... | collective-permute-start | bytes 1622024 | tf_op jit(solution)/shard_map/ppermute | solution.py:57
  26.5 1.3 collective-permute-start.2
  27.9 9.7 %collective-permute-done = f32[4,264,128]{2,1,0:T(8,128)} collective-permute-done((f32[4,264,128]{2,1,0:T(8,128)}, f32[4,264,128]{2,1,0:T(8,128)}, u32[]{:S(2)}, u32[]{:S(2)}) %collective-permute-start) | collective-permute-done | bytes 540704 | tf_op jit(solution)/shard_map/ppermute | solution.py:57
  37.6 12.8 %collective-permute-done.1 = f32[4,264,128]{2,1,0:T(8,128)} collective-permute-done((f32[4,264,128]{2,1,0:T(8,128)}, f32[4,264,128]{2,1,0:T(8,128)}, u32[]{:S(2)}, u32[]{:S(2)}) %collective-permute-start.1) | collective-permute-done | bytes 540704 | tf_op jit(solution)/shard_map/ppermute | solution.py:57
  50.4 1.8 fusion.28
  52.4 0.5 copy-done.4
  53.5 0.4 copy-done.13
  53.9 0.9 pad_maximum_fusion.4
  54.7 1.3 collective-permute-start.6
  56.4 4.6 %collective-permute-start.3 = (f32[4,136,128]{2,1,0:T(8,128)}, f32[4,136,128]{2,1,0:T(8,128)S(1)}, u32[]{:S(2)}, u32[]{:S(2)}) collective-permute-start(f32[4,136,128]{2,1,0:T(8,128)} %get-tuple-element.73), channel_id=1, source_target_pairs={{0,32},{8,40},{16,48},{24,56},{32,64},{40,72},{48,80},{56,88},{64,... | collective-permute-start | bytes 835592 | tf_op jit(solution)/shard_map/ppermute | solution.py:35
  61.0 3.7 %collective-permute-done.6 = f32[4,136,128]{2,1,0:T(8,128)} collective-permute-done((f32[4,136,128]{2,1,0:T(8,128)}, f32[4,136,128]{2,1,0:T(8,128)}, u32[]{:S(2)}, u32[]{:S(2)}) %collective-permute-start.6) | collective-permute-done | bytes 278560 | tf_op jit(solution)/shard_map/ppermute | solution.py:36
  64.6 0.8 fusion.77
  65.6 0.6 collective-permute-done.3
  66.2 1.1 multiply_add_fusion.10
  67.5 5.8 %collective-permute-start.4 = (f32[4,136,128]{2,1,0:T(8,128)S(1)}, f32[4,136,128]{2,1,0:T(8,128)S(1)}, u32[]{:S(2)}, u32[]{:S(2)}) collective-permute-start(f32[4,136,128]{2,1,0:T(8,128)S(1)} %pad_maximum_fusion.5), channel_id=1, source_target_pairs={{0,64},{8,72},{16,80},{24,88},{32,96},{40,104},{48,112},{56,120},{... | collective-permute-start | bytes 835592 | tf_op jit(solution)/shard_map/ppermute | solution.py:35
  73.4 1.3 collective-permute-start.7
  74.7 0.8 slice_reduce_fusion.2
  75.6 1.8 collective-permute-done.4
  77.5 18.1 %collective-permute-start.5 = (f32[4,136,128]{2,1,0:T(8,128)S(1)}, f32[4,136,128]{2,1,0:T(8,128)S(1)}, u32[]{:S(2)}, u32[]{:S(2)}) collective-permute-start(f32[4,136,128]{2,1,0:T(8,128)S(1)} %pad_maximum_fusion.6), channel_id=1, source_target_pairs={{0,128},{8,136},{16,144},{24,152},{32,160},{40,168},{48,176},{56,1... | collective-permute-start | bytes 835592 | tf_op jit(solution)/shard_map/ppermute | solution.py:35
  95.8 1.3 collective-permute-start.8
  97.4 2.3 %collective-permute-done.5 = f32[4,136,128]{2,1,0:T(8,128)S(1)} collective-permute-done((f32[4,136,128]{2,1,0:T(8,128)S(1)}, f32[4,136,128]{2,1,0:T(8,128)S(1)}, u32[]{:S(2)}, u32[]{:S(2)}) %collective-permute-start.5) | collective-permute-done | bytes 278560 | tf_op jit(solution)/shard_map/ppermute | solution.py:35
  99.8 9.8 %collective-permute-done.8 = f32[4,136,128]{2,1,0:T(8,128)S(1)} collective-permute-done((f32[4,136,128]{2,1,0:T(8,128)S(1)}, f32[4,136,128]{2,1,0:T(8,128)S(1)}, u32[]{:S(2)}, u32[]{:S(2)}) %collective-permute-start.8) | collective-permute-done | bytes 278560 | tf_op jit(solution)/shard_map/ppermute | solution.py:36
  109.6 1.1 multiply_add_fusion.5
  111.5 1.7 collective-permute-start.9
  113.3 4.9 %collective-permute-start.10 = (f32[4,256,128]{2,1,0:T(8,128)S(1)}, f32[4,256,128]{2,1,0:T(8,128)S(1)}, u32[]{:S(2)}, u32[]{:S(2)}) collective-permute-start(f32[4,256,128]{2,1,0:T(8,128)S(1)} %get-tuple-element.53), channel_id=1, source_target_pairs={{0,16},{8,24},{16,0},{24,8},{32,48},{40,56},{48,32},{56,40},{64,80... | collective-permute-start | bytes 1572872 | tf_op jit(solution)/shard_map/ppermute | solution.py:57
  118.1 3.7 %multiply_convert_fusion.1 = bf16[16,384,384]{2,1,0:T(8,128)(2,1)S(1)} fusion(f32[16,384]{1,0:T(8,128)S(1)} %get-tuple-element.69, pred[384,384]{1,0:T(8,128)(4,1)S(1)} %fusion.26, bf16[384,16,128]{0,2,1:T(8,128)(2,1)S(1)} %bitcast.233, bf16[384,16,128]{2,1,0:T(8,128)(2,1)S(1)} %bitcast.236), kind=kOutput, calls=%fused_computation.1 | convolution fusion | flops 615776256 | bytes 8036352 | tf_op jit(solution)/shard_map/shf,thf->hst/dot_general | solution.py:196
  121.9 7.5 %collective-permute-done.9 = f32[4,256,128]{2,1,0:T(8,128)S(1)} collective-permute-done((f32[4,256,128]{2,1,0:T(8,128)S(1)}, f32[4,256,128]{2,1,0:T(8,128)S(1)}, u32[]{:S(2)}, u32[]{:S(2)}) %collective-permute-start.9) | collective-permute-done | bytes 524320 | tf_op jit(solution)/shard_map/ppermute | solution.py:57
  129.4 5.6 %collective-permute-done.10 = f32[4,256,128]{2,1,0:T(8,128)S(1)} collective-permute-done((f32[4,256,128]{2,1,0:T(8,128)S(1)}, f32[4,256,128]{2,1,0:T(8,128)S(1)}, u32[]{:S(2)}, u32[]{:S(2)}) %collective-permute-start.10) | collective-permute-done | bytes 524320 | tf_op jit(solution)/shard_map/ppermute | solution.py:57
  135.4 1.0 fusion.21
  136.4 1.4 fusion.17
  137.9 2.7 %fusion.23 = f32[16,128,384]{2,1,0:T(8,128)} fusion(bf16[384,16,128]{0,2,1:T(8,128)(2,1)S(1)} %bitcast.223, f32[16,256,128]{2,1,0:T(8,128)S(1)} %bitcast.240), kind=kOutput, calls=%fused_computation.35 | convolution fusion | flops 603979776 | bytes 5767168 | tf_op jit(solution)/shard_map/the,hef->thf/dot_general | solution.py:204
  140.6 2.8 %fusion.10 = (f32[384,16]{0,1:T(8,128)S(1)}, bf16[384,16,128]{0,2,1:T(8,128)(2,1)}) fusion(bf16[384,16,128]{0,2,1:T(8,128)(2,1)S(1)} %bitcast.228, f32[16,128,384]{2,1,0:T(8,128)S(1)} %fusion.21, f32[384,16]{0,1:T(8,128)S(1)} %get-tuple-element.72, bf16[16,384,384]{2,1,0:T(8,128)(2,1)S(1)} %multiply_convert_fusion.1, bf16[384,16,128]{0,2,1:T(8,128)(2,1)S(1)} %bitcast.224), kind=kOutput, calls=%fused_computation.16 | convolution fusion | flops 608692224 | bytes 12632064 | tf_op jit(solution)/shard_map/hst,the->she/dot_general | solution.py:207
  143.4 2.4 %fusion.8 = (f32[384,16]{0,1:T(8,128)S(1)}, bf16[384,16,128]{0,2,1:T(8,128)(2,1)}) fusion(bf16[384,16,128]{0,2,1:T(8,128)(2,1)S(1)} %bitcast.225, f32[16,128,384]{2,1,0:T(8,128)S(1)} %fusion.17, f32[384,16]{0,1:T(8,128)S(1)} %get-tuple-element.71, bf16[384,16,128]{0,2,1:T(8,128)(2,1)S(1)} %bitcast.229, bf16[16,384,384]{2,1,0:T(8,128)(2,1)S(1)} %multiply_convert_fusion.1), kind=kOutput, calls=%fused_computation.14 | convolution fusion | flops 608692224 | bytes 12632064 | tf_op jit(solution)/shard_map/hst,she->the/dot_general | solution.py:213
  146.2 3.3 %collective-permute-start.13 = (f32[16]{0:T(128)S(1)}, f32[16]{0:T(128)S(1)}, u32[]{:S(2)}, u32[]{:S(2)}) collective-permute-start(f32[16]{0:T(128)S(1)} %multiply_reduce_fusion), channel_id=1, source_target_pairs={{0,16},{8,24},{16,0},{24,8},{32,48},{40,56},{48,32},{56,40},{64,80... | collective-permute-start | bytes 200 | tf_op jit(solution)/shard_map/ppermute | solution.py:123
  149.6 1.1 collective-permute-start.14
  150.7 7.1 %fusion.12 = bf16[384,16,128]{0,2,1:T(8,128)(2,1)} fusion(f32[16,128,384]{2,1,0:T(8,128)} %fusion.23, bf16[384,16,128]{0,2,1:T(8,128)(2,1)} %bitcast.232, f32[16,384]{1,0:T(8,128)S(1)} %get-tuple-element.69, pred[384,384]{1,0:T(8,128)(4,1)S(1)} %copy-done.17, bf16[384,16,128]{0,2,1:T(8,128)(2,1)S(1)} %bitcast.230, bf16[384,16,128]{0,2,1:T(8,128)(2,1)S(1)} %bitcast.226, ...), kind=kOutput, calls=%fused_computation.19 | convolution fusion | flops 1222115328 | bytes 9633792 | tf_op jit(solution)/shard_map/hst,shf->thf/dot_general | solution.py:201
  157.7 2.7 %copy.96 = bf16[1,384,2048]{2,1,0:T(8,128)(2,1)} copy(bf16[1,384,2048]{1,2,0:T(8,128)(2,1)} %bitcast.244) | data formatting | bytes 3145728
  160.5 2.6 %collective-permute-start.15 = (f32[16]{0:T(128)S(1)}, f32[16]{0:T(128)S(1)}, u32[]{:S(2)}, u32[]{:S(2)}) collective-permute-start(f32[16]{0:T(128)S(1)} %fusion.66), channel_id=1, source_target_pairs={{0,32},{8,40},{16,48},{24,56},{32,0},{40,8},{48,16},{56,24},{64,96... | collective-permute-start | bytes 200 | tf_op jit(solution)/shard_map/ppermute | solution.py:123
  163.1 8.8 %collective-permute-start.16 = (f32[16]{0:T(128)S(1)}, f32[16]{0:T(128)S(1)}, u32[]{:S(2)}, u32[]{:S(2)}) collective-permute-start(f32[16]{0:T(128)S(1)} %fusion.66), channel_id=1, source_target_pairs={{0,64},{8,72},{16,80},{24,88},{32,96},{40,104},{48,112},{56,120},{... | collective-permute-start | bytes 200 | tf_op jit(solution)/shard_map/ppermute | solution.py:123
  171.9 1.4 collective-permute-start.17
  173.4 3.8 %collective-permute-done.17 = f32[16]{0:T(128)S(1)} collective-permute-done((f32[16]{0:T(128)S(1)}, f32[16]{0:T(128)S(1)}, u32[]{:S(2)}, u32[]{:S(2)}) %collective-permute-start.17) | collective-permute-done | bytes 96 | tf_op jit(solution)/shard_map/ppermute | solution.py:123
  177.3 1.6 copy.97
  179.0 5.8 %collective-permute-done.18 = f32[16]{0:T(128)S(1)} collective-permute-done((f32[16]{0:T(128)S(1)}, f32[16]{0:T(128)S(1)}, u32[]{:S(2)}, u32[]{:S(2)}) %collective-permute-start.18) | collective-permute-done | bytes 96 | tf_op jit(solution)/shard_map/ppermute | solution.py:123
  184.8 0.9 collective-permute-start.20
  185.7 0.9 collective-permute-start.21
  186.6 1.7 collective-permute-done.20
  188.7 1.2 collective-permute-start.22
  189.9 1.6 copy.98
  191.5 2.3 %collective-permute-done.22 = f32[16]{0:T(128)S(1)} collective-permute-done((f32[16]{0:T(128)S(1)}, f32[16]{0:T(128)S(1)}, u32[]{:S(2)}, u32[]{:S(2)}) %collective-permute-start.22) | collective-permute-done | bytes 96 | tf_op jit(solution)/shard_map/ppermute | solution.py:123
  193.8 0.5 fusion.67
  (106 shorter events, 5.9 us)
Async XLA Ops:
  0.6 6.2 %copy-start.14 = (bf16[1,384,2048]{2,1,0:T(8,128)(2,1)S(1)}, bf16[1,384,2048]{2,1,0:T(8,128)(2,1)}, u32[]{:S(2)}) copy-start(bf16[1,384,2048]{2,1,0:T(8,128)(2,1)} %param.10) | copy-start | bytes 4718596
  6.8 1.6 copy-start.19
  6.8 1.6 copy-start.18
  14.8 2.9 %copy-start.1 = (bf16[48,8,16,128]{3,2,1,0:T(8,128)(2,1)S(1)}, bf16[48,8,16,128]{3,2,1,0:T(8,128)(2,1)}, u32[]{:S(2)}) copy-start(bf16[48,8,16,128]{3,2,1,0:T(8,128)(2,1)} %copy.105) | copy-start | bytes 4718596
  19.4 1.4 copy-start.3
  22.0 15.6 %collective-permute-start = (f32[4,264,128]{2,1,0:T(8,128)}, f32[4,264,128]{2,1,0:T(8,128)}, u32[]{:S(2)}, u32[]{:S(2)}) collective-permute-start(f32[4,264,128]{2,1,0:T(8,128)} %get-tuple-element.51), channel_id=1, source_target_pairs={{0,8},{8,16},{16,24},{24,0},{32,40},{40,48},{48,56},{56,32},{64,72... | collective-permute-start | bytes 1622024 | tf_op jit(solution)/shard_map/ppermute | solution.py:57
  23.6 26.8 %collective-permute-start.1 = (f32[4,264,128]{2,1,0:T(8,128)}, f32[4,264,128]{2,1,0:T(8,128)}, u32[]{:S(2)}, u32[]{:S(2)}) collective-permute-start(f32[4,264,128]{2,1,0:T(8,128)} %get-tuple-element.50), channel_id=1, source_target_pairs={{0,16},{8,24},{16,0},{24,8},{32,48},{40,56},{48,32},{56,40},{64,80... | collective-permute-start | bytes 1622024 | tf_op jit(solution)/shard_map/ppermute | solution.py:57
  26.5 23.9 %collective-permute-start.2 = (f32[4,264,128]{2,1,0:T(8,128)}, f32[4,264,128]{2,1,0:T(8,128)}, u32[]{:S(2)}, u32[]{:S(2)}) collective-permute-start(f32[4,264,128]{2,1,0:T(8,128)} %get-tuple-element.49), channel_id=1, source_target_pairs={{0,24},{8,0},{16,8},{24,16},{32,56},{40,32},{48,40},{56,48},{64,88... | collective-permute-start | bytes 1622024 | tf_op jit(solution)/shard_map/ppermute | solution.py:57
  52.1 0.8 copy-start.4
  52.1 1.0 copy-start.7
  52.2 1.1 copy-start.9
  52.2 1.3 copy-start.11
  53.2 0.7 copy-start.13
  54.7 9.9 %collective-permute-start.6 = (f32[4,136,128]{2,1,0:T(8,128)}, f32[4,136,128]{2,1,0:T(8,128)}, u32[]{:S(2)}, u32[]{:S(2)}) collective-permute-start(f32[4,136,128]{2,1,0:T(8,128)} %get-tuple-element.74), channel_id=1, source_target_pairs={{32,0},{40,8},{48,16},{56,24},{64,32},{72,40},{80,48},{88,56},{96,... | collective-permute-start | bytes 835592 | tf_op jit(solution)/shard_map/ppermute | solution.py:36
  56.4 61.7 %copy-start.16 = (pred[384,384]{1,0:T(8,128)(4,1)}, pred[384,384]{1,0:T(8,128)(4,1)S(1)}, u32[]{:S(2)}) copy-start(pred[384,384]{1,0:T(8,128)(4,1)S(1)} %fusion.26) | copy-start | bytes 442372
  56.4 9.8 %collective-permute-start.3 = (f32[4,136,128]{2,1,0:T(8,128)}, f32[4,136,128]{2,1,0:T(8,128)S(1)}, u32[]{:S(2)}, u32[]{:S(2)}) collective-permute-start(f32[4,136,128]{2,1,0:T(8,128)} %get-tuple-element.73), channel_id=1, source_target_pairs={{0,32},{8,40},{16,48},{24,56},{32,64},{40,72},{48,80},{56,88},{64,... | collective-permute-start | bytes 835592 | tf_op jit(solution)/shard_map/ppermute | solution.py:35
  67.3 32.4 %copy-start.12 = (f32[1,4,264,128]{3,2,1,0:T(8,128)S(1)}, f32[1,4,264,128]{3,2,1,0:T(8,128)}, u32[]{:S(2)}) copy-start(f32[1,4,264,128]{3,2,1,0:T(8,128)} %copy-done.11) | copy-start | bytes 1622020
  67.5 9.9 %collective-permute-start.4 = (f32[4,136,128]{2,1,0:T(8,128)S(1)}, f32[4,136,128]{2,1,0:T(8,128)S(1)}, u32[]{:S(2)}, u32[]{:S(2)}) collective-permute-start(f32[4,136,128]{2,1,0:T(8,128)S(1)} %pad_maximum_fusion.5), channel_id=1, source_target_pairs={{0,64},{8,72},{16,80},{24,88},{32,96},{40,104},{48,112},{56,120},{... | collective-permute-start | bytes 835592 | tf_op jit(solution)/shard_map/ppermute | solution.py:35
  73.4 22.3 %collective-permute-start.7 = (f32[4,136,128]{2,1,0:T(8,128)S(1)}, f32[4,136,128]{2,1,0:T(8,128)S(1)}, u32[]{:S(2)}, u32[]{:S(2)}) collective-permute-start(f32[4,136,128]{2,1,0:T(8,128)S(1)} %pad_maximum_fusion.7), channel_id=1, source_target_pairs={{64,0},{72,8},{80,16},{88,24},{96,32},{104,40},{112,48},{120,56},{... | collective-permute-start | bytes 835592 | tf_op jit(solution)/shard_map/ppermute | solution.py:36
  75.6 34.0 %copy-start.5 = (f32[1,4,264,128]{3,2,1,0:T(8,128)S(1)}, f32[1,4,264,128]{3,2,1,0:T(8,128)}, u32[]{:S(2)}) copy-start(f32[1,4,264,128]{3,2,1,0:T(8,128)} %copy-done.4) | copy-start | bytes 1622020
  75.6 34.0 %copy-start.8 = (f32[1,4,264,128]{3,2,1,0:T(8,128)S(1)}, f32[1,4,264,128]{3,2,1,0:T(8,128)}, u32[]{:S(2)}) copy-start(f32[1,4,264,128]{3,2,1,0:T(8,128)} %copy-done.7) | copy-start | bytes 1622020
  75.6 34.0 %copy-start.10 = (f32[1,4,264,128]{3,2,1,0:T(8,128)S(1)}, f32[1,4,264,128]{3,2,1,0:T(8,128)}, u32[]{:S(2)}) copy-start(f32[1,4,264,128]{3,2,1,0:T(8,128)} %copy-done.9) | copy-start | bytes 1622020
  77.5 22.2 %collective-permute-start.5 = (f32[4,136,128]{2,1,0:T(8,128)S(1)}, f32[4,136,128]{2,1,0:T(8,128)S(1)}, u32[]{:S(2)}, u32[]{:S(2)}) collective-permute-start(f32[4,136,128]{2,1,0:T(8,128)S(1)} %pad_maximum_fusion.6), channel_id=1, source_target_pairs={{0,128},{8,136},{16,144},{24,152},{32,160},{40,168},{48,176},{56,1... | collective-permute-start | bytes 835592 | tf_op jit(solution)/shard_map/ppermute | solution.py:35
  95.8 13.8 %collective-permute-start.8 = (f32[4,136,128]{2,1,0:T(8,128)S(1)}, f32[4,136,128]{2,1,0:T(8,128)S(1)}, u32[]{:S(2)}, u32[]{:S(2)}) collective-permute-start(f32[4,136,128]{2,1,0:T(8,128)S(1)} %pad_maximum_fusion.8), channel_id=1, source_target_pairs={{128,0},{136,8},{144,16},{152,24},{160,32},{168,40},{176,48},{184,... | collective-permute-start | bytes 835592 | tf_op jit(solution)/shard_map/ppermute | solution.py:36
  111.4 6.8 %copy-start = (bf16[1,384,2048]{1,2,0:T(8,128)(2,1)S(1)}, bf16[1,384,2048]{1,2,0:T(8,128)(2,1)}, u32[]{:S(2)}) copy-start(bf16[1,384,2048]{1,2,0:T(8,128)(2,1)} %copy.103) | copy-start | bytes 4718596
  111.4 6.8 %copy-start.2 = (bf16[48,8,16,128]{3,2,1,0:T(8,128)(2,1)S(1)}, bf16[48,8,16,128]{3,2,1,0:T(8,128)(2,1)}, u32[]{:S(2)}) copy-start(bf16[48,8,16,128]{3,2,1,0:T(8,128)(2,1)} %copy.105) | copy-start | bytes 4718596
  111.5 17.9 %collective-permute-start.9 = (f32[4,256,128]{2,1,0:T(8,128)S(1)}, f32[4,256,128]{2,1,0:T(8,128)S(1)}, u32[]{:S(2)}, u32[]{:S(2)}) collective-permute-start(f32[4,256,128]{2,1,0:T(8,128)S(1)} %get-tuple-element.54), channel_id=1, source_target_pairs={{0,8},{8,16},{16,24},{24,0},{32,40},{40,48},{48,56},{56,32},{64,72... | collective-permute-start | bytes 1572872 | tf_op jit(solution)/shard_map/ppermute | solution.py:57
  113.3 21.8 %collective-permute-start.10 = (f32[4,256,128]{2,1,0:T(8,128)S(1)}, f32[4,256,128]{2,1,0:T(8,128)S(1)}, u32[]{:S(2)}, u32[]{:S(2)}) collective-permute-start(f32[4,256,128]{2,1,0:T(8,128)S(1)} %get-tuple-element.53), channel_id=1, source_target_pairs={{0,16},{8,24},{16,0},{24,8},{32,48},{40,56},{48,32},{56,40},{64,80... | collective-permute-start | bytes 1572872 | tf_op jit(solution)/shard_map/ppermute | solution.py:57
  118.1 16.9 %collective-permute-start.11 = (f32[4,256,128]{2,1,0:T(8,128)S(1)}, f32[4,256,128]{2,1,0:T(8,128)S(1)}, u32[]{:S(2)}, u32[]{:S(2)}) collective-permute-start(f32[4,256,128]{2,1,0:T(8,128)S(1)} %get-tuple-element.52), channel_id=1, source_target_pairs={{0,24},{8,0},{16,8},{24,16},{32,56},{40,32},{48,40},{56,48},{64,88... | collective-permute-start | bytes 1572872 | tf_op jit(solution)/shard_map/ppermute | solution.py:57
  143.4 7.3 %copy-start.17 = (pred[384,384]{1,0:T(8,128)(4,1)S(1)}, pred[384,384]{1,0:T(8,128)(4,1)}, u32[]{:S(2)}) copy-start(pred[384,384]{1,0:T(8,128)(4,1)} %copy-done.16) | copy-start | bytes 442372
  145.9 14.5 %collective-permute-start.12 = (f32[16]{0:T(128)S(1)}, f32[16]{0:T(128)S(1)}, u32[]{:S(2)}, u32[]{:S(2)}) collective-permute-start(f32[16]{0:T(128)S(1)} %multiply_reduce_fusion), channel_id=1, source_target_pairs={{0,8},{8,0},{16,24},{24,16},{32,40},{40,32},{48,56},{56,48},{64,72... | collective-permute-start | bytes 200 | tf_op jit(solution)/shard_map/ppermute | solution.py:123
  146.2 14.2 %collective-permute-start.13 = (f32[16]{0:T(128)S(1)}, f32[16]{0:T(128)S(1)}, u32[]{:S(2)}, u32[]{:S(2)}) collective-permute-start(f32[16]{0:T(128)S(1)} %multiply_reduce_fusion), channel_id=1, source_target_pairs={{0,16},{8,24},{16,0},{24,8},{32,48},{40,56},{48,32},{56,40},{64,80... | collective-permute-start | bytes 200 | tf_op jit(solution)/shard_map/ppermute | solution.py:123
  149.6 10.9 %collective-permute-start.14 = (f32[16]{0:T(128)S(1)}, f32[16]{0:T(128)S(1)}, u32[]{:S(2)}, u32[]{:S(2)}) collective-permute-start(f32[16]{0:T(128)S(1)} %multiply_reduce_fusion), channel_id=1, source_target_pairs={{0,24},{8,16},{16,8},{24,0},{32,56},{40,48},{48,40},{56,32},{64,88... | collective-permute-start | bytes 200 | tf_op jit(solution)/shard_map/ppermute | solution.py:123
  157.7 19.6 %copy-start.6 = (bf16[384,16,128]{0,2,1:T(8,128)(2,1)S(1)}, bf16[384,16,128]{0,2,1:T(8,128)(2,1)}, u32[]{:S(2)}) copy-start(bf16[384,16,128]{0,2,1:T(8,128)(2,1)} %get-tuple-element.46) | copy-start | bytes 4718596
  160.4 29.5 %copy-start.15 = (bf16[384,16,128]{0,2,1:T(8,128)(2,1)S(1)}, bf16[384,16,128]{0,2,1:T(8,128)(2,1)}, u32[]{:S(2)}) copy-start(bf16[384,16,128]{0,2,1:T(8,128)(2,1)} %fusion.12) | copy-start | bytes 4718596
  160.5 12.8 %collective-permute-start.15 = (f32[16]{0:T(128)S(1)}, f32[16]{0:T(128)S(1)}, u32[]{:S(2)}, u32[]{:S(2)}) collective-permute-start(f32[16]{0:T(128)S(1)} %fusion.66), channel_id=1, source_target_pairs={{0,32},{8,40},{16,48},{24,56},{32,0},{40,8},{48,16},{56,24},{64,96... | collective-permute-start | bytes 200 | tf_op jit(solution)/shard_map/ppermute | solution.py:123
  163.1 10.3 %collective-permute-start.16 = (f32[16]{0:T(128)S(1)}, f32[16]{0:T(128)S(1)}, u32[]{:S(2)}, u32[]{:S(2)}) collective-permute-start(f32[16]{0:T(128)S(1)} %fusion.66), channel_id=1, source_target_pairs={{0,64},{8,72},{16,80},{24,88},{32,96},{40,104},{48,112},{56,120},{... | collective-permute-start | bytes 200 | tf_op jit(solution)/shard_map/ppermute | solution.py:123
  171.9 5.3 %collective-permute-start.17 = (f32[16]{0:T(128)S(1)}, f32[16]{0:T(128)S(1)}, u32[]{:S(2)}, u32[]{:S(2)}) collective-permute-start(f32[16]{0:T(128)S(1)} %fusion.66), channel_id=1, source_target_pairs={{0,96},{8,104},{16,112},{24,120},{32,64},{40,72},{48,80},{56,88},{... | collective-permute-start | bytes 200 | tf_op jit(solution)/shard_map/ppermute | solution.py:123
  177.2 7.5 %collective-permute-start.18 = (f32[16]{0:T(128)S(1)}, f32[16]{0:T(128)S(1)}, u32[]{:S(2)}, u32[]{:S(2)}) collective-permute-start(f32[16]{0:T(128)S(1)} %fusion.63), channel_id=1, source_target_pairs={{0,128},{8,136},{16,144},{24,152},{32,160},{40,168},{48,176},{56,1... | collective-permute-start | bytes 200 | tf_op jit(solution)/shard_map/ppermute | solution.py:123
  184.8 1.9 collective-permute-start.19
  184.8 3.6 %collective-permute-start.20 = (f32[16]{0:T(128)S(1)}, f32[16]{0:T(128)S(1)}, u32[]{:S(2)}, u32[]{:S(2)}) collective-permute-start(f32[16]{0:T(128)S(1)} %fusion.60), channel_id=1, source_target_pairs={{0,2},{1,3},{2,0},{3,1},{4,6},{5,7},{6,4},{7,5},{8,10},{9,11},{10,... | collective-permute-start | bytes 200 | tf_op jit(solution)/shard_map/ppermute | solution.py:123
  185.7 3.0 %collective-permute-start.21 = (f32[16]{0:T(128)S(1)}, f32[16]{0:T(128)S(1)}, u32[]{:S(2)}, u32[]{:S(2)}) collective-permute-start(f32[16]{0:T(128)S(1)} %fusion.60), channel_id=1, source_target_pairs={{0,3},{1,2},{2,1},{3,0},{4,7},{5,6},{6,5},{7,4},{8,11},{9,10},{10,... | collective-permute-start | bytes 200 | tf_op jit(solution)/shard_map/ppermute | solution.py:123
  188.7 5.1 %collective-permute-start.22 = (f32[16]{0:T(128)S(1)}, f32[16]{0:T(128)S(1)}, u32[]{:S(2)}, u32[]{:S(2)}) collective-permute-start(f32[16]{0:T(128)S(1)} %fusion.59), channel_id=1, source_target_pairs={{0,4},{1,5},{2,6},{3,7},{4,0},{5,1},{6,2},{7,3},{8,12},{9,13},{10,... | collective-permute-start | bytes 200 | tf_op jit(solution)/shard_map/ppermute | solution.py:123

commit v17 on v16

--- a/solution.py
+++ b/solution.py
@@ -72,7 +72,13 @@
     excl = [jnp.zeros_like(own_s[0])]
     excl_a = [jnp.ones_like(own_a[0])]
     for j in range(1, group):
-        excl.append(own_a[j - 1][:, None, None] * excl[j - 1] + own_s[j - 1])
+        acc = own_s[j - 1]
+        for i in range(j - 1):
+            scale = own_a[i + 1]
+            for k in range(i + 2, j):
+                scale = scale * own_a[k]
+            acc = acc + scale[:, None, None] * own_s[i]
+        excl.append(acc)
         excl_a.append(excl_a[j - 1] * own_a[j - 1])
     total = own_s[group - 1]
     for j in range(group - 1):

time: 196 us -> 196 us (level)
  no operation moved by 1% of the time
where the time goes in v17:
time: 196 us; the launch traced here: 194 us
  waiting for transfers between devices  67.9 us (35%)
  starting transfers between devices  65.5 us (33%)
  matrix products  25.4 us (13%)
  local copies, waits for them, and re-layouts  20.8 us (11%)
  other arithmetic  12.6 us (6%)
  between operations  2.1 us (1%)
    ppermute x6, waiting for transfers between devices, row_exchange(): got.append(lax.ppermute(send, axis, pairs))  35.6 us
    ppermute x3, starting transfers between devices, group_scan(): got = lax.ppermute(fwd, axis, up)  28.5 us
    ppermute x11, starting transfers between devices, digit_sum(): lax.ppermute(value, axis, [(i, i ^ k * step) for i in range(count)])  20.7 us
    unnamed x46, local copies, waits for them, and re-layouts  15.2 us
    ppermute x11, waiting for transfers between devices, digit_sum(): lax.ppermute(value, axis, [(i, i ^ k * step) for i in range(count)])  14.1 us
    ppermute x3, waiting for transfers between devices, group_scan(): rgot = lax.ppermute(bwd, axis, down)  13.5 us
    ppermute x6, starting transfers between devices, row_exchange(): got.append(lax.ppermute(send, axis, pairs))  12.4 us
    dot_general x1, matrix products, on_device(): jnp.einsum('hst,shf->thf', attn_prob, gradient_block, preferred_element_t...  7.06 us
  transfers between devices with their start and end apart: 23, of which 15 were waited for; matrix products, arithmetic and copies ran while one was open for 10% of the time, Pallas kernels for 0%

profile of v17, /device:TPU:6, one launch (start us, length us, event | category | flops | bytes accessed | tf_op | source)
XLA Modules:
  0.0 194.3 jit_solution(4249583872636223906)
XLA Ops:
  0.7 0.9 reduce-window_clone.1
  1.6 0.7 subtract_bitcast_fusion
  3.0 0.6 slice.189
  4.2 0.7 broadcast_compare_fusion
  4.9 1.9 copy.87
  6.8 1.6 copy.103
  8.5 0.9 reduce-window.24
  9.8 1.9 copy.85
  11.7 3.0 %copy.105 = bf16[48,8,16,128]{3,2,1,0:T(8,128)(2,1)} copy(bf16[48,8,16,128]{3,1,2,0:T(8,128)(2,1)} %bitcast.239) | data formatting | bytes 3145728
  14.8 2.9 %fusion.9 = f32[16,128,128]{2,1,0:T(8,128)S(1)} fusion(bf16[384,16,128]{0,2,1:T(8,128)(2,1)} %bitcast.225, bf16[384,16,128]{0,2,1:T(8,128)(2,1)S(1)} %bitcast.221, f32[384,16]{0,1:T(8,128)S(1)} %get-tuple-element.74), kind=kOutput, calls=%fused_computation.15 | convolution fusion | flops 605552640 | bytes 4218880 | tf_op jit(solution)/shard_map/she,shf->hef/dot_general | solution.py:196
  17.8 1.4 fusion.7
  19.4 1.3 copy-done.3
  20.8 1.2 dynamic-slice_bitcast_fusion
  22.0 1.6 collective-permute-start
  23.6 2.9 %collective-permute-start.1 = (f32[4,264,128]{2,1,0:T(8,128)}, f32[4,264,128]{2,1,0:T(8,128)}, u32[]{:S(2)}, u32[]{:S(2)}) collective-permute-start(f32[4,264,128]{2,1,0:T(8,128)} %get-tuple-element.52), channel_id=1, source_target_pairs={{0,16},{8,24},{16,0},{24,8},{32,48},{40,56},{48,32},{56,40},{64,80... | collective-permute-start | bytes 1622024 | tf_op jit(solution)/shard_map/ppermute | solution.py:57
  26.5 1.3 collective-permute-start.2
  27.9 9.7 %collective-permute-done = f32[4,264,128]{2,1,0:T(8,128)} collective-permute-done((f32[4,264,128]{2,1,0:T(8,128)}, f32[4,264,128]{2,1,0:T(8,128)}, u32[]{:S(2)}, u32[]{:S(2)}) %collective-permute-start) | collective-permute-done | bytes 540704 | tf_op jit(solution)/shard_map/ppermute | solution.py:57
  37.6 12.8 %collective-permute-done.1 = f32[4,264,128]{2,1,0:T(8,128)} collective-permute-done((f32[4,264,128]{2,1,0:T(8,128)}, f32[4,264,128]{2,1,0:T(8,128)}, u32[]{:S(2)}, u32[]{:S(2)}) %collective-permute-start.1) | collective-permute-done | bytes 540704 | tf_op jit(solution)/shard_map/ppermute | solution.py:57
  50.4 1.8 fusion.28
  52.4 0.5 copy-done.4
  53.5 0.4 copy-done.13
  53.9 0.9 pad_maximum_fusion.4
  54.7 1.3 collective-permute-start.6
  56.4 4.6 %collective-permute-start.3 = (f32[4,136,128]{2,1,0:T(8,128)}, f32[4,136,128]{2,1,0:T(8,128)S(1)}, u32[]{:S(2)}, u32[]{:S(2)}) collective-permute-start(f32[4,136,128]{2,1,0:T(8,128)} %get-tuple-element.75), channel_id=1, source_target_pairs={{0,32},{8,40},{16,48},{24,56},{32,64},{40,72},{48,80},{56,88},{64,... | collective-permute-start | bytes 835592 | tf_op jit(solution)/shard_map/ppermute | solution.py:35
  60.9 3.7 %collective-permute-done.6 = f32[4,136,128]{2,1,0:T(8,128)} collective-permute-done((f32[4,136,128]{2,1,0:T(8,128)}, f32[4,136,128]{2,1,0:T(8,128)}, u32[]{:S(2)}, u32[]{:S(2)}) %collective-permute-start.6) | collective-permute-done | bytes 278560 | tf_op jit(solution)/shard_map/ppermute | solution.py:36
  64.6 0.8 fusion.77
  65.5 0.6 collective-permute-done.3
  66.2 1.1 multiply_add_fusion.8
  67.4 5.8 %collective-permute-start.4 = (f32[4,136,128]{2,1,0:T(8,128)S(1)}, f32[4,136,128]{2,1,0:T(8,128)S(1)}, u32[]{:S(2)}, u32[]{:S(2)}) collective-permute-start(f32[4,136,128]{2,1,0:T(8,128)S(1)} %pad_maximum_fusion.5), channel_id=1, source_target_pairs={{0,64},{8,72},{16,80},{24,88},{32,96},{40,104},{48,112},{56,120},{... | collective-permute-start | bytes 835592 | tf_op jit(solution)/shard_map/ppermute | solution.py:35
  73.3 1.3 collective-permute-start.7
  74.6 0.8 slice_reduce_fusion.2
  75.6 1.8 collective-permute-done.4
  77.5 18.1 %collective-permute-start.5 = (f32[4,136,128]{2,1,0:T(8,128)S(1)}, f32[4,136,128]{2,1,0:T(8,128)S(1)}, u32[]{:S(2)}, u32[]{:S(2)}) collective-permute-start(f32[4,136,128]{2,1,0:T(8,128)S(1)} %pad_maximum_fusion.6), channel_id=1, source_target_pairs={{0,128},{8,136},{16,144},{24,152},{32,160},{40,168},{48,176},{56,1... | collective-permute-start | bytes 835592 | tf_op jit(solution)/shard_map/ppermute | solution.py:35
  95.8 1.3 collective-permute-start.8
  97.3 2.3 %collective-permute-done.5 = f32[4,136,128]{2,1,0:T(8,128)S(1)} collective-permute-done((f32[4,136,128]{2,1,0:T(8,128)S(1)}, f32[4,136,128]{2,1,0:T(8,128)S(1)}, u32[]{:S(2)}, u32[]{:S(2)}) %collective-permute-start.5) | collective-permute-done | bytes 278560 | tf_op jit(solution)/shard_map/ppermute | solution.py:35
  99.8 9.8 %collective-permute-done.8 = f32[4,136,128]{2,1,0:T(8,128)S(1)} collective-permute-done((f32[4,136,128]{2,1,0:T(8,128)S(1)}, f32[4,136,128]{2,1,0:T(8,128)S(1)}, u32[]{:S(2)}, u32[]{:S(2)}) %collective-permute-start.8) | collective-permute-done | bytes 278560 | tf_op jit(solution)/shard_map/ppermute | solution.py:36
  109.6 1.1 multiply_add_fusion.3
  111.5 1.7 collective-permute-start.9
  113.2 4.9 %collective-permute-start.10 = (f32[4,256,128]{2,1,0:T(8,128)S(1)}, f32[4,256,128]{2,1,0:T(8,128)S(1)}, u32[]{:S(2)}, u32[]{:S(2)}) collective-permute-start(f32[4,256,128]{2,1,0:T(8,128)S(1)} %get-tuple-element.55), channel_id=1, source_target_pairs={{0,16},{8,24},{16,0},{24,8},{32,48},{40,56},{48,32},{56,40},{64,80... | collective-permute-start | bytes 1572872 | tf_op jit(solution)/shard_map/ppermute | solution.py:57
  118.1 3.7 %multiply_convert_fusion.1 = bf16[16,384,384]{2,1,0:T(8,128)(2,1)S(1)} fusion(f32[16,384]{1,0:T(8,128)S(1)} %get-tuple-element.71, pred[384,384]{1,0:T(8,128)(4,1)S(1)} %fusion.26, bf16[384,16,128]{0,2,1:T(8,128)(2,1)S(1)} %bitcast.227, bf16[384,16,128]{2,1,0:T(8,128)(2,1)S(1)} %bitcast.230), kind=kOutput, calls=%fused_computation.1 | convolution fusion | flops 615776256 | bytes 8036352 | tf_op jit(solution)/shard_map/shf,thf->hst/dot_general | solution.py:202
  121.9 7.5 %collective-permute-done.9 = f32[4,256,128]{2,1,0:T(8,128)S(1)} collective-permute-done((f32[4,256,128]{2,1,0:T(8,128)S(1)}, f32[4,256,128]{2,1,0:T(8,128)S(1)}, u32[]{:S(2)}, u32[]{:S(2)}) %collective-permute-start.9) | collective-permute-done | bytes 524320 | tf_op jit(solution)/shard_map/ppermute | solution.py:57
  129.4 5.6 %collective-permute-done.10 = f32[4,256,128]{2,1,0:T(8,128)S(1)} collective-permute-done((f32[4,256,128]{2,1,0:T(8,128)S(1)}, f32[4,256,128]{2,1,0:T(8,128)S(1)}, u32[]{:S(2)}, u32[]{:S(2)}) %collective-permute-start.10) | collective-permute-done | bytes 524320 | tf_op jit(solution)/shard_map/ppermute | solution.py:57
  135.4 1.0 fusion.21
  136.4 1.4 fusion.17
  137.9 2.7 %fusion.23 = f32[16,128,384]{2,1,0:T(8,128)} fusion(bf16[384,16,128]{0,2,1:T(8,128)(2,1)S(1)} %bitcast.217, f32[16,256,128]{2,1,0:T(8,128)S(1)} %bitcast.234), kind=kOutput, calls=%fused_computation.35 | convolution fusion | flops 603979776 | bytes 5767168 | tf_op jit(solution)/shard_map/the,hef->thf/dot_general | solution.py:210
  140.6 2.7 %fusion.10 = (f32[384,16]{0,1:T(8,128)S(1)}, bf16[384,16,128]{0,2,1:T(8,128)(2,1)}) fusion(bf16[384,16,128]{0,2,1:T(8,128)(2,1)S(1)} %bitcast.222, f32[16,128,384]{2,1,0:T(8,128)S(1)} %fusion.21, f32[384,16]{0,1:T(8,128)S(1)} %get-tuple-element.74, bf16[16,384,384]{2,1,0:T(8,128)(2,1)S(1)} %multiply_convert_fusion.1, bf16[384,16,128]{0,2,1:T(8,128)(2,1)S(1)} %bitcast.218), kind=kOutput, calls=%fused_computation.16 | convolution fusion | flops 608692224 | bytes 12632064 | tf_op jit(solution)/shard_map/hst,the->she/dot_general | solution.py:213
  143.4 2.4 %fusion.8 = (f32[384,16]{0,1:T(8,128)S(1)}, bf16[384,16,128]{0,2,1:T(8,128)(2,1)}) fusion(bf16[384,16,128]{0,2,1:T(8,128)(2,1)S(1)} %bitcast.219, f32[16,128,384]{2,1,0:T(8,128)S(1)} %fusion.17, f32[384,16]{0,1:T(8,128)S(1)} %get-tuple-element.73, bf16[384,16,128]{0,2,1:T(8,128)(2,1)S(1)} %bitcast.223, bf16[16,384,384]{2,1,0:T(8,128)(2,1)S(1)} %multiply_convert_fusion.1), kind=kOutput, calls=%fused_computation.14 | convolution fusion | flops 608692224 | bytes 12632064 | tf_op jit(solution)/shard_map/hst,she->the/dot_general | solution.py:219
  146.2 3.3 %collective-permute-start.13 = (f32[16]{0:T(128)S(1)}, f32[16]{0:T(128)S(1)}, u32[]{:S(2)}, u32[]{:S(2)}) collective-permute-start(f32[16]{0:T(128)S(1)} %multiply_reduce_fusion), channel_id=1, source_target_pairs={{0,16},{8,24},{16,0},{24,8},{32,48},{40,56},{48,32},{56,40},{64,80... | collective-permute-start | bytes 200 | tf_op jit(solution)/shard_map/ppermute | solution.py:129
  149.6 1.1 collective-permute-start.14
  150.7 7.1 %fusion.12 = bf16[384,16,128]{0,2,1:T(8,128)(2,1)} fusion(f32[16,128,384]{2,1,0:T(8,128)} %fusion.23, bf16[384,16,128]{0,2,1:T(8,128)(2,1)} %bitcast.226, f32[16,384]{1,0:T(8,128)S(1)} %get-tuple-element.71, pred[384,384]{1,0:T(8,128)(4,1)S(1)} %copy-done.17, bf16[384,16,128]{0,2,1:T(8,128)(2,1)S(1)} %bitcast.224, bf16[384,16,128]{0,2,1:T(8,128)(2,1)S(1)} %bitcast.220, ...), kind=kOutput, calls=%fused_computation.19 | convolution fusion | flops 1222115328 | bytes 9633792 | tf_op jit(solution)/shard_map/hst,shf->thf/dot_general | solution.py:207
  157.7 2.7 %copy.96 = bf16[1,384,2048]{2,1,0:T(8,128)(2,1)} copy(bf16[1,384,2048]{1,2,0:T(8,128)(2,1)} %bitcast.238) | data formatting | bytes 3145728
  160.5 2.7 %collective-permute-start.15 = (f32[16]{0:T(128)S(1)}, f32[16]{0:T(128)S(1)}, u32[]{:S(2)}, u32[]{:S(2)}) collective-permute-start(f32[16]{0:T(128)S(1)} %fusion.65), channel_id=1, source_target_pairs={{0,32},{8,40},{16,48},{24,56},{32,0},{40,8},{48,16},{56,24},{64,96... | collective-permute-start | bytes 200 | tf_op jit(solution)/shard_map/ppermute | solution.py:129
  163.1 8.7 %collective-permute-start.16 = (f32[16]{0:T(128)S(1)}, f32[16]{0:T(128)S(1)}, u32[]{:S(2)}, u32[]{:S(2)}) collective-permute-start(f32[16]{0:T(128)S(1)} %fusion.65), channel_id=1, source_target_pairs={{0,64},{8,72},{16,80},{24,88},{32,96},{40,104},{48,112},{56,120},{... | collective-permute-start | bytes 200 | tf_op jit(solution)/shard_map/ppermute | solution.py:129
  171.9 1.4 collective-permute-start.17
  173.4 3.8 %collective-permute-done.17 = f32[16]{0:T(128)S(1)} collective-permute-done((f32[16]{0:T(128)S(1)}, f32[16]{0:T(128)S(1)}, u32[]{:S(2)}, u32[]{:S(2)}) %collective-permute-start.17) | collective-permute-done | bytes 96 | tf_op jit(solution)/shard_map/ppermute | solution.py:129
  177.3 1.6 copy.97
  178.9 5.8 %collective-permute-done.18 = f32[16]{0:T(128)S(1)} collective-permute-done((f32[16]{0:T(128)S(1)}, f32[16]{0:T(128)S(1)}, u32[]{:S(2)}, u32[]{:S(2)}) %collective-permute-start.18) | collective-permute-done | bytes 96 | tf_op jit(solution)/shard_map/ppermute | solution.py:129
  184.8 0.9 collective-permute-start.20
  185.7 0.9 collective-permute-start.21
  186.6 1.7 collective-permute-done.20
  188.7 1.2 collective-permute-start.22
  189.9 1.6 copy.98
  191.5 2.3 %collective-permute-done.22 = f32[16]{0:T(128)S(1)} collective-permute-done((f32[16]{0:T(128)S(1)}, f32[16]{0:T(128)S(1)}, u32[]{:S(2)}, u32[]{:S(2)}) %collective-permute-start.22) | collective-permute-done | bytes 96 | tf_op jit(solution)/shard_map/ppermute | solution.py:129
  193.8 0.5 fusion.66
  (106 shorter events, 5.9 us)
Async XLA Ops:
  0.6 6.2 %copy-start.14 = (bf16[1,384,2048]{2,1,0:T(8,128)(2,1)S(1)}, bf16[1,384,2048]{2,1,0:T(8,128)(2,1)}, u32[]{:S(2)}) copy-start(bf16[1,384,2048]{2,1,0:T(8,128)(2,1)} %param.10) | copy-start | bytes 4718596
  6.8 1.6 copy-start.19
  6.8 1.6 copy-start.18
  14.8 2.9 %copy-start.1 = (bf16[48,8,16,128]{3,2,1,0:T(8,128)(2,1)S(1)}, bf16[48,8,16,128]{3,2,1,0:T(8,128)(2,1)}, u32[]{:S(2)}) copy-start(bf16[48,8,16,128]{3,2,1,0:T(8,128)(2,1)} %copy.105) | copy-start | bytes 4718596
  19.4 1.4 copy-start.3
  22.0 15.6 %collective-permute-start = (f32[4,264,128]{2,1,0:T(8,128)}, f32[4,264,128]{2,1,0:T(8,128)}, u32[]{:S(2)}, u32[]{:S(2)}) collective-permute-start(f32[4,264,128]{2,1,0:T(8,128)} %get-tuple-element.53), channel_id=1, source_target_pairs={{0,8},{8,16},{16,24},{24,0},{32,40},{40,48},{48,56},{56,32},{64,72... | collective-permute-start | bytes 1622024 | tf_op jit(solution)/shard_map/ppermute | solution.py:57
  23.6 26.8 %collective-permute-start.1 = (f32[4,264,128]{2,1,0:T(8,128)}, f32[4,264,128]{2,1,0:T(8,128)}, u32[]{:S(2)}, u32[]{:S(2)}) collective-permute-start(f32[4,264,128]{2,1,0:T(8,128)} %get-tuple-element.52), channel_id=1, source_target_pairs={{0,16},{8,24},{16,0},{24,8},{32,48},{40,56},{48,32},{56,40},{64,80... | collective-permute-start | bytes 1622024 | tf_op jit(solution)/shard_map/ppermute | solution.py:57
  26.5 23.9 %collective-permute-start.2 = (f32[4,264,128]{2,1,0:T(8,128)}, f32[4,264,128]{2,1,0:T(8,128)}, u32[]{:S(2)}, u32[]{:S(2)}) collective-permute-start(f32[4,264,128]{2,1,0:T(8,128)} %get-tuple-element.51), channel_id=1, source_target_pairs={{0,24},{8,0},{16,8},{24,16},{32,56},{40,32},{48,40},{56,48},{64,88... | collective-permute-start | bytes 1622024 | tf_op jit(solution)/shard_map/ppermute | solution.py:57
  52.1 0.8 copy-start.4
  52.1 1.0 copy-start.7
  52.2 1.2 copy-start.9
  52.2 1.3 copy-start.11
  53.2 0.7 copy-start.13
  54.7 9.9 %collective-permute-start.6 = (f32[4,136,128]{2,1,0:T(8,128)}, f32[4,136,128]{2,1,0:T(8,128)}, u32[]{:S(2)}, u32[]{:S(2)}) collective-permute-start(f32[4,136,128]{2,1,0:T(8,128)} %get-tuple-element.76), channel_id=1, source_target_pairs={{32,0},{40,8},{48,16},{56,24},{64,32},{72,40},{80,48},{88,56},{96,... | collective-permute-start | bytes 835592 | tf_op jit(solution)/shard_map/ppermute | solution.py:36
  56.3 61.8 %copy-start.16 = (pred[384,384]{1,0:T(8,128)(4,1)}, pred[384,384]{1,0:T(8,128)(4,1)S(1)}, u32[]{:S(2)}) copy-start(pred[384,384]{1,0:T(8,128)(4,1)S(1)} %fusion.26) | copy-start | bytes 442372
  56.4 9.8 %collective-permute-start.3 = (f32[4,136,128]{2,1,0:T(8,128)}, f32[4,136,128]{2,1,0:T(8,128)S(1)}, u32[]{:S(2)}, u32[]{:S(2)}) collective-permute-start(f32[4,136,128]{2,1,0:T(8,128)} %get-tuple-element.75), channel_id=1, source_target_pairs={{0,32},{8,40},{16,48},{24,56},{32,64},{40,72},{48,80},{56,88},{64,... | collective-permute-start | bytes 835592 | tf_op jit(solution)/shard_map/ppermute | solution.py:35
  67.3 32.4 %copy-start.8 = (f32[1,4,264,128]{3,2,1,0:T(8,128)S(1)}, f32[1,4,264,128]{3,2,1,0:T(8,128)}, u32[]{:S(2)}) copy-start(f32[1,4,264,128]{3,2,1,0:T(8,128)} %copy-done.7) | copy-start | bytes 1622020
  67.4 9.9 %collective-permute-start.4 = (f32[4,136,128]{2,1,0:T(8,128)S(1)}, f32[4,136,128]{2,1,0:T(8,128)S(1)}, u32[]{:S(2)}, u32[]{:S(2)}) collective-permute-start(f32[4,136,128]{2,1,0:T(8,128)S(1)} %pad_maximum_fusion.5), channel_id=1, source_target_pairs={{0,64},{8,72},{16,80},{24,88},{32,96},{40,104},{48,112},{56,120},{... | collective-permute-start | bytes 835592 | tf_op jit(solution)/shard_map/ppermute | solution.py:35
  73.3 22.3 %collective-permute-start.7 = (f32[4,136,128]{2,1,0:T(8,128)S(1)}, f32[4,136,128]{2,1,0:T(8,128)S(1)}, u32[]{:S(2)}, u32[]{:S(2)}) collective-permute-start(f32[4,136,128]{2,1,0:T(8,128)S(1)} %pad_maximum_fusion.7), channel_id=1, source_target_pairs={{64,0},{72,8},{80,16},{88,24},{96,32},{104,40},{112,48},{120,56},{... | collective-permute-start | bytes 835592 | tf_op jit(solution)/shard_map/ppermute | solution.py:36
  75.6 34.0 %copy-start.5 = (f32[1,4,264,128]{3,2,1,0:T(8,128)S(1)}, f32[1,4,264,128]{3,2,1,0:T(8,128)}, u32[]{:S(2)}) copy-start(f32[1,4,264,128]{3,2,1,0:T(8,128)} %copy-done.4) | copy-start | bytes 1622020
  75.6 34.0 %copy-start.10 = (f32[1,4,264,128]{3,2,1,0:T(8,128)S(1)}, f32[1,4,264,128]{3,2,1,0:T(8,128)}, u32[]{:S(2)}) copy-start(f32[1,4,264,128]{3,2,1,0:T(8,128)} %copy-done.9) | copy-start | bytes 1622020
  75.6 34.0 %copy-start.12 = (f32[1,4,264,128]{3,2,1,0:T(8,128)S(1)}, f32[1,4,264,128]{3,2,1,0:T(8,128)}, u32[]{:S(2)}) copy-start(f32[1,4,264,128]{3,2,1,0:T(8,128)} %copy-done.11) | copy-start | bytes 1622020
  77.5 22.2 %collective-permute-start.5 = (f32[4,136,128]{2,1,0:T(8,128)S(1)}, f32[4,136,128]{2,1,0:T(8,128)S(1)}, u32[]{:S(2)}, u32[]{:S(2)}) collective-permute-start(f32[4,136,128]{2,1,0:T(8,128)S(1)} %pad_maximum_fusion.6), channel_id=1, source_target_pairs={{0,128},{8,136},{16,144},{24,152},{32,160},{40,168},{48,176},{56,1... | collective-permute-start | bytes 835592 | tf_op jit(solution)/shard_map/ppermute | solution.py:35
  95.8 13.8 %collective-permute-start.8 = (f32[4,136,128]{2,1,0:T(8,128)S(1)}, f32[4,136,128]{2,1,0:T(8,128)S(1)}, u32[]{:S(2)}, u32[]{:S(2)}) collective-permute-start(f32[4,136,128]{2,1,0:T(8,128)S(1)} %pad_maximum_fusion.8), channel_id=1, source_target_pairs={{128,0},{136,8},{144,16},{152,24},{160,32},{168,40},{176,48},{184,... | collective-permute-start | bytes 835592 | tf_op jit(solution)/shard_map/ppermute | solution.py:36
  111.3 6.8 %copy-start = (bf16[1,384,2048]{1,2,0:T(8,128)(2,1)S(1)}, bf16[1,384,2048]{1,2,0:T(8,128)(2,1)}, u32[]{:S(2)}) copy-start(bf16[1,384,2048]{1,2,0:T(8,128)(2,1)} %copy.103) | copy-start | bytes 4718596
  111.4 6.8 %copy-start.2 = (bf16[48,8,16,128]{3,2,1,0:T(8,128)(2,1)S(1)}, bf16[48,8,16,128]{3,2,1,0:T(8,128)(2,1)}, u32[]{:S(2)}) copy-start(bf16[48,8,16,128]{3,2,1,0:T(8,128)(2,1)} %copy.105) | copy-start | bytes 4718596
  111.5 17.9 %collective-permute-start.9 = (f32[4,256,128]{2,1,0:T(8,128)S(1)}, f32[4,256,128]{2,1,0:T(8,128)S(1)}, u32[]{:S(2)}, u32[]{:S(2)}) collective-permute-start(f32[4,256,128]{2,1,0:T(8,128)S(1)} %get-tuple-element.56), channel_id=1, source_target_pairs={{0,8},{8,16},{16,24},{24,0},{32,40},{40,48},{48,56},{56,32},{64,72... | collective-permute-start | bytes 1572872 | tf_op jit(solution)/shard_map/ppermute | solution.py:57
  113.2 21.8 %collective-permute-start.10 = (f32[4,256,128]{2,1,0:T(8,128)S(1)}, f32[4,256,128]{2,1,0:T(8,128)S(1)}, u32[]{:S(2)}, u32[]{:S(2)}) collective-permute-start(f32[4,256,128]{2,1,0:T(8,128)S(1)} %get-tuple-element.55), channel_id=1, source_target_pairs={{0,16},{8,24},{16,0},{24,8},{32,48},{40,56},{48,32},{56,40},{64,80... | collective-permute-start | bytes 1572872 | tf_op jit(solution)/shard_map/ppermute | solution.py:57
  118.1 16.9 %collective-permute-start.11 = (f32[4,256,128]{2,1,0:T(8,128)S(1)}, f32[4,256,128]{2,1,0:T(8,128)S(1)}, u32[]{:S(2)}, u32[]{:S(2)}) collective-permute-start(f32[4,256,128]{2,1,0:T(8,128)S(1)} %get-tuple-element.54), channel_id=1, source_target_pairs={{0,24},{8,0},{16,8},{24,16},{32,56},{40,32},{48,40},{56,48},{64,88... | collective-permute-start | bytes 1572872 | tf_op jit(solution)/shard_map/ppermute | solution.py:57
  143.4 7.3 %copy-start.17 = (pred[384,384]{1,0:T(8,128)(4,1)S(1)}, pred[384,384]{1,0:T(8,128)(4,1)}, u32[]{:S(2)}) copy-start(pred[384,384]{1,0:T(8,128)(4,1)} %copy-done.16) | copy-start | bytes 442372
  145.9 14.5 %collective-permute-start.12 = (f32[16]{0:T(128)S(1)}, f32[16]{0:T(128)S(1)}, u32[]{:S(2)}, u32[]{:S(2)}) collective-permute-start(f32[16]{0:T(128)S(1)} %multiply_reduce_fusion), channel_id=1, source_target_pairs={{0,8},{8,0},{16,24},{24,16},{32,40},{40,32},{48,56},{56,48},{64,72... | collective-permute-start | bytes 200 | tf_op jit(solution)/shard_map/ppermute | solution.py:129
  146.2 14.2 %collective-permute-start.13 = (f32[16]{0:T(128)S(1)}, f32[16]{0:T(128)S(1)}, u32[]{:S(2)}, u32[]{:S(2)}) collective-permute-start(f32[16]{0:T(128)S(1)} %multiply_reduce_fusion), channel_id=1, source_target_pairs={{0,16},{8,24},{16,0},{24,8},{32,48},{40,56},{48,32},{56,40},{64,80... | collective-permute-start | bytes 200 | tf_op jit(solution)/shard_map/ppermute | solution.py:129
  149.6 10.9 %collective-permute-start.14 = (f32[16]{0:T(128)S(1)}, f32[16]{0:T(128)S(1)}, u32[]{:S(2)}, u32[]{:S(2)}) collective-permute-start(f32[16]{0:T(128)S(1)} %multiply_reduce_fusion), channel_id=1, source_target_pairs={{0,24},{8,16},{16,8},{24,0},{32,56},{40,48},{48,40},{56,32},{64,88... | collective-permute-start | bytes 200 | tf_op jit(solution)/shard_map/ppermute | solution.py:129
  157.7 19.6 %copy-start.6 = (bf16[384,16,128]{0,2,1:T(8,128)(2,1)S(1)}, bf16[384,16,128]{0,2,1:T(8,128)(2,1)}, u32[]{:S(2)}) copy-start(bf16[384,16,128]{0,2,1:T(8,128)(2,1)} %get-tuple-element.48) | copy-start | bytes 4718596
  160.4 29.5 %copy-start.15 = (bf16[384,16,128]{0,2,1:T(8,128)(2,1)S(1)}, bf16[384,16,128]{0,2,1:T(8,128)(2,1)}, u32[]{:S(2)}) copy-start(bf16[384,16,128]{0,2,1:T(8,128)(2,1)} %fusion.12) | copy-start | bytes 4718596
  160.5 12.8 %collective-permute-start.15 = (f32[16]{0:T(128)S(1)}, f32[16]{0:T(128)S(1)}, u32[]{:S(2)}, u32[]{:S(2)}) collective-permute-start(f32[16]{0:T(128)S(1)} %fusion.65), channel_id=1, source_target_pairs={{0,32},{8,40},{16,48},{24,56},{32,0},{40,8},{48,16},{56,24},{64,96... | collective-permute-start | bytes 200 | tf_op jit(solution)/shard_map/ppermute | solution.py:129
  163.1 10.3 %collective-permute-start.16 = (f32[16]{0:T(128)S(1)}, f32[16]{0:T(128)S(1)}, u32[]{:S(2)}, u32[]{:S(2)}) collective-permute-start(f32[16]{0:T(128)S(1)} %fusion.65), channel_id=1, source_target_pairs={{0,64},{8,72},{16,80},{24,88},{32,96},{40,104},{48,112},{56,120},{... | collective-permute-start | bytes 200 | tf_op jit(solution)/shard_map/ppermute | solution.py:129
  171.9 5.3 %collective-permute-start.17 = (f32[16]{0:T(128)S(1)}, f32[16]{0:T(128)S(1)}, u32[]{:S(2)}, u32[]{:S(2)}) collective-permute-start(f32[16]{0:T(128)S(1)} %fusion.65), channel_id=1, source_target_pairs={{0,96},{8,104},{16,112},{24,120},{32,64},{40,72},{48,80},{56,88},{... | collective-permute-start | bytes 200 | tf_op jit(solution)/shard_map/ppermute | solution.py:129
  177.2 7.5 %collective-permute-start.18 = (f32[16]{0:T(128)S(1)}, f32[16]{0:T(128)S(1)}, u32[]{:S(2)}, u32[]{:S(2)}) collective-permute-start(f32[16]{0:T(128)S(1)} %fusion.62), channel_id=1, source_target_pairs={{0,128},{8,136},{16,144},{24,152},{32,160},{40,168},{48,176},{56,1... | collective-permute-start | bytes 200 | tf_op jit(solution)/shard_map/ppermute | solution.py:129
  184.7 1.9 collective-permute-start.19
  184.8 3.6 %collective-permute-start.20 = (f32[16]{0:T(128)S(1)}, f32[16]{0:T(128)S(1)}, u32[]{:S(2)}, u32[]{:S(2)}) collective-permute-start(f32[16]{0:T(128)S(1)} %fusion.59), channel_id=1, source_target_pairs={{0,2},{1,3},{2,0},{3,1},{4,6},{5,7},{6,4},{7,5},{8,10},{9,11},{10,... | collective-permute-start | bytes 200 | tf_op jit(solution)/shard_map/ppermute | solution.py:129
  185.7 3.0 %collective-permute-start.21 = (f32[16]{0:T(128)S(1)}, f32[16]{0:T(128)S(1)}, u32[]{:S(2)}, u32[]{:S(2)}) collective-permute-start(f32[16]{0:T(128)S(1)} %fusion.59), channel_id=1, source_target_pairs={{0,3},{1,2},{2,1},{3,0},{4,7},{5,6},{6,5},{7,4},{8,11},{9,10},{10,... | collective-permute-start | bytes 200 | tf_op jit(solution)/shard_map/ppermute | solution.py:129
  188.7 5.1 %collective-permute-start.22 = (f32[16]{0:T(128)S(1)}, f32[16]{0:T(128)S(1)}, u32[]{:S(2)}, u32[]{:S(2)}) collective-permute-start(f32[16]{0:T(128)S(1)} %fusion.58), channel_id=1, source_target_pairs={{0,4},{1,5},{2,6},{3,7},{4,0},{5,1},{6,2},{7,3},{8,12},{9,13},{10,... | collective-permute-start | bytes 200 | tf_op jit(solution)/shard_map/ppermute | solution.py:129
